TPU v7x, 32 devices: a whole 2x2x4 slice. The times are simulated.
32 devices in a mesh: grp: 2 (over y), lat: 4 (over z), lon: 4 (over x, core).
Axes of the slice: x: 2, y: 2, z: 4, core: 2. Of those that a mesh axis runs over, the one named last changes fastest.
Arguments:
- inputs: bfloat16 [2, 16, 256, 256], P('grp', 'lat', 'lon'), parts along dimension 0, may hold values from -6 to 6
- cotangent: bfloat16 [2, 16, 256, 256], P('grp', 'lat', 'lon'), parts along dimension 0, may hold values from -6 to 6
- weight: bfloat16 [9, 256, 256], replicated, may hold values from -0.125 to 0.125
- src_rows: int32 [16, 12], replicated, may hold values from 0 to 15, as said below
- lon_start: int32 [16, 12], replicated, may hold values from -16 to 16, as said below
- lon_span: int32 [16, 12], replicated, may hold values from 1 to 256, as said below
- basis_idx: int32 [16, 12], replicated, may hold values from 0 to 8, as said below
- quad_weight: float32 [16, 12], replicated, may hold values from -4 to 4
Outputs:
- response: float32 [2, 16, 256, 256], P('grp', 'lat', 'lon'), parts along dimension 0
- grad_input: float32 [2, 16, 256, 256], P('grp', 'lat', 'lon'), parts along dimension 0
- grad_weight: float32 [18, 256, 256], P('grp', 'lat', 'lon'), parts along dimension 0
There are 2 independent parts, one for each index of `grp`. A program takes and returns all parts, laid end to end along the dimension named above; an argument that names none is the same for every part. Nothing has to cross between parts.
Inputs may be any that keep to these rules, and one draw needn't show every extreme that they name: `src_rows`: each entry's input row lies within 2 rows of its output row; every row has entries reaching exactly 2 rows up and down, clipped at the grid's edges. `lon_start`: for an entry with span 256 the start is 0; otherwise the range lies within 16 longitudes of the output longitude on either side. `lon_span`: either 256 (a full circle, only in the first and last 2 rows) or at most 33. `basis_idx`: every basis function appears in every row.
All inputs are finite; a program needn't handle non-finite values.
Results may differ from a plain program's by a relative error of at most 0.01.
Values may be sent and summed in bfloat16 or wider, within the bound.
No kernel may reach another device: no remote copies, remote signals or barrier semaphores. Data moves between devices by JAX's collectives and lax.ppermute only.
A program may use at most 64 MiB of HBM per device.

v0:
```python
import functools

import jax
import jax.numpy as jnp
from jax import lax
from jax.experimental import pallas as pl
from jax.experimental.pallas import tpu as pltpu
from jax.sharding import PartitionSpec as P

BASIS = 9
REACH = 2
RIM = 16


def with_halo(block, sides, width, periodic):
    for axis, dim in sides:
        count = lax.axis_size(axis)
        forward = [(i, i + 1) for i in range(count - 1)]
        if periodic:
            forward.append((count - 1, 0))
        backward = [(target, source) for source, target in forward]
        low = lax.ppermute(
            lax.slice_in_dim(block, block.shape[dim] - width, None, axis=dim), axis, forward
        )
        high = lax.ppermute(lax.slice_in_dim(block, 0, width, axis=dim), axis, backward)
        block = jnp.concatenate([low, block, high], axis=dim)
    return block


def extend(grid_field, padded):
    grid_field = with_halo(grid_field, (("lat", 1),), REACH, False)
    grid_field = with_halo(grid_field, (("lon", 2),), RIM, True)
    extra = padded - grid_field.shape[2]
    return jnp.pad(grid_field, ((0, 0), (0, 0), (0, extra), (0, 0)))


def cycle_totals(widened, lon_count):
    interior = lax.slice_in_dim(widened, RIM, RIM + lon_count, axis=2)
    return lax.psum(jnp.sum(interior, axis=2, dtype=jnp.float32), "lon")


def filter_kernel(
    rows_ref, start_ref, span_ref, basis_ref, scale_ref, field_ref, total_ref, out_ref, acc_ref,
    *, slots, window_rows, lon_count, lon_total, backward,
):
    r = pl.program_id(1)
    padded = field_ref.shape[2]
    channels = field_ref.shape[3]
    acc_ref[...] = jnp.zeros(acc_ref.shape, jnp.float32)
    out_col = lax.broadcasted_iota(jnp.int32, (lon_count, padded), 0)
    in_col = lax.broadcasted_iota(jnp.int32, (lon_count, padded), 1) - RIM
    offset = out_col - in_col if backward else in_col - out_col

    def add_slot(row, table_row, slot, scale):
        start = start_ref[table_row, slot]
        span = span_ref[table_row, slot]
        basis = basis_ref[table_row, slot]
        narrow = span < lon_total
        band = ((offset >= start) & (offset < start + span) & narrow).astype(jnp.bfloat16)
        boxed = jnp.dot(band, field_ref[0, row], preferred_element_type=jnp.float32)
        full = jnp.where(narrow, 0.0, 1.0).astype(jnp.float32)
        boxed = boxed + full * total_ref[0, row]
        acc_ref[basis] = acc_ref[basis] + scale * boxed

    if backward:
        for e in range(window_rows):
            row = r + e
            for slot in range(slots):
                scale = scale_ref[r, row * slots + slot]

                @pl.when(scale != 0.0)
                def _():
                    add_slot(row, row, slot, scale)
    else:
        for slot in range(slots):
            add_slot(rows_ref[r, slot], r, slot, scale_ref[r, slot])

    for k in range(BASIS):
        out_ref[0, 0, :, k * channels:(k + 1) * channels] = acc_ref[k].astype(jnp.bfloat16)


def run_filter(tables, field, totals, lon_count, lon_total, backward):
    members, window, padded, channels = field.shape
    row_count = window - 2 * REACH
    slots = tables[1].shape[1]
    smem = pl.BlockSpec(memory_space=pltpu.SMEM)
    kernel = functools.partial(
        filter_kernel,
        slots=slots,
        window_rows=2 * REACH + 1,
        lon_count=lon_count,
        lon_total=lon_total,
        backward=backward,
    )
    return pl.pallas_call(
        kernel,
        grid=(members, row_count),
        in_specs=[smem] * 5
        + [
            pl.BlockSpec((1, window, padded, channels), lambda b, r: (b, 0, 0, 0)),
            pl.BlockSpec((1, window, 1, channels), lambda b, r: (b, 0, 0, 0)),
        ],
        out_specs=pl.BlockSpec(
            (1, 1, lon_count, BASIS * channels), lambda b, r: (b, r, 0, 0)
        ),
        out_shape=jax.ShapeDtypeStruct(
            (members, row_count, lon_count, BASIS * channels), jnp.bfloat16
        ),
        scratch_shapes=[pltpu.VMEM((BASIS, lon_count, channels), jnp.float32)],
    )(*tables, field, totals[:, :, None, :])


def on_device(inputs, cotangent, weight, src_rows, lon_start, lon_span, basis_idx, quad_weight):
    members, row_count, lon_count, channels = inputs.shape
    lon_total = lon_count * lax.axis_size("lon")
    height = row_count * lax.axis_size("lat")
    first_row = lax.axis_index("lat") * row_count
    window = row_count + 2 * REACH
    padded = -(-(lon_count + 2 * RIM) // 128) * 128
    weighting = quad_weight / jnp.sqrt(lon_span.astype(jnp.float32))

    widened = extend(inputs, padded)
    grad_wide = extend(cotangent, padded)
    totals = cycle_totals(widened, lon_count)
    grad_totals = cycle_totals(grad_wide, lon_count)

    def rows_of(table, begin, count):
        return lax.dynamic_slice_in_dim(table, begin, count, 0)

    f_tables = (
        rows_of(src_rows, first_row, row_count) - first_row + REACH,
        rows_of(lon_start, first_row, row_count),
        rows_of(lon_span, first_row, row_count),
        rows_of(basis_idx, first_row, row_count),
        rows_of(weighting, first_row, row_count),
    )
    flattened = run_filter(f_tables, widened, totals, lon_count, lon_total, False)
    w_fwd = weight.reshape(BASIS * channels, channels)
    response = jnp.einsum("brwq,qo->brwo", flattened, w_fwd, preferred_element_type=jnp.float32)

    pad_pair = ((REACH, REACH), (0, 0))
    b_src = rows_of(jnp.pad(src_rows, pad_pair, constant_values=-1), first_row, window)
    b_start = rows_of(jnp.pad(lon_start, pad_pair, constant_values=0), first_row, window)
    b_span = rows_of(jnp.pad(lon_span, pad_pair, constant_values=1), first_row, window)
    b_basis = rows_of(jnp.pad(basis_idx, pad_pair, constant_values=0), first_row, window)
    b_scale = rows_of(jnp.pad(weighting, pad_pair, constant_values=0.0), first_row, window)
    targets = first_row + jnp.arange(row_count, dtype=jnp.int32)
    b_hit = b_src[None, :, :] == targets[:, None, None]
    b_weights = jnp.where(b_hit, b_scale[None], 0.0).reshape(row_count, -1)
    b_tables = (b_src, b_start, b_span, b_basis, b_weights)
    back_filtered = run_filter(b_tables, grad_wide, grad_totals, lon_count, lon_total, True)
    w_back = jnp.transpose(weight, (0, 2, 1)).reshape(BASIS * channels, channels)
    grad_input = jnp.einsum(
        "bpwq,qc->bpwc", back_filtered, w_back, preferred_element_type=jnp.float32
    )
    partial_value = jnp.einsum(
        "brwq,brwo->qo", flattened, cotangent, preferred_element_type=jnp.float32
    )
    partial_value = partial_value.reshape(BASIS, channels, channels)
    reduced = lax.psum_scatter(partial_value, "lon", scatter_dimension=2, tiled=True)
    reduced = lax.psum_scatter(reduced, "lat", scatter_dimension=1, tiled=True)
    grad_weight = reduced / jnp.sqrt(jnp.float32(members * height * lon_total))
    return (response, grad_input, grad_weight)


def solution(mesh):
    placed = (
        P("grp", "lat", "lon", None),
        P("grp", "lat", "lon", None),
        P(),
        P(),
        P(),
        P(),
        P(),
        P(),
    )
    return jax.shard_map(
        on_device,
        mesh=mesh,
        in_specs=placed,
        out_specs=(
            P("grp", "lat", "lon", None),
            P("grp", "lat", "lon", None),
            P("grp", "lat", "lon"),
        ),
        check_vma=False,
    )
```

profile of v0, /device:TPU:0, one launch (start us, length us, event | category | flops | bytes accessed | tf_op | source)
XLA Modules:
  0.0 116.2 jit_solution(16470008672213937086)
XLA Ops:
  7.2 0.0 copy-start.4
  7.2 0.0 reduce-scatter.5.cloned.1.call-start
  7.2 0.9 fusion.28
  8.1 1.3 %collective-permute-start.1 = (bf16[1,2,64,256]{3,2,1,0:T(8,128)(2,1)S(1)}, bf16[1,2,64,256]{3,2,1,0:T(8,128)(2,1)S(1)}, u32[]{:S(2)}, u32[]{:S(2)}) collective-permute-start(bf16[1,2,64,256]{3,2,1,0:T(8,128)(2,1)S(1)} %get-tuple-element.20), channel_id=1, source_target_pairs={{4,0},{8,4},{12,8},{5,1},{9,5},{13,9},{6,2},{10,6},{14,10},{7,3},{... | collective-permute-start | bytes 196616 | tf_op jit(solution)/shard_map/ppermute | solution.py:25
  9.4 5.6 %collective-permute-start = (bf16[1,2,64,256]{3,2,1,0:T(8,128)(2,1)S(1)}, bf16[1,2,64,256]{3,2,1,0:T(8,128)(2,1)S(1)}, u32[]{:S(2)}, u32[]{:S(2)}) collective-permute-start(bf16[1,2,64,256]{3,2,1,0:T(8,128)(2,1)S(1)} %get-tuple-element.21), channel_id=1, source_target_pairs={{0,4},{4,8},{8,12},{1,5},{5,9},{9,13},{2,6},{6,10},{10,14},{3,7},{... | collective-permute-start | bytes 196616 | tf_op jit(solution)/shard_map/ppermute | solution.py:22
  15.0 0.9 fusion.27
  15.9 1.3 %collective-permute-start.5 = (bf16[1,2,64,256]{3,2,1,0:T(8,128)(2,1)S(1)}, bf16[1,2,64,256]{3,2,1,0:T(8,128)(2,1)S(1)}, u32[]{:S(2)}, u32[]{:S(2)}) collective-permute-start(bf16[1,2,64,256]{3,2,1,0:T(8,128)(2,1)S(1)} %get-tuple-element.18), channel_id=1, source_target_pairs={{4,0},{8,4},{12,8},{5,1},{9,5},{13,9},{6,2},{10,6},{14,10},{7,3},{... | collective-permute-start | bytes 196616 | tf_op jit(solution)/shard_map/ppermute | solution.py:25
  17.2 4.6 %collective-permute-start.4 = (bf16[1,2,64,256]{3,2,1,0:T(8,128)(2,1)S(1)}, bf16[1,2,64,256]{3,2,1,0:T(8,128)(2,1)S(1)}, u32[]{:S(2)}, u32[]{:S(2)}) collective-permute-start(bf16[1,2,64,256]{3,2,1,0:T(8,128)(2,1)S(1)} %get-tuple-element.19), channel_id=1, source_target_pairs={{0,4},{4,8},{8,12},{1,5},{5,9},{9,13},{2,6},{6,10},{10,14},{3,7},{... | collective-permute-start | bytes 196616 | tf_op jit(solution)/shard_map/ppermute | solution.py:22
  21.8 0.7 rsqrt_multiply_fusion
  22.5 1.3 %constant_dynamic-slice_fusion.1 = (s32[4,12]{1,0:T(4,128)}, s32[4,12]{1,0:T(4,128)}) fusion(s32[16,12]{1,0:T(8,128)} %param.14, s32[]{:T(128)S(6)} %select_n.8, s32[16,12]{1,0:T(8,128)} %param.13), kind=kLoop, calls=%fused_computation.37 | loop fusion | bytes 772 | tf_op jit(solution)/shard_map/dynamic_slice | solution.py:128
  23.8 1.3 %constant_dynamic-slice_fusion.3 = (s32[4,12]{1,0:T(4,128)}, s32[4,12]{1,0:T(4,128)}) fusion(s32[16,12]{1,0:T(8,128)} %param.12, s32[]{:T(128)S(6)} %select_n.8, s32[]{:T(128)S(6)} %mul.3, s32[16,12]{1,0:T(8,128)} %param.11), kind=kLoop, calls=%fused_computation.39 | loop fusion | flops 96 | bytes 776 | tf_op jit(solution)/shard_map/dynamic_slice | solution.py:128
  25.1 0.6 constant_dynamic-slice_fusion.scale_ref
  25.7 0.0 collective-permute-done
  25.7 0.9 constant_dynamic-update-slice_fusion.1
  26.6 0.0 collective-permute-done.1
  26.6 0.1 collective-permute-start.2
  26.7 1.7 %collective-permute-start.3 = (bf16[1,8,16,256]{3,2,1,0:T(8,128)(2,1)S(1)}, bf16[1,8,16,256]{3,2,1,0:T(8,128)(2,1)S(1)}, u32[]{:S(2)}, u32[]{:S(2)}) collective-permute-start(bf16[1,8,16,256]{3,2,1,0:T(8,128)(2,1)S(1)} %get-tuple-element.17), channel_id=1, source_target_pairs={{1,0},{2,1},{3,2},{0,3},{5,4},{6,5},{7,6},{4,7},{9,8},{10,9},{11,1... | collective-permute-start | bytes 196616 | tf_op jit(solution)/shard_map/ppermute | solution.py:25
  28.4 0.1 convert_reduce_fusion.1
  28.5 0.0 collective-permute-done.4
  28.5 0.0 copy-done.4
  28.5 0.0 collective-permute-done.5
  28.6 0.1 convert_reduce_fusion
  28.7 10.9 %all-reduce.7 = (f32[1,8,1,256]{3,2,1,0:T(1,128)}, f32[1,8,1,256]{3,2,1,0:T(1,128)}) all-reduce(f32[1,8,1,256]{3,2,1,0:T(1,128)S(1)} %broadcast_in_dim.23, f32[1,8,1,256]{3,2,1,0:T(1,128)S(1)} %broadcast_in_dim.27), channel_id=1, replica_groups=mesh['grp'=2,'lat'=4,'lon'=4] {'lon'}, use_global_device_ids=true, to_apply=%region_1.2 | all-reduce | flops 4096 | bytes 32768 | tf_op jit(solution)/shard_map/psum | solution.py:39
  39.6 0.0 collective-permute-done.2
  39.6 0.0 collective-permute-done.3
  39.6 0.8 fusion.19.field_ref
  40.5 3.5 %shard_map.103 = bf16[1,4,64,2304]{3,2,1,0:T(8,128)(2,1)} custom-call(s32[4,12]{1,0:T(4,128)} %get-tuple-element.25.rows_ref, s32[4,12]{1,0:T(4,128)} %get-tuple-element.24.start_ref, s32[4,12]{1,0:T(4,128)} %get-tuple-element.23.span_ref, s32[4,12]{1,0:T(4,128)} %get-tuple-element.22.basis_ref, f32[4,12]{1,0:T(4,128)} %constant_dynamic-slice_fusion.scale_ref, ...), custom_call_target="tpu_custom_call" | custom-call | tf_op jit(solution)/shard_map/pallas_call | solution.py:95
  44.0 3.2 %convolution_bitcast_fusion = f32[9,256,256]{1,2,0:T(8,128)} fusion(bf16[4,8,9,8,256]{4,3,2,1,0:T(8,128)(2,1)} %bitcast.40, bf16[1,4,64,256]{3,2,1,0:T(8,128)(2,1)S(1)} %copy-done.4), kind=kOutput, calls=%fused_computation | convolution fusion | flops 301989888 | bytes 3670016 | tf_op jit(solution)/shard_map/brwq,brwo->qo/dot_general | solution.py:156
  47.2 0.0 copy-start.8
  47.2 0.0 reduce-scatter.5.cloned.1.call-update
  47.2 0.0 reduce-scatter.7.cloned.1.call-start
  47.3 0.6 copy-done.8
  47.9 0.0 copy-done.9
  47.9 0.6 pad_dynamic-slice_fusion.3
  48.5 32.5 %reduce-scatter.5.cloned.1.call-done = f32[9,256,64]{1,2,0:T(8,128)} async-done(((f32[9,256,256]{1,2,0:T(8,128)}), f32[9,256,64]{1,2,0:T(8,128)}) %reduce-scatter.5.cloned.1.call-update) | async-done | bytes 589840 | tf_op jit(solution)/shard_map/reduce_scatter | solution.py:160
  81.0 2.4 %copy.20 = f32[9,256,64]{2,0,1:T(8,128)S(1)} copy(f32[9,256,64]{1,2,0:T(8,128)} %reduce-scatter.5.cloned.1.call-done) | data formatting | bytes 1179648
  83.4 0.0 copy-start.1
  83.4 1.3 %reshape.110 = f32[256,576]{1,0:T(8,128)} reshape(f32[256,9,64]{2,1,0:T(8,128)S(1)} %bitcast.41) | data formatting | bytes 1179648
  84.7 0.0 reduce-scatter.7.cloned.1.call-update
  84.7 0.1 broadcast_in_dim.24
  84.8 0.0 copy-done.6
  84.8 0.1 eq.16
  84.9 0.0 copy-done.1
  84.9 0.0 copy-start.7
  84.9 1.5 %copy.16 = bf16[9,256,256]{1,2,0:T(8,128)(2,1)} copy(bf16[9,256,256]{2,1,0:T(8,128)(2,1)S(1)} %copy-done.1) | data formatting | bytes 2359296 | tf_op args[2]
  86.4 0.6 compare_select_fusion.scale_ref
  87.1 0.1 collective-permute-start.6
  87.1 1.7 %collective-permute-start.7 = (bf16[1,8,16,256]{3,2,1,0:T(8,128)(2,1)S(1)}, bf16[1,8,16,256]{3,2,1,0:T(8,128)(2,1)S(1)}, u32[]{:S(2)}, u32[]{:S(2)}) collective-permute-start(bf16[1,8,16,256]{3,2,1,0:T(8,128)(2,1)S(1)} %get-tuple-element.15), channel_id=1, source_target_pairs={{1,0},{2,1},{3,2},{0,3},{5,4},{6,5},{7,6},{4,7},{9,8},{10,9},{11,1... | collective-permute-start | bytes 196616 | tf_op jit(solution)/shard_map/ppermute | solution.py:25
  88.9 0.0 copy-done.5
  88.9 0.0 copy-done.7
  88.9 0.6 pad_dynamic-slice_fusion.1
  89.5 1.5 %collective-permute-done.6 = bf16[1,8,16,256]{3,2,1,0:T(8,128)(2,1)S(1)} collective-permute-done((bf16[1,8,16,256]{3,2,1,0:T(8,128)(2,1)S(1)}, bf16[1,8,16,256]{3,2,1,0:T(8,128)(2,1)S(1)}, u32[]{:S(2)}, u32[]{:S(2)}) %collective-permute-start.6) | collective-permute-done | bytes 65568 | tf_op jit(solution)/shard_map/ppermute | solution.py:22
  91.0 0.0 collective-permute-done.7
  91.0 0.8 fusion.21.field_ref
  91.8 10.3 %shard_map.104 = bf16[1,4,64,2304]{3,2,1,0:T(8,128)(2,1)} custom-call(s32[8,12]{1,0:T(8,128)} %copy-done.6, s32[8,12]{1,0:T(8,128)} %get-tuple-element.28.start_ref, s32[8,12]{1,0:T(8,128)} %get-tuple-element.27.span_ref, s32[8,12]{1,0:T(8,128)} %get-tuple-element.26.basis_ref, f32[4,96]{1,0:T(4,128)} %compare_select_fusion.scale_ref, ...), custom_call_target="tpu_custom_call" | custom-call | tf_op jit(solution)/shard_map/pallas_call | solution.py:95
  102.1 0.0 copy-done
  102.1 1.2 %fusion.6 = f32[1,4,64,256]{3,2,1,0:T(8,128)} fusion(bf16[2304,256,1]{1,0,2:T(8,128)(2,1)S(1)} %bitcast.42, bf16[1,4,64,2304]{3,2,1,0:T(8,128)(2,1)S(1)} %copy-done), kind=kOutput, calls=%fused_computation.7 | convolution fusion | flops 301989888 | bytes 2621440 | tf_op jit(solution)/shard_map/brwq,qo->brwo/dot_general | solution.py:139
  103.3 0.1 copy-done.2
  103.4 0.4 copy-done.3
  103.8 1.2 %fusion.9 = f32[1,4,64,256]{3,2,1,0:T(8,128)} fusion(bf16[2304,256,1]{1,0,2:T(8,128)(2,1)S(1)} %bitcast.43, bf16[1,4,64,2304]{3,2,1,0:T(8,128)(2,1)S(1)} %copy-done.3), kind=kOutput, calls=%fused_computation.8 | convolution fusion | flops 301989888 | bytes 2621440 | tf_op jit(solution)/shard_map/bpwq,qc->bpwc/dot_general | solution.py:153
  105.0 2.2 %reduce-scatter.7.cloned.1.call-done = f32[64,576]{1,0:T(8,128)} async-done(((f32[256,576]{1,0:T(8,128)}), f32[64,576]{1,0:T(8,128)}) %reduce-scatter.7.cloned.1.call-update) | async-done | bytes 147472
  107.2 1.0 reshape.111
  108.3 0.2 copy.21
  108.5 0.9 copy.18
  (18 shorter events, 0.1 us)
Async XLA Ops:
  7.2 21.3 %copy-start.4 = (bf16[1,4,64,256]{3,2,1,0:T(8,128)(2,1)S(1)}, bf16[1,4,64,256]{3,2,1,0:T(8,128)(2,1)}, u32[]{:S(2)}) copy-start(bf16[1,4,64,256]{3,2,1,0:T(8,128)(2,1)} %param.9) | copy-start | bytes 393220
  7.2 73.8 %reduce-scatter.5.cloned.1.call-start = ((), (), s32[]{:S(2)}) async-start(), calls=%async_computation.2 | async-start | bytes 2949120 | tf_op jit(solution)/shard_map/reduce_scatter | solution.py:160
  8.1 18.5 %collective-permute-start.1 = (bf16[1,2,64,256]{3,2,1,0:T(8,128)(2,1)S(1)}, bf16[1,2,64,256]{3,2,1,0:T(8,128)(2,1)S(1)}, u32[]{:S(2)}, u32[]{:S(2)}) collective-permute-start(bf16[1,2,64,256]{3,2,1,0:T(8,128)(2,1)S(1)} %get-tuple-element.20), channel_id=1, source_target_pairs={{4,0},{8,4},{12,8},{5,1},{9,5},{13,9},{6,2},{10,6},{14,10},{7,3},{... | collective-permute-start | bytes 196616 | tf_op jit(solution)/shard_map/ppermute | solution.py:25
  9.4 16.2 %collective-permute-start = (bf16[1,2,64,256]{3,2,1,0:T(8,128)(2,1)S(1)}, bf16[1,2,64,256]{3,2,1,0:T(8,128)(2,1)S(1)}, u32[]{:S(2)}, u32[]{:S(2)}) collective-permute-start(bf16[1,2,64,256]{3,2,1,0:T(8,128)(2,1)S(1)} %get-tuple-element.21), channel_id=1, source_target_pairs={{0,4},{4,8},{8,12},{1,5},{5,9},{9,13},{2,6},{6,10},{10,14},{3,7},{... | collective-permute-start | bytes 196616 | tf_op jit(solution)/shard_map/ppermute | solution.py:22
  15.9 12.7 %collective-permute-start.5 = (bf16[1,2,64,256]{3,2,1,0:T(8,128)(2,1)S(1)}, bf16[1,2,64,256]{3,2,1,0:T(8,128)(2,1)S(1)}, u32[]{:S(2)}, u32[]{:S(2)}) collective-permute-start(bf16[1,2,64,256]{3,2,1,0:T(8,128)(2,1)S(1)} %get-tuple-element.18), channel_id=1, source_target_pairs={{4,0},{8,4},{12,8},{5,1},{9,5},{13,9},{6,2},{10,6},{14,10},{7,3},{... | collective-permute-start | bytes 196616 | tf_op jit(solution)/shard_map/ppermute | solution.py:25
  17.2 11.3 %collective-permute-start.4 = (bf16[1,2,64,256]{3,2,1,0:T(8,128)(2,1)S(1)}, bf16[1,2,64,256]{3,2,1,0:T(8,128)(2,1)S(1)}, u32[]{:S(2)}, u32[]{:S(2)}) collective-permute-start(bf16[1,2,64,256]{3,2,1,0:T(8,128)(2,1)S(1)} %get-tuple-element.19), channel_id=1, source_target_pairs={{0,4},{4,8},{8,12},{1,5},{5,9},{9,13},{2,6},{6,10},{10,14},{3,7},{... | collective-permute-start | bytes 196616 | tf_op jit(solution)/shard_map/ppermute | solution.py:22
  26.6 13.0 %collective-permute-start.2 = (bf16[1,8,16,256]{3,2,1,0:T(8,128)(2,1)S(1)}, bf16[1,8,16,256]{3,2,1,0:T(8,128)(2,1)S(1)}, u32[]{:S(2)}, u32[]{:S(2)}) collective-permute-start(bf16[1,8,16,256]{3,2,1,0:T(8,128)(2,1)S(1)} %get-tuple-element.16), channel_id=1, source_target_pairs={{0,1},{1,2},{2,3},{3,0},{4,5},{5,6},{6,7},{7,4},{8,9},{9,10},{10,1... | collective-permute-start | bytes 196616 | tf_op jit(solution)/shard_map/ppermute | solution.py:22
  26.7 12.9 %collective-permute-start.3 = (bf16[1,8,16,256]{3,2,1,0:T(8,128)(2,1)S(1)}, bf16[1,8,16,256]{3,2,1,0:T(8,128)(2,1)S(1)}, u32[]{:S(2)}, u32[]{:S(2)}) collective-permute-start(bf16[1,8,16,256]{3,2,1,0:T(8,128)(2,1)S(1)} %get-tuple-element.17), channel_id=1, source_target_pairs={{1,0},{2,1},{3,2},{0,3},{5,4},{6,5},{7,6},{4,7},{9,8},{10,9},{11,1... | collective-permute-start | bytes 196616 | tf_op jit(solution)/shard_map/ppermute | solution.py:25
  47.2 0.7 copy-start.8
  47.2 0.7 copy-start.9
  47.2 60.0 %reduce-scatter.7.cloned.1.call-start = ((), (), s32[]{:S(2)}) async-start(), calls=%async_computation.3 | async-start | bytes 819200
  48.5 36.3 %copy-start.6 = (s32[8,12]{1,0:T(8,128)}, s32[8,12]{1,0:T(8,128)S(1)}, u32[]{:S(2)}) copy-start(s32[8,12]{1,0:T(8,128)S(1)} %get-tuple-element.29.rows_ref) | copy-start | bytes 1156
  83.4 1.5 %copy-start.1 = (bf16[9,256,256]{2,1,0:T(8,128)(2,1)S(1)}, bf16[9,256,256]{2,1,0:T(8,128)(2,1)}, u32[]{:S(2)}) copy-start(bf16[9,256,256]{2,1,0:T(8,128)(2,1)} %param.10) | copy-start | bytes 3538948
  84.9 4.0 %copy-start.5 = (s32[16,12]{1,0:T(8,128)S(1)}, s32[16,12]{1,0:T(8,128)}, u32[]{:S(2)}) copy-start(s32[16,12]{1,0:T(8,128)} %param.13) | copy-start | bytes 2308
  84.9 4.0 %copy-start.7 = (s32[16,12]{1,0:T(8,128)S(1)}, s32[16,12]{1,0:T(8,128)}, u32[]{:S(2)}) copy-start(s32[16,12]{1,0:T(8,128)} %param.14) | copy-start | bytes 2308
  87.1 3.9 %collective-permute-start.6 = (bf16[1,8,16,256]{3,2,1,0:T(8,128)(2,1)S(1)}, bf16[1,8,16,256]{3,2,1,0:T(8,128)(2,1)S(1)}, u32[]{:S(2)}, u32[]{:S(2)}) collective-permute-start(bf16[1,8,16,256]{3,2,1,0:T(8,128)(2,1)S(1)} %get-tuple-element.14), channel_id=1, source_target_pairs={{0,1},{1,2},{2,3},{3,0},{4,5},{5,6},{6,7},{7,4},{8,9},{9,10},{10,1... | collective-permute-start | bytes 196616 | tf_op jit(solution)/shard_map/ppermute | solution.py:22
  87.1 3.8 %collective-permute-start.7 = (bf16[1,8,16,256]{3,2,1,0:T(8,128)(2,1)S(1)}, bf16[1,8,16,256]{3,2,1,0:T(8,128)(2,1)S(1)}, u32[]{:S(2)}, u32[]{:S(2)}) collective-permute-start(bf16[1,8,16,256]{3,2,1,0:T(8,128)(2,1)S(1)} %get-tuple-element.15), channel_id=1, source_target_pairs={{1,0},{2,1},{3,2},{0,3},{5,4},{6,5},{7,6},{4,7},{9,8},{10,9},{11,1... | collective-permute-start | bytes 196616 | tf_op jit(solution)/shard_map/ppermute | solution.py:25
  89.5 12.6 %copy-start = (bf16[1,4,64,2304]{3,2,1,0:T(8,128)(2,1)S(1)}, bf16[1,4,64,2304]{3,2,1,0:T(8,128)(2,1)}, u32[]{:S(2)}) copy-start(bf16[1,4,64,2304]{3,2,1,0:T(8,128)(2,1)} %shard_map.103) | copy-start | bytes 3538948
  102.1 1.3 %copy-start.2 = (bf16[9,256,256]{1,2,0:T(8,128)(2,1)S(1)}, bf16[9,256,256]{1,2,0:T(8,128)(2,1)}, u32[]{:S(2)}) copy-start(bf16[9,256,256]{1,2,0:T(8,128)(2,1)} %copy.16) | copy-start | bytes 3538948
  102.1 1.7 %copy-start.3 = (bf16[1,4,64,2304]{3,2,1,0:T(8,128)(2,1)S(1)}, bf16[1,4,64,2304]{3,2,1,0:T(8,128)(2,1)}, u32[]{:S(2)}) copy-start(bf16[1,4,64,2304]{3,2,1,0:T(8,128)(2,1)} %shard_map.104) | copy-start | bytes 3538948
Sparse Core Ops, SparseCore 0:
  47.3 33.6 reduce-scatter.4
  84.8 22.3 reduce-scatter.6
where the time goes:
time: 117 us; the launch traced here: 116 us
  waiting for transfers between devices  36.3 us (31%)
  starting transfers between devices  16.4 us (14%)
  local copies, waits for them, and re-layouts  14.5 us (12%)
  between operations  14.3 us (12%)
  Pallas kernels  13.8 us (12%)
  blocking collectives  10.9 us (9%)
  matrix products  5.58 us (5%)
  other arithmetic  4.47 us (4%)
    reduce_scatter x1, waiting for transfers between devices, on_device(): lax.psum_scatter(partial_value, 'lon', scatter_dimension=2, tiled=True)  32.5 us
    pallas_call x2, Pallas kernels, run_filter(): pl.pallas_call(kernel, grid=(members, row_count), in_specs=[smem] * 5 + [...  13.8 us
    psum x1, blocking collectives, cycle_totals(): return lax.psum(jnp.sum(interior, axis=2, dtype=jnp.float32), 'lon')  10.9 us
    ppermute x4, starting transfers between devices, with_halo(): lax.ppermute(lax.slice_in_dim(block, block.shape[dim] - width, None, axis...  10.2 us
    unnamed x30, local copies, waits for them, and re-layouts  9.34 us
    ppermute x4, starting transfers between devices, with_halo(): lax.ppermute(lax.slice_in_dim(block, 0, width, axis=dim), axis, backward)  6.05 us
    dot_general x1, matrix products, on_device(): jnp.einsum('brwq,brwo->qo', flattened, cotangent, preferred_element_type=...  3.22 us
    dynamic_slice x5, local copies, waits for them, and re-layouts, rows_of(): return lax.dynamic_slice_in_dim(table, begin, count, 0)  3.11 us
  transfers between devices with their start and end apart: 10, of which 3 were waited for; matrix products, arithmetic and copies ran while one was open for 11% of the time, Pallas kernels for 9%

commit v1 on v0

--- a/solution.py
+++ b/solution.py
@@ -32,11 +32,6 @@
     grid_field = with_halo(grid_field, (("lon", 2),), RIM, True)
     extra = padded - grid_field.shape[2]
     return jnp.pad(grid_field, ((0, 0), (0, 0), (0, extra), (0, 0)))
-
-
-def cycle_totals(widened, lon_count):
-    interior = lax.slice_in_dim(widened, RIM, RIM + lon_count, axis=2)
-    return lax.psum(jnp.sum(interior, axis=2, dtype=jnp.float32), "lon")
 
 
 def filter_kernel(
@@ -121,8 +116,16 @@
 
     widened = extend(inputs, padded)
     grad_wide = extend(cotangent, padded)
-    totals = cycle_totals(widened, lon_count)
-    grad_totals = cycle_totals(grad_wide, lon_count)
+    row_sums = jnp.stack(
+        [jnp.sum(inputs, axis=2, dtype=jnp.float32), jnp.sum(cotangent, axis=2, dtype=jnp.float32)]
+    )
+    gathered = lax.all_gather(row_sums, ("lat", "lon"), tiled=False)
+    lat_count = lax.axis_size("lat")
+    gathered = gathered.reshape((lat_count, lax.axis_size("lon")) + row_sums.shape)
+    whole = jnp.sum(gathered, axis=1)
+    whole = jnp.moveaxis(whole, 0, 2).reshape(2, members, height, channels)
+    whole = jnp.pad(whole, ((0, 0), (0, 0), (REACH, REACH), (0, 0)))
+    totals, grad_totals = lax.dynamic_slice_in_dim(whole, first_row, window, 2)
 
     def rows_of(table, begin, count):
         return lax.dynamic_slice_in_dim(table, begin, count, 0)
@@ -153,12 +156,20 @@
     grad_input = jnp.einsum(
         "bpwq,qc->bpwc", back_filtered, w_back, preferred_element_type=jnp.float32
     )
+    lon_parts = lax.axis_size("lon")
+    lat_parts = lax.axis_size("lat")
+    left = flattened.reshape(
+        members, row_count, lon_count, BASIS, lat_parts, channels // lat_parts
+    )
+    right = cotangent.reshape(members, row_count, lon_count, lon_parts, channels // lon_parts)
     partial_value = jnp.einsum(
-        "brwq,brwo->qo", flattened, cotangent, preferred_element_type=jnp.float32
+        "brwkic,brwjo->ijkco", left, right, preferred_element_type=jnp.float32
     )
-    partial_value = partial_value.reshape(BASIS, channels, channels)
-    reduced = lax.psum_scatter(partial_value, "lon", scatter_dimension=2, tiled=True)
-    reduced = lax.psum_scatter(reduced, "lat", scatter_dimension=1, tiled=True)
+    partial_value = partial_value.reshape(
+        (lat_parts * lon_parts, BASIS, channels // lat_parts, channels // lon_parts)
+    )
+    reduced = lax.psum_scatter(partial_value, ("lat", "lon"), scatter_dimension=0, tiled=True)
+    reduced = reduced.reshape(BASIS, channels // lat_parts, channels // lon_parts)
     grad_weight = reduced / jnp.sqrt(jnp.float32(members * height * lon_total))
     return (response, grad_input, grad_weight)
 

time: 117 us -> 139 us (1.19)
  waiting for transfers between devices: 36.3 us -> 50.6 us
  blocking collectives: 10.9 us -> 20.3 us
  matrix products: 5.58 us -> 3.16 us
  other arithmetic: 4.47 us -> 6.52 us
    all_gather x0 -> x1, blocking collectives: none -> 20.3 us  [on_device(): gathered = lax.all_gather(row_sums, ('lat', 'lon'), tiled=False)]
    reduce_scatter x1, waiting for transfers between devices: 32.5 us -> 47.3 us  [on_device(): lax.psum_scatter(partial_value, ('lat', 'lon'), scatter_dimension=0, tile...]
    psum x1 -> x0, blocking collectives: 10.9 us -> none  [cycle_totals(): return lax.psum(jnp.sum(interior, axis=2, dtype=jnp.float32), 'lon')]
    unnamed x30 -> x27, local copies, waits for them, and re-layouts: 9.34 us -> 1.76 us
    another operation x0 -> x3, local copies, waits for them, and re-layouts: none -> 5.3 us
    reshape x0 -> x1, local copies, waits for them, and re-layouts: none -> 2.85 us  [on_device(): partial_value.reshape((lat_parts * lon_parts, BASIS, channels // lat_part...]
    dot_general x1, matrix products: 3.22 us -> 0.8 us  [on_device(): jnp.einsum('brwkic,brwjo->ijkco', left, right, preferred_element_type=jnp...]
    unnamed x3 -> x1, waiting for transfers between devices: 2.26 us -> 0.02 us
  transfers between devices with their start and end apart: 10 -> 9, of which waited for: 3 -> 3; matrix products, arithmetic and copies ran while one was open for 11% -> 8% of each run, Pallas kernels for 9% -> 7%
where the time goes in v1:
time: 139 us; the launch traced here: 138 us
  waiting for transfers between devices  50.6 us (36%)
  blocking collectives  20.3 us (15%)
  starting transfers between devices  16.3 us (12%)
  between operations  14.3 us (10%)
  Pallas kernels  13.8 us (10%)
  local copies, waits for them, and re-layouts  13.5 us (10%)
  other arithmetic  6.52 us (5%)
  matrix products  3.16 us (2%)
    reduce_scatter x1, waiting for transfers between devices, on_device(): lax.psum_scatter(partial_value, ('lat', 'lon'), scatter_dimension=0, tile...  47.3 us
    all_gather x1, blocking collectives, on_device(): gathered = lax.all_gather(row_sums, ('lat', 'lon'), tiled=False)  20.3 us
    pallas_call x2, Pallas kernels, run_filter(): pl.pallas_call(kernel, grid=(members, row_count), in_specs=[smem] * 5 + [...  13.8 us
    ppermute x4, starting transfers between devices, with_halo(): lax.ppermute(lax.slice_in_dim(block, block.shape[dim] - width, None, axis...  10.6 us
    ppermute x4, starting transfers between devices, with_halo(): lax.ppermute(lax.slice_in_dim(block, 0, width, axis=dim), axis, backward)  5.72 us
    another operation x2, local copies, waits for them, and re-layouts  4.68 us
    ppermute x4, waiting for transfers between devices, with_halo(): lax.ppermute(lax.slice_in_dim(block, block.shape[dim] - width, None, axis...  3.2 us
    reshape x1, local copies, waits for them, and re-layouts, on_device(): partial_value.reshape((lat_parts * lon_parts, BASIS, channels // lat_part...  2.85 us
  transfers between devices with their start and end apart: 9, of which 3 were waited for; matrix products, arithmetic and copies ran while one was open for 8% of the time, Pallas kernels for 7%

profile of v1, /device:TPU:0, one launch (start us, length us, event | category | flops | bytes accessed | tf_op | source)
XLA Modules:
  0.0 138.4 jit_solution(15351446626290191585)
XLA Ops:
  7.2 0.0 copy-start.4
  7.2 0.0 copy-start.5
  7.2 0.0 copy-start.10
  7.2 0.0 copy-start.7
  7.2 0.0 copy-start.8
  7.2 0.0 copy-start.9
  7.2 0.0 reduce-scatter.2.cloned.1.call-start
  7.3 0.9 fusion.30
  8.2 1.3 collective-permute-start.1
  9.5 5.6 %collective-permute-start = (bf16[1,2,64,256]{3,2,1,0:T(8,128)(2,1)S(1)}, bf16[1,2,64,256]{3,2,1,0:T(8,128)(2,1)S(1)}, u32[]{:S(2)}, u32[]{:S(2)}) collective-permute-start(bf16[1,2,64,256]{3,2,1,0:T(8,128)(2,1)S(1)} %get-tuple-element.10), channel_id=1, source_target_pairs={{0,4},{4,8},{8,12},{1,5},{5,9},{9,13},{2,6},{6,10},{10,14},{3,7},{... | collective-permute-start | bytes 196616 | tf_op jit(solution)/shard_map/ppermute | solution.py:22
  15.1 0.9 convert_reduce_fusion.1
  16.0 0.9 convert_reduce_fusion
  16.9 1.1 reshape.65
  18.0 20.3 %all-gather = f32[32,1,4,256]{3,2,1,0:T(4,128)S(1)} all-gather(f32[2,1,4,256]{3,2,1,0:T(4,128)S(1)} %pad_maximum_fusion), channel_id=2, replica_groups=mesh['grp'=2,'lat'=4,'lon'=4] {'lat','lon'}, dimensions={0}, use_global_device_ids=true | all-gather | bytes 139264 | tf_op jit(solution)/shard_map/all_gather | solution.py:122
  38.4 0.0 copy-done.5
  38.4 0.0 copy-done.10
  38.4 0.0 copy-done.7
  38.4 0.6 constant_dynamic-slice_fusion.1
  39.0 0.6 fusion.24
  39.6 0.0 copy-done.8
  39.6 0.0 copy-done.9
  39.6 0.6 constant_dynamic-slice_fusion.3
  40.2 0.0 collective-permute-done
  40.2 0.0 copy-done.4
  40.3 0.0 collective-permute-done.1
  40.3 0.4 collective-permute-start.2
  40.7 1.4 %collective-permute-start.3 = (bf16[1,8,16,256]{3,2,1,0:T(8,128)(2,1)S(1)}, bf16[1,8,16,256]{3,2,1,0:T(8,128)(2,1)S(1)}, u32[]{:S(2)}, u32[]{:S(2)}) collective-permute-start(bf16[1,8,16,256]{3,2,1,0:T(8,128)(2,1)S(1)} %get-tuple-element.6), channel_id=1, source_target_pairs={{1,0},{2,1},{3,2},{0,3},{5,4},{6,5},{7,6},{4,7},{9,8},{10,9},{11,1... | collective-permute-start | bytes 196616 | tf_op jit(solution)/shard_map/ppermute | solution.py:25
  42.1 0.6 constant_dynamic-slice_fusion.scale_ref
  42.7 1.5 %collective-permute-done.2 = bf16[1,8,16,256]{3,2,1,0:T(8,128)(2,1)S(1)} collective-permute-done((bf16[1,8,16,256]{3,2,1,0:T(8,128)(2,1)S(1)}, bf16[1,8,16,256]{3,2,1,0:T(8,128)(2,1)S(1)}, u32[]{:S(2)}, u32[]{:S(2)}) %collective-permute-start.2) | collective-permute-done | bytes 65568 | tf_op jit(solution)/shard_map/ppermute | solution.py:22
  44.2 0.0 collective-permute-done.3
  44.2 0.8 fusion.19.field_ref
  45.0 3.5 %shard_map.103 = bf16[1,4,64,2304]{3,2,1,0:T(8,128)(2,1)} custom-call(s32[4,12]{1,0:T(4,128)} %get-tuple-element.16.rows_ref, s32[4,12]{1,0:T(4,128)} %get-tuple-element.15.start_ref, s32[4,12]{1,0:T(4,128)} %get-tuple-element.14.span_ref, s32[4,12]{1,0:T(4,128)} %get-tuple-element.13.basis_ref, f32[4,12]{1,0:T(4,128)} %constant_dynamic-slice_fusion.scale_ref, ...), custom_call_target="tpu_custom_call" | custom-call | tf_op jit(solution)/shard_map/pallas_call | solution.py:90
  48.6 3.6 %reshape.64 = bf16[4,64,9,4,64]{4,3,2,1,0:T(4,128)(2,1)S(1)} reshape(bf16[1,4,64,2304]{3,2,1,0:T(8,128)(2,1)} %shard_map.103) | data formatting | bytes 2359296 | tf_op jit(solution)/shard_map/reshape.5
  52.2 0.8 fusion
  53.0 2.8 %copy.30 = f32[16,9,64,64]{3,2,1,0:T(8,128)} copy(f32[16,9,64,64]{3,2,0,1:T(8,128)S(1)} %bitcast.51) | data formatting | bytes 4718592 | tf_op jit(solution)/shard_map/reshape | solution.py:168
  55.8 0.0 copy-start.3
  55.8 0.0 copy-start.1
  55.8 0.0 reduce-scatter.2.cloned.1.call-update
  55.9 0.9 copy-done.3
  56.7 1.3 collective-permute-start.5
  58.0 4.6 %collective-permute-start.4 = (bf16[1,2,64,256]{3,2,1,0:T(8,128)(2,1)S(1)}, bf16[1,2,64,256]{3,2,1,0:T(8,128)(2,1)S(1)}, u32[]{:S(2)}, u32[]{:S(2)}) collective-permute-start(bf16[1,2,64,256]{3,2,1,0:T(8,128)(2,1)S(1)} %get-tuple-element.8), channel_id=1, source_target_pairs={{0,4},{4,8},{8,12},{1,5},{5,9},{9,13},{2,6},{6,10},{10,14},{3,7},{... | collective-permute-start | bytes 196616 | tf_op jit(solution)/shard_map/ppermute | solution.py:22
  62.6 0.1 broadcast_in_dim.17
  62.7 0.6 pad_dynamic-slice_fusion.5
  63.3 0.0 copy-start.6
  63.3 0.1 eq.16
  63.4 0.7 compare_select_fusion.scale_ref
  64.1 0.0 copy-done.1
  64.1 0.7 copy.27
  64.8 0.0 copy-done.6
  64.8 0.0 collective-permute-done.4
  64.9 0.0 collective-permute-done.5
  64.9 0.1 collective-permute-start.6
  65.0 1.7 %collective-permute-start.7 = (bf16[1,8,16,256]{3,2,1,0:T(8,128)(2,1)S(1)}, bf16[1,8,16,256]{3,2,1,0:T(8,128)(2,1)S(1)}, u32[]{:S(2)}, u32[]{:S(2)}) collective-permute-start(bf16[1,8,16,256]{3,2,1,0:T(8,128)(2,1)S(1)} %get-tuple-element.4), channel_id=1, source_target_pairs={{1,0},{2,1},{3,2},{0,3},{5,4},{6,5},{7,6},{4,7},{9,8},{10,9},{11,1... | collective-permute-start | bytes 196616 | tf_op jit(solution)/shard_map/ppermute | solution.py:25
  66.7 0.6 pad_dynamic-slice_fusion.3
  67.3 1.7 %collective-permute-done.6 = bf16[1,8,16,256]{3,2,1,0:T(8,128)(2,1)S(1)} collective-permute-done((bf16[1,8,16,256]{3,2,1,0:T(8,128)(2,1)S(1)}, bf16[1,8,16,256]{3,2,1,0:T(8,128)(2,1)S(1)}, u32[]{:S(2)}, u32[]{:S(2)}) %collective-permute-start.6) | collective-permute-done | bytes 65568 | tf_op jit(solution)/shard_map/ppermute | solution.py:22
  69.0 0.0 collective-permute-done.7
  69.0 0.8 fusion.21.field_ref
  69.8 10.3 %shard_map.104 = bf16[1,4,64,2304]{3,2,1,0:T(8,128)(2,1)} custom-call(s32[8,12]{1,0:T(8,128)} %copy-done.6, s32[8,12]{1,0:T(8,128)} %get-tuple-element.19.start_ref, s32[8,12]{1,0:T(8,128)} %get-tuple-element.18.span_ref, s32[8,12]{1,0:T(8,128)} %get-tuple-element.17.basis_ref, f32[4,96]{1,0:T(4,128)} %compare_select_fusion.scale_ref, ...), custom_call_target="tpu_custom_call" | custom-call | tf_op jit(solution)/shard_map/pallas_call | solution.py:90
  80.1 0.0 copy-done
  80.1 1.2 fusion.6
  81.3 0.1 copy-done.2
  81.4 1.2 fusion.9
  82.6 47.3 %reduce-scatter.2.cloned.1.call-done = f32[1,9,64,64]{3,2,1,0:T(8,128)} async-done(((f32[16,9,64,64]{3,2,1,0:T(8,128)}), f32[1,9,64,64]{3,2,1,0:T(8,128)}) %reduce-scatter.2.cloned.1.call-update) | async-done | bytes 147472 | tf_op jit(solution)/shard_map/reduce_scatter | solution.py:171
  129.9 1.7 %multiply_bitcast_fusion = f32[9,64,64]{2,1,0:T(8,128)} fusion(f32[1,9,64,64]{3,2,1,0:T(8,128)} %reduce-scatter.2.cloned.1.call-done), kind=kLoop, calls=%fused_computation.19 | loop fusion | flops 36864 | bytes 294912 | tf_op jit(solution)/shard_map/div | solution.py:173
  (17 shorter events, 0.2 us)
Async XLA Ops:
  7.2 33.1 %copy-start.4 = (bf16[1,4,64,256]{3,2,1,0:T(8,128)(2,1)S(1)}, bf16[1,4,64,256]{3,2,1,0:T(8,128)(2,1)}, u32[]{:S(2)}) copy-start(bf16[1,4,64,256]{3,2,1,0:T(8,128)(2,1)} %param.8) | copy-start | bytes 393220
  7.2 31.2 %copy-start.5 = (s32[16,12]{1,0:T(8,128)S(1)}, s32[16,12]{1,0:T(8,128)}, u32[]{:S(2)}) copy-start(s32[16,12]{1,0:T(8,128)} %param.13) | copy-start | bytes 2308
  7.2 31.2 %copy-start.10 = (f32[16,12]{1,0:T(8,128)S(1)}, f32[16,12]{1,0:T(8,128)}, u32[]{:S(2)}) copy-start(f32[16,12]{1,0:T(8,128)} %param.15) | copy-start | bytes 2308
  7.2 31.2 %copy-start.7 = (s32[16,12]{1,0:T(8,128)S(1)}, s32[16,12]{1,0:T(8,128)}, u32[]{:S(2)}) copy-start(s32[16,12]{1,0:T(8,128)} %param.14) | copy-start | bytes 2308
  7.2 32.4 %copy-start.8 = (s32[16,12]{1,0:T(8,128)S(1)}, s32[16,12]{1,0:T(8,128)}, u32[]{:S(2)}) copy-start(s32[16,12]{1,0:T(8,128)} %param.12) | copy-start | bytes 2308
  7.2 32.4 %copy-start.9 = (s32[16,12]{1,0:T(8,128)S(1)}, s32[16,12]{1,0:T(8,128)}, u32[]{:S(2)}) copy-start(s32[16,12]{1,0:T(8,128)} %param.11) | copy-start | bytes 2308
  7.2 122.7 %reduce-scatter.2.cloned.1.call-start = ((), (), s32[]{:S(2)}) async-start(), calls=%async_computation.1 | async-start | bytes 5013504 | tf_op jit(solution)/shard_map/reduce_scatter | solution.py:171
  8.2 32.1 %collective-permute-start.1 = (bf16[1,2,64,256]{3,2,1,0:T(8,128)(2,1)S(1)}, bf16[1,2,64,256]{3,2,1,0:T(8,128)(2,1)S(1)}, u32[]{:S(2)}, u32[]{:S(2)}) collective-permute-start(bf16[1,2,64,256]{3,2,1,0:T(8,128)(2,1)S(1)} %get-tuple-element.9), channel_id=1, source_target_pairs={{4,0},{8,4},{12,8},{5,1},{9,5},{13,9},{6,2},{10,6},{14,10},{7,3},{... | collective-permute-start | bytes 196616 | tf_op jit(solution)/shard_map/ppermute | solution.py:25
  9.5 30.7 %collective-permute-start = (bf16[1,2,64,256]{3,2,1,0:T(8,128)(2,1)S(1)}, bf16[1,2,64,256]{3,2,1,0:T(8,128)(2,1)S(1)}, u32[]{:S(2)}, u32[]{:S(2)}) collective-permute-start(bf16[1,2,64,256]{3,2,1,0:T(8,128)(2,1)S(1)} %get-tuple-element.10), channel_id=1, source_target_pairs={{0,4},{4,8},{8,12},{1,5},{5,9},{9,13},{2,6},{6,10},{10,14},{3,7},{... | collective-permute-start | bytes 196616 | tf_op jit(solution)/shard_map/ppermute | solution.py:22
  40.3 3.9 %collective-permute-start.2 = (bf16[1,8,16,256]{3,2,1,0:T(8,128)(2,1)S(1)}, bf16[1,8,16,256]{3,2,1,0:T(8,128)(2,1)S(1)}, u32[]{:S(2)}, u32[]{:S(2)}) collective-permute-start(bf16[1,8,16,256]{3,2,1,0:T(8,128)(2,1)S(1)} %get-tuple-element.5), channel_id=1, source_target_pairs={{0,1},{1,2},{2,3},{3,0},{4,5},{5,6},{6,7},{7,4},{8,9},{9,10},{10,1... | collective-permute-start | bytes 196616 | tf_op jit(solution)/shard_map/ppermute | solution.py:22
  40.7 3.5 %collective-permute-start.3 = (bf16[1,8,16,256]{3,2,1,0:T(8,128)(2,1)S(1)}, bf16[1,8,16,256]{3,2,1,0:T(8,128)(2,1)S(1)}, u32[]{:S(2)}, u32[]{:S(2)}) collective-permute-start(bf16[1,8,16,256]{3,2,1,0:T(8,128)(2,1)S(1)} %get-tuple-element.6), channel_id=1, source_target_pairs={{1,0},{2,1},{3,2},{0,3},{5,4},{6,5},{7,6},{4,7},{9,8},{10,9},{11,1... | collective-permute-start | bytes 196616 | tf_op jit(solution)/shard_map/ppermute | solution.py:25
  55.8 0.9 copy-start.3
  55.8 8.3 %copy-start.1 = (bf16[9,256,256]{2,1,0:T(8,128)(2,1)S(1)}, bf16[9,256,256]{2,1,0:T(8,128)(2,1)}, u32[]{:S(2)}) copy-start(bf16[9,256,256]{2,1,0:T(8,128)(2,1)} %param.10) | copy-start | bytes 3538948
  56.7 8.1 %collective-permute-start.5 = (bf16[1,2,64,256]{3,2,1,0:T(8,128)(2,1)S(1)}, bf16[1,2,64,256]{3,2,1,0:T(8,128)(2,1)S(1)}, u32[]{:S(2)}, u32[]{:S(2)}) collective-permute-start(bf16[1,2,64,256]{3,2,1,0:T(8,128)(2,1)S(1)} %get-tuple-element.7), channel_id=1, source_target_pairs={{4,0},{8,4},{12,8},{5,1},{9,5},{13,9},{6,2},{10,6},{14,10},{7,3},{... | collective-permute-start | bytes 196616 | tf_op jit(solution)/shard_map/ppermute | solution.py:25
  58.0 6.8 %collective-permute-start.4 = (bf16[1,2,64,256]{3,2,1,0:T(8,128)(2,1)S(1)}, bf16[1,2,64,256]{3,2,1,0:T(8,128)(2,1)S(1)}, u32[]{:S(2)}, u32[]{:S(2)}) collective-permute-start(bf16[1,2,64,256]{3,2,1,0:T(8,128)(2,1)S(1)} %get-tuple-element.8), channel_id=1, source_target_pairs={{0,4},{4,8},{8,12},{1,5},{5,9},{9,13},{2,6},{6,10},{10,14},{3,7},{... | collective-permute-start | bytes 196616 | tf_op jit(solution)/shard_map/ppermute | solution.py:22
  63.3 1.5 %copy-start.6 = (s32[8,12]{1,0:T(8,128)}, s32[8,12]{1,0:T(8,128)S(1)}, u32[]{:S(2)}) copy-start(s32[8,12]{1,0:T(8,128)S(1)} %get-tuple-element.20.rows_ref) | copy-start | bytes 1156
  64.9 4.1 %collective-permute-start.6 = (bf16[1,8,16,256]{3,2,1,0:T(8,128)(2,1)S(1)}, bf16[1,8,16,256]{3,2,1,0:T(8,128)(2,1)S(1)}, u32[]{:S(2)}, u32[]{:S(2)}) collective-permute-start(bf16[1,8,16,256]{3,2,1,0:T(8,128)(2,1)S(1)} %get-tuple-element.3), channel_id=1, source_target_pairs={{0,1},{1,2},{2,3},{3,0},{4,5},{5,6},{6,7},{7,4},{8,9},{9,10},{10,1... | collective-permute-start | bytes 196616 | tf_op jit(solution)/shard_map/ppermute | solution.py:22
  65.0 4.0 %collective-permute-start.7 = (bf16[1,8,16,256]{3,2,1,0:T(8,128)(2,1)S(1)}, bf16[1,8,16,256]{3,2,1,0:T(8,128)(2,1)S(1)}, u32[]{:S(2)}, u32[]{:S(2)}) collective-permute-start(bf16[1,8,16,256]{3,2,1,0:T(8,128)(2,1)S(1)} %get-tuple-element.4), channel_id=1, source_target_pairs={{1,0},{2,1},{3,2},{0,3},{5,4},{6,5},{7,6},{4,7},{9,8},{10,9},{11,1... | collective-permute-start | bytes 196616 | tf_op jit(solution)/shard_map/ppermute | solution.py:25
  67.3 12.8 %copy-start = (bf16[1,4,64,2304]{3,2,1,0:T(8,128)(2,1)S(1)}, bf16[1,4,64,2304]{3,2,1,0:T(8,128)(2,1)}, u32[]{:S(2)}) copy-start(bf16[1,4,64,2304]{3,2,1,0:T(8,128)(2,1)} %shard_map.103) | copy-start | bytes 3538948
  80.1 1.3 copy-start.2
Sparse Core Ops, SparseCore 0:
  56.0 73.8 reduce-scatter.1

commit v2 on v0

--- a/solution.py
+++ b/solution.py
@@ -34,9 +34,30 @@
     return jnp.pad(grid_field, ((0, 0), (0, 0), (0, extra), (0, 0)))
 
 
+def ring_sum(value, axis):
+    count = lax.axis_size(axis)
+    total = value
+    for shift in range(1, count):
+        pairs = [(i, (i + shift) % count) for i in range(count)]
+        total = total + lax.ppermute(value, axis, pairs)
+    return total
+
+
 def cycle_totals(widened, lon_count):
     interior = lax.slice_in_dim(widened, RIM, RIM + lon_count, axis=2)
-    return lax.psum(jnp.sum(interior, axis=2, dtype=jnp.float32), "lon")
+    return ring_sum(jnp.sum(interior, axis=2, dtype=jnp.float32), "lon")
+
+
+def ring_scatter(value, axis, dim):
+    count = lax.axis_size(axis)
+    own = lax.axis_index(axis)
+    block = value.shape[dim] // count
+    total = lax.dynamic_slice_in_dim(value, own * block, block, dim)
+    for shift in range(1, count):
+        pairs = [(i, (i + shift) % count) for i in range(count)]
+        piece = lax.dynamic_slice_in_dim(value, ((own + shift) % count) * block, block, dim)
+        total = total + lax.ppermute(piece, axis, pairs)
+    return total
 
 
 def filter_kernel(
@@ -158,7 +179,7 @@
     )
     partial_value = partial_value.reshape(BASIS, channels, channels)
     reduced = lax.psum_scatter(partial_value, "lon", scatter_dimension=2, tiled=True)
-    reduced = lax.psum_scatter(reduced, "lat", scatter_dimension=1, tiled=True)
+    reduced = ring_scatter(reduced, "lat", 1)
     grad_weight = reduced / jnp.sqrt(jnp.float32(members * height * lon_total))
     return (response, grad_input, grad_weight)
 

time: 117 us -> 107 us (0.915)
  blocking collectives: 10.9 us -> 0 us
  starting transfers between devices: 16.4 us -> 24.7 us
  local copies, waits for them, and re-layouts: 14.5 us -> 8.24 us
  waiting for transfers between devices: 36.3 us -> 34.2 us
  other arithmetic: 4.47 us -> 5.85 us
    ppermute x0 -> x9, waiting for transfers between devices: none -> 25.8 us  [the longest x3 23.9 us: ring_scatter(): total = total + lax.ppermute(piece, axis, pairs)]
    reduce_scatter x1, waiting for transfers between devices: 32.5 us -> 7.28 us  [on_device(): lax.psum_scatter(partial_value, 'lon', scatter_dimension=2, tiled=True)]
    psum x1 -> x0, blocking collectives: 10.9 us -> none  [cycle_totals(): return lax.psum(jnp.sum(interior, axis=2, dtype=jnp.float32), 'lon')]
    ppermute x0 -> x9, starting transfers between devices: none -> 8.15 us  [the longest x3 4.57 us: ring_scatter(): total = total + lax.ppermute(piece, axis, pairs)]
    unnamed x30 -> x26, local copies, waits for them, and re-layouts: 9.34 us -> 2.57 us
    unnamed x3 -> x1, waiting for transfers between devices: 2.26 us -> 0.02 us
    ppermute x4, starting transfers between devices: 10.2 us -> 12.2 us  [with_halo(): lax.ppermute(lax.slice_in_dim(block, block.shape[dim] - width, None, axis...]
    ppermute x4, starting transfers between devices: 6.05 us -> 4.31 us  [with_halo(): lax.ppermute(lax.slice_in_dim(block, 0, width, axis=dim), axis, backward)]
  transfers between devices with their start and end apart: 10 -> 18, of which waited for: 3 -> 9; matrix products, arithmetic and copies ran while one was open for 11% -> 11% of each run, Pallas kernels for 9% -> 10%
where the time goes in v2:
time: 107 us
  waiting for transfers between devices  34.2 us (32%)
  starting transfers between devices  24.7 us (23%)
  between operations  14.3 us (13%)
  Pallas kernels  13.9 us (13%)
  local copies, waits for them, and re-layouts  8.24 us (8%)
  other arithmetic  5.85 us (5%)
  matrix products  5.57 us (5%)
    ppermute x3, waiting for transfers between devices, ring_scatter(): total = total + lax.ppermute(piece, axis, pairs)  23.9 us
    pallas_call x2, Pallas kernels, run_filter(): pl.pallas_call(kernel, grid=(members, row_count), in_specs=[smem] * 5 + [...  13.9 us
    ppermute x4, starting transfers between devices, with_halo(): lax.ppermute(lax.slice_in_dim(block, block.shape[dim] - width, None, axis...  12.2 us
    reduce_scatter x1, waiting for transfers between devices, on_device(): lax.psum_scatter(partial_value, 'lon', scatter_dimension=2, tiled=True)  7.28 us
    ppermute x3, starting transfers between devices, ring_scatter(): total = total + lax.ppermute(piece, axis, pairs)  4.57 us
    ppermute x4, starting transfers between devices, with_halo(): lax.ppermute(lax.slice_in_dim(block, 0, width, axis=dim), axis, backward)  4.31 us
    ppermute x6, starting transfers between devices, ring_sum(): total = total + lax.ppermute(value, axis, pairs)  3.58 us
    dot_general x1, matrix products, on_device(): jnp.einsum('brwq,brwo->qo', flattened, cotangent, preferred_element_type=...  3.22 us
  transfers between devices with their start and end apart: 18, of which 9 were waited for; matrix products, arithmetic and copies ran while one was open for 11% of the time, Pallas kernels for 10%

profile of v2, /device:TPU:0, one launch (start us, length us, event | category | flops | bytes accessed | tf_op | source)
XLA Modules:
  0.0 106.7 jit_solution(6842725204477278458)
XLA Ops:
  7.2 0.0 reduce-scatter.2.cloned.1.call-start
  7.2 0.9 fusion.28
  8.1 1.3 %collective-permute-start.1 = (bf16[1,2,64,256]{3,2,1,0:T(8,128)(2,1)S(1)}, bf16[1,2,64,256]{3,2,1,0:T(8,128)(2,1)S(1)}, u32[]{:S(2)}, u32[]{:S(2)}) collective-permute-start(bf16[1,2,64,256]{3,2,1,0:T(8,128)(2,1)S(1)} %get-tuple-element.18), channel_id=1, source_target_pairs={{4,0},{8,4},{12,8},{5,1},{9,5},{13,9},{6,2},{10,6},{14,10},{7,3},{... | collective-permute-start | bytes 196616 | tf_op jit(solution)/shard_map/ppermute | solution.py:25
  9.4 5.6 %collective-permute-start = (bf16[1,2,64,256]{3,2,1,0:T(8,128)(2,1)S(1)}, bf16[1,2,64,256]{3,2,1,0:T(8,128)(2,1)S(1)}, u32[]{:S(2)}, u32[]{:S(2)}) collective-permute-start(bf16[1,2,64,256]{3,2,1,0:T(8,128)(2,1)S(1)} %get-tuple-element.19), channel_id=1, source_target_pairs={{0,4},{4,8},{8,12},{1,5},{5,9},{9,13},{2,6},{6,10},{10,14},{3,7},{... | collective-permute-start | bytes 196616 | tf_op jit(solution)/shard_map/ppermute | solution.py:22
  15.0 0.7 rsqrt_multiply_fusion
  15.7 1.3 %constant_dynamic-slice_fusion.4 = (s32[4,12]{1,0:T(4,128)}, s32[4,12]{1,0:T(4,128)}) fusion(s32[16,12]{1,0:T(8,128)} %param.14, s32[]{:T(128)S(6)} %select_n.46, s32[16,12]{1,0:T(8,128)} %param.13), kind=kLoop, calls=%fused_computation.42 | loop fusion | bytes 772 | tf_op jit(solution)/shard_map/dynamic_slice | solution.py:149
  17.0 1.3 %constant_dynamic-slice_fusion.6 = (s32[4,12]{1,0:T(4,128)}, s32[4,12]{1,0:T(4,128)}) fusion(s32[16,12]{1,0:T(8,128)} %param.12, s32[]{:T(128)S(6)} %select_n.46, s32[]{:T(128)S(6)} %mul.15, s32[16,12]{1,0:T(8,128)} %param.11), kind=kLoop, calls=%fused_computation.44 | loop fusion | flops 96 | bytes 776 | tf_op jit(solution)/shard_map/dynamic_slice | solution.py:149
  18.3 0.6 constant_dynamic-slice_fusion.3.scale_ref
  18.9 0.0 collective-permute-done
  18.9 0.9 constant_dynamic-update-slice_fusion.1
  19.8 0.0 collective-permute-done.1
  19.8 0.1 convert_reduce_fusion.1
  19.9 2.0 %collective-permute-start.5 = (f32[1,8,256]{2,0,1:T(1,128)S(1)}, f32[1,8,256]{2,0,1:T(1,128)S(1)}, u32[]{:S(2)}, u32[]{:S(2)}) collective-permute-start(f32[1,8,256]{2,0,1:T(1,128)S(1)} %reduce_sum.23), channel_id=1, source_target_pairs={{0,2},{1,3},{2,0},{3,1},{4,6},{5,7},{6,4},{7,5},{8,10},{9,11},{10,... | collective-permute-start | bytes 24584 | tf_op jit(solution)/shard_map/ppermute | solution.py:42
  21.9 0.0 collective-permute-start.6
  21.9 0.5 collective-permute-start.4
  22.4 0.3 collective-permute-start.2
  22.7 1.5 %collective-permute-start.3 = (bf16[1,8,16,256]{3,2,1,0:T(8,128)(2,1)S(1)}, bf16[1,8,16,256]{3,2,1,0:T(8,128)(2,1)S(1)}, u32[]{:S(2)}, u32[]{:S(2)}) collective-permute-start(bf16[1,8,16,256]{3,2,1,0:T(8,128)(2,1)S(1)} %get-tuple-element.15), channel_id=1, source_target_pairs={{1,0},{2,1},{3,2},{0,3},{5,4},{6,5},{7,6},{4,7},{9,8},{10,9},{11,1... | collective-permute-start | bytes 196616 | tf_op jit(solution)/shard_map/ppermute | solution.py:25
  24.2 0.0 collective-permute-done.5
  24.2 0.0 collective-permute-done.6
  24.2 0.8 collective-permute-done.4
  25.0 0.6 add_bitcast_fusion.1.total_ref
  25.6 0.9 collective-permute-done.2
  26.5 0.0 collective-permute-done.3
  26.5 0.9 fusion.19.field_ref
  27.3 3.5 %shard_map.103 = bf16[1,4,64,2304]{3,2,1,0:T(8,128)(2,1)} custom-call(s32[4,12]{1,0:T(4,128)} %get-tuple-element.23.rows_ref, s32[4,12]{1,0:T(4,128)} %get-tuple-element.22.start_ref, s32[4,12]{1,0:T(4,128)} %get-tuple-element.21.span_ref, s32[4,12]{1,0:T(4,128)} %get-tuple-element.20.basis_ref, f32[4,12]{1,0:T(4,128)} %constant_dynamic-slice_fusion.3.scale_ref, ...), custom_call_target="tpu_custom_call" | custom-call | tf_op jit(solution)/shard_map/pallas_call | solution.py:116
  30.9 3.2 %convolution_bitcast_fusion = f32[9,256,256]{1,2,0:T(8,128)} fusion(bf16[4,8,9,8,256]{4,3,2,1,0:T(8,128)(2,1)} %bitcast.41, bf16[1,4,64,256]{3,2,1,0:T(8,128)(2,1)S(1)} %copy-done.4), kind=kOutput, calls=%fused_computation | convolution fusion | flops 301989888 | bytes 3670016 | tf_op jit(solution)/shard_map/brwq,brwo->qo/dot_general | solution.py:177
  34.1 0.0 reduce-scatter.2.cloned.1.call-update
  34.1 1.4 %collective-permute-start.8 = (bf16[1,2,64,256]{3,2,1,0:T(8,128)(2,1)S(1)}, bf16[1,2,64,256]{3,2,1,0:T(8,128)(2,1)S(1)}, u32[]{:S(2)}, u32[]{:S(2)}) collective-permute-start(bf16[1,2,64,256]{3,2,1,0:T(8,128)(2,1)S(1)} %get-tuple-element.16), channel_id=1, source_target_pairs={{4,0},{8,4},{12,8},{5,1},{9,5},{13,9},{6,2},{10,6},{14,10},{7,3},{... | collective-permute-start | bytes 196616 | tf_op jit(solution)/shard_map/ppermute | solution.py:25
  35.6 4.5 %collective-permute-start.7 = (bf16[1,2,64,256]{3,2,1,0:T(8,128)(2,1)S(1)}, bf16[1,2,64,256]{3,2,1,0:T(8,128)(2,1)S(1)}, u32[]{:S(2)}, u32[]{:S(2)}) collective-permute-start(bf16[1,2,64,256]{3,2,1,0:T(8,128)(2,1)S(1)} %get-tuple-element.17), channel_id=1, source_target_pairs={{0,4},{4,8},{8,12},{1,5},{5,9},{9,13},{2,6},{6,10},{10,14},{3,7},{... | collective-permute-start | bytes 196616 | tf_op jit(solution)/shard_map/ppermute | solution.py:22
  40.2 0.1 broadcast_in_dim.24
  40.3 0.6 pad_dynamic-slice_fusion.3
  40.9 0.1 eq.20
  41.0 0.0 copy-start.7
  41.0 0.7 copy.13
  41.8 0.7 compare_select_fusion.scale_ref
  42.4 0.6 pad_dynamic-slice_fusion.1
  43.0 0.0 collective-permute-done.7
  43.1 0.0 collective-permute-done.8
  43.1 0.1 convert_reduce_fusion
  43.2 0.1 collective-permute-start.12
  43.2 1.0 collective-permute-start.13
  44.2 0.0 collective-permute-start.11
  44.3 1.8 %collective-permute-start.9 = (bf16[1,8,16,256]{3,2,1,0:T(8,128)(2,1)S(1)}, bf16[1,8,16,256]{3,2,1,0:T(8,128)(2,1)S(1)}, u32[]{:S(2)}, u32[]{:S(2)}) collective-permute-start(bf16[1,8,16,256]{3,2,1,0:T(8,128)(2,1)S(1)} %get-tuple-element.12), channel_id=1, source_target_pairs={{0,1},{1,2},{2,3},{3,0},{4,5},{5,6},{6,7},{7,4},{8,9},{9,10},{10,1... | collective-permute-start | bytes 196616 | tf_op jit(solution)/shard_map/ppermute | solution.py:22
  46.0 0.1 collective-permute-start.10
  46.1 0.8 collective-permute-done.12
  46.9 0.0 collective-permute-done.13
  46.9 0.4 collective-permute-done.11
  47.3 0.6 add_bitcast_fusion.total_ref
  47.9 0.2 collective-permute-done.9
  48.1 0.0 collective-permute-done.10
  48.1 0.8 fusion.21.field_ref
  48.9 10.3 %shard_map.104 = bf16[1,4,64,2304]{3,2,1,0:T(8,128)(2,1)} custom-call(s32[8,12]{1,0:T(8,128)} %copy-done.6, s32[8,12]{1,0:T(8,128)} %get-tuple-element.26.start_ref, s32[8,12]{1,0:T(8,128)} %get-tuple-element.25.span_ref, s32[8,12]{1,0:T(8,128)} %get-tuple-element.24.basis_ref, f32[4,96]{1,0:T(4,128)} %compare_select_fusion.scale_ref, ...), custom_call_target="tpu_custom_call" | custom-call | tf_op jit(solution)/shard_map/pallas_call | solution.py:116
  59.3 1.2 %fusion.6 = f32[1,4,64,256]{3,2,1,0:T(8,128)} fusion(bf16[2304,256,1]{1,0,2:T(8,128)(2,1)S(1)} %bitcast.42, bf16[1,4,64,2304]{3,2,1,0:T(8,128)(2,1)S(1)} %copy-done), kind=kOutput, calls=%fused_computation.7 | convolution fusion | flops 301989888 | bytes 2621440 | tf_op jit(solution)/shard_map/brwq,qo->brwo/dot_general | solution.py:160
  60.5 7.3 %reduce-scatter.2.cloned.1.call-done = f32[9,256,64]{1,2,0:T(8,128)} async-done(((f32[9,256,256]{1,2,0:T(8,128)}), f32[9,256,64]{1,2,0:T(8,128)}) %reduce-scatter.2.cloned.1.call-update) | async-done | bytes 589840 | tf_op jit(solution)/shard_map/reduce_scatter | solution.py:181
  67.7 1.4 %constant_dynamic-slice_fusion.1 = (f32[9,64,64]{1,2,0:T(8,128)S(1)}, f32[9,64,64]{1,2,0:T(8,128)S(1)}, f32[9,64,64]{1,2,0:T(8,128)S(1)}) fusion(f32[9,256,64]{1,2,0:T(8,128)} %reduce-scatter.2.cloned.1.call-done, s32[]{:T(128)S(6)} %select_n.51, s32[]{:T(128)S(6)} %select_n.55, s32[]{:T(128)S(6)} %select_n.53), kind=kLoop, calls=%fused_computation.39 | loop fusion | bytes 884748 | tf_op jit(solution)/shard_map/dynamic_slice | solution.py:58
  69.2 1.5 %collective-permute-start.14 = (f32[9,64,64]{1,2,0:T(8,128)S(1)}, f32[9,64,64]{1,2,0:T(8,128)S(1)}, u32[]{:S(2)}, u32[]{:S(2)}) collective-permute-start(f32[9,64,64]{1,2,0:T(8,128)S(1)} %get-tuple-element.9), channel_id=1, source_target_pairs={{0,4},{4,8},{8,12},{12,0},{1,5},{5,9},{9,13},{13,1},{2,6},{6,10},{... | collective-permute-start | bytes 442376 | tf_op jit(solution)/shard_map/ppermute | solution.py:59
  70.7 2.4 %collective-permute-start.16 = (f32[9,64,64]{1,2,0:T(8,128)S(1)}, f32[9,64,64]{1,2,0:T(8,128)S(1)}, u32[]{:S(2)}, u32[]{:S(2)}) collective-permute-start(f32[9,64,64]{1,2,0:T(8,128)S(1)} %get-tuple-element.10), channel_id=1, source_target_pairs={{0,12},{4,0},{8,4},{12,8},{1,13},{5,1},{9,5},{13,9},{2,14},{6,2},{... | collective-permute-start | bytes 442376 | tf_op jit(solution)/shard_map/ppermute | solution.py:59
  73.1 0.7 collective-permute-start.15
  73.7 1.2 %fusion.9 = f32[1,4,64,256]{3,2,1,0:T(8,128)} fusion(bf16[2304,256,1]{1,0,2:T(8,128)(2,1)S(1)} %bitcast.43, bf16[1,4,64,2304]{3,2,1,0:T(8,128)(2,1)S(1)} %copy-done.2), kind=kOutput, calls=%fused_computation.8 | convolution fusion | flops 301989888 | bytes 2621440 | tf_op jit(solution)/shard_map/bpwq,qc->bpwc/dot_general | solution.py:174
  74.9 6.0 %collective-permute-done.14 = f32[9,64,64]{1,2,0:T(8,128)S(1)} collective-permute-done((f32[9,64,64]{1,2,0:T(8,128)S(1)}, f32[9,64,64]{1,2,0:T(8,128)S(1)}, u32[]{:S(2)}, u32[]{:S(2)}) %collective-permute-start.14) | collective-permute-done | bytes 147488 | tf_op jit(solution)/shard_map/ppermute | solution.py:59
  81.0 4.5 %collective-permute-done.16 = f32[9,64,64]{1,2,0:T(8,128)S(1)} collective-permute-done((f32[9,64,64]{1,2,0:T(8,128)S(1)}, f32[9,64,64]{1,2,0:T(8,128)S(1)}, u32[]{:S(2)}, u32[]{:S(2)}) %collective-permute-start.16) | collective-permute-done | bytes 147488 | tf_op jit(solution)/shard_map/ppermute | solution.py:59
  85.4 13.4 %collective-permute-done.15 = f32[9,64,64]{1,2,0:T(8,128)S(1)} collective-permute-done((f32[9,64,64]{1,2,0:T(8,128)S(1)}, f32[9,64,64]{1,2,0:T(8,128)S(1)}, u32[]{:S(2)}, u32[]{:S(2)}) %collective-permute-start.15) | collective-permute-done | bytes 147488 | tf_op jit(solution)/shard_map/ppermute | solution.py:59
  98.8 0.1 add_multiply_fusion
  99.0 0.9 copy.15
  (31 shorter events, 0.1 us)
Async XLA Ops:
  7.2 60.6 %reduce-scatter.2.cloned.1.call-start = ((), (), s32[]{:S(2)}) async-start(), calls=%async_computation.1 | async-start | bytes 2949120 | tf_op jit(solution)/shard_map/reduce_scatter | solution.py:181
  8.1 11.7 %collective-permute-start.1 = (bf16[1,2,64,256]{3,2,1,0:T(8,128)(2,1)S(1)}, bf16[1,2,64,256]{3,2,1,0:T(8,128)(2,1)S(1)}, u32[]{:S(2)}, u32[]{:S(2)}) collective-permute-start(bf16[1,2,64,256]{3,2,1,0:T(8,128)(2,1)S(1)} %get-tuple-element.18), channel_id=1, source_target_pairs={{4,0},{8,4},{12,8},{5,1},{9,5},{13,9},{6,2},{10,6},{14,10},{7,3},{... | collective-permute-start | bytes 196616 | tf_op jit(solution)/shard_map/ppermute | solution.py:25
  9.4 9.5 %collective-permute-start = (bf16[1,2,64,256]{3,2,1,0:T(8,128)(2,1)S(1)}, bf16[1,2,64,256]{3,2,1,0:T(8,128)(2,1)S(1)}, u32[]{:S(2)}, u32[]{:S(2)}) collective-permute-start(bf16[1,2,64,256]{3,2,1,0:T(8,128)(2,1)S(1)} %get-tuple-element.19), channel_id=1, source_target_pairs={{0,4},{4,8},{8,12},{1,5},{5,9},{9,13},{2,6},{6,10},{10,14},{3,7},{... | collective-permute-start | bytes 196616 | tf_op jit(solution)/shard_map/ppermute | solution.py:22
  19.9 4.3 %collective-permute-start.5 = (f32[1,8,256]{2,0,1:T(1,128)S(1)}, f32[1,8,256]{2,0,1:T(1,128)S(1)}, u32[]{:S(2)}, u32[]{:S(2)}) collective-permute-start(f32[1,8,256]{2,0,1:T(1,128)S(1)} %reduce_sum.23), channel_id=1, source_target_pairs={{0,2},{1,3},{2,0},{3,1},{4,6},{5,7},{6,4},{7,5},{8,10},{9,11},{10,... | collective-permute-start | bytes 24584 | tf_op jit(solution)/shard_map/ppermute | solution.py:42
  21.9 2.3 %collective-permute-start.6 = (f32[1,8,256]{2,0,1:T(1,128)S(1)}, f32[1,8,256]{2,0,1:T(1,128)S(1)}, u32[]{:S(2)}, u32[]{:S(2)}) collective-permute-start(f32[1,8,256]{2,0,1:T(1,128)S(1)} %reduce_sum.23), channel_id=1, source_target_pairs={{0,3},{1,0},{2,1},{3,2},{4,7},{5,4},{6,5},{7,6},{8,11},{9,8},{10,9... | collective-permute-start | bytes 24584 | tf_op jit(solution)/shard_map/ppermute | solution.py:42
  21.9 3.1 %collective-permute-start.4 = (f32[1,8,256]{2,0,1:T(1,128)S(1)}, f32[1,8,256]{2,0,1:T(1,128)S(1)}, u32[]{:S(2)}, u32[]{:S(2)}) collective-permute-start(f32[1,8,256]{2,0,1:T(1,128)S(1)} %reduce_sum.23), channel_id=1, source_target_pairs={{0,1},{1,2},{2,3},{3,0},{4,5},{5,6},{6,7},{7,4},{8,9},{9,10},{10,1... | collective-permute-start | bytes 24584 | tf_op jit(solution)/shard_map/ppermute | solution.py:42
  22.4 4.0 %collective-permute-start.2 = (bf16[1,8,16,256]{3,2,1,0:T(8,128)(2,1)S(1)}, bf16[1,8,16,256]{3,2,1,0:T(8,128)(2,1)S(1)}, u32[]{:S(2)}, u32[]{:S(2)}) collective-permute-start(bf16[1,8,16,256]{3,2,1,0:T(8,128)(2,1)S(1)} %get-tuple-element.14), channel_id=1, source_target_pairs={{0,1},{1,2},{2,3},{3,0},{4,5},{5,6},{6,7},{7,4},{8,9},{9,10},{10,1... | collective-permute-start | bytes 196616 | tf_op jit(solution)/shard_map/ppermute | solution.py:22
  22.7 3.8 %collective-permute-start.3 = (bf16[1,8,16,256]{3,2,1,0:T(8,128)(2,1)S(1)}, bf16[1,8,16,256]{3,2,1,0:T(8,128)(2,1)S(1)}, u32[]{:S(2)}, u32[]{:S(2)}) collective-permute-start(bf16[1,8,16,256]{3,2,1,0:T(8,128)(2,1)S(1)} %get-tuple-element.15), channel_id=1, source_target_pairs={{1,0},{2,1},{3,2},{0,3},{5,4},{6,5},{7,6},{4,7},{9,8},{10,9},{11,1... | collective-permute-start | bytes 196616 | tf_op jit(solution)/shard_map/ppermute | solution.py:25
  25.6 5.3 %copy-start.4 = (bf16[1,4,64,256]{3,2,1,0:T(8,128)(2,1)S(1)}, bf16[1,4,64,256]{3,2,1,0:T(8,128)(2,1)}, u32[]{:S(2)}) copy-start(bf16[1,4,64,256]{3,2,1,0:T(8,128)(2,1)} %param.9) | copy-start | bytes 393220
  34.1 6.2 %copy-start.8 = (s32[16,12]{1,0:T(8,128)S(1)}, s32[16,12]{1,0:T(8,128)}, u32[]{:S(2)}) copy-start(s32[16,12]{1,0:T(8,128)} %param.12) | copy-start | bytes 2308
  34.1 6.2 %copy-start.9 = (s32[16,12]{1,0:T(8,128)S(1)}, s32[16,12]{1,0:T(8,128)}, u32[]{:S(2)}) copy-start(s32[16,12]{1,0:T(8,128)} %param.11) | copy-start | bytes 2308
  34.1 6.9 %copy-start.1 = (bf16[9,256,256]{2,1,0:T(8,128)(2,1)S(1)}, bf16[9,256,256]{2,1,0:T(8,128)(2,1)}, u32[]{:S(2)}) copy-start(bf16[9,256,256]{2,1,0:T(8,128)(2,1)} %param.10) | copy-start | bytes 3538948
  34.1 8.9 %collective-permute-start.8 = (bf16[1,2,64,256]{3,2,1,0:T(8,128)(2,1)S(1)}, bf16[1,2,64,256]{3,2,1,0:T(8,128)(2,1)S(1)}, u32[]{:S(2)}, u32[]{:S(2)}) collective-permute-start(bf16[1,2,64,256]{3,2,1,0:T(8,128)(2,1)S(1)} %get-tuple-element.16), channel_id=1, source_target_pairs={{4,0},{8,4},{12,8},{5,1},{9,5},{13,9},{6,2},{10,6},{14,10},{7,3},{... | collective-permute-start | bytes 196616 | tf_op jit(solution)/shard_map/ppermute | solution.py:25
  35.6 7.5 %collective-permute-start.7 = (bf16[1,2,64,256]{3,2,1,0:T(8,128)(2,1)S(1)}, bf16[1,2,64,256]{3,2,1,0:T(8,128)(2,1)S(1)}, u32[]{:S(2)}, u32[]{:S(2)}) collective-permute-start(bf16[1,2,64,256]{3,2,1,0:T(8,128)(2,1)S(1)} %get-tuple-element.17), channel_id=1, source_target_pairs={{0,4},{4,8},{8,12},{1,5},{5,9},{9,13},{2,6},{6,10},{10,14},{3,7},{... | collective-permute-start | bytes 196616 | tf_op jit(solution)/shard_map/ppermute | solution.py:22
  40.9 0.8 copy-start.6
  41.0 1.5 %copy-start.5 = (s32[16,12]{1,0:T(8,128)S(1)}, s32[16,12]{1,0:T(8,128)}, u32[]{:S(2)}) copy-start(s32[16,12]{1,0:T(8,128)} %param.13) | copy-start | bytes 2308
  41.0 1.5 %copy-start.7 = (s32[16,12]{1,0:T(8,128)S(1)}, s32[16,12]{1,0:T(8,128)}, u32[]{:S(2)}) copy-start(s32[16,12]{1,0:T(8,128)} %param.14) | copy-start | bytes 2308
  43.2 3.7 %collective-permute-start.12 = (f32[1,8,256]{2,0,1:T(1,128)S(1)}, f32[1,8,256]{2,0,1:T(1,128)S(1)}, u32[]{:S(2)}, u32[]{:S(2)}) collective-permute-start(f32[1,8,256]{2,0,1:T(1,128)S(1)} %reduce_sum.25), channel_id=1, source_target_pairs={{0,2},{1,3},{2,0},{3,1},{4,6},{5,7},{6,4},{7,5},{8,10},{9,11},{10,... | collective-permute-start | bytes 24584 | tf_op jit(solution)/shard_map/ppermute | solution.py:42
  43.2 3.6 %collective-permute-start.13 = (f32[1,8,256]{2,0,1:T(1,128)S(1)}, f32[1,8,256]{2,0,1:T(1,128)S(1)}, u32[]{:S(2)}, u32[]{:S(2)}) collective-permute-start(f32[1,8,256]{2,0,1:T(1,128)S(1)} %reduce_sum.25), channel_id=1, source_target_pairs={{0,3},{1,0},{2,1},{3,2},{4,7},{5,4},{6,5},{7,6},{8,11},{9,8},{10,9... | collective-permute-start | bytes 24584 | tf_op jit(solution)/shard_map/ppermute | solution.py:42
  44.2 3.1 %collective-permute-start.11 = (f32[1,8,256]{2,0,1:T(1,128)S(1)}, f32[1,8,256]{2,0,1:T(1,128)S(1)}, u32[]{:S(2)}, u32[]{:S(2)}) collective-permute-start(f32[1,8,256]{2,0,1:T(1,128)S(1)} %reduce_sum.25), channel_id=1, source_target_pairs={{0,1},{1,2},{2,3},{3,0},{4,5},{5,6},{6,7},{7,4},{8,9},{9,10},{10,1... | collective-permute-start | bytes 24584 | tf_op jit(solution)/shard_map/ppermute | solution.py:42
  44.3 3.9 %collective-permute-start.9 = (bf16[1,8,16,256]{3,2,1,0:T(8,128)(2,1)S(1)}, bf16[1,8,16,256]{3,2,1,0:T(8,128)(2,1)S(1)}, u32[]{:S(2)}, u32[]{:S(2)}) collective-permute-start(bf16[1,8,16,256]{3,2,1,0:T(8,128)(2,1)S(1)} %get-tuple-element.12), channel_id=1, source_target_pairs={{0,1},{1,2},{2,3},{3,0},{4,5},{5,6},{6,7},{7,4},{8,9},{9,10},{10,1... | collective-permute-start | bytes 196616 | tf_op jit(solution)/shard_map/ppermute | solution.py:22
  46.0 2.1 %collective-permute-start.10 = (bf16[1,8,16,256]{3,2,1,0:T(8,128)(2,1)S(1)}, bf16[1,8,16,256]{3,2,1,0:T(8,128)(2,1)S(1)}, u32[]{:S(2)}, u32[]{:S(2)}) collective-permute-start(bf16[1,8,16,256]{3,2,1,0:T(8,128)(2,1)S(1)} %get-tuple-element.13), channel_id=1, source_target_pairs={{1,0},{2,1},{3,2},{0,3},{5,4},{6,5},{7,6},{4,7},{9,8},{10,9},{11,1... | collective-permute-start | bytes 196616 | tf_op jit(solution)/shard_map/ppermute | solution.py:25
  47.9 11.3 %copy-start = (bf16[1,4,64,2304]{3,2,1,0:T(8,128)(2,1)S(1)}, bf16[1,4,64,2304]{3,2,1,0:T(8,128)(2,1)}, u32[]{:S(2)}) copy-start(bf16[1,4,64,2304]{3,2,1,0:T(8,128)(2,1)} %shard_map.103) | copy-start | bytes 3538948
  60.5 13.3 %copy-start.2 = (bf16[1,4,64,2304]{3,2,1,0:T(8,128)(2,1)S(1)}, bf16[1,4,64,2304]{3,2,1,0:T(8,128)(2,1)}, u32[]{:S(2)}) copy-start(bf16[1,4,64,2304]{3,2,1,0:T(8,128)(2,1)} %shard_map.104) | copy-start | bytes 3538948
  69.2 11.8 %collective-permute-start.14 = (f32[9,64,64]{1,2,0:T(8,128)S(1)}, f32[9,64,64]{1,2,0:T(8,128)S(1)}, u32[]{:S(2)}, u32[]{:S(2)}) collective-permute-start(f32[9,64,64]{1,2,0:T(8,128)S(1)} %get-tuple-element.9), channel_id=1, source_target_pairs={{0,4},{4,8},{8,12},{12,0},{1,5},{5,9},{9,13},{13,1},{2,6},{6,10},{... | collective-permute-start | bytes 442376 | tf_op jit(solution)/shard_map/ppermute | solution.py:59
  70.7 14.8 %collective-permute-start.16 = (f32[9,64,64]{1,2,0:T(8,128)S(1)}, f32[9,64,64]{1,2,0:T(8,128)S(1)}, u32[]{:S(2)}, u32[]{:S(2)}) collective-permute-start(f32[9,64,64]{1,2,0:T(8,128)S(1)} %get-tuple-element.10), channel_id=1, source_target_pairs={{0,12},{4,0},{8,4},{12,8},{1,13},{5,1},{9,5},{13,9},{2,14},{6,2},{... | collective-permute-start | bytes 442376 | tf_op jit(solution)/shard_map/ppermute | solution.py:59
  73.1 25.8 %collective-permute-start.15 = (f32[9,64,64]{1,2,0:T(8,128)S(1)}, f32[9,64,64]{1,2,0:T(8,128)S(1)}, u32[]{:S(2)}, u32[]{:S(2)}) collective-permute-start(f32[9,64,64]{1,2,0:T(8,128)S(1)} %get-tuple-element.11), channel_id=1, source_target_pairs={{0,8},{4,12},{8,0},{12,4},{1,9},{5,13},{9,1},{13,5},{2,10},{6,14},... | collective-permute-start | bytes 442376 | tf_op jit(solution)/shard_map/ppermute | solution.py:59
  73.7 25.1 %copy-start.3 = (f32[9,256,64]{1,2,0:T(8,128)S(1)}, f32[9,256,64]{1,2,0:T(8,128)}, u32[]{:S(2)}) copy-start(f32[9,256,64]{1,2,0:T(8,128)} %reduce-scatter.2.cloned.1.call-done) | copy-start | bytes 1769476
Sparse Core Ops, SparseCore 0:
  34.2 33.4 reduce-scatter.1

commit v3 on v0

--- a/solution.py
+++ b/solution.py
@@ -34,9 +34,18 @@
     return jnp.pad(grid_field, ((0, 0), (0, 0), (0, extra), (0, 0)))
 
 
+def ring_sum(value, axis):
+    count = lax.axis_size(axis)
+    total = value
+    for shift in range(1, count):
+        pairs = [(i, (i + shift) % count) for i in range(count)]
+        total = total + lax.ppermute(value, axis, pairs)
+    return total
+
+
 def cycle_totals(widened, lon_count):
     interior = lax.slice_in_dim(widened, RIM, RIM + lon_count, axis=2)
-    return lax.psum(jnp.sum(interior, axis=2, dtype=jnp.float32), "lon")
+    return ring_sum(jnp.sum(interior, axis=2, dtype=jnp.float32), "lon")
 
 
 def filter_kernel(
@@ -79,9 +88,8 @@
         out_ref[0, 0, :, k * channels:(k + 1) * channels] = acc_ref[k].astype(jnp.bfloat16)
 
 
-def run_filter(tables, field, totals, lon_count, lon_total, backward):
+def run_filter(tables, field, totals, row_count, lon_count, lon_total, backward):
     members, window, padded, channels = field.shape
-    row_count = window - 2 * REACH
     slots = tables[1].shape[1]
     smem = pl.BlockSpec(memory_space=pltpu.SMEM)
     kernel = functools.partial(
@@ -134,7 +142,7 @@
         rows_of(basis_idx, first_row, row_count),
         rows_of(weighting, first_row, row_count),
     )
-    flattened = run_filter(f_tables, widened, totals, lon_count, lon_total, False)
+    flattened = run_filter(f_tables, widened, totals, row_count, lon_count, lon_total, False)
     w_fwd = weight.reshape(BASIS * channels, channels)
     response = jnp.einsum("brwq,qo->brwo", flattened, w_fwd, preferred_element_type=jnp.float32)
 
@@ -148,18 +156,44 @@
     b_hit = b_src[None, :, :] == targets[:, None, None]
     b_weights = jnp.where(b_hit, b_scale[None], 0.0).reshape(row_count, -1)
     b_tables = (b_src, b_start, b_span, b_basis, b_weights)
-    back_filtered = run_filter(b_tables, grad_wide, grad_totals, lon_count, lon_total, True)
+    back_filtered = run_filter(
+        b_tables, grad_wide, grad_totals, row_count, lon_count, lon_total, True
+    )
     w_back = jnp.transpose(weight, (0, 2, 1)).reshape(BASIS * channels, channels)
     grad_input = jnp.einsum(
         "bpwq,qc->bpwc", back_filtered, w_back, preferred_element_type=jnp.float32
     )
-    partial_value = jnp.einsum(
-        "brwq,brwo->qo", flattened, cotangent, preferred_element_type=jnp.float32
-    )
-    partial_value = partial_value.reshape(BASIS, channels, channels)
-    reduced = lax.psum_scatter(partial_value, "lon", scatter_dimension=2, tiled=True)
-    reduced = lax.psum_scatter(reduced, "lat", scatter_dimension=1, tiled=True)
-    grad_weight = reduced / jnp.sqrt(jnp.float32(members * height * lon_total))
+    lat_parts = lax.axis_size("lat")
+    lon_parts = lax.axis_size("lon")
+    in_block = lax.all_to_all(inputs, "lat", 3, 1, tiled=True)
+    in_block = lax.all_gather(in_block, "lon", axis=2, tiled=True)
+    out_block = lax.all_to_all(cotangent, "lon", 3, 2, tiled=True)
+    out_block = lax.all_gather(out_block, "lat", axis=1, tiled=True)
+    c_part = channels // lat_parts
+    o_part = channels // lon_parts
+    ring = jnp.concatenate(
+        [in_block[:, :, lon_total - RIM:], in_block, in_block[:, :, :RIM]], axis=2
+    )
+    span_wide = lon_count + 2 * RIM
+    stacked = jnp.concatenate(
+        [
+            jnp.pad(
+                ring[:, :, q * lon_count:q * lon_count + span_wide],
+                ((0, 0), (0, 0), (0, padded - span_wide), (0, 0)),
+            )
+            for q in range(lon_parts)
+        ],
+        axis=3,
+    )
+    ring_totals = jnp.tile(jnp.sum(in_block, axis=2, dtype=jnp.float32), (1, 1, lon_parts))
+    g_tables = (src_rows, lon_start, lon_span, basis_idx, weighting)
+    every = run_filter(g_tables, stacked, ring_totals, height, lon_count, lon_total, False)
+    every = every.reshape(members, height, lon_count, BASIS, lon_parts, c_part)
+    right = out_block.reshape(members, height, lon_parts, lon_count, o_part)
+    block_value = jnp.einsum(
+        "bhwkqc,bhqwo->kco", every, right, preferred_element_type=jnp.float32
+    )
+    grad_weight = block_value / jnp.sqrt(jnp.float32(members * height * lon_total))
     return (response, grad_input, grad_weight)
 
 

time: 117 us -> 136 us (1.16)
  waiting for transfers between devices: 36.3 us -> 0.04 us
  local copies, waits for them, and re-layouts: 14.5 us -> 33.3 us
  blocking collectives: 10.9 us -> 26.1 us
  between operations: 14.3 us -> 0.92 us
  starting transfers between devices: 16.4 us -> 29.5 us
  Pallas kernels: 13.8 us -> 24.2 us
  matrix products: 5.58 us -> 11.9 us
  other arithmetic: 4.47 us -> 9.5 us
    reduce_scatter x1 -> x0, waiting for transfers between devices: 32.5 us -> none  [on_device(): lax.psum_scatter(partial_value, 'lon', scatter_dimension=2, tiled=True)]
    all_gather x0 -> x2, blocking collectives: none -> 26.1 us  [the longest x1 16.4 us: on_device(): out_block = lax.all_gather(out_block, 'lat', axis=1, tiled=True)]
    another operation x0 -> x3, local copies, waits for them, and re-layouts: none -> 15 us
    psum x1 -> x0, blocking collectives: 10.9 us -> none  [cycle_totals(): return lax.psum(jnp.sum(interior, axis=2, dtype=jnp.float32), 'lon')]
    pallas_call x2 -> x3, Pallas kernels: 13.8 us -> 24.2 us  [run_filter(): pl.pallas_call(kernel, grid=(members, row_count), in_specs=[smem] * 5 + [...]
    all_to_all x0 -> x2, starting transfers between devices: none -> 9.26 us  [the longest x1 5.93 us: on_device(): in_block = lax.all_to_all(inputs, 'lat', 3, 1, tiled=True)]
    ppermute x0 -> x6, starting transfers between devices: none -> 5.32 us  [ring_sum(): total = total + lax.ppermute(value, axis, pairs)]
    dot_general x1, matrix products: 3.22 us -> 7 us  [on_device(): jnp.einsum('bhwkqc,bhqwo->kco', every, right, preferred_element_type=jnp....]
  transfers between devices with their start and end apart: 10 -> 16, of which waited for: 3 -> 0; matrix products, arithmetic and copies ran while one was open for 11% -> 21% of each run, Pallas kernels for 9% -> 10%
where the time goes in v3:
time: 136 us; the launch traced here: 135 us
  local copies, waits for them, and re-layouts  33.3 us (24%)
  starting transfers between devices  29.5 us (22%)
  blocking collectives  26.1 us (19%)
  Pallas kernels  24.2 us (18%)
  matrix products  11.9 us (9%)
  other arithmetic  9.5 us (7%)
    pallas_call x3, Pallas kernels, run_filter(): pl.pallas_call(kernel, grid=(members, row_count), in_specs=[smem] * 5 + [...  24.2 us
    all_gather x1, blocking collectives, on_device(): out_block = lax.all_gather(out_block, 'lat', axis=1, tiled=True)  16.4 us
    another operation x1, local copies, waits for them, and re-layouts  14.3 us
    ppermute x4, starting transfers between devices, with_halo(): lax.ppermute(lax.slice_in_dim(block, block.shape[dim] - width, None, axis...  11.5 us
    all_gather x1, blocking collectives, on_device(): in_block = lax.all_gather(in_block, 'lon', axis=2, tiled=True)  9.75 us
    dot_general x1, matrix products, on_device(): jnp.einsum('bhwkqc,bhqwo->kco', every, right, preferred_element_type=jnp....  7 us
    unnamed x25, local copies, waits for them, and re-layouts  6.92 us
    all_to_all x1, starting transfers between devices, on_device(): in_block = lax.all_to_all(inputs, 'lat', 3, 1, tiled=True)  5.93 us
  transfers between devices with their start and end apart: 16, of which 0 were waited for; matrix products, arithmetic and copies ran while one was open for 21% of the time, Pallas kernels for 10%

profile of v3, /device:TPU:0, one launch (start us, length us, event | category | flops | bytes accessed | tf_op | source)
XLA Modules:
  0.0 135.5 jit_solution(13643378952870772608)
XLA Ops:
  0.6 1.0 fusion.45
  1.6 4.9 %collective-permute-start.7 = (bf16[1,2,64,256]{3,2,1,0:T(8,128)(2,1)S(1)}, bf16[1,2,64,256]{3,2,1,0:T(8,128)(2,1)S(1)}, u32[]{:S(2)}, u32[]{:S(2)}) collective-permute-start(bf16[1,2,64,256]{3,2,1,0:T(8,128)(2,1)S(1)} %get-tuple-element.14), channel_id=1, source_target_pairs={{0,4},{4,8},{8,12},{1,5},{5,9},{9,13},{2,6},{6,10},{10,14},{3,7},{... | collective-permute-start | bytes 196616 | tf_op jit(solution)/shard_map/ppermute | solution.py:22
  6.6 1.3 collective-permute-start.8
  7.9 1.5 %fusion.46 = (bf16[1,2,64,256]{3,2,1,0:T(8,128)(2,1)}, bf16[1,2,64,256]{3,2,1,0:T(8,128)(2,1)S(1)}) fusion(bf16[1,4,64,256]{3,2,1,0:T(8,128)(2,1)} %param.8), kind=kLoop, calls=%fused_computation.69 | loop fusion | bytes 262144 | tf_op jit(solution)/shard_map/slice | solution.py:25
  9.4 5.2 %collective-permute-start = (bf16[1,2,64,256]{3,2,1,0:T(8,128)(2,1)S(1)}, bf16[1,2,64,256]{3,2,1,0:T(8,128)(2,1)}, u32[]{:S(2)}, u32[]{:S(2)}) collective-permute-start(bf16[1,2,64,256]{3,2,1,0:T(8,128)(2,1)S(1)} %get-tuple-element.16), channel_id=1, source_target_pairs={{0,4},{4,8},{8,12},{1,5},{5,9},{9,13},{2,6},{6,10},{10,14},{3,7},{... | collective-permute-start | bytes 196616 | tf_op jit(solution)/shard_map/ppermute | solution.py:22
  14.5 1.3 collective-permute-start.1
  15.8 1.1 copy.21
  16.9 0.0 copy-start.1
  16.9 0.9 reshape.121
  17.8 3.3 %all-to-all-start.1 = ((bf16[4,2,8192]{2,1,0:T(2,128)(2,1)}), bf16[4,2,8192]{2,1,0:T(2,128)(2,1)S(1)}, u32[]{:S(2)}, u32[]{:S(2)}) async-start(bf16[4,2,8192]{2,1,0:T(2,128)(2,1)} %reshape.121), calls=%async_computation.1 | async-start | bytes 262144 | tf_op jit(solution)/shard_map/all_to_all | solution.py:170
  21.2 1.3 pad_dynamic-slice_fusion.3
  22.5 1.3 constant_dynamic-slice_fusion.3
  23.8 1.3 pad_dynamic-slice_fusion.1
  25.1 1.3 constant_dynamic-slice_fusion.1
  26.4 1.1 copy.19
  27.5 0.8 rsqrt_multiply_fusion.scale_ref
  28.3 0.1 broadcast_in_dim.24
  28.4 0.1 eq.16
  28.5 0.7 copy.18
  29.2 0.9 reshape.123
  30.1 0.7 compare_select_fusion.scale_ref
  30.7 0.6 constant_dynamic-slice_fusion.scale_ref
  31.4 0.1 convert_reduce_fusion.1
  31.5 0.5 collective-permute-start.11
  32.0 1.7 %collective-permute-start.12 = (f32[1,8,256]{2,0,1:T(1,128)S(1)}, f32[1,8,256]{2,0,1:T(1,128)S(1)}, u32[]{:S(2)}, u32[]{:S(2)}) collective-permute-start(f32[1,8,256]{2,0,1:T(1,128)S(1)} %reduce_sum.34), channel_id=1, source_target_pairs={{0,2},{1,3},{2,0},{3,1},{4,6},{5,7},{6,4},{7,5},{8,10},{9,11},{10,... | collective-permute-start | bytes 24584 | tf_op jit(solution)/shard_map/ppermute | solution.py:42
  33.6 1.3 collective-permute-start.13
  34.9 0.6 fusion.43
  35.6 0.8 constant_dynamic-update-slice_fusion.2
  36.5 0.8 constant_dynamic-update-slice_fusion
  37.3 0.1 convert_reduce_fusion.2
  37.4 0.1 collective-permute-start.4
  37.5 0.4 collective-permute-start.5
  37.8 0.6 fusion.44
  38.5 1.4 %collective-permute-start.6 = (f32[1,8,256]{2,0,1:T(1,128)S(1)}, f32[1,8,256]{2,0,1:T(1,128)S(1)}, u32[]{:S(2)}, u32[]{:S(2)}) collective-permute-start(f32[1,8,256]{2,0,1:T(1,128)S(1)} %reduce_sum.32), channel_id=1, source_target_pairs={{0,3},{1,0},{2,1},{3,2},{4,7},{5,4},{6,5},{7,6},{8,11},{9,8},{10,9... | collective-permute-start | bytes 24584 | tf_op jit(solution)/shard_map/ppermute | solution.py:42
  39.9 0.4 collective-permute-start.10
  40.3 0.1 collective-permute-start.9
  40.4 0.6 add_bitcast_fusion.total_ref
  41.0 1.4 %collective-permute-start.2 = (bf16[1,8,16,256]{3,2,1,0:T(8,128)(2,1)}, bf16[1,8,16,256]{3,2,1,0:T(8,128)(2,1)}, u32[]{:S(2)}, u32[]{:S(2)}) collective-permute-start(bf16[1,8,16,256]{3,2,1,0:T(8,128)(2,1)} %get-tuple-element.11), channel_id=1, source_target_pairs={{0,1},{1,2},{2,3},{3,0},{4,5},{5,6},{6,7},{7,4},{8,9},{9,10},{10,1... | collective-permute-start | bytes 196616 | tf_op jit(solution)/shard_map/ppermute | solution.py:22
  42.4 0.4 collective-permute-start.3
  42.8 0.6 add_bitcast_fusion.1.total_ref
  43.4 5.9 %all-to-all-start = ((bf16[4,2,8192]{2,1,0:T(2,128)(2,1)}), bf16[4,2,8192]{2,1,0:T(2,128)(2,1)}, u32[]{:S(2)}, u32[]{:S(2)}) async-start(bf16[4,2,8192]{2,1,0:T(2,128)(2,1)} %reshape.123), calls=%async_computation | async-start | bytes 262144 | tf_op jit(solution)/shard_map/all_to_all | solution.py:168
  49.3 0.2 reshape.122
  49.5 0.2 copy.22
  49.7 0.2 all_to_all.33
  50.0 16.4 %all_gather.7 = bf16[1,16,256,64]{2,3,0,1:T(8,128)(2,1)S(1)} all-gather(bf16[1,4,256,64]{2,3,0,1:T(8,128)(2,1)S(1)} %all_to_all.33), channel_id=1, replica_groups=mesh['grp'=2,'lat'=4,'lon'=4] {'lat'}, dimensions={1}, use_global_device_ids=true | all-gather | bytes 655360 | tf_op jit(solution)/shard_map/all_gather | solution.py:171
  66.3 1.3 copy.23
  67.6 1.7 %fusion.36.field_ref = bf16[1,8,128,256]{3,2,1,0:T(8,128)(2,1)} fusion(bf16[1,8,16,256]{3,2,1,0:T(8,128)(2,1)} %collective-permute-done.10, bf16[1,8,64,256]{3,2,1,0:T(8,128)(2,1)S(1)} %constant_dynamic-update-slice_fusion.3, bf16[1,8,16,256]{3,2,1,0:T(8,128)(2,1)} %collective-permute-done.9), kind=kLoop, calls=%fused_computation.35 | loop fusion | flops 2621440 | bytes 917504 | tf_op jit(solution)/shard_map/concatenate | solution.py:26
  69.3 10.6 %shard_map.104 = bf16[1,4,64,2304]{3,2,1,0:T(8,128)(2,1)} custom-call(s32[8,12]{1,0:T(8,128)} %copy-done.5, s32[8,12]{1,0:T(8,128)} %get-tuple-element.23.start_ref, s32[8,12]{1,0:T(8,128)} %get-tuple-element.22.span_ref, s32[8,12]{1,0:T(8,128)} %get-tuple-element.21.basis_ref, f32[4,96]{1,0:T(4,128)} %compare_select_fusion.scale_ref, ...), custom_call_target="tpu_custom_call" | custom-call | tf_op jit(solution)/shard_map/pallas_call | solution.py:103
  80.0 2.5 %fusion.16 = f32[1,4,64,256]{3,2,1,0:T(8,128)} fusion(bf16[2304,256,1]{1,0,2:T(8,128)(2,1)S(1)} %bitcast.54, bf16[1,4,64,2304]{3,2,1,0:T(8,128)(2,1)} %shard_map.104), kind=kOutput, calls=%fused_computation.17 | convolution fusion | flops 301989888 | bytes 2621440 | tf_op jit(solution)/shard_map/bpwq,qc->bpwc/dot_general | solution.py:163
  82.4 1.7 %fusion.34.field_ref = bf16[1,8,128,256]{3,2,1,0:T(8,128)(2,1)} fusion(bf16[1,8,16,256]{3,2,1,0:T(8,128)(2,1)} %collective-permute-done.3, bf16[1,8,64,256]{3,2,1,0:T(8,128)(2,1)S(1)} %constant_dynamic-update-slice_fusion, bf16[1,8,16,256]{3,2,1,0:T(8,128)(2,1)} %collective-permute-done.2), kind=kLoop, calls=%fused_computation.33 | loop fusion | flops 2621440 | bytes 917504 | tf_op jit(solution)/shard_map/concatenate | solution.py:26
  84.1 3.5 %shard_map.103 = bf16[1,4,64,2304]{3,2,1,0:T(8,128)(2,1)} custom-call(s32[4,12]{1,0:T(4,128)} %get-tuple-element.20.rows_ref, s32[4,12]{1,0:T(4,128)} %get-tuple-element.19.start_ref, s32[4,12]{1,0:T(4,128)} %get-tuple-element.18.span_ref, s32[4,12]{1,0:T(4,128)} %get-tuple-element.17.basis_ref, f32[4,12]{1,0:T(4,128)} %constant_dynamic-slice_fusion.scale_ref, ...), custom_call_target="tpu_custom_call" | custom-call | tf_op jit(solution)/shard_map/pallas_call | solution.py:103
  87.7 2.4 %fusion.13 = f32[1,4,64,256]{3,2,1,0:T(8,128)} fusion(bf16[2304,256,1]{1,0,2:T(8,128)(2,1)S(1)} %bitcast.53, bf16[1,4,64,2304]{3,2,1,0:T(8,128)(2,1)} %shard_map.103), kind=kOutput, calls=%fused_computation.16 | convolution fusion | flops 301989888 | bytes 2621440 | tf_op jit(solution)/shard_map/brwq,qo->brwo/dot_general | solution.py:147
  90.1 1.1 reshape.124
  91.2 0.2 copy.20
  91.4 0.0 copy-start.6
  91.4 9.8 %all_gather.6 = bf16[1,16,256,64]{3,2,1,0:T(8,128)(2,1)S(1)} all-gather(bf16[1,16,64,64]{3,2,1,0:T(8,128)(2,1)S(1)} %bitcast.55), channel_id=1, replica_groups=mesh['grp'=2,'lat'=4,'lon'=4] {'lon'}, dimensions={2}, use_global_device_ids=true | all-gather | bytes 655360 | tf_op jit(solution)/shard_map/all_gather | solution.py:169
  101.2 0.1 fusion.42
  101.3 0.2 convert_reduce_fusion
  101.5 0.7 tile.9.total_ref
  102.2 0.3 fusion.38
  102.5 1.6 %fusion.23.field_ref = bf16[1,16,128,256]{3,2,1,0:T(8,128)(2,1)} fusion(bf16[1,16,96,64]{3,2,1,0:T(8,128)(2,1)S(1)} %get-tuple-element.8, bf16[1,16,96,64]{3,2,1,0:T(8,128)(2,1)S(1)} %get-tuple-element.7, bf16[1,16,128,64]{3,2,1,0:T(8,128)(2,1)S(1)} %get-tuple-element.4, bf16[1,16,128,64]{3,2,1,0:T(8,128)(2,1)S(1)} %get-tuple-element.3), kind=kLoop, calls=%fused_computation.20 | loop fusion | flops 8388608 | bytes 1966080 | tf_op jit(solution)/shard_map/concatenate | solution.py:178
  104.1 10.1 %shard_map.105 = bf16[1,16,64,2304]{3,2,1,0:T(8,128)(2,1)} custom-call(s32[16,12]{1,0:T(8,128)} %rows_ref.1, s32[16,12]{1,0:T(8,128)} %start_ref.1, s32[16,12]{1,0:T(8,128)} %span_ref.1, s32[16,12]{1,0:T(8,128)} %basis_ref.1, f32[16,12]{1,0:T(8,128)} %copy-done.4, bf16[1,16,128,256]{3,2,1,0:T(8,128)(2,1)} %fusion.23.field_ref, f32[1,16,1,256]{3,2,1,0:T(1,128)} %tile.9.total_ref), custom_call_target="tpu_custom_call" | custom-call | tf_op jit(solution)/shard_map/pallas_call | solution.py:103
  114.2 14.3 %reshape.115 = bf16[16,64,9,4,64]{4,3,2,1,0:T(4,128)(2,1)} reshape(bf16[1,16,64,2304]{3,2,1,0:T(8,128)(2,1)} %shard_map.105) | data formatting | bytes 9437184 | tf_op jit(solution)/shard_map/reshape.10
  128.5 7.0 %fusion.19 = f32[9,64,64]{2,1,0:T(8,128)} fusion(bf16[16,4,64,64,1]{3,2,1,0,4:T(8,128)(2,1)S(1)} %bitcast.56, bf16[16,64,9,4,64]{4,3,2,1,0:T(4,128)(2,1)} %reshape.115), kind=kOutput, calls=%fused_computation.18 | convolution fusion | flops 302026752 | bytes 5390336 | tf_op jit(solution)/shard_map/bhwkqc,bhqwo->kco/dot_general | solution.py:193
  (38 shorter events, 0.1 us)
Async XLA Ops:
  0.6 27.8 %copy-start = (bf16[9,256,256]{2,1,0:T(8,128)(2,1)S(1)}, bf16[9,256,256]{2,1,0:T(8,128)(2,1)}, u32[]{:S(2)}) copy-start(bf16[9,256,256]{2,1,0:T(8,128)(2,1)} %param.10) | copy-start | bytes 3538948
  1.6 29.7 %collective-permute-start.7 = (bf16[1,2,64,256]{3,2,1,0:T(8,128)(2,1)S(1)}, bf16[1,2,64,256]{3,2,1,0:T(8,128)(2,1)S(1)}, u32[]{:S(2)}, u32[]{:S(2)}) collective-permute-start(bf16[1,2,64,256]{3,2,1,0:T(8,128)(2,1)S(1)} %get-tuple-element.14), channel_id=1, source_target_pairs={{0,4},{4,8},{8,12},{1,5},{5,9},{9,13},{2,6},{6,10},{10,14},{3,7},{... | collective-permute-start | bytes 196616 | tf_op jit(solution)/shard_map/ppermute | solution.py:22
  6.6 24.8 %collective-permute-start.8 = (bf16[1,2,64,256]{3,2,1,0:T(8,128)(2,1)S(1)}, bf16[1,2,64,256]{3,2,1,0:T(8,128)(2,1)S(1)}, u32[]{:S(2)}, u32[]{:S(2)}) collective-permute-start(bf16[1,2,64,256]{3,2,1,0:T(8,128)(2,1)S(1)} %get-tuple-element.13), channel_id=1, source_target_pairs={{4,0},{8,4},{12,8},{5,1},{9,5},{13,9},{6,2},{10,6},{14,10},{7,3},{... | collective-permute-start | bytes 196616 | tf_op jit(solution)/shard_map/ppermute | solution.py:25
  9.4 26.2 %collective-permute-start = (bf16[1,2,64,256]{3,2,1,0:T(8,128)(2,1)S(1)}, bf16[1,2,64,256]{3,2,1,0:T(8,128)(2,1)}, u32[]{:S(2)}, u32[]{:S(2)}) collective-permute-start(bf16[1,2,64,256]{3,2,1,0:T(8,128)(2,1)S(1)} %get-tuple-element.16), channel_id=1, source_target_pairs={{0,4},{4,8},{8,12},{1,5},{5,9},{9,13},{2,6},{6,10},{10,14},{3,7},{... | collective-permute-start | bytes 196616 | tf_op jit(solution)/shard_map/ppermute | solution.py:22
  14.5 21.9 %collective-permute-start.1 = (bf16[1,2,64,256]{3,2,1,0:T(8,128)(2,1)}, bf16[1,2,64,256]{3,2,1,0:T(8,128)(2,1)}, u32[]{:S(2)}, u32[]{:S(2)}) collective-permute-start(bf16[1,2,64,256]{3,2,1,0:T(8,128)(2,1)} %get-tuple-element.15), channel_id=1, source_target_pairs={{4,0},{8,4},{12,8},{5,1},{9,5},{13,9},{6,2},{10,6},{14,10},{7,3},{... | collective-permute-start | bytes 196616 | tf_op jit(solution)/shard_map/ppermute | solution.py:25
  16.9 14.4 %copy-start.1 = (bf16[1,4,64,256]{3,2,1,0:T(8,128)(2,1)S(1)}, bf16[1,4,64,256]{3,2,1,0:T(8,128)(2,1)}, u32[]{:S(2)}) copy-start(bf16[1,4,64,256]{3,2,1,0:T(8,128)(2,1)} %param.9) | copy-start | bytes 393220
  17.8 25.6 %all-to-all-start.1 = ((bf16[4,2,8192]{2,1,0:T(2,128)(2,1)}), bf16[4,2,8192]{2,1,0:T(2,128)(2,1)S(1)}, u32[]{:S(2)}, u32[]{:S(2)}) async-start(bf16[4,2,8192]{2,1,0:T(2,128)(2,1)} %reshape.121), calls=%async_computation.1 | async-start | bytes 262144 | tf_op jit(solution)/shard_map/all_to_all | solution.py:170
  22.5 13.1 %copy-start.5 = (s32[8,12]{1,0:T(8,128)}, s32[8,12]{1,0:T(8,128)S(1)}, u32[]{:S(2)}) copy-start(s32[8,12]{1,0:T(8,128)S(1)} %get-tuple-element.24.rows_ref) | copy-start | bytes 1156
  27.5 8.9 %copy-start.2 = (bf16[1,4,64,256]{3,2,1,0:T(8,128)(2,1)S(1)}, bf16[1,4,64,256]{3,2,1,0:T(8,128)(2,1)}, u32[]{:S(2)}) copy-start(bf16[1,4,64,256]{3,2,1,0:T(8,128)(2,1)} %param.8) | copy-start | bytes 393220
  28.3 8.2 %copy-start.4 = (f32[16,12]{1,0:T(8,128)}, f32[16,12]{1,0:T(8,128)S(1)}, u32[]{:S(2)}) copy-start(f32[16,12]{1,0:T(8,128)S(1)} %rsqrt_multiply_fusion.scale_ref) | copy-start | bytes 2308
  31.5 7.0 %collective-permute-start.11 = (f32[1,8,256]{2,0,1:T(1,128)S(1)}, f32[1,8,256]{2,0,1:T(1,128)S(1)}, u32[]{:S(2)}, u32[]{:S(2)}) collective-permute-start(f32[1,8,256]{2,0,1:T(1,128)S(1)} %reduce_sum.34), channel_id=1, source_target_pairs={{0,1},{1,2},{2,3},{3,0},{4,5},{5,6},{6,7},{7,4},{8,9},{9,10},{10,1... | collective-permute-start | bytes 24584 | tf_op jit(solution)/shard_map/ppermute | solution.py:42
  32.0 7.9 %collective-permute-start.12 = (f32[1,8,256]{2,0,1:T(1,128)S(1)}, f32[1,8,256]{2,0,1:T(1,128)S(1)}, u32[]{:S(2)}, u32[]{:S(2)}) collective-permute-start(f32[1,8,256]{2,0,1:T(1,128)S(1)} %reduce_sum.34), channel_id=1, source_target_pairs={{0,2},{1,3},{2,0},{3,1},{4,6},{5,7},{6,4},{7,5},{8,10},{9,11},{10,... | collective-permute-start | bytes 24584 | tf_op jit(solution)/shard_map/ppermute | solution.py:42
  33.6 6.7 %collective-permute-start.13 = (f32[1,8,256]{2,0,1:T(1,128)S(1)}, f32[1,8,256]{2,0,1:T(1,128)S(1)}, u32[]{:S(2)}, u32[]{:S(2)}) collective-permute-start(f32[1,8,256]{2,0,1:T(1,128)S(1)} %reduce_sum.34), channel_id=1, source_target_pairs={{0,3},{1,0},{2,1},{3,2},{4,7},{5,4},{6,5},{7,6},{8,11},{9,8},{10,9... | collective-permute-start | bytes 24584 | tf_op jit(solution)/shard_map/ppermute | solution.py:42
  37.4 3.6 %collective-permute-start.4 = (f32[1,8,256]{2,0,1:T(1,128)S(1)}, f32[1,8,256]{2,0,1:T(1,128)S(1)}, u32[]{:S(2)}, u32[]{:S(2)}) collective-permute-start(f32[1,8,256]{2,0,1:T(1,128)S(1)} %reduce_sum.32), channel_id=1, source_target_pairs={{0,1},{1,2},{2,3},{3,0},{4,5},{5,6},{6,7},{7,4},{8,9},{9,10},{10,1... | collective-permute-start | bytes 24584 | tf_op jit(solution)/shard_map/ppermute | solution.py:42
  37.5 4.9 %collective-permute-start.5 = (f32[1,8,256]{2,0,1:T(1,128)S(1)}, f32[1,8,256]{2,0,1:T(1,128)S(1)}, u32[]{:S(2)}, u32[]{:S(2)}) collective-permute-start(f32[1,8,256]{2,0,1:T(1,128)S(1)} %reduce_sum.32), channel_id=1, source_target_pairs={{0,2},{1,3},{2,0},{3,1},{4,6},{5,7},{6,4},{7,5},{8,10},{9,11},{10,... | collective-permute-start | bytes 24584 | tf_op jit(solution)/shard_map/ppermute | solution.py:42
  38.5 4.3 %collective-permute-start.6 = (f32[1,8,256]{2,0,1:T(1,128)S(1)}, f32[1,8,256]{2,0,1:T(1,128)S(1)}, u32[]{:S(2)}, u32[]{:S(2)}) collective-permute-start(f32[1,8,256]{2,0,1:T(1,128)S(1)} %reduce_sum.32), channel_id=1, source_target_pairs={{0,3},{1,0},{2,1},{3,2},{4,7},{5,4},{6,5},{7,6},{8,11},{9,8},{10,9... | collective-permute-start | bytes 24584 | tf_op jit(solution)/shard_map/ppermute | solution.py:42
  39.9 27.7 %collective-permute-start.10 = (bf16[1,8,16,256]{3,2,1,0:T(8,128)(2,1)}, bf16[1,8,16,256]{3,2,1,0:T(8,128)(2,1)}, u32[]{:S(2)}, u32[]{:S(2)}) collective-permute-start(bf16[1,8,16,256]{3,2,1,0:T(8,128)(2,1)} %get-tuple-element.10), channel_id=1, source_target_pairs={{1,0},{2,1},{3,2},{0,3},{5,4},{6,5},{7,6},{4,7},{9,8},{10,9},{11,1... | collective-permute-start | bytes 196616 | tf_op jit(solution)/shard_map/ppermute | solution.py:25
  40.3 27.3 %collective-permute-start.9 = (bf16[1,8,16,256]{3,2,1,0:T(8,128)(2,1)}, bf16[1,8,16,256]{3,2,1,0:T(8,128)(2,1)}, u32[]{:S(2)}, u32[]{:S(2)}) collective-permute-start(bf16[1,8,16,256]{3,2,1,0:T(8,128)(2,1)} %get-tuple-element.9), channel_id=1, source_target_pairs={{0,1},{1,2},{2,3},{3,0},{4,5},{5,6},{6,7},{7,4},{8,9},{9,10},{10,1... | collective-permute-start | bytes 196616 | tf_op jit(solution)/shard_map/ppermute | solution.py:22
  41.0 41.4 %collective-permute-start.2 = (bf16[1,8,16,256]{3,2,1,0:T(8,128)(2,1)}, bf16[1,8,16,256]{3,2,1,0:T(8,128)(2,1)}, u32[]{:S(2)}, u32[]{:S(2)}) collective-permute-start(bf16[1,8,16,256]{3,2,1,0:T(8,128)(2,1)} %get-tuple-element.11), channel_id=1, source_target_pairs={{0,1},{1,2},{2,3},{3,0},{4,5},{5,6},{6,7},{7,4},{8,9},{9,10},{10,1... | collective-permute-start | bytes 196616 | tf_op jit(solution)/shard_map/ppermute | solution.py:22
  42.4 40.1 %collective-permute-start.3 = (bf16[1,8,16,256]{3,2,1,0:T(8,128)(2,1)}, bf16[1,8,16,256]{3,2,1,0:T(8,128)(2,1)}, u32[]{:S(2)}, u32[]{:S(2)}) collective-permute-start(bf16[1,8,16,256]{3,2,1,0:T(8,128)(2,1)} %get-tuple-element.12), channel_id=1, source_target_pairs={{1,0},{2,1},{3,2},{0,3},{5,4},{6,5},{7,6},{4,7},{9,8},{10,9},{11,1... | collective-permute-start | bytes 196616 | tf_op jit(solution)/shard_map/ppermute | solution.py:25
  43.4 46.7 %all-to-all-start = ((bf16[4,2,8192]{2,1,0:T(2,128)(2,1)}), bf16[4,2,8192]{2,1,0:T(2,128)(2,1)}, u32[]{:S(2)}, u32[]{:S(2)}) async-start(bf16[4,2,8192]{2,1,0:T(2,128)(2,1)} %reshape.123), calls=%async_computation | async-start | bytes 262144 | tf_op jit(solution)/shard_map/all_to_all | solution.py:168
  91.4 10.8 %copy-start.6 = (pred[128]{0:T(512)(128)(4,1)S(1)}, pred[128]{0:T(512)(128)(4,1)}, u32[]{:S(2)}) copy-start(pred[128]{0:T(512)(128)(4,1)} %constant.26.clone.1) | copy-start | bytes 388
  114.2 14.3 %copy-start.3 = (bf16[1,16,256,64]{3,2,1,0:T(8,128)(2,1)S(1)}, bf16[1,16,256,64]{3,2,1,0:T(8,128)(2,1)}, u32[]{:S(2)}) copy-start(bf16[1,16,256,64]{3,2,1,0:T(8,128)(2,1)} %copy.23) | copy-start | bytes 1572868

commit v4 on v2

--- a/solution.py
+++ b/solution.py
@@ -56,7 +56,8 @@
     for shift in range(1, count):
         pairs = [(i, (i + shift) % count) for i in range(count)]
         piece = lax.dynamic_slice_in_dim(value, ((own + shift) % count) * block, block, dim)
-        total = total + lax.ppermute(piece, axis, pairs)
+        sent = lax.ppermute(piece.astype(jnp.bfloat16), axis, pairs)
+        total = total + sent.astype(jnp.float32)
     return total
 
 
@@ -178,7 +179,7 @@
         "brwq,brwo->qo", flattened, cotangent, preferred_element_type=jnp.float32
     )
     partial_value = partial_value.reshape(BASIS, channels, channels)
-    reduced = lax.psum_scatter(partial_value, "lon", scatter_dimension=2, tiled=True)
+    reduced = ring_scatter(partial_value, "lon", 2)
     reduced = ring_scatter(reduced, "lat", 1)
     grad_weight = reduced / jnp.sqrt(jnp.float32(members * height * lon_total))
     return (response, grad_input, grad_weight)

time: 107 us -> 80.6 us (0.75)
  waiting for transfers between devices: 34.2 us -> 12.7 us
  between operations: 14.3 us -> 0.88 us
  local copies, waits for them, and re-layouts: 8.24 us -> 11.8 us
  starting transfers between devices: 24.7 us -> 27.5 us
  other arithmetic: 5.85 us -> 8.23 us
    ppermute x3 -> x6, waiting for transfers between devices: 23.9 us -> 11.3 us  [ring_scatter(): sent = lax.ppermute(piece.astype(jnp.bfloat16), axis, pairs)]
    reduce_scatter x1 -> x0, waiting for transfers between devices: 7.28 us -> none  [on_device(): lax.psum_scatter(partial_value, 'lon', scatter_dimension=2, tiled=True)]
    ppermute x3 -> x6, starting transfers between devices: 4.57 us -> 7.94 us  [ring_scatter(): sent = lax.ppermute(piece.astype(jnp.bfloat16), axis, pairs)]
    ppermute x4, starting transfers between devices: 12.2 us -> 9.49 us  [with_halo(): lax.ppermute(lax.slice_in_dim(block, block.shape[dim] - width, None, axis...]
    ppermute x6, waiting for transfers between devices: 1.96 us -> 0.02 us  [ring_sum(): total = total + lax.ppermute(value, axis, pairs)]
    ppermute x4, starting transfers between devices: 4.31 us -> 6.07 us  [with_halo(): lax.ppermute(lax.slice_in_dim(block, 0, width, axis=dim), axis, backward)]
    dot_general x1, matrix products: 3.22 us -> 1.78 us  [on_device(): jnp.einsum('brwq,brwo->qo', flattened, cotangent, preferred_element_type=...]
    dynamic_slice x1 -> x0, local copies, waits for them, and re-layouts: 1.43 us -> none  [ring_scatter(): lax.dynamic_slice_in_dim(value, (own + shift) % count * block, block, dim)]
  transfers between devices with their start and end apart: 18 -> 20, of which waited for: 9 -> 4; matrix products, arithmetic and copies ran while one was open for 11% -> 27% of each run, Pallas kernels for 10% -> 17%
where the time goes in v4:
time: 80.6 us; the launch traced here: 79.9 us
  starting transfers between devices  27.5 us (34%)
  Pallas kernels  13.4 us (17%)
  waiting for transfers between devices  12.7 us (16%)
  local copies, waits for them, and re-layouts  11.8 us (15%)
  other arithmetic  8.23 us (10%)
  matrix products  5.42 us (7%)
  between operations  0.88 us (1%)
    pallas_call x2, Pallas kernels, run_filter(): pl.pallas_call(kernel, grid=(members, row_count), in_specs=[smem] * 5 + [...  13.4 us
    ppermute x6, waiting for transfers between devices, ring_scatter(): sent = lax.ppermute(piece.astype(jnp.bfloat16), axis, pairs)  11.3 us
    ppermute x4, starting transfers between devices, with_halo(): lax.ppermute(lax.slice_in_dim(block, block.shape[dim] - width, None, axis...  9.49 us
    ppermute x6, starting transfers between devices, ring_scatter(): sent = lax.ppermute(piece.astype(jnp.bfloat16), axis, pairs)  7.94 us
    ppermute x4, starting transfers between devices, with_halo(): lax.ppermute(lax.slice_in_dim(block, 0, width, axis=dim), axis, backward)  6.07 us
    dynamic_slice x5, local copies, waits for them, and re-layouts, rows_of(): return lax.dynamic_slice_in_dim(table, begin, count, 0)  4.54 us
    ppermute x6, starting transfers between devices, ring_sum(): total = total + lax.ppermute(value, axis, pairs)  3.97 us
    unnamed x22, local copies, waits for them, and re-layouts  3.4 us
  transfers between devices with their start and end apart: 20, of which 4 were waited for; matrix products, arithmetic and copies ran while one was open for 27% of the time, Pallas kernels for 17%

profile of v4, /device:TPU:0, one launch (start us, length us, event | category | flops | bytes accessed | tf_op | source)
XLA Modules:
  0.0 79.9 jit_solution(9444081291577829961)
XLA Ops:
  0.6 0.9 %fusion.28 = (bf16[1,2,64,256]{3,2,1,0:T(8,128)(2,1)S(1)}, bf16[1,2,64,256]{3,2,1,0:T(8,128)(2,1)S(1)}) fusion(bf16[1,4,64,256]{3,2,1,0:T(8,128)(2,1)} %param.8), kind=kLoop, calls=%fused_computation.57 | loop fusion | bytes 262144 | tf_op jit(solution)/shard_map/slice | solution.py:25
  1.5 4.9 %collective-permute-start = (bf16[1,2,64,256]{3,2,1,0:T(8,128)(2,1)S(1)}, bf16[1,2,64,256]{3,2,1,0:T(8,128)(2,1)S(1)}, u32[]{:S(2)}, u32[]{:S(2)}) collective-permute-start(bf16[1,2,64,256]{3,2,1,0:T(8,128)(2,1)S(1)} %get-tuple-element.22), channel_id=1, source_target_pairs={{0,4},{4,8},{8,12},{1,5},{5,9},{9,13},{2,6},{6,10},{10,14},{3,7},{... | collective-permute-start | bytes 196616 | tf_op jit(solution)/shard_map/ppermute | solution.py:22
  6.5 1.3 %collective-permute-start.1 = (bf16[1,2,64,256]{3,2,1,0:T(8,128)(2,1)S(1)}, bf16[1,2,64,256]{3,2,1,0:T(8,128)(2,1)S(1)}, u32[]{:S(2)}, u32[]{:S(2)}) collective-permute-start(bf16[1,2,64,256]{3,2,1,0:T(8,128)(2,1)S(1)} %get-tuple-element.21), channel_id=1, source_target_pairs={{4,0},{8,4},{12,8},{5,1},{9,5},{13,9},{6,2},{10,6},{14,10},{7,3},{... | collective-permute-start | bytes 196616 | tf_op jit(solution)/shard_map/ppermute | solution.py:25
  7.8 0.9 %fusion.27 = (bf16[1,2,64,256]{3,2,1,0:T(8,128)(2,1)S(1)}, bf16[1,2,64,256]{3,2,1,0:T(8,128)(2,1)S(1)}) fusion(bf16[1,4,64,256]{3,2,1,0:T(8,128)(2,1)} %param.9), kind=kLoop, calls=%fused_computation.56 | loop fusion | bytes 262144 | tf_op jit(solution)/shard_map/slice | solution.py:25
  8.6 4.5 %collective-permute-start.7 = (bf16[1,2,64,256]{3,2,1,0:T(8,128)(2,1)S(1)}, bf16[1,2,64,256]{3,2,1,0:T(8,128)(2,1)S(1)}, u32[]{:S(2)}, u32[]{:S(2)}) collective-permute-start(bf16[1,2,64,256]{3,2,1,0:T(8,128)(2,1)S(1)} %get-tuple-element.20), channel_id=1, source_target_pairs={{0,4},{4,8},{8,12},{1,5},{5,9},{9,13},{2,6},{6,10},{10,14},{3,7},{... | collective-permute-start | bytes 196616 | tf_op jit(solution)/shard_map/ppermute | solution.py:22
  13.2 1.3 %collective-permute-start.8 = (bf16[1,2,64,256]{3,2,1,0:T(8,128)(2,1)S(1)}, bf16[1,2,64,256]{3,2,1,0:T(8,128)(2,1)S(1)}, u32[]{:S(2)}, u32[]{:S(2)}) collective-permute-start(bf16[1,2,64,256]{3,2,1,0:T(8,128)(2,1)S(1)} %get-tuple-element.19), channel_id=1, source_target_pairs={{4,0},{8,4},{12,8},{5,1},{9,5},{13,9},{6,2},{10,6},{14,10},{7,3},{... | collective-permute-start | bytes 196616 | tf_op jit(solution)/shard_map/ppermute | solution.py:25
  14.5 1.3 %constant_dynamic-slice_fusion.3 = (s32[4,12]{1,0:T(4,128)}, s32[4,12]{1,0:T(4,128)}) fusion(s32[16,12]{1,0:T(8,128)} %param.12, s32[]{:T(128)S(6)} %select_n.70, s32[]{:T(128)S(6)} %mul.27, s32[16,12]{1,0:T(8,128)} %param.11), kind=kLoop, calls=%fused_computation.48 | loop fusion | flops 96 | bytes 776 | tf_op jit(solution)/shard_map/dynamic_slice | solution.py:150
  15.8 1.3 %pad_dynamic-slice_fusion.3 = (s32[8,12]{1,0:T(8,128)}, s32[8,12]{1,0:T(8,128)S(1)}) fusion(s32[]{:T(128)S(6)} %select_n.71, s32[16,12]{1,0:T(8,128)} %param.12, s32[16,12]{1,0:T(8,128)} %param.11), kind=kLoop, calls=%fused_computation.40 | loop fusion | bytes 2308 | tf_op jit(solution)/shard_map/dynamic_slice | solution.py:150
  17.1 1.3 %constant_dynamic-slice_fusion.1 = (s32[4,12]{1,0:T(4,128)}, s32[4,12]{1,0:T(4,128)}) fusion(s32[16,12]{1,0:T(8,128)} %param.14, s32[]{:T(128)S(6)} %select_n.70, s32[16,12]{1,0:T(8,128)} %param.13), kind=kLoop, calls=%fused_computation.46 | loop fusion | bytes 772 | tf_op jit(solution)/shard_map/dynamic_slice | solution.py:150
  18.4 1.3 %pad_dynamic-slice_fusion.1 = (s32[8,12]{1,0:T(8,128)}, s32[8,12]{1,0:T(8,128)}) fusion(s32[]{:T(128)S(6)} %select_n.71, s32[16,12]{1,0:T(8,128)} %param.14, s32[16,12]{1,0:T(8,128)} %param.13), kind=kLoop, calls=%fused_computation.38 | loop fusion | bytes 2308 | tf_op jit(solution)/shard_map/dynamic_slice | solution.py:150
  19.8 0.7 rsqrt_multiply_fusion
  20.5 2.4 %copy.13 = bf16[9,256,256]{1,2,0:T(8,128)(2,1)} copy(bf16[9,256,256]{2,1,0:T(8,128)(2,1)} %param.10) | data formatting | bytes 2359296 | tf_op args[2]
  22.9 0.1 broadcast_in_dim.24
  23.0 0.1 eq.23
  23.1 0.7 compare_select_fusion.scale_ref
  23.8 0.6 constant_dynamic-slice_fusion.scale_ref
  24.4 0.0 collective-permute-done.1
  24.5 0.1 convert_reduce_fusion.1
  24.5 0.1 collective-permute-start.6
  24.7 1.5 %collective-permute-start.5 = (f32[1,8,256]{2,0,1:T(1,128)S(1)}, f32[1,8,256]{2,0,1:T(1,128)S(1)}, u32[]{:S(2)}, u32[]{:S(2)}) collective-permute-start(f32[1,8,256]{2,0,1:T(1,128)S(1)} %reduce_sum.23), channel_id=1, source_target_pairs={{0,2},{1,3},{2,0},{3,1},{4,6},{5,7},{6,4},{7,5},{8,10},{9,11},{10,... | collective-permute-start | bytes 24584 | tf_op jit(solution)/shard_map/ppermute | solution.py:42
  26.1 0.2 collective-permute-start.4
  26.4 0.0 copy-start.3
  26.4 0.7 fusion.25
  27.1 0.0 copy-done.3
  27.1 0.1 convert_reduce_fusion
  27.2 1.6 %collective-permute-start.13 = (f32[1,8,256]{2,0,1:T(1,128)S(1)}, f32[1,8,256]{2,0,1:T(1,128)S(1)}, u32[]{:S(2)}, u32[]{:S(2)}) collective-permute-start(f32[1,8,256]{2,0,1:T(1,128)S(1)} %reduce_sum.25), channel_id=1, source_target_pairs={{0,3},{1,0},{2,1},{3,2},{4,7},{5,4},{6,5},{7,6},{8,11},{9,8},{10,9... | collective-permute-start | bytes 24584 | tf_op jit(solution)/shard_map/ppermute | solution.py:42
  28.8 0.5 collective-permute-start.12
  29.4 0.0 collective-permute-done.6
  29.4 0.0 collective-permute-start.11
  29.4 0.0 collective-permute-done.5
  29.4 1.7 %collective-permute-start.3 = (bf16[1,8,16,256]{3,2,1,0:T(8,128)(2,1)S(1)}, bf16[1,8,16,256]{3,2,1,0:T(8,128)(2,1)S(1)}, u32[]{:S(2)}, u32[]{:S(2)}) collective-permute-start(bf16[1,8,16,256]{3,2,1,0:T(8,128)(2,1)S(1)} %get-tuple-element.18), channel_id=1, source_target_pairs={{1,0},{2,1},{3,2},{0,3},{5,4},{6,5},{7,6},{4,7},{9,8},{10,9},{11,1... | collective-permute-start | bytes 196616 | tf_op jit(solution)/shard_map/ppermute | solution.py:25
  31.1 0.6 add_bitcast_fusion.1.total_ref
  31.8 0.0 collective-permute-done.13
  31.8 1.7 %collective-permute-start.10 = (bf16[1,8,16,256]{3,2,1,0:T(8,128)(2,1)}, bf16[1,8,16,256]{3,2,1,0:T(8,128)(2,1)}, u32[]{:S(2)}, u32[]{:S(2)}) collective-permute-start(bf16[1,8,16,256]{3,2,1,0:T(8,128)(2,1)} %get-tuple-element.16), channel_id=1, source_target_pairs={{1,0},{2,1},{3,2},{0,3},{5,4},{6,5},{7,6},{4,7},{9,8},{10,9},{11,1... | collective-permute-start | bytes 196616 | tf_op jit(solution)/shard_map/ppermute | solution.py:25
  33.5 0.0 collective-permute-done.12
  33.5 0.0 collective-permute-start.9
  33.5 0.6 add_bitcast_fusion.total_ref
  34.1 0.0 collective-permute-done.3
  34.1 1.4 %collective-permute-done.2 = bf16[1,8,16,256]{3,2,1,0:T(8,128)(2,1)S(1)} collective-permute-done((bf16[1,8,16,256]{3,2,1,0:T(8,128)(2,1)S(1)}, bf16[1,8,16,256]{3,2,1,0:T(8,128)(2,1)S(1)}, u32[]{:S(2)}, u32[]{:S(2)}) %collective-permute-start.2) | collective-permute-done | bytes 65568 | tf_op jit(solution)/shard_map/ppermute | solution.py:22
  35.5 0.8 %fusion.19.field_ref = bf16[1,8,128,256]{3,2,1,0:T(8,128)(2,1)} fusion(bf16[1,8,16,256]{3,2,1,0:T(8,128)(2,1)S(1)} %collective-permute-done.3, bf16[1,8,64,256]{3,2,1,0:T(8,128)(2,1)S(1)} %constant_dynamic-update-slice_fusion, bf16[1,8,16,256]{3,2,1,0:T(8,128)(2,1)S(1)} %collective-permute-done.2), kind=kLoop, calls=%fused_computation.21 | loop fusion | flops 2621440 | bytes 917504 | tf_op jit(solution)/shard_map/concatenate | solution.py:26
  36.3 3.5 %shard_map.103 = bf16[1,4,64,2304]{3,2,1,0:T(8,128)(2,1)} custom-call(s32[4,12]{1,0:T(4,128)} %get-tuple-element.26.rows_ref, s32[4,12]{1,0:T(4,128)} %get-tuple-element.25.start_ref, s32[4,12]{1,0:T(4,128)} %get-tuple-element.24.span_ref, s32[4,12]{1,0:T(4,128)} %get-tuple-element.23.basis_ref, f32[4,12]{1,0:T(4,128)} %constant_dynamic-slice_fusion.scale_ref, ...), custom_call_target="tpu_custom_call" | custom-call | tf_op jit(solution)/shard_map/pallas_call | solution.py:117
  39.9 1.8 %convolution_bitcast_fusion = f32[9,256,256]{1,2,0:T(8,128)S(1)} fusion(bf16[4,8,9,8,256]{4,3,2,1,0:T(8,128)(2,1)} %bitcast.41, bf16[1,4,64,256]{3,2,1,0:T(8,128)(2,1)S(1)} %copy-done.5), kind=kOutput, calls=%fused_computation | convolution fusion | flops 301989888 | bytes 3670016 | tf_op jit(solution)/shard_map/brwq,brwo->qo/dot_general | solution.py:178
  41.7 0.0 copy-start.4
  41.7 1.0 %dynamic-slice_convert_fusion.2 = (bf16[9,256,64]{1,2,0:T(8,128)(2,1)}, bf16[9,256,64]{1,2,0:T(8,128)(2,1)}, bf16[9,256,64]{1,2,0:T(8,128)(2,1)}) fusion(f32[9,256,256]{1,2,0:T(8,128)S(1)} %convolution_bitcast_fusion, s32[]{:T(128)S(6)} %select_n.75, s32[]{:T(128)S(6)} %select_n.79, s32[]{:T(128)S(6)} %select_n.77), kind=kLoop, calls=%fused_computation.19 | loop fusion | bytes 1769484 | tf_op jit(solution)/shard_map/convert_element_type | solution.py:59
  42.7 0.4 collective-permute-start.16
  43.0 1.5 %collective-permute-start.15 = (bf16[9,256,64]{1,2,0:T(8,128)(2,1)}, bf16[9,256,64]{1,2,0:T(8,128)(2,1)}, u32[]{:S(2)}, u32[]{:S(2)}) collective-permute-start(bf16[9,256,64]{1,2,0:T(8,128)(2,1)} %get-tuple-element.11), channel_id=1, source_target_pairs={{0,2},{1,3},{2,0},{3,1},{4,6},{5,7},{6,4},{7,5},{8,10},{9,11},{10,... | collective-permute-start | bytes 884744 | tf_op jit(solution)/shard_map/ppermute | solution.py:59
  44.5 0.0 collective-permute-start.14
  44.5 0.0 collective-permute-done.10
  44.5 1.8 %fusion.21.field_ref = bf16[1,8,128,256]{3,2,1,0:T(8,128)(2,1)} fusion(bf16[1,8,16,256]{3,2,1,0:T(8,128)(2,1)} %collective-permute-done.10, bf16[1,8,64,256]{3,2,1,0:T(8,128)(2,1)S(1)} %copy-done.4, bf16[1,8,16,256]{3,2,1,0:T(8,128)(2,1)} %collective-permute-done.9), kind=kLoop, calls=%fused_computation.23 | loop fusion | flops 2621440 | bytes 917504 | tf_op jit(solution)/shard_map/concatenate | solution.py:26
  46.3 9.8 %shard_map.104 = bf16[1,4,64,2304]{3,2,1,0:T(8,128)(2,1)} custom-call(s32[8,12]{1,0:T(8,128)} %copy-done.7, s32[8,12]{1,0:T(8,128)} %get-tuple-element.29.start_ref, s32[8,12]{1,0:T(8,128)} %get-tuple-element.28.span_ref, s32[8,12]{1,0:T(8,128)} %get-tuple-element.27.basis_ref, f32[4,96]{1,0:T(4,128)} %compare_select_fusion.scale_ref, ...), custom_call_target="tpu_custom_call" | custom-call | tf_op jit(solution)/shard_map/pallas_call | solution.py:117
  56.2 2.5 %fusion.6 = f32[1,4,64,256]{3,2,1,0:T(8,128)} fusion(bf16[2304,256,1]{1,0,2:T(8,128)(2,1)} %bitcast.42, bf16[1,4,64,2304]{3,2,1,0:T(8,128)(2,1)S(1)} %copy-done), kind=kOutput, calls=%fused_computation.7 | convolution fusion | flops 301989888 | bytes 2621440 | tf_op jit(solution)/shard_map/brwq,qo->brwo/dot_general | solution.py:161
  58.6 0.1 collective-permute-done.15
  58.7 0.0 collective-permute-done.14
  58.7 1.4 %convert_add_fusion = f32[9,256,64]{1,2,0:T(8,128)S(1)} fusion(bf16[9,256,64]{1,2,0:T(8,128)(2,1)} %collective-permute-done.16, bf16[9,256,64]{1,2,0:T(8,128)(2,1)} %collective-permute-done.15, bf16[9,256,64]{1,2,0:T(8,128)(2,1)} %collective-permute-done.14, f32[9,256,256]{1,2,0:T(8,128)S(1)} %convolution_bitcast_fusion, s32[]{:T(128)S(6)} %select_n.73), kind=kLoop, calls=%fused_computation.16 | loop fusion | flops 884736 | bytes 2064388 | tf_op jit(solution)/shard_map/add | solution.py:60
  60.2 0.2 dynamic-slice_convert_fusion.5
  60.4 5.3 %collective-permute-start.19 = (bf16[9,64,64]{1,2,0:T(8,128)(2,1)S(1)}, bf16[9,64,64]{1,2,0:T(8,128)(2,1)S(1)}, u32[]{:S(2)}, u32[]{:S(2)}) collective-permute-start(bf16[9,64,64]{1,2,0:T(8,128)(2,1)S(1)} %get-tuple-element.13), channel_id=1, source_target_pairs={{0,12},{4,0},{8,4},{12,8},{1,13},{5,1},{9,5},{13,9},{2,14},{6,2},{... | collective-permute-start | bytes 221192 | tf_op jit(solution)/shard_map/ppermute | solution.py:59
  65.6 0.0 collective-permute-start.18
  65.6 0.8 %collective-permute-start.17 = (bf16[9,64,64]{1,2,0:T(8,128)(2,1)S(1)}, bf16[9,64,64]{1,2,0:T(8,128)(2,1)S(1)}, u32[]{:S(2)}, u32[]{:S(2)}) collective-permute-start(bf16[9,64,64]{1,2,0:T(8,128)(2,1)S(1)} %get-tuple-element.12), channel_id=1, source_target_pairs={{0,4},{4,8},{8,12},{12,0},{1,5},{5,9},{9,13},{13,1},{2,6},{6,10},{... | collective-permute-start | bytes 221192 | tf_op jit(solution)/shard_map/ppermute | solution.py:59
  66.5 1.2 %fusion.9 = f32[1,4,64,256]{3,2,1,0:T(8,128)} fusion(bf16[2304,256,1]{1,0,2:T(8,128)(2,1)S(1)} %bitcast.43, bf16[1,4,64,2304]{3,2,1,0:T(8,128)(2,1)S(1)} %copy-done.2), kind=kOutput, calls=%fused_computation.8 | convolution fusion | flops 301989888 | bytes 2621440 | tf_op jit(solution)/shard_map/bpwq,qc->bpwc/dot_general | solution.py:175
  67.6 2.2 %collective-permute-done.19 = bf16[9,64,64]{1,2,0:T(8,128)(2,1)S(1)} collective-permute-done((bf16[9,64,64]{1,2,0:T(8,128)(2,1)S(1)}, bf16[9,64,64]{1,2,0:T(8,128)(2,1)S(1)}, u32[]{:S(2)}, u32[]{:S(2)}) %collective-permute-start.19) | collective-permute-done | bytes 73760 | tf_op jit(solution)/shard_map/ppermute | solution.py:59
  69.9 9.0 %collective-permute-done.18 = bf16[9,64,64]{1,2,0:T(8,128)(2,1)S(1)} collective-permute-done((bf16[9,64,64]{1,2,0:T(8,128)(2,1)S(1)}, bf16[9,64,64]{1,2,0:T(8,128)(2,1)S(1)}, u32[]{:S(2)}, u32[]{:S(2)}) %collective-permute-start.18) | collective-permute-done | bytes 73760 | tf_op jit(solution)/shard_map/ppermute | solution.py:59
  78.9 0.0 collective-permute-done.17
  78.9 0.1 add_multiply_fusion
  79.0 0.9 %copy.15 = f32[9,64,64]{2,1,0:T(8,128)} copy(f32[9,64,64]{1,2,0:T(8,128)S(1)} %add_multiply_fusion) | data formatting | bytes 294912
  (32 shorter events, 0.1 us)
Async XLA Ops:
  1.5 22.9 %collective-permute-start = (bf16[1,2,64,256]{3,2,1,0:T(8,128)(2,1)S(1)}, bf16[1,2,64,256]{3,2,1,0:T(8,128)(2,1)S(1)}, u32[]{:S(2)}, u32[]{:S(2)}) collective-permute-start(bf16[1,2,64,256]{3,2,1,0:T(8,128)(2,1)S(1)} %get-tuple-element.22), channel_id=1, source_target_pairs={{0,4},{4,8},{8,12},{1,5},{5,9},{9,13},{2,6},{6,10},{10,14},{3,7},{... | collective-permute-start | bytes 196616 | tf_op jit(solution)/shard_map/ppermute | solution.py:22
  6.5 18.0 %collective-permute-start.1 = (bf16[1,2,64,256]{3,2,1,0:T(8,128)(2,1)S(1)}, bf16[1,2,64,256]{3,2,1,0:T(8,128)(2,1)S(1)}, u32[]{:S(2)}, u32[]{:S(2)}) collective-permute-start(bf16[1,2,64,256]{3,2,1,0:T(8,128)(2,1)S(1)} %get-tuple-element.21), channel_id=1, source_target_pairs={{4,0},{8,4},{12,8},{5,1},{9,5},{13,9},{6,2},{10,6},{14,10},{7,3},{... | collective-permute-start | bytes 196616 | tf_op jit(solution)/shard_map/ppermute | solution.py:25
  8.6 17.7 %collective-permute-start.7 = (bf16[1,2,64,256]{3,2,1,0:T(8,128)(2,1)S(1)}, bf16[1,2,64,256]{3,2,1,0:T(8,128)(2,1)S(1)}, u32[]{:S(2)}, u32[]{:S(2)}) collective-permute-start(bf16[1,2,64,256]{3,2,1,0:T(8,128)(2,1)S(1)} %get-tuple-element.20), channel_id=1, source_target_pairs={{0,4},{4,8},{8,12},{1,5},{5,9},{9,13},{2,6},{6,10},{10,14},{3,7},{... | collective-permute-start | bytes 196616 | tf_op jit(solution)/shard_map/ppermute | solution.py:22
  13.2 13.2 %collective-permute-start.8 = (bf16[1,2,64,256]{3,2,1,0:T(8,128)(2,1)S(1)}, bf16[1,2,64,256]{3,2,1,0:T(8,128)(2,1)S(1)}, u32[]{:S(2)}, u32[]{:S(2)}) collective-permute-start(bf16[1,2,64,256]{3,2,1,0:T(8,128)(2,1)S(1)} %get-tuple-element.19), channel_id=1, source_target_pairs={{4,0},{8,4},{12,8},{5,1},{9,5},{13,9},{6,2},{10,6},{14,10},{7,3},{... | collective-permute-start | bytes 196616 | tf_op jit(solution)/shard_map/ppermute | solution.py:25
  17.1 5.9 %copy-start.7 = (s32[8,12]{1,0:T(8,128)}, s32[8,12]{1,0:T(8,128)S(1)}, u32[]{:S(2)}) copy-start(s32[8,12]{1,0:T(8,128)S(1)} %get-tuple-element.30.rows_ref) | copy-start | bytes 1156
  20.5 3.9 %copy-start.6 = (bf16[1,4,64,256]{3,2,1,0:T(8,128)(2,1)S(1)}, bf16[1,4,64,256]{3,2,1,0:T(8,128)(2,1)}, u32[]{:S(2)}) copy-start(bf16[1,4,64,256]{3,2,1,0:T(8,128)(2,1)} %param.8) | copy-start | bytes 393220
  22.9 3.4 %copy-start.5 = (bf16[1,4,64,256]{3,2,1,0:T(8,128)(2,1)S(1)}, bf16[1,4,64,256]{3,2,1,0:T(8,128)(2,1)}, u32[]{:S(2)}) copy-start(bf16[1,4,64,256]{3,2,1,0:T(8,128)(2,1)} %param.9) | copy-start | bytes 393220
  24.5 4.9 %collective-permute-start.6 = (f32[1,8,256]{2,0,1:T(1,128)S(1)}, f32[1,8,256]{2,0,1:T(1,128)S(1)}, u32[]{:S(2)}, u32[]{:S(2)}) collective-permute-start(f32[1,8,256]{2,0,1:T(1,128)S(1)} %reduce_sum.23), channel_id=1, source_target_pairs={{0,3},{1,0},{2,1},{3,2},{4,7},{5,4},{6,5},{7,6},{8,11},{9,8},{10,9... | collective-permute-start | bytes 24584 | tf_op jit(solution)/shard_map/ppermute | solution.py:42
  24.7 4.7 %collective-permute-start.5 = (f32[1,8,256]{2,0,1:T(1,128)S(1)}, f32[1,8,256]{2,0,1:T(1,128)S(1)}, u32[]{:S(2)}, u32[]{:S(2)}) collective-permute-start(f32[1,8,256]{2,0,1:T(1,128)S(1)} %reduce_sum.23), channel_id=1, source_target_pairs={{0,2},{1,3},{2,0},{3,1},{4,6},{5,7},{6,4},{7,5},{8,10},{9,11},{10,... | collective-permute-start | bytes 24584 | tf_op jit(solution)/shard_map/ppermute | solution.py:42
  26.1 5.0 %collective-permute-start.4 = (f32[1,8,256]{2,0,1:T(1,128)S(1)}, f32[1,8,256]{2,0,1:T(1,128)S(1)}, u32[]{:S(2)}, u32[]{:S(2)}) collective-permute-start(f32[1,8,256]{2,0,1:T(1,128)S(1)} %reduce_sum.23), channel_id=1, source_target_pairs={{0,1},{1,2},{2,3},{3,0},{4,5},{5,6},{6,7},{7,4},{8,9},{9,10},{10,1... | collective-permute-start | bytes 24584 | tf_op jit(solution)/shard_map/ppermute | solution.py:42
  26.4 0.7 copy-start.3
  27.2 4.6 %collective-permute-start.13 = (f32[1,8,256]{2,0,1:T(1,128)S(1)}, f32[1,8,256]{2,0,1:T(1,128)S(1)}, u32[]{:S(2)}, u32[]{:S(2)}) collective-permute-start(f32[1,8,256]{2,0,1:T(1,128)S(1)} %reduce_sum.25), channel_id=1, source_target_pairs={{0,3},{1,0},{2,1},{3,2},{4,7},{5,4},{6,5},{7,6},{8,11},{9,8},{10,9... | collective-permute-start | bytes 24584 | tf_op jit(solution)/shard_map/ppermute | solution.py:42
  28.8 4.7 %collective-permute-start.12 = (f32[1,8,256]{2,0,1:T(1,128)S(1)}, f32[1,8,256]{2,0,1:T(1,128)S(1)}, u32[]{:S(2)}, u32[]{:S(2)}) collective-permute-start(f32[1,8,256]{2,0,1:T(1,128)S(1)} %reduce_sum.25), channel_id=1, source_target_pairs={{0,2},{1,3},{2,0},{3,1},{4,6},{5,7},{6,4},{7,5},{8,10},{9,11},{10,... | collective-permute-start | bytes 24584 | tf_op jit(solution)/shard_map/ppermute | solution.py:42
  29.4 4.1 %collective-permute-start.11 = (f32[1,8,256]{2,0,1:T(1,128)S(1)}, f32[1,8,256]{2,0,1:T(1,128)S(1)}, u32[]{:S(2)}, u32[]{:S(2)}) collective-permute-start(f32[1,8,256]{2,0,1:T(1,128)S(1)} %reduce_sum.25), channel_id=1, source_target_pairs={{0,1},{1,2},{2,3},{3,0},{4,5},{5,6},{6,7},{7,4},{8,9},{9,10},{10,1... | collective-permute-start | bytes 24584 | tf_op jit(solution)/shard_map/ppermute | solution.py:42
  29.4 4.7 %collective-permute-start.3 = (bf16[1,8,16,256]{3,2,1,0:T(8,128)(2,1)S(1)}, bf16[1,8,16,256]{3,2,1,0:T(8,128)(2,1)S(1)}, u32[]{:S(2)}, u32[]{:S(2)}) collective-permute-start(bf16[1,8,16,256]{3,2,1,0:T(8,128)(2,1)S(1)} %get-tuple-element.18), channel_id=1, source_target_pairs={{1,0},{2,1},{3,2},{0,3},{5,4},{6,5},{7,6},{4,7},{9,8},{10,9},{11,1... | collective-permute-start | bytes 196616 | tf_op jit(solution)/shard_map/ppermute | solution.py:25
  31.1 4.4 %collective-permute-start.2 = (bf16[1,8,16,256]{3,2,1,0:T(8,128)(2,1)S(1)}, bf16[1,8,16,256]{3,2,1,0:T(8,128)(2,1)S(1)}, u32[]{:S(2)}, u32[]{:S(2)}) collective-permute-start(bf16[1,8,16,256]{3,2,1,0:T(8,128)(2,1)S(1)} %get-tuple-element.17), channel_id=1, source_target_pairs={{0,1},{1,2},{2,3},{3,0},{4,5},{5,6},{6,7},{7,4},{8,9},{9,10},{10,1... | collective-permute-start | bytes 196616 | tf_op jit(solution)/shard_map/ppermute | solution.py:22
  31.8 12.8 %collective-permute-start.10 = (bf16[1,8,16,256]{3,2,1,0:T(8,128)(2,1)}, bf16[1,8,16,256]{3,2,1,0:T(8,128)(2,1)}, u32[]{:S(2)}, u32[]{:S(2)}) collective-permute-start(bf16[1,8,16,256]{3,2,1,0:T(8,128)(2,1)} %get-tuple-element.16), channel_id=1, source_target_pairs={{1,0},{2,1},{3,2},{0,3},{5,4},{6,5},{7,6},{4,7},{9,8},{10,9},{11,1... | collective-permute-start | bytes 196616 | tf_op jit(solution)/shard_map/ppermute | solution.py:25
  33.5 11.0 %collective-permute-start.9 = (bf16[1,8,16,256]{3,2,1,0:T(8,128)(2,1)}, bf16[1,8,16,256]{3,2,1,0:T(8,128)(2,1)}, u32[]{:S(2)}, u32[]{:S(2)}) collective-permute-start(bf16[1,8,16,256]{3,2,1,0:T(8,128)(2,1)} %get-tuple-element.15), channel_id=1, source_target_pairs={{0,1},{1,2},{2,3},{3,0},{4,5},{5,6},{6,7},{7,4},{8,9},{9,10},{10,1... | collective-permute-start | bytes 196616 | tf_op jit(solution)/shard_map/ppermute | solution.py:22
  41.7 2.9 %copy-start.4 = (bf16[1,8,64,256]{3,2,1,0:T(8,128)(2,1)S(1)}, bf16[1,8,64,256]{3,2,1,0:T(8,128)(2,1)}, u32[]{:S(2)}) copy-start(bf16[1,8,64,256]{3,2,1,0:T(8,128)(2,1)} %copy-done.3) | copy-start | bytes 786436
  42.7 16.0 %collective-permute-start.16 = (bf16[9,256,64]{1,2,0:T(8,128)(2,1)}, bf16[9,256,64]{1,2,0:T(8,128)(2,1)}, u32[]{:S(2)}, u32[]{:S(2)}) collective-permute-start(bf16[9,256,64]{1,2,0:T(8,128)(2,1)} %get-tuple-element.10), channel_id=1, source_target_pairs={{0,3},{1,0},{2,1},{3,2},{4,7},{5,4},{6,5},{7,6},{8,11},{9,8},{10,9... | collective-permute-start | bytes 884744 | tf_op jit(solution)/shard_map/ppermute | solution.py:59
  43.0 15.7 %collective-permute-start.15 = (bf16[9,256,64]{1,2,0:T(8,128)(2,1)}, bf16[9,256,64]{1,2,0:T(8,128)(2,1)}, u32[]{:S(2)}, u32[]{:S(2)}) collective-permute-start(bf16[9,256,64]{1,2,0:T(8,128)(2,1)} %get-tuple-element.11), channel_id=1, source_target_pairs={{0,2},{1,3},{2,0},{3,1},{4,6},{5,7},{6,4},{7,5},{8,10},{9,11},{10,... | collective-permute-start | bytes 884744 | tf_op jit(solution)/shard_map/ppermute | solution.py:59
  44.5 11.7 %copy-start = (bf16[1,4,64,2304]{3,2,1,0:T(8,128)(2,1)S(1)}, bf16[1,4,64,2304]{3,2,1,0:T(8,128)(2,1)}, u32[]{:S(2)}) copy-start(bf16[1,4,64,2304]{3,2,1,0:T(8,128)(2,1)} %shard_map.103) | copy-start | bytes 3538948
  44.5 14.2 %collective-permute-start.14 = (bf16[9,256,64]{1,2,0:T(8,128)(2,1)}, bf16[9,256,64]{1,2,0:T(8,128)(2,1)}, u32[]{:S(2)}, u32[]{:S(2)}) collective-permute-start(bf16[9,256,64]{1,2,0:T(8,128)(2,1)} %get-tuple-element.9), channel_id=1, source_target_pairs={{0,1},{1,2},{2,3},{3,0},{4,5},{5,6},{6,7},{7,4},{8,9},{9,10},{10,1... | collective-permute-start | bytes 884744 | tf_op jit(solution)/shard_map/ppermute | solution.py:59
  58.6 7.8 %copy-start.1 = (bf16[9,256,256]{1,2,0:T(8,128)(2,1)S(1)}, bf16[9,256,256]{1,2,0:T(8,128)(2,1)}, u32[]{:S(2)}) copy-start(bf16[9,256,256]{1,2,0:T(8,128)(2,1)} %copy.13) | copy-start | bytes 3538948
  58.6 7.8 %copy-start.2 = (bf16[1,4,64,2304]{3,2,1,0:T(8,128)(2,1)S(1)}, bf16[1,4,64,2304]{3,2,1,0:T(8,128)(2,1)}, u32[]{:S(2)}) copy-start(bf16[1,4,64,2304]{3,2,1,0:T(8,128)(2,1)} %shard_map.104) | copy-start | bytes 3538948
  60.4 9.5 %collective-permute-start.19 = (bf16[9,64,64]{1,2,0:T(8,128)(2,1)S(1)}, bf16[9,64,64]{1,2,0:T(8,128)(2,1)S(1)}, u32[]{:S(2)}, u32[]{:S(2)}) collective-permute-start(bf16[9,64,64]{1,2,0:T(8,128)(2,1)S(1)} %get-tuple-element.13), channel_id=1, source_target_pairs={{0,12},{4,0},{8,4},{12,8},{1,13},{5,1},{9,5},{13,9},{2,14},{6,2},{... | collective-permute-start | bytes 221192 | tf_op jit(solution)/shard_map/ppermute | solution.py:59
  65.6 13.2 %collective-permute-start.18 = (bf16[9,64,64]{1,2,0:T(8,128)(2,1)S(1)}, bf16[9,64,64]{1,2,0:T(8,128)(2,1)S(1)}, u32[]{:S(2)}, u32[]{:S(2)}) collective-permute-start(bf16[9,64,64]{1,2,0:T(8,128)(2,1)S(1)} %get-tuple-element.14), channel_id=1, source_target_pairs={{0,8},{4,12},{8,0},{12,4},{1,9},{5,13},{9,1},{13,5},{2,10},{6,14},... | collective-permute-start | bytes 221192 | tf_op jit(solution)/shard_map/ppermute | solution.py:59
  65.6 13.2 %collective-permute-start.17 = (bf16[9,64,64]{1,2,0:T(8,128)(2,1)S(1)}, bf16[9,64,64]{1,2,0:T(8,128)(2,1)S(1)}, u32[]{:S(2)}, u32[]{:S(2)}) collective-permute-start(bf16[9,64,64]{1,2,0:T(8,128)(2,1)S(1)} %get-tuple-element.12), channel_id=1, source_target_pairs={{0,4},{4,8},{8,12},{12,0},{1,5},{5,9},{9,13},{13,1},{2,6},{6,10},{... | collective-permute-start | bytes 221192 | tf_op jit(solution)/shard_map/ppermute | solution.py:59

commit v5 on v4

--- a/solution.py
+++ b/solution.py
@@ -10,28 +10,37 @@
 BASIS = 9
 REACH = 2
 RIM = 16
-
-
-def with_halo(block, sides, width, periodic):
-    for axis, dim in sides:
-        count = lax.axis_size(axis)
-        forward = [(i, i + 1) for i in range(count - 1)]
-        if periodic:
-            forward.append((count - 1, 0))
-        backward = [(target, source) for source, target in forward]
-        low = lax.ppermute(
-            lax.slice_in_dim(block, block.shape[dim] - width, None, axis=dim), axis, forward
-        )
-        high = lax.ppermute(lax.slice_in_dim(block, 0, width, axis=dim), axis, backward)
-        block = jnp.concatenate([low, block, high], axis=dim)
-    return block
-
-
-def extend(grid_field, padded):
-    grid_field = with_halo(grid_field, (("lat", 1),), REACH, False)
-    grid_field = with_halo(grid_field, (("lon", 2),), RIM, True)
-    extra = padded - grid_field.shape[2]
-    return jnp.pad(grid_field, ((0, 0), (0, 0), (0, extra), (0, 0)))
+POLAR = 2
+
+
+def extend(block, padded):
+    lat_count = lax.axis_size("lat")
+    lon_count = lax.axis_size("lon")
+    rows = block.shape[1]
+    cols = block.shape[2]
+
+    def fetch(piece, d_lat, d_lon):
+        pairs = []
+        for lat in range(lat_count):
+            source = lat - d_lat
+            if 0 <= source < lat_count:
+                for lon in range(lon_count):
+                    pairs.append(
+                        (source * lon_count + (lon - d_lon) % lon_count, lat * lon_count + lon)
+                    )
+        return lax.ppermute(piece, ("lat", "lon"), pairs)
+
+    top = block[:, rows - REACH:]
+    bottom = block[:, :REACH]
+    bands = []
+    for d_lat, part in ((1, top), (0, block), (-1, bottom)):
+        left = fetch(part[:, :, cols - RIM:], d_lat, 1)
+        right = fetch(part[:, :, :RIM], d_lat, -1)
+        middle = part if d_lat == 0 else fetch(part, d_lat, 0)
+        bands.append(jnp.concatenate([left, middle, right], axis=2))
+    field = jnp.concatenate(bands, axis=1)
+    extra = padded - field.shape[2]
+    return jnp.pad(field, ((0, 0), (0, 0), (0, extra), (0, 0)))
 
 
 def ring_sum(value, axis):
@@ -43,9 +52,14 @@
     return total
 
 
-def cycle_totals(widened, lon_count):
-    interior = lax.slice_in_dim(widened, RIM, RIM + lon_count, axis=2)
-    return ring_sum(jnp.sum(interior, axis=2, dtype=jnp.float32), "lon")
+def with_lat_halo(value):
+    count = lax.axis_size("lat")
+    forward = [(i, i + 1) for i in range(count - 1)]
+    backward = [(t, f) for f, t in forward]
+    rows = value.shape[2]
+    low = lax.ppermute(value[:, :, rows - REACH:], "lat", forward)
+    high = lax.ppermute(value[:, :, :REACH], "lat", backward)
+    return jnp.concatenate([low, value, high], axis=2)
 
 
 def ring_scatter(value, axis, dim):
@@ -143,8 +157,15 @@
 
     widened = extend(inputs, padded)
     grad_wide = extend(cotangent, padded)
-    totals = cycle_totals(widened, lon_count)
-    grad_totals = cycle_totals(grad_wide, lon_count)
+    row_sums = jnp.stack(
+        [jnp.sum(inputs, axis=2, dtype=jnp.float32), jnp.sum(cotangent, axis=2, dtype=jnp.float32)]
+    )
+    local_totals = ring_sum(row_sums, "lon")
+    if row_count >= POLAR + REACH:
+        framed = jnp.pad(local_totals, ((0, 0), (0, 0), (REACH, REACH), (0, 0)))
+    else:
+        framed = with_lat_halo(local_totals)
+    totals, grad_totals = framed[0], framed[1]
 
     def rows_of(table, begin, count):
         return lax.dynamic_slice_in_dim(table, begin, count, 0)

time: 80.6 us -> 105 us (1.30)
  starting transfers between devices: 27.5 us -> 48.3 us
  local copies, waits for them, and re-layouts: 11.8 us -> 13.7 us
    ppermute x8 -> x16, starting transfers between devices: 15.6 us -> 39.6 us  [fetch(): return lax.ppermute(piece, ('lat', 'lon'), pairs)]
    ppermute x6, starting transfers between devices: 7.94 us -> 5.46 us  [ring_scatter(): sent = lax.ppermute(piece.astype(jnp.bfloat16), axis, pairs)]
    slice x4 -> x6, local copies, waits for them, and re-layouts: 2.49 us -> 4.75 us  [the longest x2 2.41 us: extend(): top = block[:, rows - REACH:]]
    reduce_sum x2, other arithmetic: 0.1 us -> 1.97 us  [the longest x1 1.04 us: on_device(): jnp.sum(cotangent, axis=2, dtype=jnp.float32)]
    broadcast_in_dim x2 -> x0, other arithmetic: 1.23 us -> none  [run_filter(): totals[:, :, None, :]]
    unnamed x22 -> x26, local copies, waits for them, and re-layouts: 3.4 us -> 2.47 us
    ppermute x6 -> x3, starting transfers between devices: 3.97 us -> 3.23 us  [ring_sum(): total = total + lax.ppermute(value, axis, pairs)]
  transfers between devices with their start and end apart: 20 -> 25, of which waited for: 4 -> 4; matrix products, arithmetic and copies ran while one was open for 27% -> 22% of each run, Pallas kernels for 17% -> 13%
where the time goes in v5:
time: 105 us; the launch traced here: 104 us
  starting transfers between devices  48.3 us (46%)
  Pallas kernels  13.8 us (13%)
  local copies, waits for them, and re-layouts  13.7 us (13%)
  waiting for transfers between devices  13.6 us (13%)
  other arithmetic  8.19 us (8%)
  matrix products  5.42 us (5%)
  between operations  1.06 us (1%)
    ppermute x16, starting transfers between devices, fetch(): return lax.ppermute(piece, ('lat', 'lon'), pairs)  39.6 us
    pallas_call x2, Pallas kernels, run_filter(): pl.pallas_call(kernel, grid=(members, row_count), in_specs=[smem] * 5 + [...  13.8 us
    ppermute x6, waiting for transfers between devices, ring_scatter(): sent = lax.ppermute(piece.astype(jnp.bfloat16), axis, pairs)  12.3 us
    ppermute x6, starting transfers between devices, ring_scatter(): sent = lax.ppermute(piece.astype(jnp.bfloat16), axis, pairs)  5.46 us
    dynamic_slice x5, local copies, waits for them, and re-layouts, rows_of(): return lax.dynamic_slice_in_dim(table, begin, count, 0)  4.55 us
    ppermute x3, starting transfers between devices, ring_sum(): total = total + lax.ppermute(value, axis, pairs)  3.23 us
    concatenate x2, other arithmetic, extend(): field = jnp.concatenate(bands, axis=1)  2.63 us
    unnamed x26, local copies, waits for them, and re-layouts  2.47 us
  transfers between devices with their start and end apart: 25, of which 4 were waited for; matrix products, arithmetic and copies ran while one was open for 22% of the time, Pallas kernels for 13%

profile of v5, /device:TPU:0, one launch (start us, length us, event | category | flops | bytes accessed | tf_op | source)
XLA Modules:
  0.0 104.2 jit_solution(9473266989766051110)
XLA Ops:
  0.6 0.0 copy-start.4
  0.6 0.0 copy-start.7
  0.7 0.0 copy-start.1
  0.7 1.0 convert_reduce_fusion
  1.7 0.9 convert_reduce_fusion.1
  2.7 2.4 %collective-permute-start.10 = (f32[2,1,4,256]{3,0,2,1:T(2,128)S(1)}, f32[2,1,4,256]{3,0,2,1:T(2,128)S(1)}, u32[]{:S(2)}, u32[]{:S(2)}) collective-permute-start(f32[2,1,4,256]{3,0,2,1:T(2,128)S(1)} %pad_maximum_fusion), channel_id=1, source_target_pairs={{0,3},{1,0},{2,1},{3,2},{4,7},{5,4},{6,5},{7,6},{8,11},{9,8},{10,9... | collective-permute-start | bytes 24584 | tf_op jit(solution)/shard_map/ppermute | solution.py:51
  5.1 0.6 collective-permute-start.9
  5.8 0.2 collective-permute-start.8
  5.9 0.8 fusion.54
  6.7 1.3 %collective-permute-start.7 = (bf16[1,2,16,256]{3,2,1,0:T(8,128)(2,1)S(1)}, bf16[1,2,16,256]{3,2,1,0:T(8,128)(2,1)S(1)}, u32[]{:S(2)}, u32[]{:S(2)}) collective-permute-start(bf16[1,2,16,256]{3,2,1,0:T(8,128)(2,1)S(1)} %get-tuple-element.26), channel_id=1, source_target_pairs={{5,0},{6,1},{7,2},{4,3},{9,4},{10,5},{11,6},{8,7},{13,8},{14,9},{1... | collective-permute-start | bytes 49160 | tf_op jit(solution)/shard_map/ppermute | solution.py:31
  8.0 0.9 fusion.55
  8.9 1.3 %collective-permute-start.6 = (bf16[1,2,64,256]{3,2,1,0:T(8,128)(2,1)S(1)}, bf16[1,2,64,256]{3,2,1,0:T(8,128)(2,1)S(1)}, u32[]{:S(2)}, u32[]{:S(2)}) collective-permute-start(bf16[1,2,64,256]{3,2,1,0:T(8,128)(2,1)S(1)} %get-tuple-element.28), channel_id=1, source_target_pairs={{4,0},{5,1},{6,2},{7,3},{8,4},{9,5},{10,6},{11,7},{12,8},{13,9},{1... | collective-permute-start | bytes 196616 | tf_op jit(solution)/shard_map/ppermute | solution.py:31
  10.2 0.8 fusion.56
  11.0 1.3 %constant_dynamic-slice_fusion.3 = (s32[4,12]{1,0:T(4,128)}, s32[4,12]{1,0:T(4,128)}) fusion(s32[16,12]{1,0:T(8,128)} %param.12, s32[]{:T(128)S(6)} %select_n.70, s32[]{:T(128)S(6)} %mul.27, s32[16,12]{1,0:T(8,128)} %param.11), kind=kLoop, calls=%fused_computation.70 | loop fusion | flops 96 | bytes 776 | tf_op jit(solution)/shard_map/dynamic_slice | solution.py:171
  12.3 1.3 %pad_dynamic-slice_fusion.3 = (s32[8,12]{1,0:T(8,128)}, s32[8,12]{1,0:T(8,128)S(1)}) fusion(s32[]{:T(128)S(6)} %select_n.71, s32[16,12]{1,0:T(8,128)} %param.12, s32[16,12]{1,0:T(8,128)} %param.11), kind=kLoop, calls=%fused_computation.60 | loop fusion | bytes 2308 | tf_op jit(solution)/shard_map/dynamic_slice | solution.py:171
  13.6 1.3 %constant_dynamic-slice_fusion.1 = (s32[4,12]{1,0:T(4,128)}, s32[4,12]{1,0:T(4,128)}) fusion(s32[16,12]{1,0:T(8,128)} %param.14, s32[]{:T(128)S(6)} %select_n.70, s32[16,12]{1,0:T(8,128)} %param.13), kind=kLoop, calls=%fused_computation.68 | loop fusion | bytes 772 | tf_op jit(solution)/shard_map/dynamic_slice | solution.py:171
  14.9 1.3 %pad_dynamic-slice_fusion.1 = (s32[8,12]{1,0:T(8,128)}, s32[8,12]{1,0:T(8,128)}) fusion(s32[]{:T(128)S(6)} %select_n.71, s32[16,12]{1,0:T(8,128)} %param.14, s32[16,12]{1,0:T(8,128)} %param.13), kind=kLoop, calls=%fused_computation.58 | loop fusion | bytes 2308 | tf_op jit(solution)/shard_map/dynamic_slice | solution.py:171
  16.2 0.8 fusion.51
  17.0 1.5 %fusion.52 = (bf16[1,2,64,256]{3,2,1,0:T(8,128)(2,1)}, bf16[1,2,64,256]{3,2,1,0:T(8,128)(2,1)}) fusion(bf16[1,4,64,256]{3,2,1,0:T(8,128)(2,1)} %param.9), kind=kLoop, calls=%fused_computation.77 | loop fusion | bytes 262144 | tf_op jit(solution)/shard_map/slice | solution.py:33
  18.6 0.1 broadcast_in_dim.17
  18.7 0.1 eq.23
  18.8 0.7 compare_select_fusion.scale_ref
  19.4 0.6 constant_dynamic-slice_fusion.scale_ref
  20.0 1.5 %copy.15 = bf16[9,256,256]{1,2,0:T(8,128)(2,1)} copy(bf16[9,256,256]{2,1,0:T(8,128)(2,1)S(1)} %copy-done.1) | data formatting | bytes 2359296 | tf_op args[2]
  21.6 0.0 collective-permute-done.10
  21.6 1.3 %collective-permute-start.5 = (bf16[1,2,16,256]{3,2,1,0:T(8,128)(2,1)S(1)}, bf16[1,2,16,256]{3,2,1,0:T(8,128)(2,1)S(1)}, u32[]{:S(2)}, u32[]{:S(2)}) collective-permute-start(bf16[1,2,16,256]{3,2,1,0:T(8,128)(2,1)S(1)} %get-tuple-element.24), channel_id=1, source_target_pairs={{7,0},{4,1},{5,2},{6,3},{11,4},{8,5},{9,6},{10,7},{15,8},{12,9},{1... | collective-permute-start | bytes 49160 | tf_op jit(solution)/shard_map/ppermute | solution.py:31
  22.9 0.0 collective-permute-done.9
  22.9 1.6 %collective-permute-start.4 = (bf16[1,4,16,256]{3,2,1,0:T(8,128)(2,1)S(1)}, bf16[1,4,16,256]{3,2,1,0:T(8,128)(2,1)S(1)}, u32[]{:S(2)}, u32[]{:S(2)}) collective-permute-start(bf16[1,4,16,256]{3,2,1,0:T(8,128)(2,1)S(1)} %get-tuple-element.30), channel_id=1, source_target_pairs={{1,0},{2,1},{3,2},{0,3},{5,4},{6,5},{7,6},{4,7},{9,8},{10,9},{11,1... | collective-permute-start | bytes 98312 | tf_op jit(solution)/shard_map/ppermute | solution.py:31
  24.5 0.0 collective-permute-done.8
  24.5 6.2 %collective-permute-start.2 = (bf16[1,2,16,256]{3,2,1,0:T(8,128)(2,1)S(1)}, bf16[1,2,16,256]{3,2,1,0:T(8,128)(2,1)S(1)}, u32[]{:S(2)}, u32[]{:S(2)}) collective-permute-start(bf16[1,2,16,256]{3,2,1,0:T(8,128)(2,1)S(1)} %get-tuple-element.25), channel_id=1, source_target_pairs={{1,4},{2,5},{3,6},{0,7},{5,8},{6,9},{7,10},{4,11},{9,12},{10,13},{... | collective-permute-start | bytes 49160 | tf_op jit(solution)/shard_map/ppermute | solution.py:31
  30.7 0.1 collective-permute-start.3
  30.8 4.3 %collective-permute-start.1 = (bf16[1,2,64,256]{3,2,1,0:T(8,128)(2,1)S(1)}, bf16[1,2,64,256]{3,2,1,0:T(8,128)(2,1)S(1)}, u32[]{:S(2)}, u32[]{:S(2)}) collective-permute-start(bf16[1,2,64,256]{3,2,1,0:T(8,128)(2,1)S(1)} %get-tuple-element.27), channel_id=1, source_target_pairs={{0,4},{1,5},{2,6},{3,7},{4,8},{5,9},{6,10},{7,11},{8,12},{9,13},{1... | collective-permute-start | bytes 196616 | tf_op jit(solution)/shard_map/ppermute | solution.py:31
  35.1 4.1 %collective-permute-start = (bf16[1,2,16,256]{3,2,1,0:T(8,128)(2,1)S(1)}, bf16[1,2,16,256]{3,2,1,0:T(8,128)(2,1)S(1)}, u32[]{:S(2)}, u32[]{:S(2)}) collective-permute-start(bf16[1,2,16,256]{3,2,1,0:T(8,128)(2,1)S(1)} %get-tuple-element.23), channel_id=1, source_target_pairs={{3,4},{0,5},{1,6},{2,7},{7,8},{4,9},{5,10},{6,11},{11,12},{8,13},{... | collective-permute-start | bytes 49160 | tf_op jit(solution)/shard_map/ppermute | solution.py:31
  39.2 0.6 fusion.48
  39.8 0.8 collective-permute-done
  40.6 1.3 %collective-permute-start.18 = (bf16[1,2,16,256]{3,2,1,0:T(8,128)(2,1)S(1)}, bf16[1,2,16,256]{3,2,1,0:T(8,128)(2,1)S(1)}, u32[]{:S(2)}, u32[]{:S(2)}) collective-permute-start(bf16[1,2,16,256]{3,2,1,0:T(8,128)(2,1)S(1)} %get-tuple-element.18), channel_id=1, source_target_pairs={{5,0},{6,1},{7,2},{4,3},{9,4},{10,5},{11,6},{8,7},{13,8},{14,9},{1... | collective-permute-start | bytes 49160 | tf_op jit(solution)/shard_map/ppermute | solution.py:31
  41.9 1.3 %collective-permute-start.17 = (bf16[1,2,64,256]{3,2,1,0:T(8,128)(2,1)}, bf16[1,2,64,256]{3,2,1,0:T(8,128)(2,1)}, u32[]{:S(2)}, u32[]{:S(2)}) collective-permute-start(bf16[1,2,64,256]{3,2,1,0:T(8,128)(2,1)} %get-tuple-element.20), channel_id=1, source_target_pairs={{4,0},{5,1},{6,2},{7,3},{8,4},{9,5},{10,6},{11,7},{12,8},{13,9},{1... | collective-permute-start | bytes 196616 | tf_op jit(solution)/shard_map/ppermute | solution.py:31
  43.2 1.3 %collective-permute-start.16 = (bf16[1,2,16,256]{3,2,1,0:T(8,128)(2,1)S(1)}, bf16[1,2,16,256]{3,2,1,0:T(8,128)(2,1)S(1)}, u32[]{:S(2)}, u32[]{:S(2)}) collective-permute-start(bf16[1,2,16,256]{3,2,1,0:T(8,128)(2,1)S(1)} %get-tuple-element.16), channel_id=1, source_target_pairs={{7,0},{4,1},{5,2},{6,3},{11,4},{8,5},{9,6},{10,7},{15,8},{12,9},{1... | collective-permute-start | bytes 49160 | tf_op jit(solution)/shard_map/ppermute | solution.py:31
  44.5 0.5 collective-permute-start.15
  45.0 6.8 %collective-permute-start.13 = (bf16[1,2,16,256]{3,2,1,0:T(8,128)(2,1)S(1)}, bf16[1,2,16,256]{3,2,1,0:T(8,128)(2,1)S(1)}, u32[]{:S(2)}, u32[]{:S(2)}) collective-permute-start(bf16[1,2,16,256]{3,2,1,0:T(8,128)(2,1)S(1)} %get-tuple-element.17), channel_id=1, source_target_pairs={{1,4},{2,5},{3,6},{0,7},{5,8},{6,9},{7,10},{4,11},{9,12},{10,13},{... | collective-permute-start | bytes 49160 | tf_op jit(solution)/shard_map/ppermute | solution.py:31
  51.9 0.8 fusion.33.field_ref
  52.7 3.5 %shard_map.103 = bf16[1,4,64,2304]{3,2,1,0:T(8,128)(2,1)} custom-call(s32[4,12]{1,0:T(4,128)} %get-tuple-element.36.rows_ref, s32[4,12]{1,0:T(4,128)} %get-tuple-element.35.start_ref, s32[4,12]{1,0:T(4,128)} %get-tuple-element.34.span_ref, s32[4,12]{1,0:T(4,128)} %get-tuple-element.33.basis_ref, f32[4,12]{1,0:T(4,128)} %constant_dynamic-slice_fusion.scale_ref, ...), custom_call_target="tpu_custom_call" | custom-call | tf_op jit(solution)/shard_map/pallas_call | solution.py:131
  56.2 1.8 %convolution_bitcast_fusion = f32[9,256,256]{1,2,0:T(8,128)S(1)} fusion(bf16[4,8,9,8,256]{4,3,2,1,0:T(8,128)(2,1)} %bitcast.43, bf16[1,4,64,256]{3,2,1,0:T(8,128)(2,1)S(1)} %copy-done.4), kind=kOutput, calls=%fused_computation | convolution fusion | flops 301989888 | bytes 3670016 | tf_op jit(solution)/shard_map/brwq,brwo->qo/dot_general | solution.py:199
  58.0 0.0 copy-start.5
  58.0 0.1 collective-permute-start.14
  58.1 4.3 %collective-permute-start.12 = (bf16[1,2,64,256]{3,2,1,0:T(8,128)(2,1)}, bf16[1,2,64,256]{3,2,1,0:T(8,128)(2,1)S(1)}, u32[]{:S(2)}, u32[]{:S(2)}) collective-permute-start(bf16[1,2,64,256]{3,2,1,0:T(8,128)(2,1)} %get-tuple-element.19), channel_id=1, source_target_pairs={{0,4},{1,5},{2,6},{3,7},{4,8},{5,9},{6,10},{7,11},{8,12},{9,13},{1... | collective-permute-start | bytes 196616 | tf_op jit(solution)/shard_map/ppermute | solution.py:31
  62.4 4.1 %collective-permute-start.11 = (bf16[1,2,16,256]{3,2,1,0:T(8,128)(2,1)S(1)}, bf16[1,2,16,256]{3,2,1,0:T(8,128)(2,1)S(1)}, u32[]{:S(2)}, u32[]{:S(2)}) collective-permute-start(bf16[1,2,16,256]{3,2,1,0:T(8,128)(2,1)S(1)} %get-tuple-element.15), channel_id=1, source_target_pairs={{3,4},{0,5},{1,6},{2,7},{7,8},{4,9},{5,10},{6,11},{11,12},{8,13},{... | collective-permute-start | bytes 49160 | tf_op jit(solution)/shard_map/ppermute | solution.py:31
  66.5 1.0 dynamic-slice_convert_fusion.2
  67.5 0.5 collective-permute-done.11
  67.9 0.5 collective-permute-start.21
  68.5 1.4 %collective-permute-start.20 = (bf16[9,256,64]{1,2,0:T(8,128)(2,1)}, bf16[9,256,64]{1,2,0:T(8,128)(2,1)}, u32[]{:S(2)}, u32[]{:S(2)}) collective-permute-start(bf16[9,256,64]{1,2,0:T(8,128)(2,1)} %get-tuple-element.11), channel_id=1, source_target_pairs={{0,2},{1,3},{2,0},{3,1},{4,6},{5,7},{6,4},{7,5},{8,10},{9,11},{10,... | collective-permute-start | bytes 884744 | tf_op jit(solution)/shard_map/ppermute | solution.py:73
  69.9 0.1 collective-permute-start.19
  70.0 1.8 %fusion.41.field_ref = bf16[1,8,128,256]{3,2,1,0:T(8,128)(2,1)} fusion(bf16[1,2,16,256]{3,2,1,0:T(8,128)(2,1)S(1)} %collective-permute-done.18, bf16[1,2,64,256]{3,2,1,0:T(8,128)(2,1)} %collective-permute-done.17, bf16[1,2,16,256]{3,2,1,0:T(8,128)(2,1)} %copy-done.9, bf16[1,4,16,256]{3,2,1,0:T(8,128)(2,1)} %collective-permute-done.15, ...), kind=kLoop, calls=%fused_computation.43 | loop fusion | flops 7340032 | bytes 917504 | tf_op jit(solution)/shard_map/concatenate | solution.py:41
  71.8 10.3 %shard_map.104 = bf16[1,4,64,2304]{3,2,1,0:T(8,128)(2,1)} custom-call(s32[8,12]{1,0:T(8,128)} %copy-done.8, s32[8,12]{1,0:T(8,128)} %get-tuple-element.39.start_ref, s32[8,12]{1,0:T(8,128)} %get-tuple-element.38.span_ref, s32[8,12]{1,0:T(8,128)} %get-tuple-element.37.basis_ref, f32[4,96]{1,0:T(4,128)} %compare_select_fusion.scale_ref, ...), custom_call_target="tpu_custom_call" | custom-call | tf_op jit(solution)/shard_map/pallas_call | solution.py:131
  82.1 2.5 %fusion.6 = f32[1,4,64,256]{3,2,1,0:T(8,128)} fusion(bf16[2304,256,1]{1,0,2:T(8,128)(2,1)} %bitcast.44, bf16[1,4,64,2304]{3,2,1,0:T(8,128)(2,1)S(1)} %copy-done), kind=kOutput, calls=%fused_computation.7 | convolution fusion | flops 301989888 | bytes 2621440 | tf_op jit(solution)/shard_map/brwq,qo->brwo/dot_general | solution.py:182
  84.6 1.4 %convert_add_fusion = f32[9,256,64]{1,2,0:T(8,128)S(1)} fusion(bf16[9,256,64]{1,2,0:T(8,128)(2,1)} %collective-permute-done.21, bf16[9,256,64]{1,2,0:T(8,128)(2,1)} %collective-permute-done.20, bf16[9,256,64]{1,2,0:T(8,128)(2,1)} %collective-permute-done.19, f32[9,256,256]{1,2,0:T(8,128)S(1)} %convolution_bitcast_fusion, s32[]{:T(128)S(6)} %select_n.73), kind=kLoop, calls=%fused_computation.28 | loop fusion | flops 884736 | bytes 2064388 | tf_op jit(solution)/shard_map/add | solution.py:74
  86.0 0.2 dynamic-slice_convert_fusion.5
  86.2 0.8 collective-permute-start.24
  87.0 2.7 %collective-permute-start.23 = (bf16[9,64,64]{1,2,0:T(8,128)(2,1)S(1)}, bf16[9,64,64]{1,2,0:T(8,128)(2,1)S(1)}, u32[]{:S(2)}, u32[]{:S(2)}) collective-permute-start(bf16[9,64,64]{1,2,0:T(8,128)(2,1)S(1)} %get-tuple-element.14), channel_id=1, source_target_pairs={{0,8},{4,12},{8,0},{12,4},{1,9},{5,13},{9,1},{13,5},{2,10},{6,14},... | collective-permute-start | bytes 221192 | tf_op jit(solution)/shard_map/ppermute | solution.py:73
  89.7 1.2 %fusion.9 = f32[1,4,64,256]{3,2,1,0:T(8,128)} fusion(bf16[2304,256,1]{1,0,2:T(8,128)(2,1)S(1)} %bitcast.45, bf16[1,4,64,2304]{3,2,1,0:T(8,128)(2,1)S(1)} %copy-done.3), kind=kOutput, calls=%fused_computation.8 | convolution fusion | flops 301989888 | bytes 2621440 | tf_op jit(solution)/shard_map/bpwq,qc->bpwc/dot_general | solution.py:196
  90.9 1.8 %collective-permute-done.24 = bf16[9,64,64]{1,2,0:T(8,128)(2,1)S(1)} collective-permute-done((bf16[9,64,64]{1,2,0:T(8,128)(2,1)S(1)}, bf16[9,64,64]{1,2,0:T(8,128)(2,1)S(1)}, u32[]{:S(2)}, u32[]{:S(2)}) %collective-permute-start.24) | collective-permute-done | bytes 73760 | tf_op jit(solution)/shard_map/ppermute | solution.py:73
  92.6 10.5 %collective-permute-done.23 = bf16[9,64,64]{1,2,0:T(8,128)(2,1)S(1)} collective-permute-done((bf16[9,64,64]{1,2,0:T(8,128)(2,1)S(1)}, bf16[9,64,64]{1,2,0:T(8,128)(2,1)S(1)}, u32[]{:S(2)}, u32[]{:S(2)}) %collective-permute-start.23) | collective-permute-done | bytes 73760 | tf_op jit(solution)/shard_map/ppermute | solution.py:73
  103.2 0.1 add_multiply_fusion
  103.3 0.9 copy.17
  (47 shorter events, 0.2 us)
Async XLA Ops:
  0.6 17.9 %copy-start.4 = (bf16[1,4,64,256]{3,2,1,0:T(8,128)(2,1)S(1)}, bf16[1,4,64,256]{3,2,1,0:T(8,128)(2,1)}, u32[]{:S(2)}) copy-start(bf16[1,4,64,256]{3,2,1,0:T(8,128)(2,1)} %param.9) | copy-start | bytes 393220
  0.6 17.9 %copy-start.7 = (s32[16,12]{1,0:T(8,128)S(1)}, s32[16,12]{1,0:T(8,128)}, u32[]{:S(2)}) copy-start(s32[16,12]{1,0:T(8,128)} %param.13) | copy-start | bytes 2308
  0.7 17.9 %copy-start.11 = (f32[16,12]{1,0:T(8,128)S(1)}, f32[16,12]{1,0:T(8,128)}, u32[]{:S(2)}) copy-start(f32[16,12]{1,0:T(8,128)} %param.15) | copy-start | bytes 2308
  0.7 19.4 %copy-start.1 = (bf16[9,256,256]{2,1,0:T(8,128)(2,1)S(1)}, bf16[9,256,256]{2,1,0:T(8,128)(2,1)}, u32[]{:S(2)}) copy-start(bf16[9,256,256]{2,1,0:T(8,128)(2,1)} %param.10) | copy-start | bytes 3538948
  2.7 18.9 %collective-permute-start.10 = (f32[2,1,4,256]{3,0,2,1:T(2,128)S(1)}, f32[2,1,4,256]{3,0,2,1:T(2,128)S(1)}, u32[]{:S(2)}, u32[]{:S(2)}) collective-permute-start(f32[2,1,4,256]{3,0,2,1:T(2,128)S(1)} %pad_maximum_fusion), channel_id=1, source_target_pairs={{0,3},{1,0},{2,1},{3,2},{4,7},{5,4},{6,5},{7,6},{8,11},{9,8},{10,9... | collective-permute-start | bytes 24584 | tf_op jit(solution)/shard_map/ppermute | solution.py:51
  5.1 17.7 %collective-permute-start.9 = (f32[2,1,4,256]{3,0,2,1:T(2,128)S(1)}, f32[2,1,4,256]{3,0,2,1:T(2,128)S(1)}, u32[]{:S(2)}, u32[]{:S(2)}) collective-permute-start(f32[2,1,4,256]{3,0,2,1:T(2,128)S(1)} %pad_maximum_fusion), channel_id=1, source_target_pairs={{0,2},{1,3},{2,0},{3,1},{4,6},{5,7},{6,4},{7,5},{8,10},{9,11},{10,... | collective-permute-start | bytes 24584 | tf_op jit(solution)/shard_map/ppermute | solution.py:51
  5.8 18.7 %collective-permute-start.8 = (f32[2,1,4,256]{3,0,2,1:T(2,128)S(1)}, f32[2,1,4,256]{3,0,2,1:T(2,128)S(1)}, u32[]{:S(2)}, u32[]{:S(2)}) collective-permute-start(f32[2,1,4,256]{3,0,2,1:T(2,128)S(1)} %pad_maximum_fusion), channel_id=1, source_target_pairs={{0,1},{1,2},{2,3},{3,0},{4,5},{5,6},{6,7},{7,4},{8,9},{9,10},{10,1... | collective-permute-start | bytes 24584 | tf_op jit(solution)/shard_map/ppermute | solution.py:51
  6.7 24.0 %collective-permute-start.7 = (bf16[1,2,16,256]{3,2,1,0:T(8,128)(2,1)S(1)}, bf16[1,2,16,256]{3,2,1,0:T(8,128)(2,1)S(1)}, u32[]{:S(2)}, u32[]{:S(2)}) collective-permute-start(bf16[1,2,16,256]{3,2,1,0:T(8,128)(2,1)S(1)} %get-tuple-element.26), channel_id=1, source_target_pairs={{5,0},{6,1},{7,2},{4,3},{9,4},{10,5},{11,6},{8,7},{13,8},{14,9},{1... | collective-permute-start | bytes 49160 | tf_op jit(solution)/shard_map/ppermute | solution.py:31
  8.9 35.6 %collective-permute-start.6 = (bf16[1,2,64,256]{3,2,1,0:T(8,128)(2,1)S(1)}, bf16[1,2,64,256]{3,2,1,0:T(8,128)(2,1)S(1)}, u32[]{:S(2)}, u32[]{:S(2)}) collective-permute-start(bf16[1,2,64,256]{3,2,1,0:T(8,128)(2,1)S(1)} %get-tuple-element.28), channel_id=1, source_target_pairs={{4,0},{5,1},{6,2},{7,3},{8,4},{9,5},{10,6},{11,7},{12,8},{13,9},{1... | collective-permute-start | bytes 196616 | tf_op jit(solution)/shard_map/ppermute | solution.py:31
  13.6 8.0 %copy-start.8 = (s32[8,12]{1,0:T(8,128)}, s32[8,12]{1,0:T(8,128)S(1)}, u32[]{:S(2)}) copy-start(s32[8,12]{1,0:T(8,128)S(1)} %get-tuple-element.40.rows_ref) | copy-start | bytes 1156
  20.0 31.8 %copy-start.6 = (bf16[1,4,64,256]{3,2,1,0:T(8,128)(2,1)S(1)}, bf16[1,4,64,256]{3,2,1,0:T(8,128)(2,1)}, u32[]{:S(2)}) copy-start(bf16[1,4,64,256]{3,2,1,0:T(8,128)(2,1)} %param.8) | copy-start | bytes 393220
  21.6 9.2 %collective-permute-start.5 = (bf16[1,2,16,256]{3,2,1,0:T(8,128)(2,1)S(1)}, bf16[1,2,16,256]{3,2,1,0:T(8,128)(2,1)S(1)}, u32[]{:S(2)}, u32[]{:S(2)}) collective-permute-start(bf16[1,2,16,256]{3,2,1,0:T(8,128)(2,1)S(1)} %get-tuple-element.24), channel_id=1, source_target_pairs={{7,0},{4,1},{5,2},{6,3},{11,4},{8,5},{9,6},{10,7},{15,8},{12,9},{1... | collective-permute-start | bytes 49160 | tf_op jit(solution)/shard_map/ppermute | solution.py:31
  22.9 19.0 %collective-permute-start.4 = (bf16[1,4,16,256]{3,2,1,0:T(8,128)(2,1)S(1)}, bf16[1,4,16,256]{3,2,1,0:T(8,128)(2,1)S(1)}, u32[]{:S(2)}, u32[]{:S(2)}) collective-permute-start(bf16[1,4,16,256]{3,2,1,0:T(8,128)(2,1)S(1)} %get-tuple-element.30), channel_id=1, source_target_pairs={{1,0},{2,1},{3,2},{0,3},{5,4},{6,5},{7,6},{4,7},{9,8},{10,9},{11,1... | collective-permute-start | bytes 98312 | tf_op jit(solution)/shard_map/ppermute | solution.py:31
  24.5 10.6 %collective-permute-start.2 = (bf16[1,2,16,256]{3,2,1,0:T(8,128)(2,1)S(1)}, bf16[1,2,16,256]{3,2,1,0:T(8,128)(2,1)S(1)}, u32[]{:S(2)}, u32[]{:S(2)}) collective-permute-start(bf16[1,2,16,256]{3,2,1,0:T(8,128)(2,1)S(1)} %get-tuple-element.25), channel_id=1, source_target_pairs={{1,4},{2,5},{3,6},{0,7},{5,8},{6,9},{7,10},{4,11},{9,12},{10,13},{... | collective-permute-start | bytes 49160 | tf_op jit(solution)/shard_map/ppermute | solution.py:31
  30.7 12.5 %collective-permute-start.3 = (bf16[1,4,16,256]{3,2,1,0:T(8,128)(2,1)S(1)}, bf16[1,4,16,256]{3,2,1,0:T(8,128)(2,1)S(1)}, u32[]{:S(2)}, u32[]{:S(2)}) collective-permute-start(bf16[1,4,16,256]{3,2,1,0:T(8,128)(2,1)S(1)} %get-tuple-element.29), channel_id=1, source_target_pairs={{3,0},{0,1},{1,2},{2,3},{7,4},{4,5},{5,6},{6,7},{11,8},{8,9},{9,10... | collective-permute-start | bytes 98312 | tf_op jit(solution)/shard_map/ppermute | solution.py:31
  30.8 14.2 %collective-permute-start.1 = (bf16[1,2,64,256]{3,2,1,0:T(8,128)(2,1)S(1)}, bf16[1,2,64,256]{3,2,1,0:T(8,128)(2,1)S(1)}, u32[]{:S(2)}, u32[]{:S(2)}) collective-permute-start(bf16[1,2,64,256]{3,2,1,0:T(8,128)(2,1)S(1)} %get-tuple-element.27), channel_id=1, source_target_pairs={{0,4},{1,5},{2,6},{3,7},{4,8},{5,9},{6,10},{7,11},{8,12},{9,13},{1... | collective-permute-start | bytes 196616 | tf_op jit(solution)/shard_map/ppermute | solution.py:31
  35.1 5.5 %collective-permute-start = (bf16[1,2,16,256]{3,2,1,0:T(8,128)(2,1)S(1)}, bf16[1,2,16,256]{3,2,1,0:T(8,128)(2,1)S(1)}, u32[]{:S(2)}, u32[]{:S(2)}) collective-permute-start(bf16[1,2,16,256]{3,2,1,0:T(8,128)(2,1)S(1)} %get-tuple-element.23), channel_id=1, source_target_pairs={{3,4},{0,5},{1,6},{2,7},{7,8},{4,9},{5,10},{6,11},{11,12},{8,13},{... | collective-permute-start | bytes 49160 | tf_op jit(solution)/shard_map/ppermute | solution.py:31
  40.6 17.4 %collective-permute-start.18 = (bf16[1,2,16,256]{3,2,1,0:T(8,128)(2,1)S(1)}, bf16[1,2,16,256]{3,2,1,0:T(8,128)(2,1)S(1)}, u32[]{:S(2)}, u32[]{:S(2)}) collective-permute-start(bf16[1,2,16,256]{3,2,1,0:T(8,128)(2,1)S(1)} %get-tuple-element.18), channel_id=1, source_target_pairs={{5,0},{6,1},{7,2},{4,3},{9,4},{10,5},{11,6},{8,7},{13,8},{14,9},{1... | collective-permute-start | bytes 49160 | tf_op jit(solution)/shard_map/ppermute | solution.py:31
  41.9 28.0 %collective-permute-start.17 = (bf16[1,2,64,256]{3,2,1,0:T(8,128)(2,1)}, bf16[1,2,64,256]{3,2,1,0:T(8,128)(2,1)}, u32[]{:S(2)}, u32[]{:S(2)}) collective-permute-start(bf16[1,2,64,256]{3,2,1,0:T(8,128)(2,1)} %get-tuple-element.20), channel_id=1, source_target_pairs={{4,0},{5,1},{6,2},{7,3},{8,4},{9,5},{10,6},{11,7},{12,8},{13,9},{1... | collective-permute-start | bytes 196616 | tf_op jit(solution)/shard_map/ppermute | solution.py:31
  43.2 14.9 %collective-permute-start.16 = (bf16[1,2,16,256]{3,2,1,0:T(8,128)(2,1)S(1)}, bf16[1,2,16,256]{3,2,1,0:T(8,128)(2,1)S(1)}, u32[]{:S(2)}, u32[]{:S(2)}) collective-permute-start(bf16[1,2,16,256]{3,2,1,0:T(8,128)(2,1)S(1)} %get-tuple-element.16), channel_id=1, source_target_pairs={{7,0},{4,1},{5,2},{6,3},{11,4},{8,5},{9,6},{10,7},{15,8},{12,9},{1... | collective-permute-start | bytes 49160 | tf_op jit(solution)/shard_map/ppermute | solution.py:31
  44.5 24.0 %collective-permute-start.15 = (bf16[1,4,16,256]{3,2,1,0:T(8,128)(2,1)S(1)}, bf16[1,4,16,256]{3,2,1,0:T(8,128)(2,1)}, u32[]{:S(2)}, u32[]{:S(2)}) collective-permute-start(bf16[1,4,16,256]{3,2,1,0:T(8,128)(2,1)S(1)} %get-tuple-element.22), channel_id=1, source_target_pairs={{1,0},{2,1},{3,2},{0,3},{5,4},{6,5},{7,6},{4,7},{9,8},{10,9},{11,1... | collective-permute-start | bytes 98312 | tf_op jit(solution)/shard_map/ppermute | solution.py:31
  45.0 17.4 %collective-permute-start.13 = (bf16[1,2,16,256]{3,2,1,0:T(8,128)(2,1)S(1)}, bf16[1,2,16,256]{3,2,1,0:T(8,128)(2,1)S(1)}, u32[]{:S(2)}, u32[]{:S(2)}) collective-permute-start(bf16[1,2,16,256]{3,2,1,0:T(8,128)(2,1)S(1)} %get-tuple-element.17), channel_id=1, source_target_pairs={{1,4},{2,5},{3,6},{0,7},{5,8},{6,9},{7,10},{4,11},{9,12},{10,13},{... | collective-permute-start | bytes 49160 | tf_op jit(solution)/shard_map/ppermute | solution.py:31
  58.0 11.9 %copy-start.5 = (bf16[1,4,64,256]{3,2,1,0:T(8,128)(2,1)S(1)}, bf16[1,4,64,256]{3,2,1,0:T(8,128)(2,1)}, u32[]{:S(2)}) copy-start(bf16[1,4,64,256]{3,2,1,0:T(8,128)(2,1)} %param.9) | copy-start | bytes 393220
  58.0 11.8 %collective-permute-start.14 = (bf16[1,4,16,256]{3,2,1,0:T(8,128)(2,1)S(1)}, bf16[1,4,16,256]{3,2,1,0:T(8,128)(2,1)S(1)}, u32[]{:S(2)}, u32[]{:S(2)}) collective-permute-start(bf16[1,4,16,256]{3,2,1,0:T(8,128)(2,1)S(1)} %get-tuple-element.21), channel_id=1, source_target_pairs={{3,0},{0,1},{1,2},{2,3},{7,4},{4,5},{5,6},{6,7},{11,8},{8,9},{9,10... | collective-permute-start | bytes 98312 | tf_op jit(solution)/shard_map/ppermute | solution.py:31
  58.1 11.7 %copy-start.9 = (bf16[1,2,16,256]{3,2,1,0:T(8,128)(2,1)}, bf16[1,2,16,256]{3,2,1,0:T(8,128)(2,1)S(1)}, u32[]{:S(2)}) copy-start(bf16[1,2,16,256]{3,2,1,0:T(8,128)(2,1)S(1)} %collective-permute-done.16) | copy-start | bytes 49156
  58.1 11.8 %collective-permute-start.12 = (bf16[1,2,64,256]{3,2,1,0:T(8,128)(2,1)}, bf16[1,2,64,256]{3,2,1,0:T(8,128)(2,1)S(1)}, u32[]{:S(2)}, u32[]{:S(2)}) collective-permute-start(bf16[1,2,64,256]{3,2,1,0:T(8,128)(2,1)} %get-tuple-element.19), channel_id=1, source_target_pairs={{0,4},{1,5},{2,6},{3,7},{4,8},{5,9},{6,10},{7,11},{8,12},{9,13},{1... | collective-permute-start | bytes 196616 | tf_op jit(solution)/shard_map/ppermute | solution.py:31
  62.4 7.5 %copy-start.10 = (bf16[1,2,16,256]{3,2,1,0:T(8,128)(2,1)}, bf16[1,2,16,256]{3,2,1,0:T(8,128)(2,1)S(1)}, u32[]{:S(2)}) copy-start(bf16[1,2,16,256]{3,2,1,0:T(8,128)(2,1)S(1)} %collective-permute-done.13) | copy-start | bytes 49156
  62.4 5.5 %collective-permute-start.11 = (bf16[1,2,16,256]{3,2,1,0:T(8,128)(2,1)S(1)}, bf16[1,2,16,256]{3,2,1,0:T(8,128)(2,1)S(1)}, u32[]{:S(2)}, u32[]{:S(2)}) collective-permute-start(bf16[1,2,16,256]{3,2,1,0:T(8,128)(2,1)S(1)} %get-tuple-element.15), channel_id=1, source_target_pairs={{3,4},{0,5},{1,6},{2,7},{7,8},{4,9},{5,10},{6,11},{11,12},{8,13},{... | collective-permute-start | bytes 49160 | tf_op jit(solution)/shard_map/ppermute | solution.py:31
  67.9 16.6 %collective-permute-start.21 = (bf16[9,256,64]{1,2,0:T(8,128)(2,1)}, bf16[9,256,64]{1,2,0:T(8,128)(2,1)}, u32[]{:S(2)}, u32[]{:S(2)}) collective-permute-start(bf16[9,256,64]{1,2,0:T(8,128)(2,1)} %get-tuple-element.10), channel_id=1, source_target_pairs={{0,3},{1,0},{2,1},{3,2},{4,7},{5,4},{6,5},{7,6},{8,11},{9,8},{10,9... | collective-permute-start | bytes 884744 | tf_op jit(solution)/shard_map/ppermute | solution.py:73
  68.5 16.1 %collective-permute-start.20 = (bf16[9,256,64]{1,2,0:T(8,128)(2,1)}, bf16[9,256,64]{1,2,0:T(8,128)(2,1)}, u32[]{:S(2)}, u32[]{:S(2)}) collective-permute-start(bf16[9,256,64]{1,2,0:T(8,128)(2,1)} %get-tuple-element.11), channel_id=1, source_target_pairs={{0,2},{1,3},{2,0},{3,1},{4,6},{5,7},{6,4},{7,5},{8,10},{9,11},{10,... | collective-permute-start | bytes 884744 | tf_op jit(solution)/shard_map/ppermute | solution.py:73
  69.9 12.2 %copy-start = (bf16[1,4,64,2304]{3,2,1,0:T(8,128)(2,1)S(1)}, bf16[1,4,64,2304]{3,2,1,0:T(8,128)(2,1)}, u32[]{:S(2)}) copy-start(bf16[1,4,64,2304]{3,2,1,0:T(8,128)(2,1)} %shard_map.103) | copy-start | bytes 3538948
  69.9 14.7 %collective-permute-start.19 = (bf16[9,256,64]{1,2,0:T(8,128)(2,1)}, bf16[9,256,64]{1,2,0:T(8,128)(2,1)}, u32[]{:S(2)}, u32[]{:S(2)}) collective-permute-start(bf16[9,256,64]{1,2,0:T(8,128)(2,1)} %get-tuple-element.9), channel_id=1, source_target_pairs={{0,1},{1,2},{2,3},{3,0},{4,5},{5,6},{6,7},{7,4},{8,9},{9,10},{10,1... | collective-permute-start | bytes 884744 | tf_op jit(solution)/shard_map/ppermute | solution.py:73
  84.5 5.1 %copy-start.2 = (bf16[9,256,256]{1,2,0:T(8,128)(2,1)S(1)}, bf16[9,256,256]{1,2,0:T(8,128)(2,1)}, u32[]{:S(2)}) copy-start(bf16[9,256,256]{1,2,0:T(8,128)(2,1)} %copy.15) | copy-start | bytes 3538948
  84.5 5.1 %copy-start.3 = (bf16[1,4,64,2304]{3,2,1,0:T(8,128)(2,1)S(1)}, bf16[1,4,64,2304]{3,2,1,0:T(8,128)(2,1)}, u32[]{:S(2)}) copy-start(bf16[1,4,64,2304]{3,2,1,0:T(8,128)(2,1)} %shard_map.104) | copy-start | bytes 3538948
  86.2 6.5 %collective-permute-start.24 = (bf16[9,64,64]{1,2,0:T(8,128)(2,1)S(1)}, bf16[9,64,64]{1,2,0:T(8,128)(2,1)S(1)}, u32[]{:S(2)}, u32[]{:S(2)}) collective-permute-start(bf16[9,64,64]{1,2,0:T(8,128)(2,1)S(1)} %get-tuple-element.13), channel_id=1, source_target_pairs={{0,12},{4,0},{8,4},{12,8},{1,13},{5,1},{9,5},{13,9},{2,14},{6,2},{... | collective-permute-start | bytes 221192 | tf_op jit(solution)/shard_map/ppermute | solution.py:73
  87.0 16.2 %collective-permute-start.23 = (bf16[9,64,64]{1,2,0:T(8,128)(2,1)S(1)}, bf16[9,64,64]{1,2,0:T(8,128)(2,1)S(1)}, u32[]{:S(2)}, u32[]{:S(2)}) collective-permute-start(bf16[9,64,64]{1,2,0:T(8,128)(2,1)S(1)} %get-tuple-element.14), channel_id=1, source_target_pairs={{0,8},{4,12},{8,0},{12,4},{1,9},{5,13},{9,1},{13,5},{2,10},{6,14},... | collective-permute-start | bytes 221192 | tf_op jit(solution)/shard_map/ppermute | solution.py:73
  89.7 13.5 %collective-permute-start.22 = (bf16[9,64,64]{1,2,0:T(8,128)(2,1)S(1)}, bf16[9,64,64]{1,2,0:T(8,128)(2,1)S(1)}, u32[]{:S(2)}, u32[]{:S(2)}) collective-permute-start(bf16[9,64,64]{1,2,0:T(8,128)(2,1)S(1)} %get-tuple-element.12), channel_id=1, source_target_pairs={{0,4},{4,8},{8,12},{12,0},{1,5},{5,9},{9,13},{13,1},{2,6},{6,10},{... | collective-permute-start | bytes 221192 | tf_op jit(solution)/shard_map/ppermute | solution.py:73

commit v6 on v4

--- a/solution.py
+++ b/solution.py
@@ -10,6 +10,7 @@
 BASIS = 9
 REACH = 2
 RIM = 16
+POLAR = 2
 
 
 def with_halo(block, sides, width, periodic):
@@ -43,11 +44,6 @@
     return total
 
 
-def cycle_totals(widened, lon_count):
-    interior = lax.slice_in_dim(widened, RIM, RIM + lon_count, axis=2)
-    return ring_sum(jnp.sum(interior, axis=2, dtype=jnp.float32), "lon")
-
-
 def ring_scatter(value, axis, dim):
     count = lax.axis_size(axis)
     own = lax.axis_index(axis)
@@ -62,10 +58,11 @@
 
 
 def filter_kernel(
-    rows_ref, start_ref, span_ref, basis_ref, scale_ref, field_ref, total_ref, out_ref, acc_ref,
-    *, slots, window_rows, lon_count, lon_total, backward,
+    first_ref, src_ref, start_ref, span_ref, basis_ref, scale_ref, field_ref, total_ref,
+    out_ref, acc_ref, *, slots, height, lon_count, lon_total, backward,
 ):
     r = pl.program_id(1)
+    first_row = first_ref[0]
     padded = field_ref.shape[2]
     channels = field_ref.shape[3]
     acc_ref[...] = jnp.zeros(acc_ref.shape, jnp.float32)
@@ -85,31 +82,37 @@
         acc_ref[basis] = acc_ref[basis] + scale * boxed
 
     if backward:
-        for e in range(window_rows):
+        target = first_row + r
+        for e in range(2 * REACH + 1):
             row = r + e
+            global_row = target + e - REACH
+            inside = (global_row >= 0) & (global_row < height)
+            table_row = jnp.clip(global_row, 0, height - 1)
             for slot in range(slots):
-                scale = scale_ref[r, row * slots + slot]
-
-                @pl.when(scale != 0.0)
+                scale = scale_ref[table_row, slot]
+                hit = inside & (src_ref[table_row, slot] == target) & (scale != 0.0)
+
+                @pl.when(hit)
                 def _():
-                    add_slot(row, row, slot, scale)
+                    add_slot(row, table_row, slot, scale)
     else:
+        table_row = first_row + r
         for slot in range(slots):
-            add_slot(rows_ref[r, slot], r, slot, scale_ref[r, slot])
+            row = src_ref[table_row, slot] - first_row + REACH
+            add_slot(row, table_row, slot, scale_ref[table_row, slot])
 
     for k in range(BASIS):
         out_ref[0, 0, :, k * channels:(k + 1) * channels] = acc_ref[k].astype(jnp.bfloat16)
 
 
-def run_filter(tables, field, totals, lon_count, lon_total, backward):
+def run_filter(first, tables, field, totals, row_count, lon_count, lon_total, backward):
     members, window, padded, channels = field.shape
-    row_count = window - 2 * REACH
-    slots = tables[1].shape[1]
+    height, slots = tables[0].shape
     smem = pl.BlockSpec(memory_space=pltpu.SMEM)
     kernel = functools.partial(
         filter_kernel,
         slots=slots,
-        window_rows=2 * REACH + 1,
+        height=height,
         lon_count=lon_count,
         lon_total=lon_total,
         backward=backward,
@@ -117,7 +120,7 @@
     return pl.pallas_call(
         kernel,
         grid=(members, row_count),
-        in_specs=[smem] * 5
+        in_specs=[smem] * 6
         + [
             pl.BlockSpec((1, window, padded, channels), lambda b, r: (b, 0, 0, 0)),
             pl.BlockSpec((1, window, 1, channels), lambda b, r: (b, 0, 0, 0)),
@@ -129,7 +132,7 @@
             (members, row_count, lon_count, BASIS * channels), jnp.bfloat16
         ),
         scratch_shapes=[pltpu.VMEM((BASIS, lon_count, channels), jnp.float32)],
-    )(*tables, field, totals[:, :, None, :])
+    )(first, *tables, field, totals[:, :, None, :])
 
 
 def on_device(inputs, cotangent, weight, src_rows, lon_start, lon_span, basis_idx, quad_weight):
@@ -137,40 +140,31 @@
     lon_total = lon_count * lax.axis_size("lon")
     height = row_count * lax.axis_size("lat")
     first_row = lax.axis_index("lat") * row_count
-    window = row_count + 2 * REACH
     padded = -(-(lon_count + 2 * RIM) // 128) * 128
     weighting = quad_weight / jnp.sqrt(lon_span.astype(jnp.float32))
-
-    widened = extend(inputs, padded)
-    grad_wide = extend(cotangent, padded)
-    totals = cycle_totals(widened, lon_count)
-    grad_totals = cycle_totals(grad_wide, lon_count)
-
-    def rows_of(table, begin, count):
-        return lax.dynamic_slice_in_dim(table, begin, count, 0)
-
-    f_tables = (
-        rows_of(src_rows, first_row, row_count) - first_row + REACH,
-        rows_of(lon_start, first_row, row_count),
-        rows_of(lon_span, first_row, row_count),
-        rows_of(basis_idx, first_row, row_count),
-        rows_of(weighting, first_row, row_count),
-    )
-    flattened = run_filter(f_tables, widened, totals, lon_count, lon_total, False)
+    first = jnp.reshape(first_row, (1,)).astype(jnp.int32)
+    tables = (src_rows, lon_start, lon_span, basis_idx, weighting)
+
+    both = extend(jnp.concatenate([inputs, cotangent], axis=3), padded)
+    widened = both[..., :channels]
+    grad_wide = both[..., channels:]
+    row_sums = jnp.stack(
+        [jnp.sum(inputs, axis=2, dtype=jnp.float32), jnp.sum(cotangent, axis=2, dtype=jnp.float32)]
+    )
+    local_totals = ring_sum(row_sums, "lon")
+    if row_count >= POLAR + REACH:
+        framed = jnp.pad(local_totals, ((0, 0), (0, 0), (REACH, REACH), (0, 0)))
+    else:
+        framed = with_halo(local_totals, (("lat", 2),), REACH, False)
+    totals, grad_totals = framed[0], framed[1]
+
+    flattened = run_filter(first, tables, widened, totals, row_count, lon_count, lon_total, False)
     w_fwd = weight.reshape(BASIS * channels, channels)
     response = jnp.einsum("brwq,qo->brwo", flattened, w_fwd, preferred_element_type=jnp.float32)
 
-    pad_pair = ((REACH, REACH), (0, 0))
-    b_src = rows_of(jnp.pad(src_rows, pad_pair, constant_values=-1), first_row, window)
-    b_start = rows_of(jnp.pad(lon_start, pad_pair, constant_values=0), first_row, window)
-    b_span = rows_of(jnp.pad(lon_span, pad_pair, constant_values=1), first_row, window)
-    b_basis = rows_of(jnp.pad(basis_idx, pad_pair, constant_values=0), first_row, window)
-    b_scale = rows_of(jnp.pad(weighting, pad_pair, constant_values=0.0), first_row, window)
-    targets = first_row + jnp.arange(row_count, dtype=jnp.int32)
-    b_hit = b_src[None, :, :] == targets[:, None, None]
-    b_weights = jnp.where(b_hit, b_scale[None], 0.0).reshape(row_count, -1)
-    b_tables = (b_src, b_start, b_span, b_basis, b_weights)
-    back_filtered = run_filter(b_tables, grad_wide, grad_totals, lon_count, lon_total, True)
+    back_filtered = run_filter(
+        first, tables, grad_wide, grad_totals, row_count, lon_count, lon_total, True
+    )
     w_back = jnp.transpose(weight, (0, 2, 1)).reshape(BASIS * channels, channels)
     grad_input = jnp.einsum(
         "bpwq,qc->bpwc", back_filtered, w_back, preferred_element_type=jnp.float32

time: 80.6 us -> 68 us (0.84)
  starting transfers between devices: 27.5 us -> 17.2 us
  waiting for transfers between devices: 12.7 us -> 18.2 us
  local copies, waits for them, and re-layouts: 11.8 us -> 7.15 us
  other arithmetic: 8.23 us -> 4.21 us
  Pallas kernels: 13.4 us -> 14.5 us
    ppermute x4 -> x2, starting transfers between devices: 6.07 us -> 1.45 us  [with_halo(): lax.ppermute(lax.slice_in_dim(block, 0, width, axis=dim), axis, backward)]
    dynamic_slice x5 -> x0, local copies, waits for them, and re-layouts: 4.54 us -> none  [rows_of(): return lax.dynamic_slice_in_dim(table, begin, count, 0)]
    ppermute x4 -> x2, starting transfers between devices: 9.49 us -> 4.96 us  [with_halo(): lax.ppermute(lax.slice_in_dim(block, block.shape[dim] - width, None, axis...]
    ppermute x4 -> x2, waiting for transfers between devices: 1.38 us -> 4.56 us  [with_halo(): lax.ppermute(lax.slice_in_dim(block, block.shape[dim] - width, None, axis...]
    ppermute x4 -> x2, waiting for transfers between devices: 0.01 us -> 3.01 us  [with_halo(): lax.ppermute(lax.slice_in_dim(block, 0, width, axis=dim), axis, backward)]
    concatenate x2 -> x1, other arithmetic: 2.64 us -> 0.09 us  [with_halo(): block = jnp.concatenate([low, block, high], axis=dim)]
    reduce_sum x2, other arithmetic: 0.1 us -> 1.88 us  [the longest x1 0.95 us: on_device(): jnp.sum(cotangent, axis=2, dtype=jnp.float32)]
    dynamic_slice x1 -> x0, other arithmetic: 1.31 us -> none  [rows_of(): return lax.dynamic_slice_in_dim(table, begin, count, 0)]
  transfers between devices with their start and end apart: 20 -> 13, of which waited for: 4 -> 6; matrix products, arithmetic and copies ran while one was open for 27% -> 12% of each run, Pallas kernels for 17% -> 16%
where the time goes in v6:
time: 68 us; the launch traced here: 67.5 us
  waiting for transfers between devices  18.2 us (27%)
  starting transfers between devices  17.2 us (25%)
  Pallas kernels  14.5 us (21%)
  local copies, waits for them, and re-layouts  7.15 us (11%)
  matrix products  5.42 us (8%)
  other arithmetic  4.21 us (6%)
  between operations  0.85 us (1%)
    pallas_call x2, Pallas kernels, run_filter(): pl.pallas_call(kernel, grid=(members, row_count), in_specs=[smem] * 6 + [...  14.5 us
    ppermute x6, waiting for transfers between devices, ring_scatter(): sent = lax.ppermute(piece.astype(jnp.bfloat16), axis, pairs)  10.7 us
    ppermute x6, starting transfers between devices, ring_scatter(): sent = lax.ppermute(piece.astype(jnp.bfloat16), axis, pairs)  7.51 us
    ppermute x2, starting transfers between devices, with_halo(): lax.ppermute(lax.slice_in_dim(block, block.shape[dim] - width, None, axis...  4.96 us
    ppermute x2, waiting for transfers between devices, with_halo(): lax.ppermute(lax.slice_in_dim(block, block.shape[dim] - width, None, axis...  4.56 us
    unnamed x17, local copies, waits for them, and re-layouts  3.34 us
    ppermute x3, starting transfers between devices, ring_sum(): total = total + lax.ppermute(value, axis, pairs)  3.23 us
    ppermute x2, waiting for transfers between devices, with_halo(): lax.ppermute(lax.slice_in_dim(block, 0, width, axis=dim), axis, backward)  3.01 us
  transfers between devices with their start and end apart: 13, of which 6 were waited for; matrix products, arithmetic and copies ran while one was open for 12% of the time, Pallas kernels for 16%

profile of v6, /device:TPU:0, one launch (start us, length us, event | category | flops | bytes accessed | tf_op | source)
XLA Modules:
  0.0 67.5 jit_solution(6755829894899711361)
XLA Ops:
  0.6 0.0 copy-start.5
  0.6 0.0 copy-start.6
  0.7 0.9 %convert_reduce_fusion = f32[4,256]{1,0:T(4,128)S(1)} fusion(bf16[1,4,64,256]{3,2,1,0:T(8,128)(2,1)} %param.9), kind=kLoop, calls=%fused_computation.27 | loop fusion | flops 130048 | bytes 135168 | tf_op jit(solution)/shard_map/reduce_sum | solution.py:152
  1.6 0.9 %convert_reduce_fusion.1 = f32[4,256]{1,0:T(4,128)S(1)} fusion(bf16[1,4,64,256]{3,2,1,0:T(8,128)(2,1)} %param.8), kind=kLoop, calls=%fused_computation.28 | loop fusion | flops 130048 | bytes 135168 | tf_op jit(solution)/shard_map/reduce_sum | solution.py:152
  2.6 2.4 %collective-permute-start.6 = (f32[2,1,4,256]{3,0,2,1:T(2,128)S(1)}, f32[2,1,4,256]{3,0,2,1:T(2,128)S(1)}, u32[]{:S(2)}, u32[]{:S(2)}) collective-permute-start(f32[2,1,4,256]{3,0,2,1:T(2,128)S(1)} %pad_maximum_fusion.3), channel_id=1, source_target_pairs={{0,3},{1,0},{2,1},{3,2},{4,7},{5,4},{6,5},{7,6},{8,11},{9,8},{10,9... | collective-permute-start | bytes 24584 | tf_op jit(solution)/shard_map/ppermute | solution.py:43
  5.0 0.6 collective-permute-start.5
  5.7 0.2 collective-permute-start.4
  5.8 0.9 %constant_dynamic-update-slice_fusion.1 = bf16[1,4,64,512]{3,2,1,0:T(8,128)(2,1)S(1)} fusion(bf16[1,4,64,256]{3,2,1,0:T(8,128)(2,1)} %param.8), kind=kLoop, calls=%fused_computation.41 | loop fusion | bytes 262144
  6.7 0.9 %constant_dynamic-update-slice_fusion = bf16[1,4,64,512]{3,2,1,0:T(8,128)(2,1)S(1)} fusion(bf16[1,4,64,512]{3,2,1,0:T(8,128)(2,1)S(1)} %constant_dynamic-update-slice_fusion.1, bf16[1,4,64,256]{3,2,1,0:T(8,128)(2,1)} %param.9), kind=kLoop, calls=%fused_computation.40 | loop fusion | bytes 262144 | tf_op jit(solution)/shard_map/concatenate | solution.py:148
  7.7 1.3 %collective-permute-start.1 = (bf16[1,2,64,512]{3,2,1,0:T(8,128)(2,1)S(1)}, bf16[1,2,64,512]{3,2,1,0:T(8,128)(2,1)S(1)}, u32[]{:S(2)}, u32[]{:S(2)}) collective-permute-start(bf16[1,2,64,512]{3,2,1,0:T(8,128)(2,1)S(1)} %get-tuple-element.20), channel_id=1, source_target_pairs={{4,0},{8,4},{12,8},{5,1},{9,5},{13,9},{6,2},{10,6},{14,10},{7,3},{... | collective-permute-start | bytes 393224 | tf_op jit(solution)/shard_map/ppermute | solution.py:26
  9.0 4.6 %collective-permute-start = (bf16[1,2,64,512]{3,2,1,0:T(8,128)(2,1)S(1)}, bf16[1,2,64,512]{3,2,1,0:T(8,128)(2,1)S(1)}, u32[]{:S(2)}, u32[]{:S(2)}) collective-permute-start(bf16[1,2,64,512]{3,2,1,0:T(8,128)(2,1)S(1)} %get-tuple-element.19), channel_id=1, source_target_pairs={{0,4},{4,8},{8,12},{1,5},{5,9},{9,13},{2,6},{6,10},{10,14},{3,7},{... | collective-permute-start | bytes 393224 | tf_op jit(solution)/shard_map/ppermute | solution.py:23
  13.6 0.0 copy-done.5
  13.6 0.0 copy-done.6
  13.6 0.6 rsqrt_multiply_fusion.scale_ref
  14.2 1.5 %collective-permute-done.1 = bf16[1,2,64,512]{3,2,1,0:T(8,128)(2,1)S(1)} collective-permute-done((bf16[1,2,64,512]{3,2,1,0:T(8,128)(2,1)S(1)}, bf16[1,2,64,512]{3,2,1,0:T(8,128)(2,1)S(1)}, u32[]{:S(2)}, u32[]{:S(2)}) %collective-permute-start.1) | collective-permute-done | bytes 131104 | tf_op jit(solution)/shard_map/ppermute | solution.py:26
  15.7 1.6 %collective-permute-done = bf16[1,2,64,512]{3,2,1,0:T(8,128)(2,1)S(1)} collective-permute-done((bf16[1,2,64,512]{3,2,1,0:T(8,128)(2,1)S(1)}, bf16[1,2,64,512]{3,2,1,0:T(8,128)(2,1)S(1)}, u32[]{:S(2)}, u32[]{:S(2)}) %collective-permute-start) | collective-permute-done | bytes 131104 | tf_op jit(solution)/shard_map/ppermute | solution.py:23
  17.3 0.2 collective-permute-start.3
  17.5 0.4 collective-permute-start.2
  17.9 0.0 collective-permute-done.6
  17.9 0.0 collective-permute-done.5
  17.9 0.0 collective-permute-done.4
  17.9 0.6 fusion.23
  18.6 1.6 %collective-permute-done.3 = bf16[1,8,16,512]{3,2,1,0:T(8,128)(2,1)S(1)} collective-permute-done((bf16[1,8,16,512]{3,2,1,0:T(8,128)(2,1)S(1)}, bf16[1,8,16,512]{3,2,1,0:T(8,128)(2,1)S(1)}, u32[]{:S(2)}, u32[]{:S(2)}) %collective-permute-start.3) | collective-permute-done | bytes 131104 | tf_op jit(solution)/shard_map/ppermute | solution.py:26
  20.1 2.9 %collective-permute-done.2 = bf16[1,8,16,512]{3,2,1,0:T(8,128)(2,1)S(1)} collective-permute-done((bf16[1,8,16,512]{3,2,1,0:T(8,128)(2,1)S(1)}, bf16[1,8,16,512]{3,2,1,0:T(8,128)(2,1)S(1)}, u32[]{:S(2)}, u32[]{:S(2)}) %collective-permute-start.2) | collective-permute-done | bytes 131104 | tf_op jit(solution)/shard_map/ppermute | solution.py:23
  23.0 0.1 fusion.18
  23.1 1.1 %fusion.24 = (bf16[1,8,128,256]{3,2,1,0:T(8,128)(2,1)}, bf16[1,8,128,256]{3,2,1,0:T(8,128)(2,1)}) fusion(bf16[1,8,128,512]{3,2,1,0:T(8,128)(2,1)S(1)} %fusion.18), kind=kLoop, calls=%fused_computation.42 | loop fusion | bytes 2097152 | tf_op jit(solution)/shard_map/slice | solution.py:150
  24.2 0.0 copy-start.4
  24.2 3.9 %shard_map.103 = bf16[1,4,64,2304]{3,2,1,0:T(8,128)(2,1)} custom-call(s32[1]{0:T(128)} %bitcast.first_ref, s32[16,12]{1,0:T(8,128)} %src_ref.3, s32[16,12]{1,0:T(8,128)} %start_ref.3, s32[16,12]{1,0:T(8,128)} %span_ref.3, s32[16,12]{1,0:T(8,128)} %basis_ref.3, f32[16,12]{1,0:T(8,128)} %rsqrt_multiply_fusion.scale_ref, ...), custom_call_target="tpu_custom_call" | custom-call | tf_op jit(solution)/shard_map/pallas_call | solution.py:120
  28.2 0.0 copy-done.4
  28.2 1.8 %convolution_bitcast_fusion = f32[9,256,256]{1,2,0:T(8,128)S(1)} fusion(bf16[4,8,9,8,256]{4,3,2,1,0:T(8,128)(2,1)} %bitcast.44, bf16[1,4,64,256]{3,2,1,0:T(8,128)(2,1)S(1)} %copy-done.4), kind=kOutput, calls=%fused_computation.6 | convolution fusion | flops 301989888 | bytes 3670016 | tf_op jit(solution)/shard_map/brwq,brwo->qo/dot_general | solution.py:172
  30.0 0.0 copy-start.2
  30.0 1.0 %dynamic-slice_convert_fusion.2 = (bf16[9,256,64]{1,2,0:T(8,128)(2,1)}, bf16[9,256,64]{1,2,0:T(8,128)(2,1)}, bf16[9,256,64]{1,2,0:T(8,128)(2,1)}) fusion(f32[9,256,256]{1,2,0:T(8,128)S(1)} %convolution_bitcast_fusion, s32[]{:T(128)S(6)} %select_n.53, s32[]{:T(128)S(6)} %select_n.57, s32[]{:T(128)S(6)} %select_n.55), kind=kLoop, calls=%fused_computation.22 | loop fusion | bytes 1769484 | tf_op jit(solution)/shard_map/convert_element_type | solution.py:55
  30.9 0.0 collective-permute-start.9
  30.9 1.7 %collective-permute-start.8 = (bf16[9,256,64]{1,2,0:T(8,128)(2,1)}, bf16[9,256,64]{1,2,0:T(8,128)(2,1)}, u32[]{:S(2)}, u32[]{:S(2)}) collective-permute-start(bf16[9,256,64]{1,2,0:T(8,128)(2,1)} %get-tuple-element.11), channel_id=1, source_target_pairs={{0,2},{1,3},{2,0},{3,1},{4,6},{5,7},{6,4},{7,5},{8,10},{9,11},{10,... | collective-permute-start | bytes 884744 | tf_op jit(solution)/shard_map/ppermute | solution.py:55
  32.7 0.0 collective-permute-start.7
  32.7 0.0 copy-done.2
  32.7 1.5 %copy.15 = bf16[9,256,256]{1,2,0:T(8,128)(2,1)} copy(bf16[9,256,256]{2,1,0:T(8,128)(2,1)S(1)} %copy-done.2) | data formatting | bytes 2359296 | tf_op args[2]
  34.2 0.0 copy-start
  34.2 10.6 %shard_map.104 = bf16[1,4,64,2304]{3,2,1,0:T(8,128)(2,1)} custom-call(s32[1]{0:T(128)} %bitcast.first_ref, s32[16,12]{1,0:T(8,128)} %src_ref.3, s32[16,12]{1,0:T(8,128)} %start_ref.3, s32[16,12]{1,0:T(8,128)} %span_ref.3, s32[16,12]{1,0:T(8,128)} %basis_ref.3, f32[16,12]{1,0:T(8,128)} %rsqrt_multiply_fusion.scale_ref, ...), custom_call_target="tpu_custom_call" | custom-call | tf_op jit(solution)/shard_map/pallas_call | solution.py:120
  44.8 0.0 copy-done
  44.8 2.5 %fusion.11 = f32[1,4,64,256]{3,2,1,0:T(8,128)} fusion(bf16[2304,256,1]{1,0,2:T(8,128)(2,1)} %bitcast.45, bf16[1,4,64,2304]{3,2,1,0:T(8,128)(2,1)S(1)} %copy-done), kind=kOutput, calls=%fused_computation.13 | convolution fusion | flops 301989888 | bytes 2621440 | tf_op jit(solution)/shard_map/brwq,qo->brwo/dot_general | solution.py:163
  47.2 0.0 copy-start.1
  47.2 0.0 copy-start.3
  47.2 0.0 collective-permute-done.9
  47.2 0.0 collective-permute-done.8
  47.2 0.0 collective-permute-done.7
  47.3 1.4 %convert_add_fusion = f32[9,256,64]{1,2,0:T(8,128)S(1)} fusion(bf16[9,256,64]{1,2,0:T(8,128)(2,1)} %collective-permute-done.9, bf16[9,256,64]{1,2,0:T(8,128)(2,1)} %collective-permute-done.8, bf16[9,256,64]{1,2,0:T(8,128)(2,1)} %collective-permute-done.7, f32[9,256,256]{1,2,0:T(8,128)S(1)} %convolution_bitcast_fusion, s32[]{:T(128)S(6)} %select_n.51), kind=kLoop, calls=%fused_computation.19 | loop fusion | flops 884736 | bytes 2064388 | tf_op jit(solution)/shard_map/add | solution.py:56
  48.7 0.2 dynamic-slice_convert_fusion.5
  48.9 4.6 %collective-permute-start.12 = (bf16[9,64,64]{1,2,0:T(8,128)(2,1)S(1)}, bf16[9,64,64]{1,2,0:T(8,128)(2,1)S(1)}, u32[]{:S(2)}, u32[]{:S(2)}) collective-permute-start(bf16[9,64,64]{1,2,0:T(8,128)(2,1)S(1)} %get-tuple-element.15), channel_id=1, source_target_pairs={{0,12},{4,0},{8,4},{12,8},{1,13},{5,1},{9,5},{13,9},{2,14},{6,2},{... | collective-permute-start | bytes 221192 | tf_op jit(solution)/shard_map/ppermute | solution.py:55
  53.4 0.0 collective-permute-start.11
  53.4 1.2 %collective-permute-start.10 = (bf16[9,64,64]{1,2,0:T(8,128)(2,1)S(1)}, bf16[9,64,64]{1,2,0:T(8,128)(2,1)S(1)}, u32[]{:S(2)}, u32[]{:S(2)}) collective-permute-start(bf16[9,64,64]{1,2,0:T(8,128)(2,1)S(1)} %get-tuple-element.14), channel_id=1, source_target_pairs={{0,4},{4,8},{8,12},{12,0},{1,5},{5,9},{9,13},{13,1},{2,6},{6,10},{... | collective-permute-start | bytes 221192 | tf_op jit(solution)/shard_map/ppermute | solution.py:55
  54.7 0.0 copy-done.1
  54.7 0.0 copy-done.3
  54.7 1.2 %fusion.14 = f32[1,4,64,256]{3,2,1,0:T(8,128)} fusion(bf16[2304,256,1]{1,0,2:T(8,128)(2,1)S(1)} %bitcast.46, bf16[1,4,64,2304]{3,2,1,0:T(8,128)(2,1)S(1)} %copy-done.1), kind=kOutput, calls=%fused_computation.14 | convolution fusion | flops 301989888 | bytes 2621440 | tf_op jit(solution)/shard_map/bpwq,qc->bpwc/dot_general | solution.py:169
  55.8 1.9 %collective-permute-done.12 = bf16[9,64,64]{1,2,0:T(8,128)(2,1)S(1)} collective-permute-done((bf16[9,64,64]{1,2,0:T(8,128)(2,1)S(1)}, bf16[9,64,64]{1,2,0:T(8,128)(2,1)S(1)}, u32[]{:S(2)}, u32[]{:S(2)}) %collective-permute-start.12) | collective-permute-done | bytes 73760 | tf_op jit(solution)/shard_map/ppermute | solution.py:55
  57.7 8.8 %collective-permute-done.11 = bf16[9,64,64]{1,2,0:T(8,128)(2,1)S(1)} collective-permute-done((bf16[9,64,64]{1,2,0:T(8,128)(2,1)S(1)}, bf16[9,64,64]{1,2,0:T(8,128)(2,1)S(1)}, u32[]{:S(2)}, u32[]{:S(2)}) %collective-permute-start.11) | collective-permute-done | bytes 73760 | tf_op jit(solution)/shard_map/ppermute | solution.py:55
  66.5 0.0 collective-permute-done.10
  66.5 0.1 add_multiply_fusion
  66.7 0.9 %copy.17 = f32[9,64,64]{2,1,0:T(8,128)} copy(f32[9,64,64]{1,2,0:T(8,128)S(1)} %add_multiply_fusion) | data formatting | bytes 294912
  (6 shorter events, 0.1 us)
Async XLA Ops:
  0.6 13.0 %copy-start.5 = (s32[16,12]{1,0:T(8,128)S(1)}, s32[16,12]{1,0:T(8,128)}, u32[]{:S(2)}) copy-start(s32[16,12]{1,0:T(8,128)} %span_ref.3) | copy-start | bytes 2308
  0.6 13.0 %copy-start.6 = (f32[16,12]{1,0:T(8,128)S(1)}, f32[16,12]{1,0:T(8,128)}, u32[]{:S(2)}) copy-start(f32[16,12]{1,0:T(8,128)} %param.15) | copy-start | bytes 2308
  2.6 15.3 %collective-permute-start.6 = (f32[2,1,4,256]{3,0,2,1:T(2,128)S(1)}, f32[2,1,4,256]{3,0,2,1:T(2,128)S(1)}, u32[]{:S(2)}, u32[]{:S(2)}) collective-permute-start(f32[2,1,4,256]{3,0,2,1:T(2,128)S(1)} %pad_maximum_fusion.3), channel_id=1, source_target_pairs={{0,3},{1,0},{2,1},{3,2},{4,7},{5,4},{6,5},{7,6},{8,11},{9,8},{10,9... | collective-permute-start | bytes 24584 | tf_op jit(solution)/shard_map/ppermute | solution.py:43
  5.0 12.9 %collective-permute-start.5 = (f32[2,1,4,256]{3,0,2,1:T(2,128)S(1)}, f32[2,1,4,256]{3,0,2,1:T(2,128)S(1)}, u32[]{:S(2)}, u32[]{:S(2)}) collective-permute-start(f32[2,1,4,256]{3,0,2,1:T(2,128)S(1)} %pad_maximum_fusion.3), channel_id=1, source_target_pairs={{0,2},{1,3},{2,0},{3,1},{4,6},{5,7},{6,4},{7,5},{8,10},{9,11},{10,... | collective-permute-start | bytes 24584 | tf_op jit(solution)/shard_map/ppermute | solution.py:43
  5.7 12.3 %collective-permute-start.4 = (f32[2,1,4,256]{3,0,2,1:T(2,128)S(1)}, f32[2,1,4,256]{3,0,2,1:T(2,128)S(1)}, u32[]{:S(2)}, u32[]{:S(2)}) collective-permute-start(f32[2,1,4,256]{3,0,2,1:T(2,128)S(1)} %pad_maximum_fusion.3), channel_id=1, source_target_pairs={{0,1},{1,2},{2,3},{3,0},{4,5},{5,6},{6,7},{7,4},{8,9},{9,10},{10,1... | collective-permute-start | bytes 24584 | tf_op jit(solution)/shard_map/ppermute | solution.py:43
  7.7 8.0 %collective-permute-start.1 = (bf16[1,2,64,512]{3,2,1,0:T(8,128)(2,1)S(1)}, bf16[1,2,64,512]{3,2,1,0:T(8,128)(2,1)S(1)}, u32[]{:S(2)}, u32[]{:S(2)}) collective-permute-start(bf16[1,2,64,512]{3,2,1,0:T(8,128)(2,1)S(1)} %get-tuple-element.20), channel_id=1, source_target_pairs={{4,0},{8,4},{12,8},{5,1},{9,5},{13,9},{6,2},{10,6},{14,10},{7,3},{... | collective-permute-start | bytes 393224 | tf_op jit(solution)/shard_map/ppermute | solution.py:26
  9.0 8.3 %collective-permute-start = (bf16[1,2,64,512]{3,2,1,0:T(8,128)(2,1)S(1)}, bf16[1,2,64,512]{3,2,1,0:T(8,128)(2,1)S(1)}, u32[]{:S(2)}, u32[]{:S(2)}) collective-permute-start(bf16[1,2,64,512]{3,2,1,0:T(8,128)(2,1)S(1)} %get-tuple-element.19), channel_id=1, source_target_pairs={{0,4},{4,8},{8,12},{1,5},{5,9},{9,13},{2,6},{6,10},{10,14},{3,7},{... | collective-permute-start | bytes 393224 | tf_op jit(solution)/shard_map/ppermute | solution.py:23
  17.3 2.8 %collective-permute-start.3 = (bf16[1,8,16,512]{3,2,1,0:T(8,128)(2,1)S(1)}, bf16[1,8,16,512]{3,2,1,0:T(8,128)(2,1)S(1)}, u32[]{:S(2)}, u32[]{:S(2)}) collective-permute-start(bf16[1,8,16,512]{3,2,1,0:T(8,128)(2,1)S(1)} %get-tuple-element.18), channel_id=1, source_target_pairs={{1,0},{2,1},{3,2},{0,3},{5,4},{6,5},{7,6},{4,7},{9,8},{10,9},{11,1... | collective-permute-start | bytes 393224 | tf_op jit(solution)/shard_map/ppermute | solution.py:26
  17.5 5.5 %collective-permute-start.2 = (bf16[1,8,16,512]{3,2,1,0:T(8,128)(2,1)S(1)}, bf16[1,8,16,512]{3,2,1,0:T(8,128)(2,1)S(1)}, u32[]{:S(2)}, u32[]{:S(2)}) collective-permute-start(bf16[1,8,16,512]{3,2,1,0:T(8,128)(2,1)S(1)} %get-tuple-element.17), channel_id=1, source_target_pairs={{0,1},{1,2},{2,3},{3,0},{4,5},{5,6},{6,7},{7,4},{8,9},{9,10},{10,1... | collective-permute-start | bytes 393224 | tf_op jit(solution)/shard_map/ppermute | solution.py:23
  24.2 3.9 %copy-start.4 = (bf16[1,4,64,256]{3,2,1,0:T(8,128)(2,1)S(1)}, bf16[1,4,64,256]{3,2,1,0:T(8,128)(2,1)}, u32[]{:S(2)}) copy-start(bf16[1,4,64,256]{3,2,1,0:T(8,128)(2,1)} %param.9) | copy-start | bytes 393220
  30.0 2.7 %copy-start.2 = (bf16[9,256,256]{2,1,0:T(8,128)(2,1)S(1)}, bf16[9,256,256]{2,1,0:T(8,128)(2,1)}, u32[]{:S(2)}) copy-start(bf16[9,256,256]{2,1,0:T(8,128)(2,1)} %param.10) | copy-start | bytes 3538948
  30.9 16.3 %collective-permute-start.9 = (bf16[9,256,64]{1,2,0:T(8,128)(2,1)}, bf16[9,256,64]{1,2,0:T(8,128)(2,1)}, u32[]{:S(2)}, u32[]{:S(2)}) collective-permute-start(bf16[9,256,64]{1,2,0:T(8,128)(2,1)} %get-tuple-element.10), channel_id=1, source_target_pairs={{0,3},{1,0},{2,1},{3,2},{4,7},{5,4},{6,5},{7,6},{8,11},{9,8},{10,9... | collective-permute-start | bytes 884744 | tf_op jit(solution)/shard_map/ppermute | solution.py:55
  30.9 16.3 %collective-permute-start.8 = (bf16[9,256,64]{1,2,0:T(8,128)(2,1)}, bf16[9,256,64]{1,2,0:T(8,128)(2,1)}, u32[]{:S(2)}, u32[]{:S(2)}) collective-permute-start(bf16[9,256,64]{1,2,0:T(8,128)(2,1)} %get-tuple-element.11), channel_id=1, source_target_pairs={{0,2},{1,3},{2,0},{3,1},{4,6},{5,7},{6,4},{7,5},{8,10},{9,11},{10,... | collective-permute-start | bytes 884744 | tf_op jit(solution)/shard_map/ppermute | solution.py:55
  32.7 14.6 %collective-permute-start.7 = (bf16[9,256,64]{1,2,0:T(8,128)(2,1)}, bf16[9,256,64]{1,2,0:T(8,128)(2,1)}, u32[]{:S(2)}, u32[]{:S(2)}) collective-permute-start(bf16[9,256,64]{1,2,0:T(8,128)(2,1)} %get-tuple-element.9), channel_id=1, source_target_pairs={{0,1},{1,2},{2,3},{3,0},{4,5},{5,6},{6,7},{7,4},{8,9},{9,10},{10,1... | collective-permute-start | bytes 884744 | tf_op jit(solution)/shard_map/ppermute | solution.py:55
  34.2 10.6 %copy-start = (bf16[1,4,64,2304]{3,2,1,0:T(8,128)(2,1)S(1)}, bf16[1,4,64,2304]{3,2,1,0:T(8,128)(2,1)}, u32[]{:S(2)}) copy-start(bf16[1,4,64,2304]{3,2,1,0:T(8,128)(2,1)} %shard_map.103) | copy-start | bytes 3538948
  47.2 7.4 %copy-start.1 = (bf16[1,4,64,2304]{3,2,1,0:T(8,128)(2,1)S(1)}, bf16[1,4,64,2304]{3,2,1,0:T(8,128)(2,1)}, u32[]{:S(2)}) copy-start(bf16[1,4,64,2304]{3,2,1,0:T(8,128)(2,1)} %shard_map.104) | copy-start | bytes 3538948
  47.2 7.4 %copy-start.3 = (bf16[9,256,256]{1,2,0:T(8,128)(2,1)S(1)}, bf16[9,256,256]{1,2,0:T(8,128)(2,1)}, u32[]{:S(2)}) copy-start(bf16[9,256,256]{1,2,0:T(8,128)(2,1)} %copy.15) | copy-start | bytes 3538948
  48.9 8.8 %collective-permute-start.12 = (bf16[9,64,64]{1,2,0:T(8,128)(2,1)S(1)}, bf16[9,64,64]{1,2,0:T(8,128)(2,1)S(1)}, u32[]{:S(2)}, u32[]{:S(2)}) collective-permute-start(bf16[9,64,64]{1,2,0:T(8,128)(2,1)S(1)} %get-tuple-element.15), channel_id=1, source_target_pairs={{0,12},{4,0},{8,4},{12,8},{1,13},{5,1},{9,5},{13,9},{2,14},{6,2},{... | collective-permute-start | bytes 221192 | tf_op jit(solution)/shard_map/ppermute | solution.py:55
  53.4 13.1 %collective-permute-start.11 = (bf16[9,64,64]{1,2,0:T(8,128)(2,1)S(1)}, bf16[9,64,64]{1,2,0:T(8,128)(2,1)S(1)}, u32[]{:S(2)}, u32[]{:S(2)}) collective-permute-start(bf16[9,64,64]{1,2,0:T(8,128)(2,1)S(1)} %get-tuple-element.16), channel_id=1, source_target_pairs={{0,8},{4,12},{8,0},{12,4},{1,9},{5,13},{9,1},{13,5},{2,10},{6,14},... | collective-permute-start | bytes 221192 | tf_op jit(solution)/shard_map/ppermute | solution.py:55
  53.4 13.1 %collective-permute-start.10 = (bf16[9,64,64]{1,2,0:T(8,128)(2,1)S(1)}, bf16[9,64,64]{1,2,0:T(8,128)(2,1)S(1)}, u32[]{:S(2)}, u32[]{:S(2)}) collective-permute-start(bf16[9,64,64]{1,2,0:T(8,128)(2,1)S(1)} %get-tuple-element.14), channel_id=1, source_target_pairs={{0,4},{4,8},{8,12},{12,0},{1,5},{5,9},{9,13},{13,1},{2,6},{6,10},{... | collective-permute-start | bytes 221192 | tf_op jit(solution)/shard_map/ppermute | solution.py:55

commit v7 on v6

--- a/solution.py
+++ b/solution.py
@@ -52,6 +52,32 @@
     for shift in range(1, count):
         pairs = [(i, (i + shift) % count) for i in range(count)]
         piece = lax.dynamic_slice_in_dim(value, ((own + shift) % count) * block, block, dim)
+        sent = lax.ppermute(piece.astype(jnp.bfloat16), axis, pairs)
+        total = total + sent.astype(jnp.float32)
+    return total
+
+
+def paired_scatter(value, axis, dim):
+    count = lax.axis_size(axis)
+    if count % 2:
+        return ring_scatter(value, axis, dim)
+    own = lax.axis_index(axis)
+    parity = own % 2
+    group = own // 2
+    groups = count // 2
+    block = value.shape[dim] // count
+    shape = value.shape[:dim] + (groups, 2, block) + value.shape[dim + 1:]
+    split = value.reshape(shape)
+    keep = lax.dynamic_index_in_dim(split, parity, dim + 1, keepdims=False)
+    give = lax.dynamic_index_in_dim(split, 1 - parity, dim + 1, keepdims=False)
+    swap = [(i, i ^ 1) for i in range(count)]
+    merged = keep + lax.ppermute(give, axis, swap)
+    total = lax.dynamic_index_in_dim(merged, group, dim, keepdims=False)
+    for shift in range(1, groups):
+        pairs = [
+            (2 * g + p, 2 * ((g + shift) % groups) + p) for g in range(groups) for p in range(2)
+        ]
+        piece = lax.dynamic_index_in_dim(merged, (group + shift) % groups, dim, keepdims=False)
         sent = lax.ppermute(piece.astype(jnp.bfloat16), axis, pairs)
         total = total + sent.astype(jnp.float32)
     return total
@@ -173,7 +199,7 @@
         "brwq,brwo->qo", flattened, cotangent, preferred_element_type=jnp.float32
     )
     partial_value = partial_value.reshape(BASIS, channels, channels)
-    reduced = ring_scatter(partial_value, "lon", 2)
+    reduced = paired_scatter(partial_value, "lon", 2)
     reduced = ring_scatter(reduced, "lat", 1)
     grad_weight = reduced / jnp.sqrt(jnp.float32(members * height * lon_total))
     return (response, grad_input, grad_weight)

time: 68 us -> 74.6 us (1.097)
  local copies, waits for them, and re-layouts: 7.15 us -> 11.2 us
  waiting for transfers between devices: 18.2 us -> 21.1 us
  other arithmetic: 4.21 us -> 5.45 us
    dot_general x0 -> x3, local copies, waits for them, and re-layouts: none -> 3.91 us  [on_device(): jnp.einsum('brwq,brwo->qo', flattened, cotangent, preferred_element_type=...]
    ppermute x0 -> x2, waiting for transfers between devices: none -> 2.85 us  [the longest x1 2.85 us: paired_scatter(): merged = keep + lax.ppermute(give, axis, swap)]
    ppermute x6 -> x3, starting transfers between devices: 7.51 us -> 5.97 us  [ring_scatter(): sent = lax.ppermute(piece.astype(jnp.bfloat16), axis, pairs)]
    dot_general x1, matrix products: 2.45 us -> 1.18 us  [on_device(): jnp.einsum('brwq,qo->brwo', flattened, w_fwd, preferred_element_type=jnp....]
    add x1 -> x2, other arithmetic: 1.43 us -> 2.62 us  [the longest x1 1.52 us: paired_scatter(): merged = keep + lax.ppermute(give, axis, swap)]
    ppermute x0 -> x2, starting transfers between devices: none -> 1.05 us  [the longest x1 0.85 us: paired_scatter(): sent = lax.ppermute(piece.astype(jnp.bfloat16), axis, pairs)]
    convert_element_type x2 -> x1, local copies, waits for them, and re-layouts: 1.15 us -> 0.2 us  [ring_scatter(): sent = lax.ppermute(piece.astype(jnp.bfloat16), axis, pairs)]
    ppermute x6 -> x3, waiting for transfers between devices: 10.7 us -> 11 us  [ring_scatter(): sent = lax.ppermute(piece.astype(jnp.bfloat16), axis, pairs)]
  transfers between devices with their start and end apart: 13 -> 12, of which waited for: 6 -> 7; matrix products, arithmetic and copies ran while one was open for 12% -> 9% of each run, Pallas kernels for 16% -> 14%
where the time goes in v7:
time: 74.6 us; the launch traced here: 74 us
  waiting for transfers between devices  21.1 us (28%)
  starting transfers between devices  16.7 us (22%)
  Pallas kernels  13.9 us (19%)
  local copies, waits for them, and re-layouts  11.2 us (15%)
  other arithmetic  5.45 us (7%)
  matrix products  4.77 us (6%)
  between operations  0.89 us (1%)
    pallas_call x2, Pallas kernels, run_filter(): pl.pallas_call(kernel, grid=(members, row_count), in_specs=[smem] * 6 + [...  13.9 us
    ppermute x3, waiting for transfers between devices, ring_scatter(): sent = lax.ppermute(piece.astype(jnp.bfloat16), axis, pairs)  11 us
    ppermute x3, starting transfers between devices, ring_scatter(): sent = lax.ppermute(piece.astype(jnp.bfloat16), axis, pairs)  5.97 us
    ppermute x2, starting transfers between devices, with_halo(): lax.ppermute(lax.slice_in_dim(block, block.shape[dim] - width, None, axis...  4.96 us
    ppermute x2, waiting for transfers between devices, with_halo(): lax.ppermute(lax.slice_in_dim(block, block.shape[dim] - width, None, axis...  4.56 us
    dot_general x3, local copies, waits for them, and re-layouts, on_device(): jnp.einsum('brwq,brwo->qo', flattened, cotangent, preferred_element_type=...  3.91 us
    unnamed x19, local copies, waits for them, and re-layouts  3.64 us
    ppermute x3, starting transfers between devices, ring_sum(): total = total + lax.ppermute(value, axis, pairs)  3.23 us
  transfers between devices with their start and end apart: 12, of which 7 were waited for; matrix products, arithmetic and copies ran while one was open for 9% of the time, Pallas kernels for 14%

profile of v7, /device:TPU:0, one launch (start us, length us, event | category | flops | bytes accessed | tf_op | source)
XLA Modules:
  0.0 74.0 jit_solution(7899949043499694781)
XLA Ops:
  0.6 0.0 copy-start.5
  0.6 0.0 copy-start.6
  0.7 0.0 copy-start.7
  0.7 1.0 %convert_reduce_fusion = f32[4,256]{1,0:T(4,128)S(1)} fusion(bf16[1,4,64,256]{3,2,1,0:T(8,128)(2,1)} %param.9), kind=kLoop, calls=%fused_computation.28 | loop fusion | flops 130048 | bytes 135168 | tf_op jit(solution)/shard_map/reduce_sum | solution.py:178
  1.7 0.9 %convert_reduce_fusion.1 = f32[4,256]{1,0:T(4,128)S(1)} fusion(bf16[1,4,64,256]{3,2,1,0:T(8,128)(2,1)} %param.8), kind=kLoop, calls=%fused_computation.29 | loop fusion | flops 130048 | bytes 135168 | tf_op jit(solution)/shard_map/reduce_sum | solution.py:178
  2.6 2.4 %collective-permute-start.6 = (f32[2,1,4,256]{3,0,2,1:T(2,128)S(1)}, f32[2,1,4,256]{3,0,2,1:T(2,128)S(1)}, u32[]{:S(2)}, u32[]{:S(2)}) collective-permute-start(f32[2,1,4,256]{3,0,2,1:T(2,128)S(1)} %pad_maximum_fusion.3), channel_id=1, source_target_pairs={{0,3},{1,0},{2,1},{3,2},{4,7},{5,4},{6,5},{7,6},{8,11},{9,8},{10,9... | collective-permute-start | bytes 24584 | tf_op jit(solution)/shard_map/ppermute | solution.py:43
  5.1 0.6 collective-permute-start.5
  5.7 0.2 collective-permute-start.4
  5.9 0.9 %constant_dynamic-update-slice_fusion.1 = bf16[1,4,64,512]{3,2,1,0:T(8,128)(2,1)S(1)} fusion(bf16[1,4,64,256]{3,2,1,0:T(8,128)(2,1)} %param.8), kind=kLoop, calls=%fused_computation.41 | loop fusion | bytes 262144
  6.8 0.9 %constant_dynamic-update-slice_fusion = bf16[1,4,64,512]{3,2,1,0:T(8,128)(2,1)S(1)} fusion(bf16[1,4,64,512]{3,2,1,0:T(8,128)(2,1)S(1)} %constant_dynamic-update-slice_fusion.1, bf16[1,4,64,256]{3,2,1,0:T(8,128)(2,1)} %param.9), kind=kLoop, calls=%fused_computation.40 | loop fusion | bytes 262144 | tf_op jit(solution)/shard_map/concatenate | solution.py:174
  7.7 1.3 %collective-permute-start.1 = (bf16[1,2,64,512]{3,2,1,0:T(8,128)(2,1)S(1)}, bf16[1,2,64,512]{3,2,1,0:T(8,128)(2,1)S(1)}, u32[]{:S(2)}, u32[]{:S(2)}) collective-permute-start(bf16[1,2,64,512]{3,2,1,0:T(8,128)(2,1)S(1)} %get-tuple-element.14), channel_id=1, source_target_pairs={{4,0},{8,4},{12,8},{5,1},{9,5},{13,9},{6,2},{10,6},{14,10},{7,3},{... | collective-permute-start | bytes 393224 | tf_op jit(solution)/shard_map/ppermute | solution.py:26
  9.0 4.6 %collective-permute-start = (bf16[1,2,64,512]{3,2,1,0:T(8,128)(2,1)S(1)}, bf16[1,2,64,512]{3,2,1,0:T(8,128)(2,1)S(1)}, u32[]{:S(2)}, u32[]{:S(2)}) collective-permute-start(bf16[1,2,64,512]{3,2,1,0:T(8,128)(2,1)S(1)} %get-tuple-element.13), channel_id=1, source_target_pairs={{0,4},{4,8},{8,12},{1,5},{5,9},{9,13},{2,6},{6,10},{10,14},{3,7},{... | collective-permute-start | bytes 393224 | tf_op jit(solution)/shard_map/ppermute | solution.py:23
  13.6 0.0 copy-done.5
  13.6 0.2 dot_general.28
  13.8 0.2 copy.17
  14.0 0.0 copy-done.6
  14.0 0.0 copy-done.7
  14.0 0.6 rsqrt_multiply_fusion.scale_ref
  14.6 1.1 %collective-permute-done.1 = bf16[1,2,64,512]{3,2,1,0:T(8,128)(2,1)S(1)} collective-permute-done((bf16[1,2,64,512]{3,2,1,0:T(8,128)(2,1)S(1)}, bf16[1,2,64,512]{3,2,1,0:T(8,128)(2,1)S(1)}, u32[]{:S(2)}, u32[]{:S(2)}) %collective-permute-start.1) | collective-permute-done | bytes 131104 | tf_op jit(solution)/shard_map/ppermute | solution.py:26
  15.7 1.6 %collective-permute-done = bf16[1,2,64,512]{3,2,1,0:T(8,128)(2,1)S(1)} collective-permute-done((bf16[1,2,64,512]{3,2,1,0:T(8,128)(2,1)S(1)}, bf16[1,2,64,512]{3,2,1,0:T(8,128)(2,1)S(1)}, u32[]{:S(2)}, u32[]{:S(2)}) %collective-permute-start) | collective-permute-done | bytes 131104 | tf_op jit(solution)/shard_map/ppermute | solution.py:23
  17.4 0.2 collective-permute-start.3
  17.6 0.4 collective-permute-start.2
  18.0 0.0 collective-permute-done.6
  18.0 0.0 collective-permute-done.5
  18.0 0.0 collective-permute-done.4
  18.0 0.6 fusion.23
  18.6 1.6 %collective-permute-done.3 = bf16[1,8,16,512]{3,2,1,0:T(8,128)(2,1)S(1)} collective-permute-done((bf16[1,8,16,512]{3,2,1,0:T(8,128)(2,1)S(1)}, bf16[1,8,16,512]{3,2,1,0:T(8,128)(2,1)S(1)}, u32[]{:S(2)}, u32[]{:S(2)}) %collective-permute-start.3) | collective-permute-done | bytes 131104 | tf_op jit(solution)/shard_map/ppermute | solution.py:26
  20.2 2.9 %collective-permute-done.2 = bf16[1,8,16,512]{3,2,1,0:T(8,128)(2,1)S(1)} collective-permute-done((bf16[1,8,16,512]{3,2,1,0:T(8,128)(2,1)S(1)}, bf16[1,8,16,512]{3,2,1,0:T(8,128)(2,1)S(1)}, u32[]{:S(2)}, u32[]{:S(2)}) %collective-permute-start.2) | collective-permute-done | bytes 131104 | tf_op jit(solution)/shard_map/ppermute | solution.py:23
  23.1 0.1 fusion.17
  23.2 1.1 %fusion.24 = (bf16[1,8,128,256]{3,2,1,0:T(8,128)(2,1)}, bf16[1,8,128,256]{3,2,1,0:T(8,128)(2,1)}) fusion(bf16[1,8,128,512]{3,2,1,0:T(8,128)(2,1)S(1)} %fusion.17), kind=kLoop, calls=%fused_computation.42 | loop fusion | bytes 2097152 | tf_op jit(solution)/shard_map/slice | solution.py:176
  24.3 3.8 %shard_map.103 = bf16[1,4,64,2304]{3,2,1,0:T(8,128)(2,1)} custom-call(s32[1]{0:T(128)} %bitcast.first_ref, s32[16,12]{1,0:T(8,128)} %src_ref.3, s32[16,12]{1,0:T(8,128)} %start_ref.3, s32[16,12]{1,0:T(8,128)} %span_ref.3, s32[16,12]{1,0:T(8,128)} %basis_ref.3, f32[16,12]{1,0:T(8,128)} %rsqrt_multiply_fusion.scale_ref, ...), custom_call_target="tpu_custom_call" | custom-call | tf_op jit(solution)/shard_map/pallas_call | solution.py:146
  28.1 3.5 %dot_general.26 = bf16[9,256,4,64]{1,0,3,2:T(8,128)(2,1)} reshape(bf16[2304,4,64]{0,2,1:T(8,128)(2,1)} %bitcast.55) | data formatting | bytes 2359296 | tf_op jit(solution)/shard_map/brwq,brwo->qo/dot_general | solution.py:198
  31.6 2.4 %convolution_bitcast_fusion = f32[9,256,2,2,64]{1,4,3,2,0:T(8,128)S(1)} fusion(bf16[9,256,4,64,1,1]{1,0,3,2,5,4:T(8,128)(2,1)} %bitcast.56, bf16[2,2,64,4,64]{4,2,3,1,0:T(8,128)(2,1)S(1)} %copy.17), kind=kOutput, calls=%fused_computation.6 | convolution fusion | flops 301989888 | bytes 3670016 | tf_op jit(solution)/shard_map/brwq,brwo->qo/dot_general | solution.py:198
  34.0 0.1 dynamic-slice_bitcast_fusion
  34.1 0.2 collective-permute-start.7
  34.3 2.8 %collective-permute-done.7 = f32[9,256,2,64]{1,3,2,0:T(8,128)} collective-permute-done((f32[9,256,2,64]{1,3,2,0:T(8,128)S(1)}, f32[9,256,2,64]{1,3,2,0:T(8,128)}, u32[]{:S(2)}, u32[]{:S(2)}) %collective-permute-start.7) | collective-permute-done | bytes 1179680 | tf_op jit(solution)/shard_map/ppermute | solution.py:74
  37.2 0.0 copy-start.2
  37.2 1.5 %bitcast_add_fusion = f32[9,256,2,64]{1,3,2,0:T(8,128)S(1)} fusion(f32[9,256,2,64]{1,3,2,0:T(8,128)} %collective-permute-done.7, f32[9,256,2,2,64]{1,4,3,2,0:T(8,128)S(1)} %convolution_bitcast_fusion, s32[]{:T(128)S(6)} %select_n.54), kind=kLoop, calls=%fused_computation.7 | loop fusion | flops 294912 | bytes 3538948 | tf_op jit(solution)/shard_map/add | solution.py:74
  38.7 0.0 copy-start.3
  38.7 1.0 %copy-done.3 = f32[9,256,2,64]{1,3,2,0:T(8,128)} copy-done((f32[9,256,2,64]{1,3,2,0:T(8,128)}, f32[9,256,2,64]{1,3,2,0:T(8,128)S(1)}, u32[]{:S(2)}) %copy-start.3) | copy-done | bytes 1179672
  39.7 0.7 %fusion.20 = bf16[9,256,64]{1,2,0:T(8,128)(2,1)} fusion(f32[9,256,2,64]{1,3,2,0:T(8,128)S(1)} %bitcast_add_fusion, s32[]{:T(128)S(6)} %select_n.59), kind=kLoop, calls=%fused_computation.22 | loop fusion | bytes 589828 | tf_op jit(solution)/shard_map/convert_element_type | solution.py:81
  40.5 0.8 %collective-permute-start.8 = (bf16[9,256,64]{1,2,0:T(8,128)(2,1)}, bf16[9,256,64]{1,2,0:T(8,128)(2,1)}, u32[]{:S(2)}, u32[]{:S(2)}) collective-permute-start(bf16[9,256,64]{1,2,0:T(8,128)(2,1)} %fusion.20), channel_id=1, source_target_pairs={{0,2},{1,3},{2,0},{3,1},{4,6},{5,7},{6,4},{7,5},{8,10},{9,11},{10,... | collective-permute-start | bytes 884744 | tf_op jit(solution)/shard_map/ppermute | solution.py:81
  41.3 0.0 copy-done.2
  41.3 0.7 copy.15
  42.1 0.0 copy-start
  42.1 10.1 %shard_map.104 = bf16[1,4,64,2304]{3,2,1,0:T(8,128)(2,1)} custom-call(s32[1]{0:T(128)} %bitcast.first_ref, s32[16,12]{1,0:T(8,128)} %src_ref.3, s32[16,12]{1,0:T(8,128)} %start_ref.3, s32[16,12]{1,0:T(8,128)} %span_ref.3, s32[16,12]{1,0:T(8,128)} %basis_ref.3, f32[16,12]{1,0:T(8,128)} %rsqrt_multiply_fusion.scale_ref, ...), custom_call_target="tpu_custom_call" | custom-call | tf_op jit(solution)/shard_map/pallas_call | solution.py:146
  52.2 0.0 copy-done
  52.2 0.0 copy-start.4
  52.2 1.2 %fusion.10 = f32[1,4,64,256]{3,2,1,0:T(8,128)} fusion(bf16[2304,256,1]{1,0,2:T(8,128)(2,1)S(1)} %bitcast.57, bf16[1,4,64,2304]{3,2,1,0:T(8,128)(2,1)S(1)} %copy-done), kind=kOutput, calls=%fused_computation.14 | convolution fusion | flops 301989888 | bytes 2621440 | tf_op jit(solution)/shard_map/brwq,qo->brwo/dot_general | solution.py:189
  53.4 0.0 copy-start.1
  53.4 0.0 collective-permute-done.8
  53.4 0.1 copy-done.4
  53.5 1.1 %bitcast_add_fusion.1 = f32[9,256,64]{1,2,0:T(8,128)S(1)} fusion(bf16[9,256,64]{1,2,0:T(8,128)(2,1)} %collective-permute-done.8, f32[9,256,2,64]{1,3,2,0:T(8,128)S(1)} %copy-done.4, s32[]{:T(128)S(6)} %select_n.57), kind=kLoop, calls=%fused_computation.20 | loop fusion | flops 294912 | bytes 1474564 | tf_op jit(solution)/shard_map/add | solution.py:82
  54.6 0.2 dynamic-slice_convert_fusion.3
  54.8 5.3 %collective-permute-start.11 = (bf16[9,64,64]{1,2,0:T(8,128)(2,1)S(1)}, bf16[9,64,64]{1,2,0:T(8,128)(2,1)S(1)}, u32[]{:S(2)}, u32[]{:S(2)}) collective-permute-start(bf16[9,64,64]{1,2,0:T(8,128)(2,1)S(1)} %get-tuple-element.9), channel_id=1, source_target_pairs={{0,12},{4,0},{8,4},{12,8},{1,13},{5,1},{9,5},{13,9},{2,14},{6,2},{... | collective-permute-start | bytes 221192 | tf_op jit(solution)/shard_map/ppermute | solution.py:55
  60.1 0.0 collective-permute-start.10
  60.1 0.6 collective-permute-start.9
  60.8 0.0 copy-done.1
  60.8 1.2 %fusion.13 = f32[1,4,64,256]{3,2,1,0:T(8,128)} fusion(bf16[2304,256,1]{1,0,2:T(8,128)(2,1)S(1)} %bitcast.58, bf16[1,4,64,2304]{3,2,1,0:T(8,128)(2,1)S(1)} %copy-done.1), kind=kOutput, calls=%fused_computation.15 | convolution fusion | flops 301989888 | bytes 2621440 | tf_op jit(solution)/shard_map/bpwq,qc->bpwc/dot_general | solution.py:195
  62.0 2.5 %collective-permute-done.11 = bf16[9,64,64]{1,2,0:T(8,128)(2,1)S(1)} collective-permute-done((bf16[9,64,64]{1,2,0:T(8,128)(2,1)S(1)}, bf16[9,64,64]{1,2,0:T(8,128)(2,1)S(1)}, u32[]{:S(2)}, u32[]{:S(2)}) %collective-permute-start.11) | collective-permute-done | bytes 73760 | tf_op jit(solution)/shard_map/ppermute | solution.py:55
  64.4 8.6 %collective-permute-done.10 = bf16[9,64,64]{1,2,0:T(8,128)(2,1)S(1)} collective-permute-done((bf16[9,64,64]{1,2,0:T(8,128)(2,1)S(1)}, bf16[9,64,64]{1,2,0:T(8,128)(2,1)S(1)}, u32[]{:S(2)}, u32[]{:S(2)}) %collective-permute-start.10) | collective-permute-done | bytes 73760 | tf_op jit(solution)/shard_map/ppermute | solution.py:55
  73.0 0.0 collective-permute-done.9
  73.0 0.1 add_multiply_fusion
  73.1 0.9 %copy.18 = f32[9,64,64]{2,1,0:T(8,128)} copy(f32[9,64,64]{1,2,0:T(8,128)S(1)} %add_multiply_fusion) | data formatting | bytes 294912
  (6 shorter events, 0.1 us)
Async XLA Ops:
  0.6 13.0 %copy-start.5 = (bf16[1,4,64,256]{3,2,1,0:T(8,128)(2,1)S(1)}, bf16[1,4,64,256]{3,2,1,0:T(8,128)(2,1)}, u32[]{:S(2)}) copy-start(bf16[1,4,64,256]{3,2,1,0:T(8,128)(2,1)} %param.9) | copy-start | bytes 393220
  0.6 13.4 %copy-start.6 = (s32[16,12]{1,0:T(8,128)S(1)}, s32[16,12]{1,0:T(8,128)}, u32[]{:S(2)}) copy-start(s32[16,12]{1,0:T(8,128)} %span_ref.3) | copy-start | bytes 2308
  0.7 13.4 %copy-start.7 = (f32[16,12]{1,0:T(8,128)S(1)}, f32[16,12]{1,0:T(8,128)}, u32[]{:S(2)}) copy-start(f32[16,12]{1,0:T(8,128)} %param.15) | copy-start | bytes 2308
  2.6 15.3 %collective-permute-start.6 = (f32[2,1,4,256]{3,0,2,1:T(2,128)S(1)}, f32[2,1,4,256]{3,0,2,1:T(2,128)S(1)}, u32[]{:S(2)}, u32[]{:S(2)}) collective-permute-start(f32[2,1,4,256]{3,0,2,1:T(2,128)S(1)} %pad_maximum_fusion.3), channel_id=1, source_target_pairs={{0,3},{1,0},{2,1},{3,2},{4,7},{5,4},{6,5},{7,6},{8,11},{9,8},{10,9... | collective-permute-start | bytes 24584 | tf_op jit(solution)/shard_map/ppermute | solution.py:43
  5.1 12.9 %collective-permute-start.5 = (f32[2,1,4,256]{3,0,2,1:T(2,128)S(1)}, f32[2,1,4,256]{3,0,2,1:T(2,128)S(1)}, u32[]{:S(2)}, u32[]{:S(2)}) collective-permute-start(f32[2,1,4,256]{3,0,2,1:T(2,128)S(1)} %pad_maximum_fusion.3), channel_id=1, source_target_pairs={{0,2},{1,3},{2,0},{3,1},{4,6},{5,7},{6,4},{7,5},{8,10},{9,11},{10,... | collective-permute-start | bytes 24584 | tf_op jit(solution)/shard_map/ppermute | solution.py:43
  5.7 12.3 %collective-permute-start.4 = (f32[2,1,4,256]{3,0,2,1:T(2,128)S(1)}, f32[2,1,4,256]{3,0,2,1:T(2,128)S(1)}, u32[]{:S(2)}, u32[]{:S(2)}) collective-permute-start(f32[2,1,4,256]{3,0,2,1:T(2,128)S(1)} %pad_maximum_fusion.3), channel_id=1, source_target_pairs={{0,1},{1,2},{2,3},{3,0},{4,5},{5,6},{6,7},{7,4},{8,9},{9,10},{10,1... | collective-permute-start | bytes 24584 | tf_op jit(solution)/shard_map/ppermute | solution.py:43
  7.7 8.0 %collective-permute-start.1 = (bf16[1,2,64,512]{3,2,1,0:T(8,128)(2,1)S(1)}, bf16[1,2,64,512]{3,2,1,0:T(8,128)(2,1)S(1)}, u32[]{:S(2)}, u32[]{:S(2)}) collective-permute-start(bf16[1,2,64,512]{3,2,1,0:T(8,128)(2,1)S(1)} %get-tuple-element.14), channel_id=1, source_target_pairs={{4,0},{8,4},{12,8},{5,1},{9,5},{13,9},{6,2},{10,6},{14,10},{7,3},{... | collective-permute-start | bytes 393224 | tf_op jit(solution)/shard_map/ppermute | solution.py:26
  9.0 8.3 %collective-permute-start = (bf16[1,2,64,512]{3,2,1,0:T(8,128)(2,1)S(1)}, bf16[1,2,64,512]{3,2,1,0:T(8,128)(2,1)S(1)}, u32[]{:S(2)}, u32[]{:S(2)}) collective-permute-start(bf16[1,2,64,512]{3,2,1,0:T(8,128)(2,1)S(1)} %get-tuple-element.13), channel_id=1, source_target_pairs={{0,4},{4,8},{8,12},{1,5},{5,9},{9,13},{2,6},{6,10},{10,14},{3,7},{... | collective-permute-start | bytes 393224 | tf_op jit(solution)/shard_map/ppermute | solution.py:23
  17.4 2.8 %collective-permute-start.3 = (bf16[1,8,16,512]{3,2,1,0:T(8,128)(2,1)S(1)}, bf16[1,8,16,512]{3,2,1,0:T(8,128)(2,1)S(1)}, u32[]{:S(2)}, u32[]{:S(2)}) collective-permute-start(bf16[1,8,16,512]{3,2,1,0:T(8,128)(2,1)S(1)} %get-tuple-element.12), channel_id=1, source_target_pairs={{1,0},{2,1},{3,2},{0,3},{5,4},{6,5},{7,6},{4,7},{9,8},{10,9},{11,1... | collective-permute-start | bytes 393224 | tf_op jit(solution)/shard_map/ppermute | solution.py:26
  17.6 5.5 %collective-permute-start.2 = (bf16[1,8,16,512]{3,2,1,0:T(8,128)(2,1)S(1)}, bf16[1,8,16,512]{3,2,1,0:T(8,128)(2,1)S(1)}, u32[]{:S(2)}, u32[]{:S(2)}) collective-permute-start(bf16[1,8,16,512]{3,2,1,0:T(8,128)(2,1)S(1)} %get-tuple-element.11), channel_id=1, source_target_pairs={{0,1},{1,2},{2,3},{3,0},{4,5},{5,6},{6,7},{7,4},{8,9},{9,10},{10,1... | collective-permute-start | bytes 393224 | tf_op jit(solution)/shard_map/ppermute | solution.py:23
  34.1 3.0 %collective-permute-start.7 = (f32[9,256,2,64]{1,3,2,0:T(8,128)S(1)}, f32[9,256,2,64]{1,3,2,0:T(8,128)}, u32[]{:S(2)}, u32[]{:S(2)}) collective-permute-start(f32[9,256,2,64]{1,3,2,0:T(8,128)S(1)} %dynamic-slice_bitcast_fusion), channel_id=1, source_target_pairs={{0,1},{1,0},{2,3},{3,2},{4,5},{5,4},{6,7},{7,6},{8,9},{9,8},{10,11... | collective-permute-start | bytes 3538952 | tf_op jit(solution)/shard_map/ppermute | solution.py:74
  37.2 4.2 %copy-start.2 = (bf16[9,256,256]{2,1,0:T(8,128)(2,1)S(1)}, bf16[9,256,256]{2,1,0:T(8,128)(2,1)}, u32[]{:S(2)}) copy-start(bf16[9,256,256]{2,1,0:T(8,128)(2,1)} %param.10) | copy-start | bytes 3538948
  38.7 1.0 %copy-start.3 = (f32[9,256,2,64]{1,3,2,0:T(8,128)}, f32[9,256,2,64]{1,3,2,0:T(8,128)S(1)}, u32[]{:S(2)}) copy-start(f32[9,256,2,64]{1,3,2,0:T(8,128)S(1)} %bitcast_add_fusion) | copy-start | bytes 3538948
  40.5 12.9 %collective-permute-start.8 = (bf16[9,256,64]{1,2,0:T(8,128)(2,1)}, bf16[9,256,64]{1,2,0:T(8,128)(2,1)}, u32[]{:S(2)}, u32[]{:S(2)}) collective-permute-start(bf16[9,256,64]{1,2,0:T(8,128)(2,1)} %fusion.20), channel_id=1, source_target_pairs={{0,2},{1,3},{2,0},{3,1},{4,6},{5,7},{6,4},{7,5},{8,10},{9,11},{10,... | collective-permute-start | bytes 884744 | tf_op jit(solution)/shard_map/ppermute | solution.py:81
  42.1 10.2 %copy-start = (bf16[1,4,64,2304]{3,2,1,0:T(8,128)(2,1)S(1)}, bf16[1,4,64,2304]{3,2,1,0:T(8,128)(2,1)}, u32[]{:S(2)}) copy-start(bf16[1,4,64,2304]{3,2,1,0:T(8,128)(2,1)} %shard_map.103) | copy-start | bytes 3538948
  52.2 1.3 %copy-start.4 = (f32[9,256,2,64]{1,3,2,0:T(8,128)S(1)}, f32[9,256,2,64]{1,3,2,0:T(8,128)}, u32[]{:S(2)}) copy-start(f32[9,256,2,64]{1,3,2,0:T(8,128)} %copy-done.3) | copy-start | bytes 3538948
  53.4 7.4 %copy-start.1 = (bf16[1,4,64,2304]{3,2,1,0:T(8,128)(2,1)S(1)}, bf16[1,4,64,2304]{3,2,1,0:T(8,128)(2,1)}, u32[]{:S(2)}) copy-start(bf16[1,4,64,2304]{3,2,1,0:T(8,128)(2,1)} %shard_map.104) | copy-start | bytes 3538948
  54.8 9.6 %collective-permute-start.11 = (bf16[9,64,64]{1,2,0:T(8,128)(2,1)S(1)}, bf16[9,64,64]{1,2,0:T(8,128)(2,1)S(1)}, u32[]{:S(2)}, u32[]{:S(2)}) collective-permute-start(bf16[9,64,64]{1,2,0:T(8,128)(2,1)S(1)} %get-tuple-element.9), channel_id=1, source_target_pairs={{0,12},{4,0},{8,4},{12,8},{1,13},{5,1},{9,5},{13,9},{2,14},{6,2},{... | collective-permute-start | bytes 221192 | tf_op jit(solution)/shard_map/ppermute | solution.py:55
  60.1 12.8 %collective-permute-start.10 = (bf16[9,64,64]{1,2,0:T(8,128)(2,1)S(1)}, bf16[9,64,64]{1,2,0:T(8,128)(2,1)S(1)}, u32[]{:S(2)}, u32[]{:S(2)}) collective-permute-start(bf16[9,64,64]{1,2,0:T(8,128)(2,1)S(1)} %get-tuple-element.10), channel_id=1, source_target_pairs={{0,8},{4,12},{8,0},{12,4},{1,9},{5,13},{9,1},{13,5},{2,10},{6,14},... | collective-permute-start | bytes 221192 | tf_op jit(solution)/shard_map/ppermute | solution.py:55
  60.1 12.8 %collective-permute-start.9 = (bf16[9,64,64]{1,2,0:T(8,128)(2,1)S(1)}, bf16[9,64,64]{1,2,0:T(8,128)(2,1)S(1)}, u32[]{:S(2)}, u32[]{:S(2)}) collective-permute-start(bf16[9,64,64]{1,2,0:T(8,128)(2,1)S(1)} %get-tuple-element.8), channel_id=1, source_target_pairs={{0,4},{4,8},{8,12},{12,0},{1,5},{5,9},{9,13},{13,1},{2,6},{6,10},{... | collective-permute-start | bytes 221192 | tf_op jit(solution)/shard_map/ppermute | solution.py:55

commit v8 on v6

--- a/solution.py
+++ b/solution.py
@@ -59,7 +59,7 @@
 
 def filter_kernel(
     first_ref, src_ref, start_ref, span_ref, basis_ref, scale_ref, field_ref, total_ref,
-    out_ref, acc_ref, *, slots, height, lon_count, lon_total, backward,
+    out_ref, acc_ref, *hits_ref, slots, height, lon_count, lon_total, backward,
 ):
     r = pl.program_id(1)
     first_row = first_ref[0]
@@ -83,18 +83,30 @@
 
     if backward:
         target = first_row + r
-        for e in range(2 * REACH + 1):
-            row = r + e
+        list_ref = hits_ref[0]
+
+        def collect(i, count):
+            e = i // slots
+            slot = i % slots
             global_row = target + e - REACH
             inside = (global_row >= 0) & (global_row < height)
             table_row = jnp.clip(global_row, 0, height - 1)
-            for slot in range(slots):
-                scale = scale_ref[table_row, slot]
-                hit = inside & (src_ref[table_row, slot] == target) & (scale != 0.0)
-
-                @pl.when(hit)
-                def _():
-                    add_slot(row, table_row, slot, scale)
+            scale = scale_ref[table_row, slot]
+            hit = inside & (src_ref[table_row, slot] == target) & (scale != 0.0)
+            list_ref[count] = i
+            return count + hit.astype(jnp.int32)
+
+        count = lax.fori_loop(0, (2 * REACH + 1) * slots, collect, jnp.int32(0))
+
+        def accumulate(j, carry):
+            i = list_ref[j]
+            e = i // slots
+            slot = i % slots
+            table_row = target + e - REACH
+            add_slot(r + e, table_row, slot, scale_ref[table_row, slot])
+            return carry
+
+        lax.fori_loop(0, count, accumulate, jnp.int32(0))
     else:
         table_row = first_row + r
         for slot in range(slots):
@@ -131,7 +143,8 @@
         out_shape=jax.ShapeDtypeStruct(
             (members, row_count, lon_count, BASIS * channels), jnp.bfloat16
         ),
-        scratch_shapes=[pltpu.VMEM((BASIS, lon_count, channels), jnp.float32)],
+        scratch_shapes=[pltpu.VMEM((BASIS, lon_count, channels), jnp.float32)]
+        + ([pltpu.SMEM(((2 * REACH + 1) * slots,), jnp.int32)] if backward else []),
     )(first, *tables, field, totals[:, :, None, :])
 
 

time: 68 us -> 73.5 us (1.081)
  Pallas kernels: 14.5 us -> 19.6 us
    pallas_call x2, Pallas kernels: 14.5 us -> 19.6 us  [run_filter(): pl.pallas_call(kernel, grid=(members, row_count), in_specs=[smem] * 6 + [...]
  transfers between devices with their start and end apart: 13 -> 13, of which waited for: 6 -> 6; matrix products, arithmetic and copies ran while one was open for 12% -> 11% of each run, Pallas kernels for 16% -> 21%
where the time goes in v8:
time: 73.5 us; the launch traced here: 73.2 us
  Pallas kernels  19.6 us (27%)
  waiting for transfers between devices  18.8 us (26%)
  starting transfers between devices  17.2 us (23%)
  local copies, waits for them, and re-layouts  7.15 us (10%)
  matrix products  5.41 us (7%)
  other arithmetic  4.21 us (6%)
  between operations  0.85 us (1%)
    pallas_call x2, Pallas kernels, run_filter(): pl.pallas_call(kernel, grid=(members, row_count), in_specs=[smem] * 6 + [...  19.6 us
    ppermute x6, waiting for transfers between devices, ring_scatter(): sent = lax.ppermute(piece.astype(jnp.bfloat16), axis, pairs)  11.2 us
    ppermute x6, starting transfers between devices, ring_scatter(): sent = lax.ppermute(piece.astype(jnp.bfloat16), axis, pairs)  7.52 us
    ppermute x2, starting transfers between devices, with_halo(): lax.ppermute(lax.slice_in_dim(block, block.shape[dim] - width, None, axis...  4.96 us
    ppermute x2, waiting for transfers between devices, with_halo(): lax.ppermute(lax.slice_in_dim(block, block.shape[dim] - width, None, axis...  4.56 us
    unnamed x17, local copies, waits for them, and re-layouts  3.34 us
    ppermute x3, starting transfers between devices, ring_sum(): total = total + lax.ppermute(value, axis, pairs)  3.23 us
    ppermute x2, waiting for transfers between devices, with_halo(): lax.ppermute(lax.slice_in_dim(block, 0, width, axis=dim), axis, backward)  3.01 us
  transfers between devices with their start and end apart: 13, of which 6 were waited for; matrix products, arithmetic and copies ran while one was open for 11% of the time, Pallas kernels for 21%

profile of v8, /device:TPU:0, one launch (start us, length us, event | category | flops | bytes accessed | tf_op | source)
XLA Modules:
  0.0 73.2 jit_solution(10030057942398247449)
XLA Ops:
  0.6 0.0 copy-start.5
  0.6 0.0 copy-start.6
  0.7 0.9 %convert_reduce_fusion = f32[4,256]{1,0:T(4,128)S(1)} fusion(bf16[1,4,64,256]{3,2,1,0:T(8,128)(2,1)} %param.9), kind=kLoop, calls=%fused_computation.27 | loop fusion | flops 130048 | bytes 135168 | tf_op jit(solution)/shard_map/reduce_sum | solution.py:165
  1.6 0.9 %convert_reduce_fusion.1 = f32[4,256]{1,0:T(4,128)S(1)} fusion(bf16[1,4,64,256]{3,2,1,0:T(8,128)(2,1)} %param.8), kind=kLoop, calls=%fused_computation.28 | loop fusion | flops 130048 | bytes 135168 | tf_op jit(solution)/shard_map/reduce_sum | solution.py:165
  2.6 2.4 %collective-permute-start.6 = (f32[2,1,4,256]{3,0,2,1:T(2,128)S(1)}, f32[2,1,4,256]{3,0,2,1:T(2,128)S(1)}, u32[]{:S(2)}, u32[]{:S(2)}) collective-permute-start(f32[2,1,4,256]{3,0,2,1:T(2,128)S(1)} %pad_maximum_fusion.3), channel_id=1, source_target_pairs={{0,3},{1,0},{2,1},{3,2},{4,7},{5,4},{6,5},{7,6},{8,11},{9,8},{10,9... | collective-permute-start | bytes 24584 | tf_op jit(solution)/shard_map/ppermute | solution.py:43
  5.0 0.6 collective-permute-start.5
  5.7 0.2 collective-permute-start.4
  5.8 0.9 %constant_dynamic-update-slice_fusion.1 = bf16[1,4,64,512]{3,2,1,0:T(8,128)(2,1)S(1)} fusion(bf16[1,4,64,256]{3,2,1,0:T(8,128)(2,1)} %param.8), kind=kLoop, calls=%fused_computation.41 | loop fusion | bytes 262144
  6.7 0.9 %constant_dynamic-update-slice_fusion = bf16[1,4,64,512]{3,2,1,0:T(8,128)(2,1)S(1)} fusion(bf16[1,4,64,512]{3,2,1,0:T(8,128)(2,1)S(1)} %constant_dynamic-update-slice_fusion.1, bf16[1,4,64,256]{3,2,1,0:T(8,128)(2,1)} %param.9), kind=kLoop, calls=%fused_computation.40 | loop fusion | bytes 262144 | tf_op jit(solution)/shard_map/concatenate | solution.py:161
  7.7 1.3 %collective-permute-start.1 = (bf16[1,2,64,512]{3,2,1,0:T(8,128)(2,1)S(1)}, bf16[1,2,64,512]{3,2,1,0:T(8,128)(2,1)S(1)}, u32[]{:S(2)}, u32[]{:S(2)}) collective-permute-start(bf16[1,2,64,512]{3,2,1,0:T(8,128)(2,1)S(1)} %get-tuple-element.20), channel_id=1, source_target_pairs={{4,0},{8,4},{12,8},{5,1},{9,5},{13,9},{6,2},{10,6},{14,10},{7,3},{... | collective-permute-start | bytes 393224 | tf_op jit(solution)/shard_map/ppermute | solution.py:26
  9.0 4.6 %collective-permute-start = (bf16[1,2,64,512]{3,2,1,0:T(8,128)(2,1)S(1)}, bf16[1,2,64,512]{3,2,1,0:T(8,128)(2,1)S(1)}, u32[]{:S(2)}, u32[]{:S(2)}) collective-permute-start(bf16[1,2,64,512]{3,2,1,0:T(8,128)(2,1)S(1)} %get-tuple-element.19), channel_id=1, source_target_pairs={{0,4},{4,8},{8,12},{1,5},{5,9},{9,13},{2,6},{6,10},{10,14},{3,7},{... | collective-permute-start | bytes 393224 | tf_op jit(solution)/shard_map/ppermute | solution.py:23
  13.6 0.0 copy-done.5
  13.6 0.0 copy-done.6
  13.6 0.6 rsqrt_multiply_fusion.scale_ref
  14.2 1.5 %collective-permute-done.1 = bf16[1,2,64,512]{3,2,1,0:T(8,128)(2,1)S(1)} collective-permute-done((bf16[1,2,64,512]{3,2,1,0:T(8,128)(2,1)S(1)}, bf16[1,2,64,512]{3,2,1,0:T(8,128)(2,1)S(1)}, u32[]{:S(2)}, u32[]{:S(2)}) %collective-permute-start.1) | collective-permute-done | bytes 131104 | tf_op jit(solution)/shard_map/ppermute | solution.py:26
  15.7 1.6 %collective-permute-done = bf16[1,2,64,512]{3,2,1,0:T(8,128)(2,1)S(1)} collective-permute-done((bf16[1,2,64,512]{3,2,1,0:T(8,128)(2,1)S(1)}, bf16[1,2,64,512]{3,2,1,0:T(8,128)(2,1)S(1)}, u32[]{:S(2)}, u32[]{:S(2)}) %collective-permute-start) | collective-permute-done | bytes 131104 | tf_op jit(solution)/shard_map/ppermute | solution.py:23
  17.3 0.2 collective-permute-start.3
  17.5 0.4 collective-permute-start.2
  17.9 0.0 collective-permute-done.6
  17.9 0.0 collective-permute-done.5
  17.9 0.0 collective-permute-done.4
  17.9 0.6 fusion.23
  18.6 1.6 %collective-permute-done.3 = bf16[1,8,16,512]{3,2,1,0:T(8,128)(2,1)S(1)} collective-permute-done((bf16[1,8,16,512]{3,2,1,0:T(8,128)(2,1)S(1)}, bf16[1,8,16,512]{3,2,1,0:T(8,128)(2,1)S(1)}, u32[]{:S(2)}, u32[]{:S(2)}) %collective-permute-start.3) | collective-permute-done | bytes 131104 | tf_op jit(solution)/shard_map/ppermute | solution.py:26
  20.1 2.9 %collective-permute-done.2 = bf16[1,8,16,512]{3,2,1,0:T(8,128)(2,1)S(1)} collective-permute-done((bf16[1,8,16,512]{3,2,1,0:T(8,128)(2,1)S(1)}, bf16[1,8,16,512]{3,2,1,0:T(8,128)(2,1)S(1)}, u32[]{:S(2)}, u32[]{:S(2)}) %collective-permute-start.2) | collective-permute-done | bytes 131104 | tf_op jit(solution)/shard_map/ppermute | solution.py:23
  23.0 0.1 fusion.18
  23.1 1.1 %fusion.24 = (bf16[1,8,128,256]{3,2,1,0:T(8,128)(2,1)}, bf16[1,8,128,256]{3,2,1,0:T(8,128)(2,1)}) fusion(bf16[1,8,128,512]{3,2,1,0:T(8,128)(2,1)S(1)} %fusion.18), kind=kLoop, calls=%fused_computation.42 | loop fusion | bytes 2097152 | tf_op jit(solution)/shard_map/slice | solution.py:163
  24.2 0.0 copy-start.4
  24.2 3.9 %shard_map.103 = bf16[1,4,64,2304]{3,2,1,0:T(8,128)(2,1)} custom-call(s32[1]{0:T(128)} %bitcast.first_ref, s32[16,12]{1,0:T(8,128)} %src_ref.3, s32[16,12]{1,0:T(8,128)} %start_ref.3, s32[16,12]{1,0:T(8,128)} %span_ref.3, s32[16,12]{1,0:T(8,128)} %basis_ref.3, f32[16,12]{1,0:T(8,128)} %rsqrt_multiply_fusion.scale_ref, ...), custom_call_target="tpu_custom_call" | custom-call | tf_op jit(solution)/shard_map/pallas_call | solution.py:132
  28.2 0.0 copy-done.4
  28.2 1.8 %convolution_bitcast_fusion = f32[9,256,256]{1,2,0:T(8,128)S(1)} fusion(bf16[4,8,9,8,256]{4,3,2,1,0:T(8,128)(2,1)} %bitcast.44, bf16[1,4,64,256]{3,2,1,0:T(8,128)(2,1)S(1)} %copy-done.4), kind=kOutput, calls=%fused_computation.6 | convolution fusion | flops 301989888 | bytes 3670016 | tf_op jit(solution)/shard_map/brwq,brwo->qo/dot_general | solution.py:185
  30.0 0.0 copy-start.2
  30.0 1.0 %dynamic-slice_convert_fusion.2 = (bf16[9,256,64]{1,2,0:T(8,128)(2,1)}, bf16[9,256,64]{1,2,0:T(8,128)(2,1)}, bf16[9,256,64]{1,2,0:T(8,128)(2,1)}) fusion(f32[9,256,256]{1,2,0:T(8,128)S(1)} %convolution_bitcast_fusion, s32[]{:T(128)S(6)} %select_n.53, s32[]{:T(128)S(6)} %select_n.57, s32[]{:T(128)S(6)} %select_n.55), kind=kLoop, calls=%fused_computation.22 | loop fusion | bytes 1769484 | tf_op jit(solution)/shard_map/convert_element_type | solution.py:55
  30.9 0.0 collective-permute-start.9
  30.9 1.8 %collective-permute-start.8 = (bf16[9,256,64]{1,2,0:T(8,128)(2,1)}, bf16[9,256,64]{1,2,0:T(8,128)(2,1)}, u32[]{:S(2)}, u32[]{:S(2)}) collective-permute-start(bf16[9,256,64]{1,2,0:T(8,128)(2,1)} %get-tuple-element.11), channel_id=1, source_target_pairs={{0,2},{1,3},{2,0},{3,1},{4,6},{5,7},{6,4},{7,5},{8,10},{9,11},{10,... | collective-permute-start | bytes 884744 | tf_op jit(solution)/shard_map/ppermute | solution.py:55
  32.7 0.0 collective-permute-start.7
  32.7 0.0 copy-done.2
  32.7 1.5 %copy.15 = bf16[9,256,256]{1,2,0:T(8,128)(2,1)} copy(bf16[9,256,256]{2,1,0:T(8,128)(2,1)S(1)} %copy-done.2) | data formatting | bytes 2359296 | tf_op args[2]
  34.2 0.0 copy-start
  34.2 15.7 %shard_map.104 = bf16[1,4,64,2304]{3,2,1,0:T(8,128)(2,1)} custom-call(s32[1]{0:T(128)} %bitcast.first_ref, s32[16,12]{1,0:T(8,128)} %src_ref.3, s32[16,12]{1,0:T(8,128)} %start_ref.3, s32[16,12]{1,0:T(8,128)} %span_ref.3, s32[16,12]{1,0:T(8,128)} %basis_ref.3, f32[16,12]{1,0:T(8,128)} %rsqrt_multiply_fusion.scale_ref, ...), custom_call_target="tpu_custom_call" | custom-call | tf_op jit(solution)/shard_map/pallas_call | solution.py:132
  49.9 0.0 copy-done
  49.9 2.4 %fusion.11 = f32[1,4,64,256]{3,2,1,0:T(8,128)} fusion(bf16[2304,256,1]{1,0,2:T(8,128)(2,1)} %bitcast.45, bf16[1,4,64,2304]{3,2,1,0:T(8,128)(2,1)S(1)} %copy-done), kind=kOutput, calls=%fused_computation.13 | convolution fusion | flops 301989888 | bytes 2621440 | tf_op jit(solution)/shard_map/brwq,qo->brwo/dot_general | solution.py:176
  52.4 0.0 copy-start.1
  52.4 0.0 copy-start.3
  52.4 0.0 collective-permute-done.9
  52.4 0.0 collective-permute-done.8
  52.4 0.0 collective-permute-done.7
  52.4 1.4 %convert_add_fusion = f32[9,256,64]{1,2,0:T(8,128)S(1)} fusion(bf16[9,256,64]{1,2,0:T(8,128)(2,1)} %collective-permute-done.9, bf16[9,256,64]{1,2,0:T(8,128)(2,1)} %collective-permute-done.8, bf16[9,256,64]{1,2,0:T(8,128)(2,1)} %collective-permute-done.7, f32[9,256,256]{1,2,0:T(8,128)S(1)} %convolution_bitcast_fusion, s32[]{:T(128)S(6)} %select_n.51), kind=kLoop, calls=%fused_computation.19 | loop fusion | flops 884736 | bytes 2064388 | tf_op jit(solution)/shard_map/add | solution.py:56
  53.8 0.2 dynamic-slice_convert_fusion.5
  54.0 5.1 %collective-permute-start.12 = (bf16[9,64,64]{1,2,0:T(8,128)(2,1)S(1)}, bf16[9,64,64]{1,2,0:T(8,128)(2,1)S(1)}, u32[]{:S(2)}, u32[]{:S(2)}) collective-permute-start(bf16[9,64,64]{1,2,0:T(8,128)(2,1)S(1)} %get-tuple-element.15), channel_id=1, source_target_pairs={{0,12},{4,0},{8,4},{12,8},{1,13},{5,1},{9,5},{13,9},{2,14},{6,2},{... | collective-permute-start | bytes 221192 | tf_op jit(solution)/shard_map/ppermute | solution.py:55
  59.2 0.0 collective-permute-start.11
  59.2 0.6 collective-permute-start.10
  59.8 0.0 copy-done.1
  59.8 0.0 copy-done.3
  59.8 1.2 %fusion.14 = f32[1,4,64,256]{3,2,1,0:T(8,128)} fusion(bf16[2304,256,1]{1,0,2:T(8,128)(2,1)S(1)} %bitcast.46, bf16[1,4,64,2304]{3,2,1,0:T(8,128)(2,1)S(1)} %copy-done.1), kind=kOutput, calls=%fused_computation.14 | convolution fusion | flops 301989888 | bytes 2621440 | tf_op jit(solution)/shard_map/bpwq,qc->bpwc/dot_general | solution.py:182
  61.0 2.4 %collective-permute-done.12 = bf16[9,64,64]{1,2,0:T(8,128)(2,1)S(1)} collective-permute-done((bf16[9,64,64]{1,2,0:T(8,128)(2,1)S(1)}, bf16[9,64,64]{1,2,0:T(8,128)(2,1)S(1)}, u32[]{:S(2)}, u32[]{:S(2)}) %collective-permute-start.12) | collective-permute-done | bytes 73760 | tf_op jit(solution)/shard_map/ppermute | solution.py:55
  63.4 8.8 %collective-permute-done.11 = bf16[9,64,64]{1,2,0:T(8,128)(2,1)S(1)} collective-permute-done((bf16[9,64,64]{1,2,0:T(8,128)(2,1)S(1)}, bf16[9,64,64]{1,2,0:T(8,128)(2,1)S(1)}, u32[]{:S(2)}, u32[]{:S(2)}) %collective-permute-start.11) | collective-permute-done | bytes 73760 | tf_op jit(solution)/shard_map/ppermute | solution.py:55
  72.2 0.0 collective-permute-done.10
  72.2 0.1 add_multiply_fusion
  72.4 0.9 %copy.17 = f32[9,64,64]{2,1,0:T(8,128)} copy(f32[9,64,64]{1,2,0:T(8,128)S(1)} %add_multiply_fusion) | data formatting | bytes 294912
  (6 shorter events, 0.1 us)
Async XLA Ops:
  0.6 13.0 %copy-start.5 = (s32[16,12]{1,0:T(8,128)S(1)}, s32[16,12]{1,0:T(8,128)}, u32[]{:S(2)}) copy-start(s32[16,12]{1,0:T(8,128)} %span_ref.3) | copy-start | bytes 2308
  0.6 13.0 %copy-start.6 = (f32[16,12]{1,0:T(8,128)S(1)}, f32[16,12]{1,0:T(8,128)}, u32[]{:S(2)}) copy-start(f32[16,12]{1,0:T(8,128)} %param.15) | copy-start | bytes 2308
  2.6 15.3 %collective-permute-start.6 = (f32[2,1,4,256]{3,0,2,1:T(2,128)S(1)}, f32[2,1,4,256]{3,0,2,1:T(2,128)S(1)}, u32[]{:S(2)}, u32[]{:S(2)}) collective-permute-start(f32[2,1,4,256]{3,0,2,1:T(2,128)S(1)} %pad_maximum_fusion.3), channel_id=1, source_target_pairs={{0,3},{1,0},{2,1},{3,2},{4,7},{5,4},{6,5},{7,6},{8,11},{9,8},{10,9... | collective-permute-start | bytes 24584 | tf_op jit(solution)/shard_map/ppermute | solution.py:43
  5.0 12.9 %collective-permute-start.5 = (f32[2,1,4,256]{3,0,2,1:T(2,128)S(1)}, f32[2,1,4,256]{3,0,2,1:T(2,128)S(1)}, u32[]{:S(2)}, u32[]{:S(2)}) collective-permute-start(f32[2,1,4,256]{3,0,2,1:T(2,128)S(1)} %pad_maximum_fusion.3), channel_id=1, source_target_pairs={{0,2},{1,3},{2,0},{3,1},{4,6},{5,7},{6,4},{7,5},{8,10},{9,11},{10,... | collective-permute-start | bytes 24584 | tf_op jit(solution)/shard_map/ppermute | solution.py:43
  5.7 12.3 %collective-permute-start.4 = (f32[2,1,4,256]{3,0,2,1:T(2,128)S(1)}, f32[2,1,4,256]{3,0,2,1:T(2,128)S(1)}, u32[]{:S(2)}, u32[]{:S(2)}) collective-permute-start(f32[2,1,4,256]{3,0,2,1:T(2,128)S(1)} %pad_maximum_fusion.3), channel_id=1, source_target_pairs={{0,1},{1,2},{2,3},{3,0},{4,5},{5,6},{6,7},{7,4},{8,9},{9,10},{10,1... | collective-permute-start | bytes 24584 | tf_op jit(solution)/shard_map/ppermute | solution.py:43
  7.7 8.0 %collective-permute-start.1 = (bf16[1,2,64,512]{3,2,1,0:T(8,128)(2,1)S(1)}, bf16[1,2,64,512]{3,2,1,0:T(8,128)(2,1)S(1)}, u32[]{:S(2)}, u32[]{:S(2)}) collective-permute-start(bf16[1,2,64,512]{3,2,1,0:T(8,128)(2,1)S(1)} %get-tuple-element.20), channel_id=1, source_target_pairs={{4,0},{8,4},{12,8},{5,1},{9,5},{13,9},{6,2},{10,6},{14,10},{7,3},{... | collective-permute-start | bytes 393224 | tf_op jit(solution)/shard_map/ppermute | solution.py:26
  9.0 8.3 %collective-permute-start = (bf16[1,2,64,512]{3,2,1,0:T(8,128)(2,1)S(1)}, bf16[1,2,64,512]{3,2,1,0:T(8,128)(2,1)S(1)}, u32[]{:S(2)}, u32[]{:S(2)}) collective-permute-start(bf16[1,2,64,512]{3,2,1,0:T(8,128)(2,1)S(1)} %get-tuple-element.19), channel_id=1, source_target_pairs={{0,4},{4,8},{8,12},{1,5},{5,9},{9,13},{2,6},{6,10},{10,14},{3,7},{... | collective-permute-start | bytes 393224 | tf_op jit(solution)/shard_map/ppermute | solution.py:23
  17.3 2.8 %collective-permute-start.3 = (bf16[1,8,16,512]{3,2,1,0:T(8,128)(2,1)S(1)}, bf16[1,8,16,512]{3,2,1,0:T(8,128)(2,1)S(1)}, u32[]{:S(2)}, u32[]{:S(2)}) collective-permute-start(bf16[1,8,16,512]{3,2,1,0:T(8,128)(2,1)S(1)} %get-tuple-element.18), channel_id=1, source_target_pairs={{1,0},{2,1},{3,2},{0,3},{5,4},{6,5},{7,6},{4,7},{9,8},{10,9},{11,1... | collective-permute-start | bytes 393224 | tf_op jit(solution)/shard_map/ppermute | solution.py:26
  17.5 5.5 %collective-permute-start.2 = (bf16[1,8,16,512]{3,2,1,0:T(8,128)(2,1)S(1)}, bf16[1,8,16,512]{3,2,1,0:T(8,128)(2,1)S(1)}, u32[]{:S(2)}, u32[]{:S(2)}) collective-permute-start(bf16[1,8,16,512]{3,2,1,0:T(8,128)(2,1)S(1)} %get-tuple-element.17), channel_id=1, source_target_pairs={{0,1},{1,2},{2,3},{3,0},{4,5},{5,6},{6,7},{7,4},{8,9},{9,10},{10,1... | collective-permute-start | bytes 393224 | tf_op jit(solution)/shard_map/ppermute | solution.py:23
  24.2 3.9 %copy-start.4 = (bf16[1,4,64,256]{3,2,1,0:T(8,128)(2,1)S(1)}, bf16[1,4,64,256]{3,2,1,0:T(8,128)(2,1)}, u32[]{:S(2)}) copy-start(bf16[1,4,64,256]{3,2,1,0:T(8,128)(2,1)} %param.9) | copy-start | bytes 393220
  30.0 2.7 %copy-start.2 = (bf16[9,256,256]{2,1,0:T(8,128)(2,1)S(1)}, bf16[9,256,256]{2,1,0:T(8,128)(2,1)}, u32[]{:S(2)}) copy-start(bf16[9,256,256]{2,1,0:T(8,128)(2,1)} %param.10) | copy-start | bytes 3538948
  30.9 21.5 %collective-permute-start.9 = (bf16[9,256,64]{1,2,0:T(8,128)(2,1)}, bf16[9,256,64]{1,2,0:T(8,128)(2,1)}, u32[]{:S(2)}, u32[]{:S(2)}) collective-permute-start(bf16[9,256,64]{1,2,0:T(8,128)(2,1)} %get-tuple-element.10), channel_id=1, source_target_pairs={{0,3},{1,0},{2,1},{3,2},{4,7},{5,4},{6,5},{7,6},{8,11},{9,8},{10,9... | collective-permute-start | bytes 884744 | tf_op jit(solution)/shard_map/ppermute | solution.py:55
  30.9 21.5 %collective-permute-start.8 = (bf16[9,256,64]{1,2,0:T(8,128)(2,1)}, bf16[9,256,64]{1,2,0:T(8,128)(2,1)}, u32[]{:S(2)}, u32[]{:S(2)}) collective-permute-start(bf16[9,256,64]{1,2,0:T(8,128)(2,1)} %get-tuple-element.11), channel_id=1, source_target_pairs={{0,2},{1,3},{2,0},{3,1},{4,6},{5,7},{6,4},{7,5},{8,10},{9,11},{10,... | collective-permute-start | bytes 884744 | tf_op jit(solution)/shard_map/ppermute | solution.py:55
  32.7 19.7 %collective-permute-start.7 = (bf16[9,256,64]{1,2,0:T(8,128)(2,1)}, bf16[9,256,64]{1,2,0:T(8,128)(2,1)}, u32[]{:S(2)}, u32[]{:S(2)}) collective-permute-start(bf16[9,256,64]{1,2,0:T(8,128)(2,1)} %get-tuple-element.9), channel_id=1, source_target_pairs={{0,1},{1,2},{2,3},{3,0},{4,5},{5,6},{6,7},{7,4},{8,9},{9,10},{10,1... | collective-permute-start | bytes 884744 | tf_op jit(solution)/shard_map/ppermute | solution.py:55
  34.2 15.7 %copy-start = (bf16[1,4,64,2304]{3,2,1,0:T(8,128)(2,1)S(1)}, bf16[1,4,64,2304]{3,2,1,0:T(8,128)(2,1)}, u32[]{:S(2)}) copy-start(bf16[1,4,64,2304]{3,2,1,0:T(8,128)(2,1)} %shard_map.103) | copy-start | bytes 3538948
  52.4 7.4 %copy-start.1 = (bf16[1,4,64,2304]{3,2,1,0:T(8,128)(2,1)S(1)}, bf16[1,4,64,2304]{3,2,1,0:T(8,128)(2,1)}, u32[]{:S(2)}) copy-start(bf16[1,4,64,2304]{3,2,1,0:T(8,128)(2,1)} %shard_map.104) | copy-start | bytes 3538948
  52.4 7.4 %copy-start.3 = (bf16[9,256,256]{1,2,0:T(8,128)(2,1)S(1)}, bf16[9,256,256]{1,2,0:T(8,128)(2,1)}, u32[]{:S(2)}) copy-start(bf16[9,256,256]{1,2,0:T(8,128)(2,1)} %copy.15) | copy-start | bytes 3538948
  54.0 9.4 %collective-permute-start.12 = (bf16[9,64,64]{1,2,0:T(8,128)(2,1)S(1)}, bf16[9,64,64]{1,2,0:T(8,128)(2,1)S(1)}, u32[]{:S(2)}, u32[]{:S(2)}) collective-permute-start(bf16[9,64,64]{1,2,0:T(8,128)(2,1)S(1)} %get-tuple-element.15), channel_id=1, source_target_pairs={{0,12},{4,0},{8,4},{12,8},{1,13},{5,1},{9,5},{13,9},{2,14},{6,2},{... | collective-permute-start | bytes 221192 | tf_op jit(solution)/shard_map/ppermute | solution.py:55
  59.2 13.1 %collective-permute-start.11 = (bf16[9,64,64]{1,2,0:T(8,128)(2,1)S(1)}, bf16[9,64,64]{1,2,0:T(8,128)(2,1)S(1)}, u32[]{:S(2)}, u32[]{:S(2)}) collective-permute-start(bf16[9,64,64]{1,2,0:T(8,128)(2,1)S(1)} %get-tuple-element.16), channel_id=1, source_target_pairs={{0,8},{4,12},{8,0},{12,4},{1,9},{5,13},{9,1},{13,5},{2,10},{6,14},... | collective-permute-start | bytes 221192 | tf_op jit(solution)/shard_map/ppermute | solution.py:55
  59.2 13.1 %collective-permute-start.10 = (bf16[9,64,64]{1,2,0:T(8,128)(2,1)S(1)}, bf16[9,64,64]{1,2,0:T(8,128)(2,1)S(1)}, u32[]{:S(2)}, u32[]{:S(2)}) collective-permute-start(bf16[9,64,64]{1,2,0:T(8,128)(2,1)S(1)} %get-tuple-element.14), channel_id=1, source_target_pairs={{0,4},{4,8},{8,12},{12,0},{1,5},{5,9},{9,13},{13,1},{2,6},{6,10},{... | collective-permute-start | bytes 221192 | tf_op jit(solution)/shard_map/ppermute | solution.py:55

commit v9 on v6

--- a/solution.py
+++ b/solution.py
@@ -162,6 +162,13 @@
     w_fwd = weight.reshape(BASIS * channels, channels)
     response = jnp.einsum("brwq,qo->brwo", flattened, w_fwd, preferred_element_type=jnp.float32)
 
+    partial_value = jnp.einsum(
+        "brwq,brwo->qo", flattened, cotangent, preferred_element_type=jnp.float32
+    )
+    partial_value = partial_value.reshape(BASIS, channels, channels)
+    reduced = ring_scatter(partial_value, "lon", 2)
+    grad_wide, grad_totals, reduced = lax.optimization_barrier((grad_wide, grad_totals, reduced))
+    reduced = ring_scatter(reduced, "lat", 1)
     back_filtered = run_filter(
         first, tables, grad_wide, grad_totals, row_count, lon_count, lon_total, True
     )
@@ -169,12 +176,6 @@
     grad_input = jnp.einsum(
         "bpwq,qc->bpwc", back_filtered, w_back, preferred_element_type=jnp.float32
     )
-    partial_value = jnp.einsum(
-        "brwq,brwo->qo", flattened, cotangent, preferred_element_type=jnp.float32
-    )
-    partial_value = partial_value.reshape(BASIS, channels, channels)
-    reduced = ring_scatter(partial_value, "lon", 2)
-    reduced = ring_scatter(reduced, "lat", 1)
     grad_weight = reduced / jnp.sqrt(jnp.float32(members * height * lon_total))
     return (response, grad_input, grad_weight)
 

time: 68 us -> 68 us (level)
  waiting for transfers between devices: 18.2 us -> 14.5 us
  starting transfers between devices: 17.2 us -> 18.6 us
  matrix products: 5.42 us -> 6.69 us
  local copies, waits for them, and re-layouts: 7.15 us -> 8.08 us
    ppermute x6, waiting for transfers between devices: 10.7 us -> 7.07 us  [ring_scatter(): sent = lax.ppermute(piece.astype(jnp.bfloat16), axis, pairs)]
    ppermute x2, starting transfers between devices: 1.45 us -> 3.02 us  [with_halo(): lax.ppermute(lax.slice_in_dim(block, 0, width, axis=dim), axis, backward)]
    ppermute x2, waiting for transfers between devices: 4.56 us -> 3.09 us  [with_halo(): lax.ppermute(lax.slice_in_dim(block, block.shape[dim] - width, None, axis...]
    ppermute x2, starting transfers between devices: 4.96 us -> 3.54 us  [with_halo(): lax.ppermute(lax.slice_in_dim(block, block.shape[dim] - width, None, axis...]
    ppermute x2, waiting for transfers between devices: 3.01 us -> 4.37 us  [with_halo(): lax.ppermute(lax.slice_in_dim(block, 0, width, axis=dim), axis, backward)]
    dot_general x1, matrix products: 1.18 us -> 2.45 us  [on_device(): jnp.einsum('bpwq,qc->bpwc', back_filtered, w_back, preferred_element_type...]
    ppermute x3, starting transfers between devices: 3.23 us -> 4.46 us  [ring_sum(): total = total + lax.ppermute(value, axis, pairs)]
    unnamed x17 -> x13, local copies, waits for them, and re-layouts: 3.34 us -> 4.28 us
  transfers between devices with their start and end apart: 13 -> 13, of which waited for: 6 -> 6; matrix products, arithmetic and copies ran while one was open for 12% -> 16% of each run, Pallas kernels for 16% -> 16%
where the time goes in v9:
time: 68 us; the launch traced here: 67.3 us
  starting transfers between devices  18.6 us (27%)
  Pallas kernels  14.6 us (21%)
  waiting for transfers between devices  14.5 us (21%)
  local copies, waits for them, and re-layouts  8.08 us (12%)
  matrix products  6.69 us (10%)
  other arithmetic  4.05 us (6%)
  between operations  0.84 us (1%)
    pallas_call x2, Pallas kernels, run_filter(): pl.pallas_call(kernel, grid=(members, row_count), in_specs=[smem] * 6 + [...  14.6 us
    ppermute x6, starting transfers between devices, ring_scatter(): sent = lax.ppermute(piece.astype(jnp.bfloat16), axis, pairs)  7.55 us
    ppermute x6, waiting for transfers between devices, ring_scatter(): sent = lax.ppermute(piece.astype(jnp.bfloat16), axis, pairs)  7.07 us
    ppermute x3, starting transfers between devices, ring_sum(): total = total + lax.ppermute(value, axis, pairs)  4.46 us
    ppermute x2, waiting for transfers between devices, with_halo(): lax.ppermute(lax.slice_in_dim(block, 0, width, axis=dim), axis, backward)  4.37 us
    unnamed x13, local copies, waits for them, and re-layouts  4.28 us
    ppermute x2, starting transfers between devices, with_halo(): lax.ppermute(lax.slice_in_dim(block, block.shape[dim] - width, None, axis...  3.54 us
    ppermute x2, waiting for transfers between devices, with_halo(): lax.ppermute(lax.slice_in_dim(block, block.shape[dim] - width, None, axis...  3.09 us
  transfers between devices with their start and end apart: 13, of which 6 were waited for; matrix products, arithmetic and copies ran while one was open for 16% of the time, Pallas kernels for 16%

profile of v9, /device:TPU:0, one launch (start us, length us, event | category | flops | bytes accessed | tf_op | source)
XLA Modules:
  0.0 67.3 jit_solution(14076010966405747104)
XLA Ops:
  0.6 0.0 copy-start.3
  0.6 0.0 copy-start.4
  0.7 0.9 %convert_reduce_fusion = f32[4,256]{1,0:T(4,128)S(1)} fusion(bf16[1,4,64,256]{3,2,1,0:T(8,128)(2,1)} %param.9), kind=kLoop, calls=%fused_computation.27 | loop fusion | flops 130048 | bytes 135168 | tf_op jit(solution)/shard_map/reduce_sum | solution.py:152
  1.6 0.9 %convert_reduce_fusion.1 = f32[4,256]{1,0:T(4,128)S(1)} fusion(bf16[1,4,64,256]{3,2,1,0:T(8,128)(2,1)} %param.8), kind=kLoop, calls=%fused_computation.28 | loop fusion | flops 130048 | bytes 135168 | tf_op jit(solution)/shard_map/reduce_sum | solution.py:152
  2.6 0.5 collective-permute-start.4
  3.1 2.6 %collective-permute-start.5 = (f32[2,1,4,256]{3,0,2,1:T(2,128)S(1)}, f32[2,1,4,256]{3,0,2,1:T(2,128)S(1)}, u32[]{:S(2)}, u32[]{:S(2)}) collective-permute-start(f32[2,1,4,256]{3,0,2,1:T(2,128)S(1)} %pad_maximum_fusion.3), channel_id=1, source_target_pairs={{0,2},{1,3},{2,0},{3,1},{4,6},{5,7},{6,4},{7,5},{8,10},{9,11},{10,... | collective-permute-start | bytes 24584 | tf_op jit(solution)/shard_map/ppermute | solution.py:43
  5.7 1.4 %collective-permute-start.6 = (f32[2,1,4,256]{3,0,2,1:T(2,128)S(1)}, f32[2,1,4,256]{3,0,2,1:T(2,128)S(1)}, u32[]{:S(2)}, u32[]{:S(2)}) collective-permute-start(f32[2,1,4,256]{3,0,2,1:T(2,128)S(1)} %pad_maximum_fusion.3), channel_id=1, source_target_pairs={{0,3},{1,0},{2,1},{3,2},{4,7},{5,4},{6,5},{7,6},{8,11},{9,8},{10,9... | collective-permute-start | bytes 24584 | tf_op jit(solution)/shard_map/ppermute | solution.py:43
  7.0 0.9 %constant_dynamic-update-slice_fusion.1 = bf16[1,4,64,512]{3,2,1,0:T(8,128)(2,1)S(1)} fusion(bf16[1,4,64,256]{3,2,1,0:T(8,128)(2,1)} %param.8), kind=kLoop, calls=%fused_computation.41 | loop fusion | bytes 262144
  8.0 0.9 %constant_dynamic-update-slice_fusion = bf16[1,4,64,512]{3,2,1,0:T(8,128)(2,1)S(1)} fusion(bf16[1,4,64,512]{3,2,1,0:T(8,128)(2,1)S(1)} %constant_dynamic-update-slice_fusion.1, bf16[1,4,64,256]{3,2,1,0:T(8,128)(2,1)} %param.9), kind=kLoop, calls=%fused_computation.40 | loop fusion | bytes 262144 | tf_op jit(solution)/shard_map/concatenate | solution.py:148
  8.9 3.5 %collective-permute-start = (bf16[1,2,64,512]{3,2,1,0:T(8,128)(2,1)S(1)}, bf16[1,2,64,512]{3,2,1,0:T(8,128)(2,1)S(1)}, u32[]{:S(2)}, u32[]{:S(2)}) collective-permute-start(bf16[1,2,64,512]{3,2,1,0:T(8,128)(2,1)S(1)} %get-tuple-element.25), channel_id=1, source_target_pairs={{0,4},{4,8},{8,12},{1,5},{5,9},{9,13},{2,6},{6,10},{10,14},{3,7},{... | collective-permute-start | bytes 393224 | tf_op jit(solution)/shard_map/ppermute | solution.py:23
  12.4 1.3 %collective-permute-start.1 = (bf16[1,2,64,512]{3,2,1,0:T(8,128)(2,1)S(1)}, bf16[1,2,64,512]{3,2,1,0:T(8,128)(2,1)S(1)}, u32[]{:S(2)}, u32[]{:S(2)}) collective-permute-start(bf16[1,2,64,512]{3,2,1,0:T(8,128)(2,1)S(1)} %get-tuple-element.26), channel_id=1, source_target_pairs={{4,0},{8,4},{12,8},{5,1},{9,5},{13,9},{6,2},{10,6},{14,10},{7,3},{... | collective-permute-start | bytes 393224 | tf_op jit(solution)/shard_map/ppermute | solution.py:26
  13.7 0.0 copy-done.3
  13.8 0.0 copy-done.4
  13.8 0.6 rsqrt_multiply_fusion.scale_ref
  14.4 0.5 collective-permute-done
  14.9 4.4 %collective-permute-done.1 = bf16[1,2,64,512]{3,2,1,0:T(8,128)(2,1)S(1)} collective-permute-done((bf16[1,2,64,512]{3,2,1,0:T(8,128)(2,1)S(1)}, bf16[1,2,64,512]{3,2,1,0:T(8,128)(2,1)S(1)}, u32[]{:S(2)}, u32[]{:S(2)}) %collective-permute-start.1) | collective-permute-done | bytes 131104 | tf_op jit(solution)/shard_map/ppermute | solution.py:26
  19.3 0.1 collective-permute-start.2
  19.3 1.7 %collective-permute-start.3 = (bf16[1,8,16,512]{3,2,1,0:T(8,128)(2,1)S(1)}, bf16[1,8,16,512]{3,2,1,0:T(8,128)(2,1)S(1)}, u32[]{:S(2)}, u32[]{:S(2)}) collective-permute-start(bf16[1,8,16,512]{3,2,1,0:T(8,128)(2,1)S(1)} %get-tuple-element.24), channel_id=1, source_target_pairs={{1,0},{2,1},{3,2},{0,3},{5,4},{6,5},{7,6},{4,7},{9,8},{10,9},{11,1... | collective-permute-start | bytes 393224 | tf_op jit(solution)/shard_map/ppermute | solution.py:26
  21.1 0.0 collective-permute-done.4
  21.1 0.0 collective-permute-done.5
  21.1 0.0 collective-permute-done.6
  21.1 0.6 fusion.23
  21.7 2.6 %collective-permute-done.2 = bf16[1,8,16,512]{3,2,1,0:T(8,128)(2,1)S(1)} collective-permute-done((bf16[1,8,16,512]{3,2,1,0:T(8,128)(2,1)S(1)}, bf16[1,8,16,512]{3,2,1,0:T(8,128)(2,1)S(1)}, u32[]{:S(2)}, u32[]{:S(2)}) %collective-permute-start.2) | collective-permute-done | bytes 131104 | tf_op jit(solution)/shard_map/ppermute | solution.py:23
  24.3 0.0 collective-permute-done.3
  24.3 0.1 fusion.18
  24.4 1.1 %fusion.24 = (bf16[1,8,128,256]{3,2,1,0:T(8,128)(2,1)}, bf16[1,8,128,256]{3,2,1,0:T(8,128)(2,1)}) fusion(bf16[1,8,128,512]{3,2,1,0:T(8,128)(2,1)S(1)} %fusion.18), kind=kLoop, calls=%fused_computation.42 | loop fusion | bytes 2097152 | tf_op jit(solution)/shard_map/slice | solution.py:150
  25.5 0.0 copy-start.2
  25.5 3.9 %shard_map.103 = bf16[1,4,64,2304]{3,2,1,0:T(8,128)(2,1)} custom-call(s32[1]{0:T(128)} %bitcast.first_ref, s32[16,12]{1,0:T(8,128)} %src_ref.3, s32[16,12]{1,0:T(8,128)} %start_ref.3, s32[16,12]{1,0:T(8,128)} %span_ref.3, s32[16,12]{1,0:T(8,128)} %basis_ref.3, f32[16,12]{1,0:T(8,128)} %rsqrt_multiply_fusion.scale_ref, ...), custom_call_target="tpu_custom_call" | custom-call | tf_op jit(solution)/shard_map/pallas_call | solution.py:120
  29.4 0.0 copy-done.2
  29.4 1.8 %convolution_bitcast_fusion = f32[9,256,256]{1,2,0:T(8,128)S(1)} fusion(bf16[4,8,9,8,256]{4,3,2,1,0:T(8,128)(2,1)} %bitcast.45, bf16[1,4,64,256]{3,2,1,0:T(8,128)(2,1)S(1)} %copy-done.2), kind=kOutput, calls=%fused_computation.6 | convolution fusion | flops 301989888 | bytes 3670016 | tf_op jit(solution)/shard_map/brwq,brwo->qo/dot_general | solution.py:165
  31.2 0.9 %dynamic-slice_convert_fusion.2 = (bf16[9,256,64]{1,2,0:T(8,128)(2,1)}, bf16[9,256,64]{1,2,0:T(8,128)(2,1)}, bf16[9,256,64]{1,2,0:T(8,128)(2,1)}) fusion(f32[9,256,256]{1,2,0:T(8,128)S(1)} %convolution_bitcast_fusion, s32[]{:T(128)S(6)} %select_n.53, s32[]{:T(128)S(6)} %select_n.57, s32[]{:T(128)S(6)} %select_n.55), kind=kLoop, calls=%fused_computation.22 | loop fusion | bytes 1769484 | tf_op jit(solution)/shard_map/convert_element_type | solution.py:55
  32.2 0.6 collective-permute-start.7
  32.8 0.9 %collective-permute-start.8 = (bf16[9,256,64]{1,2,0:T(8,128)(2,1)}, bf16[9,256,64]{1,2,0:T(8,128)(2,1)}, u32[]{:S(2)}, u32[]{:S(2)}) collective-permute-start(bf16[9,256,64]{1,2,0:T(8,128)(2,1)} %get-tuple-element.17), channel_id=1, source_target_pairs={{0,2},{1,3},{2,0},{3,1},{4,6},{5,7},{6,4},{7,5},{8,10},{9,11},{10,... | collective-permute-start | bytes 884744 | tf_op jit(solution)/shard_map/ppermute | solution.py:55
  33.7 0.4 collective-permute-start.9
  34.2 0.0 copy-start
  34.2 2.5 %copy.16 = bf16[9,256,256]{1,2,0:T(8,128)(2,1)} copy(bf16[9,256,256]{2,1,0:T(8,128)(2,1)} %param.10) | data formatting | bytes 2359296 | tf_op args[2]
  36.7 0.0 copy-done
  36.7 2.5 %fusion.11 = f32[1,4,64,256]{3,2,1,0:T(8,128)} fusion(bf16[2304,256,1]{1,0,2:T(8,128)(2,1)} %bitcast.46, bf16[1,4,64,2304]{3,2,1,0:T(8,128)(2,1)S(1)} %copy-done), kind=kOutput, calls=%fused_computation.13 | convolution fusion | flops 301989888 | bytes 2621440 | tf_op jit(solution)/shard_map/brwq,qo->brwo/dot_general | solution.py:163
  39.1 1.4 %collective-permute-done.7 = bf16[9,256,64]{1,2,0:T(8,128)(2,1)} collective-permute-done((bf16[9,256,64]{1,2,0:T(8,128)(2,1)}, bf16[9,256,64]{1,2,0:T(8,128)(2,1)}, u32[]{:S(2)}, u32[]{:S(2)}) %collective-permute-start.7) | collective-permute-done | bytes 294944 | tf_op jit(solution)/shard_map/ppermute | solution.py:55
  40.5 2.5 %collective-permute-done.8 = bf16[9,256,64]{1,2,0:T(8,128)(2,1)} collective-permute-done((bf16[9,256,64]{1,2,0:T(8,128)(2,1)}, bf16[9,256,64]{1,2,0:T(8,128)(2,1)}, u32[]{:S(2)}, u32[]{:S(2)}) %collective-permute-start.8) | collective-permute-done | bytes 294944 | tf_op jit(solution)/shard_map/ppermute | solution.py:55
  43.0 3.1 %collective-permute-done.9 = bf16[9,256,64]{1,2,0:T(8,128)(2,1)} collective-permute-done((bf16[9,256,64]{1,2,0:T(8,128)(2,1)}, bf16[9,256,64]{1,2,0:T(8,128)(2,1)}, u32[]{:S(2)}, u32[]{:S(2)}) %collective-permute-start.9) | collective-permute-done | bytes 294944 | tf_op jit(solution)/shard_map/ppermute | solution.py:55
  46.2 1.3 %convert_add_fusion = f32[9,256,64]{1,2,0:T(8,128)S(1)} fusion(bf16[9,256,64]{1,2,0:T(8,128)(2,1)} %collective-permute-done.9, bf16[9,256,64]{1,2,0:T(8,128)(2,1)} %collective-permute-done.8, bf16[9,256,64]{1,2,0:T(8,128)(2,1)} %collective-permute-done.7, f32[9,256,256]{1,2,0:T(8,128)S(1)} %convolution_bitcast_fusion, s32[]{:T(128)S(6)} %select_n.51), kind=kLoop, calls=%fused_computation.19 | loop fusion | flops 884736 | bytes 2064388 | tf_op jit(solution)/shard_map/add | solution.py:56
  47.4 0.0 copy-start.1
  47.4 0.2 dynamic-slice_convert_fusion.5
  47.6 1.6 %collective-permute-start.10 = (bf16[9,64,64]{1,2,0:T(8,128)(2,1)S(1)}, bf16[9,64,64]{1,2,0:T(8,128)(2,1)S(1)}, u32[]{:S(2)}, u32[]{:S(2)}) collective-permute-start(bf16[9,64,64]{1,2,0:T(8,128)(2,1)S(1)} %get-tuple-element.20), channel_id=1, source_target_pairs={{0,4},{4,8},{8,12},{12,0},{1,5},{5,9},{9,13},{13,1},{2,6},{6,10},{... | collective-permute-start | bytes 221192 | tf_op jit(solution)/shard_map/ppermute | solution.py:55
  49.3 1.1 %collective-permute-start.11 = (bf16[9,64,64]{1,2,0:T(8,128)(2,1)S(1)}, bf16[9,64,64]{1,2,0:T(8,128)(2,1)S(1)}, u32[]{:S(2)}, u32[]{:S(2)}) collective-permute-start(bf16[9,64,64]{1,2,0:T(8,128)(2,1)S(1)} %get-tuple-element.22), channel_id=1, source_target_pairs={{0,8},{4,12},{8,0},{12,4},{1,9},{5,13},{9,1},{13,5},{2,10},{6,14},... | collective-permute-start | bytes 221192 | tf_op jit(solution)/shard_map/ppermute | solution.py:55
  50.4 2.8 %collective-permute-start.12 = (bf16[9,64,64]{1,2,0:T(8,128)(2,1)S(1)}, bf16[9,64,64]{1,2,0:T(8,128)(2,1)S(1)}, u32[]{:S(2)}, u32[]{:S(2)}) collective-permute-start(bf16[9,64,64]{1,2,0:T(8,128)(2,1)S(1)} %get-tuple-element.21), channel_id=1, source_target_pairs={{0,12},{4,0},{8,4},{12,8},{1,13},{5,1},{9,5},{13,9},{2,14},{6,2},{... | collective-permute-start | bytes 221192 | tf_op jit(solution)/shard_map/ppermute | solution.py:55
  53.2 10.6 %shard_map.104 = bf16[1,4,64,2304]{3,2,1,0:T(8,128)(2,1)} custom-call(s32[1]{0:T(128)} %bitcast.first_ref, s32[16,12]{1,0:T(8,128)} %src_ref.3, s32[16,12]{1,0:T(8,128)} %start_ref.3, s32[16,12]{1,0:T(8,128)} %span_ref.3, s32[16,12]{1,0:T(8,128)} %basis_ref.3, f32[16,12]{1,0:T(8,128)} %rsqrt_multiply_fusion.scale_ref, ...), custom_call_target="tpu_custom_call" | custom-call | tf_op jit(solution)/shard_map/pallas_call | solution.py:120
  63.8 0.0 copy-done.1
  63.8 2.5 %fusion.14 = f32[1,4,64,256]{3,2,1,0:T(8,128)} fusion(bf16[2304,256,1]{1,0,2:T(8,128)(2,1)S(1)} %bitcast.47, bf16[1,4,64,2304]{3,2,1,0:T(8,128)(2,1)} %shard_map.104), kind=kOutput, calls=%fused_computation.14 | convolution fusion | flops 301989888 | bytes 2621440 | tf_op jit(solution)/shard_map/bpwq,qc->bpwc/dot_general | solution.py:176
  66.3 0.0 collective-permute-done.10
  66.3 0.0 collective-permute-done.11
  66.3 0.0 collective-permute-done.12
  66.3 0.2 add_multiply_fusion
  66.5 0.9 %copy.17 = f32[9,64,64]{2,1,0:T(8,128)} copy(f32[9,64,64]{1,2,0:T(8,128)S(1)} %add_multiply_fusion) | data formatting | bytes 294912
  (6 shorter events, 0.1 us)
Async XLA Ops:
  0.6 13.1 %copy-start.3 = (s32[16,12]{1,0:T(8,128)S(1)}, s32[16,12]{1,0:T(8,128)}, u32[]{:S(2)}) copy-start(s32[16,12]{1,0:T(8,128)} %span_ref.3) | copy-start | bytes 2308
  0.6 13.1 %copy-start.4 = (f32[16,12]{1,0:T(8,128)S(1)}, f32[16,12]{1,0:T(8,128)}, u32[]{:S(2)}) copy-start(f32[16,12]{1,0:T(8,128)} %param.15) | copy-start | bytes 2308
  2.6 18.5 %collective-permute-start.4 = (f32[2,1,4,256]{3,0,2,1:T(2,128)S(1)}, f32[2,1,4,256]{3,0,2,1:T(2,128)S(1)}, u32[]{:S(2)}, u32[]{:S(2)}) collective-permute-start(f32[2,1,4,256]{3,0,2,1:T(2,128)S(1)} %pad_maximum_fusion.3), channel_id=1, source_target_pairs={{0,1},{1,2},{2,3},{3,0},{4,5},{5,6},{6,7},{7,4},{8,9},{9,10},{10,1... | collective-permute-start | bytes 24584 | tf_op jit(solution)/shard_map/ppermute | solution.py:43
  3.1 18.0 %collective-permute-start.5 = (f32[2,1,4,256]{3,0,2,1:T(2,128)S(1)}, f32[2,1,4,256]{3,0,2,1:T(2,128)S(1)}, u32[]{:S(2)}, u32[]{:S(2)}) collective-permute-start(f32[2,1,4,256]{3,0,2,1:T(2,128)S(1)} %pad_maximum_fusion.3), channel_id=1, source_target_pairs={{0,2},{1,3},{2,0},{3,1},{4,6},{5,7},{6,4},{7,5},{8,10},{9,11},{10,... | collective-permute-start | bytes 24584 | tf_op jit(solution)/shard_map/ppermute | solution.py:43
  5.7 15.4 %collective-permute-start.6 = (f32[2,1,4,256]{3,0,2,1:T(2,128)S(1)}, f32[2,1,4,256]{3,0,2,1:T(2,128)S(1)}, u32[]{:S(2)}, u32[]{:S(2)}) collective-permute-start(f32[2,1,4,256]{3,0,2,1:T(2,128)S(1)} %pad_maximum_fusion.3), channel_id=1, source_target_pairs={{0,3},{1,0},{2,1},{3,2},{4,7},{5,4},{6,5},{7,6},{8,11},{9,8},{10,9... | collective-permute-start | bytes 24584 | tf_op jit(solution)/shard_map/ppermute | solution.py:43
  8.9 6.0 %collective-permute-start = (bf16[1,2,64,512]{3,2,1,0:T(8,128)(2,1)S(1)}, bf16[1,2,64,512]{3,2,1,0:T(8,128)(2,1)S(1)}, u32[]{:S(2)}, u32[]{:S(2)}) collective-permute-start(bf16[1,2,64,512]{3,2,1,0:T(8,128)(2,1)S(1)} %get-tuple-element.25), channel_id=1, source_target_pairs={{0,4},{4,8},{8,12},{1,5},{5,9},{9,13},{2,6},{6,10},{10,14},{3,7},{... | collective-permute-start | bytes 393224 | tf_op jit(solution)/shard_map/ppermute | solution.py:23
  12.4 6.9 %collective-permute-start.1 = (bf16[1,2,64,512]{3,2,1,0:T(8,128)(2,1)S(1)}, bf16[1,2,64,512]{3,2,1,0:T(8,128)(2,1)S(1)}, u32[]{:S(2)}, u32[]{:S(2)}) collective-permute-start(bf16[1,2,64,512]{3,2,1,0:T(8,128)(2,1)S(1)} %get-tuple-element.26), channel_id=1, source_target_pairs={{4,0},{8,4},{12,8},{5,1},{9,5},{13,9},{6,2},{10,6},{14,10},{7,3},{... | collective-permute-start | bytes 393224 | tf_op jit(solution)/shard_map/ppermute | solution.py:26
  19.3 5.0 %collective-permute-start.2 = (bf16[1,8,16,512]{3,2,1,0:T(8,128)(2,1)S(1)}, bf16[1,8,16,512]{3,2,1,0:T(8,128)(2,1)S(1)}, u32[]{:S(2)}, u32[]{:S(2)}) collective-permute-start(bf16[1,8,16,512]{3,2,1,0:T(8,128)(2,1)S(1)} %get-tuple-element.23), channel_id=1, source_target_pairs={{0,1},{1,2},{2,3},{3,0},{4,5},{5,6},{6,7},{7,4},{8,9},{9,10},{10,1... | collective-permute-start | bytes 393224 | tf_op jit(solution)/shard_map/ppermute | solution.py:23
  19.3 5.0 %collective-permute-start.3 = (bf16[1,8,16,512]{3,2,1,0:T(8,128)(2,1)S(1)}, bf16[1,8,16,512]{3,2,1,0:T(8,128)(2,1)S(1)}, u32[]{:S(2)}, u32[]{:S(2)}) collective-permute-start(bf16[1,8,16,512]{3,2,1,0:T(8,128)(2,1)S(1)} %get-tuple-element.24), channel_id=1, source_target_pairs={{1,0},{2,1},{3,2},{0,3},{5,4},{6,5},{7,6},{4,7},{9,8},{10,9},{11,1... | collective-permute-start | bytes 393224 | tf_op jit(solution)/shard_map/ppermute | solution.py:26
  25.5 3.9 %copy-start.2 = (bf16[1,4,64,256]{3,2,1,0:T(8,128)(2,1)S(1)}, bf16[1,4,64,256]{3,2,1,0:T(8,128)(2,1)}, u32[]{:S(2)}) copy-start(bf16[1,4,64,256]{3,2,1,0:T(8,128)(2,1)} %param.9) | copy-start | bytes 393220
  32.2 8.4 %collective-permute-start.7 = (bf16[9,256,64]{1,2,0:T(8,128)(2,1)}, bf16[9,256,64]{1,2,0:T(8,128)(2,1)}, u32[]{:S(2)}, u32[]{:S(2)}) collective-permute-start(bf16[9,256,64]{1,2,0:T(8,128)(2,1)} %get-tuple-element.15), channel_id=1, source_target_pairs={{0,1},{1,2},{2,3},{3,0},{4,5},{5,6},{6,7},{7,4},{8,9},{9,10},{10,1... | collective-permute-start | bytes 884744 | tf_op jit(solution)/shard_map/ppermute | solution.py:55
  32.8 10.2 %collective-permute-start.8 = (bf16[9,256,64]{1,2,0:T(8,128)(2,1)}, bf16[9,256,64]{1,2,0:T(8,128)(2,1)}, u32[]{:S(2)}, u32[]{:S(2)}) collective-permute-start(bf16[9,256,64]{1,2,0:T(8,128)(2,1)} %get-tuple-element.17), channel_id=1, source_target_pairs={{0,2},{1,3},{2,0},{3,1},{4,6},{5,7},{6,4},{7,5},{8,10},{9,11},{10,... | collective-permute-start | bytes 884744 | tf_op jit(solution)/shard_map/ppermute | solution.py:55
  33.7 12.4 %collective-permute-start.9 = (bf16[9,256,64]{1,2,0:T(8,128)(2,1)}, bf16[9,256,64]{1,2,0:T(8,128)(2,1)}, u32[]{:S(2)}, u32[]{:S(2)}) collective-permute-start(bf16[9,256,64]{1,2,0:T(8,128)(2,1)} %get-tuple-element.16), channel_id=1, source_target_pairs={{0,3},{1,0},{2,1},{3,2},{4,7},{5,4},{6,5},{7,6},{8,11},{9,8},{10,9... | collective-permute-start | bytes 884744 | tf_op jit(solution)/shard_map/ppermute | solution.py:55
  34.2 2.5 %copy-start = (bf16[1,4,64,2304]{3,2,1,0:T(8,128)(2,1)S(1)}, bf16[1,4,64,2304]{3,2,1,0:T(8,128)(2,1)}, u32[]{:S(2)}) copy-start(bf16[1,4,64,2304]{3,2,1,0:T(8,128)(2,1)} %shard_map.103) | copy-start | bytes 3538948
  47.4 16.4 %copy-start.1 = (bf16[9,256,256]{1,2,0:T(8,128)(2,1)S(1)}, bf16[9,256,256]{1,2,0:T(8,128)(2,1)}, u32[]{:S(2)}) copy-start(bf16[9,256,256]{1,2,0:T(8,128)(2,1)} %copy.16) | copy-start | bytes 3538948
  47.6 18.6 %collective-permute-start.10 = (bf16[9,64,64]{1,2,0:T(8,128)(2,1)S(1)}, bf16[9,64,64]{1,2,0:T(8,128)(2,1)S(1)}, u32[]{:S(2)}, u32[]{:S(2)}) collective-permute-start(bf16[9,64,64]{1,2,0:T(8,128)(2,1)S(1)} %get-tuple-element.20), channel_id=1, source_target_pairs={{0,4},{4,8},{8,12},{12,0},{1,5},{5,9},{9,13},{13,1},{2,6},{6,10},{... | collective-permute-start | bytes 221192 | tf_op jit(solution)/shard_map/ppermute | solution.py:55
  49.3 17.0 %collective-permute-start.11 = (bf16[9,64,64]{1,2,0:T(8,128)(2,1)S(1)}, bf16[9,64,64]{1,2,0:T(8,128)(2,1)S(1)}, u32[]{:S(2)}, u32[]{:S(2)}) collective-permute-start(bf16[9,64,64]{1,2,0:T(8,128)(2,1)S(1)} %get-tuple-element.22), channel_id=1, source_target_pairs={{0,8},{4,12},{8,0},{12,4},{1,9},{5,13},{9,1},{13,5},{2,10},{6,14},... | collective-permute-start | bytes 221192 | tf_op jit(solution)/shard_map/ppermute | solution.py:55
  50.4 15.9 %collective-permute-start.12 = (bf16[9,64,64]{1,2,0:T(8,128)(2,1)S(1)}, bf16[9,64,64]{1,2,0:T(8,128)(2,1)S(1)}, u32[]{:S(2)}, u32[]{:S(2)}) collective-permute-start(bf16[9,64,64]{1,2,0:T(8,128)(2,1)S(1)} %get-tuple-element.21), channel_id=1, source_target_pairs={{0,12},{4,0},{8,4},{12,8},{1,13},{5,1},{9,5},{13,9},{2,14},{6,2},{... | collective-permute-start | bytes 221192 | tf_op jit(solution)/shard_map/ppermute | solution.py:55

commit v10 on v9

--- a/solution.py
+++ b/solution.py
@@ -52,6 +52,29 @@
     for shift in range(1, count):
         pairs = [(i, (i + shift) % count) for i in range(count)]
         piece = lax.dynamic_slice_in_dim(value, ((own + shift) % count) * block, block, dim)
+        sent = lax.ppermute(piece.astype(jnp.bfloat16), axis, pairs)
+        total = total + sent.astype(jnp.float32)
+    return total
+
+
+def paired_scatter(value, axis, dim):
+    count = lax.axis_size(axis)
+    own = lax.axis_index(axis)
+    parity = own % 2
+    group = own // 2
+    groups = count // 2
+    half = value.shape[dim] // 2
+    block = half // groups
+    keep = lax.dynamic_slice_in_dim(value, parity * half, half, dim)
+    give = lax.dynamic_slice_in_dim(value, (1 - parity) * half, half, dim)
+    swap = [(i, i ^ 1) for i in range(count)]
+    merged = keep + lax.ppermute(give.astype(jnp.bfloat16), axis, swap).astype(jnp.float32)
+    total = lax.dynamic_slice_in_dim(merged, group * block, block, dim)
+    for shift in range(1, groups):
+        pairs = [
+            (2 * g + p, 2 * ((g + shift) % groups) + p) for g in range(groups) for p in range(2)
+        ]
+        piece = lax.dynamic_slice_in_dim(merged, ((group + shift) % groups) * block, block, dim)
         sent = lax.ppermute(piece.astype(jnp.bfloat16), axis, pairs)
         total = total + sent.astype(jnp.float32)
     return total
@@ -162,11 +185,21 @@
     w_fwd = weight.reshape(BASIS * channels, channels)
     response = jnp.einsum("brwq,qo->brwo", flattened, w_fwd, preferred_element_type=jnp.float32)
 
+    lon_parts = lax.axis_size("lon")
+    if lon_parts % 2 == 0:
+        o_block = channels // lon_parts
+        mixed = cotangent.reshape(members, row_count, lon_count, lon_parts // 2, 2, o_block)
+        mixed = jnp.swapaxes(mixed, 3, 4).reshape(cotangent.shape)
+    else:
+        mixed = cotangent
     partial_value = jnp.einsum(
-        "brwq,brwo->qo", flattened, cotangent, preferred_element_type=jnp.float32
+        "brwq,brwo->qo", flattened, mixed, preferred_element_type=jnp.float32
     )
     partial_value = partial_value.reshape(BASIS, channels, channels)
-    reduced = ring_scatter(partial_value, "lon", 2)
+    if lon_parts % 2 == 0:
+        reduced = paired_scatter(partial_value, "lon", 2)
+    else:
+        reduced = ring_scatter(partial_value, "lon", 2)
     grad_wide, grad_totals, reduced = lax.optimization_barrier((grad_wide, grad_totals, reduced))
     reduced = ring_scatter(reduced, "lat", 1)
     back_filtered = run_filter(

time: 68 us -> 67.9 us (level)
  starting transfers between devices: 18.6 us -> 17.3 us
  matrix products: 6.69 us -> 5.41 us
  local copies, waits for them, and re-layouts: 8.08 us -> 9.16 us
  other arithmetic: 4.05 us -> 5.05 us
    ppermute x0 -> x2, waiting for transfers between devices: none -> 8.19 us  [the longest x1 6.22 us: paired_scatter(): sent = lax.ppermute(piece.astype(jnp.bfloat16), axis, pairs)]
    ppermute x6 -> x3, waiting for transfers between devices: 7.07 us -> 0.01 us  [ring_scatter(): sent = lax.ppermute(piece.astype(jnp.bfloat16), axis, pairs)]
    ppermute x6 -> x3, starting transfers between devices: 7.55 us -> 4.68 us  [ring_scatter(): sent = lax.ppermute(piece.astype(jnp.bfloat16), axis, pairs)]
    convert_element_type x0 -> x2, local copies, waits for them, and re-layouts: none -> 1.68 us  [the longest x1 0.93 us: paired_scatter(): give.astype(jnp.bfloat16)]
    ppermute x0 -> x2, starting transfers between devices: none -> 1.58 us  [the longest x1 0.93 us: paired_scatter(): sent = lax.ppermute(piece.astype(jnp.bfloat16), axis, pairs)]
    dot_general x1, matrix products: 2.45 us -> 1.18 us  [on_device(): jnp.einsum('brwq,qo->brwo', flattened, w_fwd, preferred_element_type=jnp....]
    add x1 -> x2, other arithmetic: 1.26 us -> 2.21 us  [the longest x1 1.18 us: paired_scatter(): keep + lax.ppermute(give.astype(jnp.bfloat16), axis, swap).astype(jnp.flo...]
    convert_element_type x2 -> x1, local copies, waits for them, and re-layouts: 1.14 us -> 0.2 us  [ring_scatter(): sent = lax.ppermute(piece.astype(jnp.bfloat16), axis, pairs)]
  transfers between devices with their start and end apart: 13 -> 12, of which waited for: 6 -> 4; matrix products, arithmetic and copies ran while one was open for 16% -> 12% of each run, Pallas kernels for 16% -> 16%
where the time goes in v10:
time: 67.9 us; the launch traced here: 67.5 us
  starting transfers between devices  17.3 us (25%)
  waiting for transfers between devices  15.1 us (22%)
  Pallas kernels  14.6 us (22%)
  local copies, waits for them, and re-layouts  9.16 us (13%)
  matrix products  5.41 us (8%)
  other arithmetic  5.05 us (7%)
  between operations  0.91 us (1%)
    pallas_call x2, Pallas kernels, run_filter(): pl.pallas_call(kernel, grid=(members, row_count), in_specs=[smem] * 6 + [...  14.6 us
    ppermute x1, waiting for transfers between devices, paired_scatter(): sent = lax.ppermute(piece.astype(jnp.bfloat16), axis, pairs)  6.22 us
    ppermute x3, starting transfers between devices, ring_scatter(): sent = lax.ppermute(piece.astype(jnp.bfloat16), axis, pairs)  4.68 us
    ppermute x3, starting transfers between devices, ring_sum(): total = total + lax.ppermute(value, axis, pairs)  4.46 us
    ppermute x2, waiting for transfers between devices, with_halo(): lax.ppermute(lax.slice_in_dim(block, 0, width, axis=dim), axis, backward)  4.32 us
    unnamed x17, local copies, waits for them, and re-layouts  4.05 us
    ppermute x2, starting transfers between devices, with_halo(): lax.ppermute(lax.slice_in_dim(block, block.shape[dim] - width, None, axis...  3.54 us
    ppermute x2, starting transfers between devices, with_halo(): lax.ppermute(lax.slice_in_dim(block, 0, width, axis=dim), axis, backward)  3.02 us
  transfers between devices with their start and end apart: 12, of which 4 were waited for; matrix products, arithmetic and copies ran while one was open for 12% of the time, Pallas kernels for 16%

profile of v10, /device:TPU:0, one launch (start us, length us, event | category | flops | bytes accessed | tf_op | source)
XLA Modules:
  0.0 67.5 jit_solution(17023261047799865012)
XLA Ops:
  0.6 0.0 copy-start.4
  0.6 1.0 %convert_reduce_fusion = f32[4,256]{1,0:T(4,128)S(1)} fusion(bf16[1,4,64,256]{3,2,1,0:T(8,128)(2,1)} %param.9), kind=kLoop, calls=%fused_computation.27 | loop fusion | flops 130048 | bytes 135168 | tf_op jit(solution)/shard_map/reduce_sum | solution.py:175
  1.7 0.9 %convert_reduce_fusion.1 = f32[4,256]{1,0:T(4,128)S(1)} fusion(bf16[1,4,64,256]{3,2,1,0:T(8,128)(2,1)} %param.8), kind=kLoop, calls=%fused_computation.28 | loop fusion | flops 130048 | bytes 135168 | tf_op jit(solution)/shard_map/reduce_sum | solution.py:175
  2.6 0.0 copy-start.5
  2.6 0.0 copy-start.6
  2.6 0.5 collective-permute-start.4
  3.2 2.6 %collective-permute-start.5 = (f32[2,1,4,256]{3,0,2,1:T(2,128)S(1)}, f32[2,1,4,256]{3,0,2,1:T(2,128)S(1)}, u32[]{:S(2)}, u32[]{:S(2)}) collective-permute-start(f32[2,1,4,256]{3,0,2,1:T(2,128)S(1)} %pad_maximum_fusion.3), channel_id=1, source_target_pairs={{0,2},{1,3},{2,0},{3,1},{4,6},{5,7},{6,4},{7,5},{8,10},{9,11},{10,... | collective-permute-start | bytes 24584 | tf_op jit(solution)/shard_map/ppermute | solution.py:43
  5.7 1.4 %collective-permute-start.6 = (f32[2,1,4,256]{3,0,2,1:T(2,128)S(1)}, f32[2,1,4,256]{3,0,2,1:T(2,128)S(1)}, u32[]{:S(2)}, u32[]{:S(2)}) collective-permute-start(f32[2,1,4,256]{3,0,2,1:T(2,128)S(1)} %pad_maximum_fusion.3), channel_id=1, source_target_pairs={{0,3},{1,0},{2,1},{3,2},{4,7},{5,4},{6,5},{7,6},{8,11},{9,8},{10,9... | collective-permute-start | bytes 24584 | tf_op jit(solution)/shard_map/ppermute | solution.py:43
  7.1 0.9 %constant_dynamic-update-slice_fusion.1 = bf16[1,4,64,512]{3,2,1,0:T(8,128)(2,1)S(1)} fusion(bf16[1,4,64,256]{3,2,1,0:T(8,128)(2,1)} %param.8), kind=kLoop, calls=%fused_computation.40 | loop fusion | bytes 262144
  8.0 0.9 %constant_dynamic-update-slice_fusion = bf16[1,4,64,512]{3,2,1,0:T(8,128)(2,1)S(1)} fusion(bf16[1,4,64,512]{3,2,1,0:T(8,128)(2,1)S(1)} %constant_dynamic-update-slice_fusion.1, bf16[1,4,64,256]{3,2,1,0:T(8,128)(2,1)} %param.9), kind=kLoop, calls=%fused_computation.39 | loop fusion | bytes 262144 | tf_op jit(solution)/shard_map/concatenate | solution.py:171
  9.0 3.5 %collective-permute-start = (bf16[1,2,64,512]{3,2,1,0:T(8,128)(2,1)S(1)}, bf16[1,2,64,512]{3,2,1,0:T(8,128)(2,1)S(1)}, u32[]{:S(2)}, u32[]{:S(2)}) collective-permute-start(bf16[1,2,64,512]{3,2,1,0:T(8,128)(2,1)S(1)} %get-tuple-element.22), channel_id=1, source_target_pairs={{0,4},{4,8},{8,12},{1,5},{5,9},{9,13},{2,6},{6,10},{10,14},{3,7},{... | collective-permute-start | bytes 393224 | tf_op jit(solution)/shard_map/ppermute | solution.py:23
  12.5 1.3 %collective-permute-start.1 = (bf16[1,2,64,512]{3,2,1,0:T(8,128)(2,1)S(1)}, bf16[1,2,64,512]{3,2,1,0:T(8,128)(2,1)S(1)}, u32[]{:S(2)}, u32[]{:S(2)}) collective-permute-start(bf16[1,2,64,512]{3,2,1,0:T(8,128)(2,1)S(1)} %get-tuple-element.23), channel_id=1, source_target_pairs={{4,0},{8,4},{12,8},{5,1},{9,5},{13,9},{6,2},{10,6},{14,10},{7,3},{... | collective-permute-start | bytes 393224 | tf_op jit(solution)/shard_map/ppermute | solution.py:26
  13.8 0.0 copy-done.4
  13.8 0.2 reshape.41
  14.0 0.2 copy.16
  14.2 0.2 reshape.46
  14.4 0.0 copy-done.5
  14.4 0.0 copy-done.6
  14.4 0.6 rsqrt_multiply_fusion.scale_ref
  15.0 0.0 collective-permute-done
  15.0 4.3 %collective-permute-done.1 = bf16[1,2,64,512]{3,2,1,0:T(8,128)(2,1)S(1)} collective-permute-done((bf16[1,2,64,512]{3,2,1,0:T(8,128)(2,1)S(1)}, bf16[1,2,64,512]{3,2,1,0:T(8,128)(2,1)S(1)}, u32[]{:S(2)}, u32[]{:S(2)}) %collective-permute-start.1) | collective-permute-done | bytes 131104 | tf_op jit(solution)/shard_map/ppermute | solution.py:26
  19.3 0.1 collective-permute-start.2
  19.4 1.7 %collective-permute-start.3 = (bf16[1,8,16,512]{3,2,1,0:T(8,128)(2,1)S(1)}, bf16[1,8,16,512]{3,2,1,0:T(8,128)(2,1)S(1)}, u32[]{:S(2)}, u32[]{:S(2)}) collective-permute-start(bf16[1,8,16,512]{3,2,1,0:T(8,128)(2,1)S(1)} %get-tuple-element.21), channel_id=1, source_target_pairs={{1,0},{2,1},{3,2},{0,3},{5,4},{6,5},{7,6},{4,7},{9,8},{10,9},{11,1... | collective-permute-start | bytes 393224 | tf_op jit(solution)/shard_map/ppermute | solution.py:26
  21.1 0.0 collective-permute-done.4
  21.1 0.0 collective-permute-done.5
  21.2 0.0 collective-permute-done.6
  21.2 0.6 fusion.22
  21.8 2.6 %collective-permute-done.2 = bf16[1,8,16,512]{3,2,1,0:T(8,128)(2,1)S(1)} collective-permute-done((bf16[1,8,16,512]{3,2,1,0:T(8,128)(2,1)S(1)}, bf16[1,8,16,512]{3,2,1,0:T(8,128)(2,1)S(1)}, u32[]{:S(2)}, u32[]{:S(2)}) %collective-permute-start.2) | collective-permute-done | bytes 131104 | tf_op jit(solution)/shard_map/ppermute | solution.py:23
  24.4 0.0 collective-permute-done.3
  24.4 0.1 fusion.18
  24.5 1.1 %fusion.23 = (bf16[1,8,128,256]{3,2,1,0:T(8,128)(2,1)}, bf16[1,8,128,256]{3,2,1,0:T(8,128)(2,1)}) fusion(bf16[1,8,128,512]{3,2,1,0:T(8,128)(2,1)S(1)} %fusion.18), kind=kLoop, calls=%fused_computation.41 | loop fusion | bytes 2097152 | tf_op jit(solution)/shard_map/slice | solution.py:173
  25.6 3.8 %shard_map.103 = bf16[1,4,64,2304]{3,2,1,0:T(8,128)(2,1)} custom-call(s32[1]{0:T(128)} %bitcast.first_ref, s32[16,12]{1,0:T(8,128)} %src_ref.3, s32[16,12]{1,0:T(8,128)} %start_ref.3, s32[16,12]{1,0:T(8,128)} %span_ref.3, s32[16,12]{1,0:T(8,128)} %basis_ref.3, f32[16,12]{1,0:T(8,128)} %rsqrt_multiply_fusion.scale_ref, ...), custom_call_target="tpu_custom_call" | custom-call | tf_op jit(solution)/shard_map/pallas_call | solution.py:143
  29.4 1.8 %convolution_bitcast_fusion = f32[9,256,256]{1,2,0:T(8,128)S(1)} fusion(bf16[4,64,256,1]{2,1,0,3:T(8,128)(2,1)S(1)} %reshape.46, bf16[4,8,9,8,256]{4,3,2,1,0:T(8,128)(2,1)} %bitcast.45), kind=kOutput, calls=%fused_computation.6 | convolution fusion | flops 301989888 | bytes 3670016 | tf_op jit(solution)/shard_map/brwq,brwo->qo/dot_general | solution.py:195
  31.2 0.9 %dynamic-slice_convert_fusion = bf16[9,256,128]{1,2,0:T(8,128)(2,1)} fusion(f32[9,256,256]{1,2,0:T(8,128)S(1)} %convolution_bitcast_fusion, s32[]{:T(128)S(6)} %select_n.53), kind=kLoop, calls=%fused_computation.14 | loop fusion | bytes 1179652 | tf_op jit(solution)/shard_map/convert_element_type | solution.py:71
  32.1 0.6 collective-permute-start.7
  32.8 0.0 copy-start.1
  32.8 2.0 %collective-permute-done.7 = bf16[9,256,128]{1,2,0:T(8,128)(2,1)} collective-permute-done((bf16[9,256,128]{1,2,0:T(8,128)(2,1)}, bf16[9,256,128]{1,2,0:T(8,128)(2,1)}, u32[]{:S(2)}, u32[]{:S(2)}) %collective-permute-start.7) | collective-permute-done | bytes 589856 | tf_op jit(solution)/shard_map/ppermute | solution.py:71
  34.7 1.2 %convert_add_fusion = f32[9,256,128]{1,2,0:T(8,128)S(1)} fusion(bf16[9,256,128]{1,2,0:T(8,128)(2,1)} %collective-permute-done.7, f32[9,256,256]{1,2,0:T(8,128)S(1)} %convolution_bitcast_fusion, s32[]{:T(128)S(6)} %select_n.52), kind=kLoop, calls=%fused_computation.13 | loop fusion | flops 589824 | bytes 2949124 | tf_op jit(solution)/shard_map/add | solution.py:71
  35.9 0.0 copy-start.2
  35.9 1.0 %copy-done.2 = f32[9,256,128]{1,2,0:T(8,128)} copy-done((f32[9,256,128]{1,2,0:T(8,128)}, f32[9,256,128]{1,2,0:T(8,128)S(1)}, u32[]{:S(2)}) %copy-start.2) | copy-done | bytes 1179672
  36.9 0.7 %dynamic-slice_convert_fusion.1 = bf16[9,256,64]{1,2,0:T(8,128)(2,1)} fusion(f32[9,256,128]{1,2,0:T(8,128)S(1)} %convert_add_fusion, s32[]{:T(128)S(6)} %select_n.57), kind=kLoop, calls=%fused_computation.22 | loop fusion | bytes 589828 | tf_op jit(solution)/shard_map/convert_element_type | solution.py:78
  37.7 0.9 %collective-permute-start.8 = (bf16[9,256,64]{1,2,0:T(8,128)(2,1)}, bf16[9,256,64]{1,2,0:T(8,128)(2,1)}, u32[]{:S(2)}, u32[]{:S(2)}) collective-permute-start(bf16[9,256,64]{1,2,0:T(8,128)(2,1)} %dynamic-slice_convert_fusion.1), channel_id=1, source_target_pairs={{0,2},{1,3},{2,0},{3,1},{4,6},{5,7},{6,4},{7,5},{8,10},{9,11},{10,... | collective-permute-start | bytes 884744 | tf_op jit(solution)/shard_map/ppermute | solution.py:78
  38.6 0.0 copy-done.1
  38.6 0.0 copy-start
  38.6 0.7 %copy.18 = bf16[9,256,256]{1,2,0:T(8,128)(2,1)S(1)} copy(bf16[9,256,256]{2,1,0:T(8,128)(2,1)S(1)} %copy-done.1) | data formatting | bytes 2359296 | tf_op args[2]
  39.4 0.5 copy-done
  39.9 0.0 copy-start.3
  39.9 1.2 %fusion.11 = f32[1,4,64,256]{3,2,1,0:T(8,128)} fusion(bf16[2304,256,1]{1,0,2:T(8,128)(2,1)S(1)} %bitcast.46, bf16[1,4,64,2304]{3,2,1,0:T(8,128)(2,1)S(1)} %copy-done), kind=kOutput, calls=%fused_computation.15 | convolution fusion | flops 301989888 | bytes 2621440 | tf_op jit(solution)/shard_map/brwq,qo->brwo/dot_general | solution.py:186
  41.1 6.2 %collective-permute-done.8 = bf16[9,256,64]{1,2,0:T(8,128)(2,1)} collective-permute-done((bf16[9,256,64]{1,2,0:T(8,128)(2,1)}, bf16[9,256,64]{1,2,0:T(8,128)(2,1)}, u32[]{:S(2)}, u32[]{:S(2)}) %collective-permute-start.8) | collective-permute-done | bytes 294944 | tf_op jit(solution)/shard_map/ppermute | solution.py:78
  47.3 0.0 copy-done.3
  47.3 1.0 %convert_add_fusion.1 = f32[9,256,64]{1,2,0:T(8,128)S(1)} fusion(bf16[9,256,64]{1,2,0:T(8,128)(2,1)} %collective-permute-done.8, f32[9,256,128]{1,2,0:T(8,128)S(1)} %copy-done.3, s32[]{:T(128)S(6)} %select_n.55), kind=kLoop, calls=%fused_computation.21 | loop fusion | flops 294912 | bytes 1474564 | tf_op jit(solution)/shard_map/add | solution.py:79
  48.3 0.2 dynamic-slice_convert_fusion.4
  48.5 2.6 %collective-permute-start.10 = (bf16[9,64,64]{1,2,0:T(8,128)(2,1)S(1)}, bf16[9,64,64]{1,2,0:T(8,128)(2,1)S(1)}, u32[]{:S(2)}, u32[]{:S(2)}) collective-permute-start(bf16[9,64,64]{1,2,0:T(8,128)(2,1)S(1)} %get-tuple-element.19), channel_id=1, source_target_pairs={{0,8},{4,12},{8,0},{12,4},{1,9},{5,13},{9,1},{13,5},{2,10},{6,14},... | collective-permute-start | bytes 221192 | tf_op jit(solution)/shard_map/ppermute | solution.py:55
  51.2 1.4 %collective-permute-start.11 = (bf16[9,64,64]{1,2,0:T(8,128)(2,1)S(1)}, bf16[9,64,64]{1,2,0:T(8,128)(2,1)S(1)}, u32[]{:S(2)}, u32[]{:S(2)}) collective-permute-start(bf16[9,64,64]{1,2,0:T(8,128)(2,1)S(1)} %get-tuple-element.18), channel_id=1, source_target_pairs={{0,12},{4,0},{8,4},{12,8},{1,13},{5,1},{9,5},{13,9},{2,14},{6,2},{... | collective-permute-start | bytes 221192 | tf_op jit(solution)/shard_map/ppermute | solution.py:55
  52.5 0.7 collective-permute-start.9
  53.2 10.8 %shard_map.104 = bf16[1,4,64,2304]{3,2,1,0:T(8,128)(2,1)} custom-call(s32[1]{0:T(128)} %bitcast.first_ref, s32[16,12]{1,0:T(8,128)} %src_ref.3, s32[16,12]{1,0:T(8,128)} %start_ref.3, s32[16,12]{1,0:T(8,128)} %span_ref.3, s32[16,12]{1,0:T(8,128)} %basis_ref.3, f32[16,12]{1,0:T(8,128)} %rsqrt_multiply_fusion.scale_ref, ...), custom_call_target="tpu_custom_call" | custom-call | tf_op jit(solution)/shard_map/pallas_call | solution.py:143
  64.0 2.5 %fusion.14 = f32[1,4,64,256]{3,2,1,0:T(8,128)} fusion(bf16[2304,256,1]{1,0,2:T(8,128)(2,1)S(1)} %bitcast.47, bf16[1,4,64,2304]{3,2,1,0:T(8,128)(2,1)} %shard_map.104), kind=kOutput, calls=%fused_computation.16 | convolution fusion | flops 301989888 | bytes 2621440 | tf_op jit(solution)/shard_map/bpwq,qc->bpwc/dot_general | solution.py:209
  66.5 0.0 collective-permute-done.10
  66.5 0.0 collective-permute-done.11
  66.5 0.0 collective-permute-done.9
  66.5 0.2 add_multiply_fusion
  66.6 0.9 %copy.19 = f32[9,64,64]{2,1,0:T(8,128)} copy(f32[9,64,64]{1,2,0:T(8,128)S(1)} %add_multiply_fusion) | data formatting | bytes 294912
  (6 shorter events, 0.1 us)
Async XLA Ops:
  0.6 13.1 %copy-start.4 = (bf16[1,4,64,256]{3,2,1,0:T(8,128)(2,1)S(1)}, bf16[1,4,64,256]{3,2,1,0:T(8,128)(2,1)}, u32[]{:S(2)}) copy-start(bf16[1,4,64,256]{3,2,1,0:T(8,128)(2,1)} %param.9) | copy-start | bytes 393220
  2.6 11.8 %copy-start.5 = (s32[16,12]{1,0:T(8,128)S(1)}, s32[16,12]{1,0:T(8,128)}, u32[]{:S(2)}) copy-start(s32[16,12]{1,0:T(8,128)} %span_ref.3) | copy-start | bytes 2308
  2.6 11.8 %copy-start.6 = (f32[16,12]{1,0:T(8,128)S(1)}, f32[16,12]{1,0:T(8,128)}, u32[]{:S(2)}) copy-start(f32[16,12]{1,0:T(8,128)} %param.15) | copy-start | bytes 2308
  2.6 18.5 %collective-permute-start.4 = (f32[2,1,4,256]{3,0,2,1:T(2,128)S(1)}, f32[2,1,4,256]{3,0,2,1:T(2,128)S(1)}, u32[]{:S(2)}, u32[]{:S(2)}) collective-permute-start(f32[2,1,4,256]{3,0,2,1:T(2,128)S(1)} %pad_maximum_fusion.3), channel_id=1, source_target_pairs={{0,1},{1,2},{2,3},{3,0},{4,5},{5,6},{6,7},{7,4},{8,9},{9,10},{10,1... | collective-permute-start | bytes 24584 | tf_op jit(solution)/shard_map/ppermute | solution.py:43
  3.2 18.0 %collective-permute-start.5 = (f32[2,1,4,256]{3,0,2,1:T(2,128)S(1)}, f32[2,1,4,256]{3,0,2,1:T(2,128)S(1)}, u32[]{:S(2)}, u32[]{:S(2)}) collective-permute-start(f32[2,1,4,256]{3,0,2,1:T(2,128)S(1)} %pad_maximum_fusion.3), channel_id=1, source_target_pairs={{0,2},{1,3},{2,0},{3,1},{4,6},{5,7},{6,4},{7,5},{8,10},{9,11},{10,... | collective-permute-start | bytes 24584 | tf_op jit(solution)/shard_map/ppermute | solution.py:43
  5.7 15.4 %collective-permute-start.6 = (f32[2,1,4,256]{3,0,2,1:T(2,128)S(1)}, f32[2,1,4,256]{3,0,2,1:T(2,128)S(1)}, u32[]{:S(2)}, u32[]{:S(2)}) collective-permute-start(f32[2,1,4,256]{3,0,2,1:T(2,128)S(1)} %pad_maximum_fusion.3), channel_id=1, source_target_pairs={{0,3},{1,0},{2,1},{3,2},{4,7},{5,4},{6,5},{7,6},{8,11},{9,8},{10,9... | collective-permute-start | bytes 24584 | tf_op jit(solution)/shard_map/ppermute | solution.py:43
  9.0 6.0 %collective-permute-start = (bf16[1,2,64,512]{3,2,1,0:T(8,128)(2,1)S(1)}, bf16[1,2,64,512]{3,2,1,0:T(8,128)(2,1)S(1)}, u32[]{:S(2)}, u32[]{:S(2)}) collective-permute-start(bf16[1,2,64,512]{3,2,1,0:T(8,128)(2,1)S(1)} %get-tuple-element.22), channel_id=1, source_target_pairs={{0,4},{4,8},{8,12},{1,5},{5,9},{9,13},{2,6},{6,10},{10,14},{3,7},{... | collective-permute-start | bytes 393224 | tf_op jit(solution)/shard_map/ppermute | solution.py:23
  12.5 6.9 %collective-permute-start.1 = (bf16[1,2,64,512]{3,2,1,0:T(8,128)(2,1)S(1)}, bf16[1,2,64,512]{3,2,1,0:T(8,128)(2,1)S(1)}, u32[]{:S(2)}, u32[]{:S(2)}) collective-permute-start(bf16[1,2,64,512]{3,2,1,0:T(8,128)(2,1)S(1)} %get-tuple-element.23), channel_id=1, source_target_pairs={{4,0},{8,4},{12,8},{5,1},{9,5},{13,9},{6,2},{10,6},{14,10},{7,3},{... | collective-permute-start | bytes 393224 | tf_op jit(solution)/shard_map/ppermute | solution.py:26
  19.3 5.0 %collective-permute-start.2 = (bf16[1,8,16,512]{3,2,1,0:T(8,128)(2,1)S(1)}, bf16[1,8,16,512]{3,2,1,0:T(8,128)(2,1)S(1)}, u32[]{:S(2)}, u32[]{:S(2)}) collective-permute-start(bf16[1,8,16,512]{3,2,1,0:T(8,128)(2,1)S(1)} %get-tuple-element.20), channel_id=1, source_target_pairs={{0,1},{1,2},{2,3},{3,0},{4,5},{5,6},{6,7},{7,4},{8,9},{9,10},{10,1... | collective-permute-start | bytes 393224 | tf_op jit(solution)/shard_map/ppermute | solution.py:23
  19.4 5.0 %collective-permute-start.3 = (bf16[1,8,16,512]{3,2,1,0:T(8,128)(2,1)S(1)}, bf16[1,8,16,512]{3,2,1,0:T(8,128)(2,1)S(1)}, u32[]{:S(2)}, u32[]{:S(2)}) collective-permute-start(bf16[1,8,16,512]{3,2,1,0:T(8,128)(2,1)S(1)} %get-tuple-element.21), channel_id=1, source_target_pairs={{1,0},{2,1},{3,2},{0,3},{5,4},{6,5},{7,6},{4,7},{9,8},{10,9},{11,1... | collective-permute-start | bytes 393224 | tf_op jit(solution)/shard_map/ppermute | solution.py:26
  32.1 2.6 %collective-permute-start.7 = (bf16[9,256,128]{1,2,0:T(8,128)(2,1)}, bf16[9,256,128]{1,2,0:T(8,128)(2,1)}, u32[]{:S(2)}, u32[]{:S(2)}) collective-permute-start(bf16[9,256,128]{1,2,0:T(8,128)(2,1)} %dynamic-slice_convert_fusion), channel_id=1, source_target_pairs={{0,1},{1,0},{2,3},{3,2},{4,5},{5,4},{6,7},{7,6},{8,9},{9,8},{10,11... | collective-permute-start | bytes 1769480 | tf_op jit(solution)/shard_map/ppermute | solution.py:71
  32.8 5.9 %copy-start.1 = (bf16[9,256,256]{2,1,0:T(8,128)(2,1)S(1)}, bf16[9,256,256]{2,1,0:T(8,128)(2,1)}, u32[]{:S(2)}) copy-start(bf16[9,256,256]{2,1,0:T(8,128)(2,1)} %param.10) | copy-start | bytes 3538948
  35.9 1.0 %copy-start.2 = (f32[9,256,128]{1,2,0:T(8,128)}, f32[9,256,128]{1,2,0:T(8,128)S(1)}, u32[]{:S(2)}) copy-start(f32[9,256,128]{1,2,0:T(8,128)S(1)} %convert_add_fusion) | copy-start | bytes 3538948
  37.7 9.6 %collective-permute-start.8 = (bf16[9,256,64]{1,2,0:T(8,128)(2,1)}, bf16[9,256,64]{1,2,0:T(8,128)(2,1)}, u32[]{:S(2)}, u32[]{:S(2)}) collective-permute-start(bf16[9,256,64]{1,2,0:T(8,128)(2,1)} %dynamic-slice_convert_fusion.1), channel_id=1, source_target_pairs={{0,2},{1,3},{2,0},{3,1},{4,6},{5,7},{6,4},{7,5},{8,10},{9,11},{10,... | collective-permute-start | bytes 884744 | tf_op jit(solution)/shard_map/ppermute | solution.py:78
  38.6 1.3 %copy-start = (bf16[1,4,64,2304]{3,2,1,0:T(8,128)(2,1)S(1)}, bf16[1,4,64,2304]{3,2,1,0:T(8,128)(2,1)}, u32[]{:S(2)}) copy-start(bf16[1,4,64,2304]{3,2,1,0:T(8,128)(2,1)} %shard_map.103) | copy-start | bytes 3538948
  39.9 7.4 %copy-start.3 = (f32[9,256,128]{1,2,0:T(8,128)S(1)}, f32[9,256,128]{1,2,0:T(8,128)}, u32[]{:S(2)}) copy-start(f32[9,256,128]{1,2,0:T(8,128)} %copy-done.2) | copy-start | bytes 3538948
  48.5 17.9 %collective-permute-start.10 = (bf16[9,64,64]{1,2,0:T(8,128)(2,1)S(1)}, bf16[9,64,64]{1,2,0:T(8,128)(2,1)S(1)}, u32[]{:S(2)}, u32[]{:S(2)}) collective-permute-start(bf16[9,64,64]{1,2,0:T(8,128)(2,1)S(1)} %get-tuple-element.19), channel_id=1, source_target_pairs={{0,8},{4,12},{8,0},{12,4},{1,9},{5,13},{9,1},{13,5},{2,10},{6,14},... | collective-permute-start | bytes 221192 | tf_op jit(solution)/shard_map/ppermute | solution.py:55
  51.2 15.3 %collective-permute-start.11 = (bf16[9,64,64]{1,2,0:T(8,128)(2,1)S(1)}, bf16[9,64,64]{1,2,0:T(8,128)(2,1)S(1)}, u32[]{:S(2)}, u32[]{:S(2)}) collective-permute-start(bf16[9,64,64]{1,2,0:T(8,128)(2,1)S(1)} %get-tuple-element.18), channel_id=1, source_target_pairs={{0,12},{4,0},{8,4},{12,8},{1,13},{5,1},{9,5},{13,9},{2,14},{6,2},{... | collective-permute-start | bytes 221192 | tf_op jit(solution)/shard_map/ppermute | solution.py:55
  52.5 13.9 %collective-permute-start.9 = (bf16[9,64,64]{1,2,0:T(8,128)(2,1)S(1)}, bf16[9,64,64]{1,2,0:T(8,128)(2,1)S(1)}, u32[]{:S(2)}, u32[]{:S(2)}) collective-permute-start(bf16[9,64,64]{1,2,0:T(8,128)(2,1)S(1)} %get-tuple-element.17), channel_id=1, source_target_pairs={{0,4},{4,8},{8,12},{12,0},{1,5},{5,9},{9,13},{13,1},{2,6},{6,10},{... | collective-permute-start | bytes 221192 | tf_op jit(solution)/shard_map/ppermute | solution.py:55

commit v11 on v9

--- a/solution.py
+++ b/solution.py
@@ -59,9 +59,9 @@
 
 def filter_kernel(
     first_ref, src_ref, start_ref, span_ref, basis_ref, scale_ref, field_ref, total_ref,
-    out_ref, acc_ref, *, slots, height, lon_count, lon_total, backward,
+    out_ref, acc_ref, *, slots, height, lon_count, lon_total, backward, row_offset,
 ):
-    r = pl.program_id(1)
+    r = pl.program_id(1) + row_offset
     first_row = first_ref[0]
     padded = field_ref.shape[2]
     channels = field_ref.shape[3]
@@ -105,7 +105,9 @@
         out_ref[0, 0, :, k * channels:(k + 1) * channels] = acc_ref[k].astype(jnp.bfloat16)
 
 
-def run_filter(first, tables, field, totals, row_count, lon_count, lon_total, backward):
+def run_filter(
+    first, tables, field, totals, row_count, lon_count, lon_total, backward, row_offset=0
+):
     members, window, padded, channels = field.shape
     height, slots = tables[0].shape
     smem = pl.BlockSpec(memory_space=pltpu.SMEM)
@@ -116,6 +118,7 @@
         lon_count=lon_count,
         lon_total=lon_total,
         backward=backward,
+        row_offset=row_offset,
     )
     return pl.pallas_call(
         kernel,
@@ -166,16 +169,26 @@
         "brwq,brwo->qo", flattened, cotangent, preferred_element_type=jnp.float32
     )
     partial_value = partial_value.reshape(BASIS, channels, channels)
+    w_back = jnp.transpose(weight, (0, 2, 1)).reshape(BASIS * channels, channels)
+
+    def backward_rows(field, field_totals, begin, count):
+        back_filtered = run_filter(
+            first, tables, field, field_totals, count, lon_count, lon_total, True, begin
+        )
+        return jnp.einsum(
+            "bpwq,qc->bpwc", back_filtered, w_back, preferred_element_type=jnp.float32
+        )
+
+    early_rows = row_count // 2
+    early_wide, early_totals, partial_value = lax.optimization_barrier(
+        (grad_wide, grad_totals, partial_value)
+    )
+    early_input = backward_rows(early_wide, early_totals, 0, early_rows)
     reduced = ring_scatter(partial_value, "lon", 2)
     grad_wide, grad_totals, reduced = lax.optimization_barrier((grad_wide, grad_totals, reduced))
     reduced = ring_scatter(reduced, "lat", 1)
-    back_filtered = run_filter(
-        first, tables, grad_wide, grad_totals, row_count, lon_count, lon_total, True
-    )
-    w_back = jnp.transpose(weight, (0, 2, 1)).reshape(BASIS * channels, channels)
-    grad_input = jnp.einsum(
-        "bpwq,qc->bpwc", back_filtered, w_back, preferred_element_type=jnp.float32
-    )
+    late_input = backward_rows(grad_wide, grad_totals, early_rows, row_count - early_rows)
+    grad_input = jnp.concatenate([early_input, late_input], axis=1)
     grad_weight = reduced / jnp.sqrt(jnp.float32(members * height * lon_total))
     return (response, grad_input, grad_weight)
 

time: 68 us -> 73.8 us (1.085)
  waiting for transfers between devices: 14.5 us -> 6.85 us
  local copies, waits for them, and re-layouts: 8.08 us -> 15.1 us
  other arithmetic: 4.05 us -> 6.98 us
  Pallas kernels: 14.6 us -> 16.2 us
  matrix products: 6.69 us -> 7.81 us
    ppermute x6, waiting for transfers between devices: 7.07 us -> 0.22 us  [ring_scatter(): sent = lax.ppermute(piece.astype(jnp.bfloat16), axis, pairs)]
    ppermute x0 -> x3, local copies, waits for them, and re-layouts: none -> 6.1 us  [ring_scatter(): sent = lax.ppermute(piece.astype(jnp.bfloat16), axis, pairs)]
    pallas_call x2 -> x3, Pallas kernels: 14.6 us -> 16.2 us  [run_filter(): pl.pallas_call(kernel, grid=(members, row_count), in_specs=[smem] * 6 + [...]
    div x1, other arithmetic: 0.15 us -> 1.75 us  [on_device(): grad_weight = reduced / jnp.sqrt(jnp.float32(members * height * lon_total))]
    unnamed x13 -> x14, local copies, waits for them, and re-layouts: 4.28 us -> 2.71 us
    optimization_barrier x0 -> x1, local copies, waits for them, and re-layouts: none -> 1.47 us  [on_device(): lax.optimization_barrier((grad_wide, grad_totals, partial_value))]
    dot_general x1 -> x2, matrix products: 2.45 us -> 3.56 us  [backward_rows(): jnp.einsum('bpwq,qc->bpwc', back_filtered, w_back, preferred_element_type...]
    convert_element_type x2, local copies, waits for them, and re-layouts: 1.14 us -> 2.13 us  [ring_scatter(): sent = lax.ppermute(piece.astype(jnp.bfloat16), axis, pairs)]
  transfers between devices with their start and end apart: 13 -> 13, of which waited for: 6 -> 3; matrix products, arithmetic and copies ran while one was open for 16% -> 20% of each run, Pallas kernels for 16% -> 17%
where the time goes in v11:
time: 73.8 us; the launch traced here: 73 us
  starting transfers between devices  19.1 us (26%)
  Pallas kernels  16.2 us (22%)
  local copies, waits for them, and re-layouts  15.1 us (20%)
  matrix products  7.81 us (11%)
  other arithmetic  6.98 us (9%)
  waiting for transfers between devices  6.85 us (9%)
  between operations  0.95 us (1%)
    pallas_call x3, Pallas kernels, run_filter(): pl.pallas_call(kernel, grid=(members, row_count), in_specs=[smem] * 6 + [...  16.2 us
    ppermute x6, starting transfers between devices, ring_scatter(): sent = lax.ppermute(piece.astype(jnp.bfloat16), axis, pairs)  8.05 us
    ppermute x3, local copies, waits for them, and re-layouts, ring_scatter(): sent = lax.ppermute(piece.astype(jnp.bfloat16), axis, pairs)  6.1 us
    ppermute x3, starting transfers between devices, ring_sum(): total = total + lax.ppermute(value, axis, pairs)  4.46 us
    ppermute x2, waiting for transfers between devices, with_halo(): lax.ppermute(lax.slice_in_dim(block, 0, width, axis=dim), axis, backward)  4.05 us
    dot_general x2, matrix products, backward_rows(): jnp.einsum('bpwq,qc->bpwc', back_filtered, w_back, preferred_element_type...  3.56 us
    ppermute x2, starting transfers between devices, with_halo(): lax.ppermute(lax.slice_in_dim(block, block.shape[dim] - width, None, axis...  3.54 us
    ppermute x2, starting transfers between devices, with_halo(): lax.ppermute(lax.slice_in_dim(block, 0, width, axis=dim), axis, backward)  3.02 us
  transfers between devices with their start and end apart: 13, of which 3 were waited for; matrix products, arithmetic and copies ran while one was open for 20% of the time, Pallas kernels for 17%

profile of v11, /device:TPU:0, one launch (start us, length us, event | category | flops | bytes accessed | tf_op | source)
XLA Modules:
  0.0 73.0 jit_solution(15758730280217143807)
XLA Ops:
  0.6 0.0 copy-start.1
  0.6 1.0 %convert_reduce_fusion = f32[4,256]{1,0:T(4,128)S(1)} fusion(bf16[1,4,64,256]{3,2,1,0:T(8,128)(2,1)} %param.9), kind=kLoop, calls=%fused_computation.29 | loop fusion | flops 130048 | bytes 135168 | tf_op jit(solution)/shard_map/reduce_sum | solution.py:155
  1.7 0.9 %convert_reduce_fusion.1 = f32[4,256]{1,0:T(4,128)S(1)} fusion(bf16[1,4,64,256]{3,2,1,0:T(8,128)(2,1)} %param.8), kind=kLoop, calls=%fused_computation.30 | loop fusion | flops 130048 | bytes 135168 | tf_op jit(solution)/shard_map/reduce_sum | solution.py:155
  2.7 0.5 collective-permute-start.4
  3.2 2.6 %collective-permute-start.5 = (f32[2,1,4,256]{3,0,2,1:T(2,128)S(1)}, f32[2,1,4,256]{3,0,2,1:T(2,128)S(1)}, u32[]{:S(2)}, u32[]{:S(2)}) collective-permute-start(f32[2,1,4,256]{3,0,2,1:T(2,128)S(1)} %pad_maximum_fusion.4), channel_id=1, source_target_pairs={{0,2},{1,3},{2,0},{3,1},{4,6},{5,7},{6,4},{7,5},{8,10},{9,11},{10,... | collective-permute-start | bytes 24584 | tf_op jit(solution)/shard_map/ppermute | solution.py:43
  5.7 1.4 %collective-permute-start.6 = (f32[2,1,4,256]{3,0,2,1:T(2,128)S(1)}, f32[2,1,4,256]{3,0,2,1:T(2,128)S(1)}, u32[]{:S(2)}, u32[]{:S(2)}) collective-permute-start(f32[2,1,4,256]{3,0,2,1:T(2,128)S(1)} %pad_maximum_fusion.4), channel_id=1, source_target_pairs={{0,3},{1,0},{2,1},{3,2},{4,7},{5,4},{6,5},{7,6},{8,11},{9,8},{10,9... | collective-permute-start | bytes 24584 | tf_op jit(solution)/shard_map/ppermute | solution.py:43
  7.1 0.9 %constant_dynamic-update-slice_fusion.1 = bf16[1,4,64,512]{3,2,1,0:T(8,128)(2,1)S(1)} fusion(bf16[1,4,64,256]{3,2,1,0:T(8,128)(2,1)} %param.8), kind=kLoop, calls=%fused_computation.43 | loop fusion | bytes 262144
  8.0 0.9 %constant_dynamic-update-slice_fusion = bf16[1,4,64,512]{3,2,1,0:T(8,128)(2,1)S(1)} fusion(bf16[1,4,64,512]{3,2,1,0:T(8,128)(2,1)S(1)} %constant_dynamic-update-slice_fusion.1, bf16[1,4,64,256]{3,2,1,0:T(8,128)(2,1)} %param.9), kind=kLoop, calls=%fused_computation.42 | loop fusion | bytes 262144 | tf_op jit(solution)/shard_map/concatenate | solution.py:151
  9.0 3.5 %collective-permute-start = (bf16[1,2,64,512]{3,2,1,0:T(8,128)(2,1)S(1)}, bf16[1,2,64,512]{3,2,1,0:T(8,128)(2,1)S(1)}, u32[]{:S(2)}, u32[]{:S(2)}) collective-permute-start(bf16[1,2,64,512]{3,2,1,0:T(8,128)(2,1)S(1)} %get-tuple-element.25), channel_id=1, source_target_pairs={{0,4},{4,8},{8,12},{1,5},{5,9},{9,13},{2,6},{6,10},{10,14},{3,7},{... | collective-permute-start | bytes 393224 | tf_op jit(solution)/shard_map/ppermute | solution.py:23
  12.5 1.3 %collective-permute-start.1 = (bf16[1,2,64,512]{3,2,1,0:T(8,128)(2,1)S(1)}, bf16[1,2,64,512]{3,2,1,0:T(8,128)(2,1)S(1)}, u32[]{:S(2)}, u32[]{:S(2)}) collective-permute-start(bf16[1,2,64,512]{3,2,1,0:T(8,128)(2,1)S(1)} %get-tuple-element.26), channel_id=1, source_target_pairs={{4,0},{8,4},{12,8},{5,1},{9,5},{13,9},{6,2},{10,6},{14,10},{7,3},{... | collective-permute-start | bytes 393224 | tf_op jit(solution)/shard_map/ppermute | solution.py:26
  13.9 0.0 copy-done.1
  13.9 0.0 copy-start.4
  13.9 0.0 copy-start.5
  13.9 0.7 copy.31
  14.7 0.0 copy-done.4
  14.7 0.0 copy-done.5
  14.7 0.6 rsqrt_multiply_fusion.scale_ref
  15.3 0.0 collective-permute-done
  15.3 4.0 %collective-permute-done.1 = bf16[1,2,64,512]{3,2,1,0:T(8,128)(2,1)S(1)} collective-permute-done((bf16[1,2,64,512]{3,2,1,0:T(8,128)(2,1)S(1)}, bf16[1,2,64,512]{3,2,1,0:T(8,128)(2,1)S(1)}, u32[]{:S(2)}, u32[]{:S(2)}) %collective-permute-start.1) | collective-permute-done | bytes 131104 | tf_op jit(solution)/shard_map/ppermute | solution.py:26
  19.4 0.1 collective-permute-start.2
  19.4 1.7 %collective-permute-start.3 = (bf16[1,8,16,512]{3,2,1,0:T(8,128)(2,1)S(1)}, bf16[1,8,16,512]{3,2,1,0:T(8,128)(2,1)S(1)}, u32[]{:S(2)}, u32[]{:S(2)}) collective-permute-start(bf16[1,8,16,512]{3,2,1,0:T(8,128)(2,1)S(1)} %get-tuple-element.24), channel_id=1, source_target_pairs={{1,0},{2,1},{3,2},{0,3},{5,4},{6,5},{7,6},{4,7},{9,8},{10,9},{11,1... | collective-permute-start | bytes 393224 | tf_op jit(solution)/shard_map/ppermute | solution.py:26
  21.2 0.0 collective-permute-done.4
  21.2 0.0 collective-permute-done.5
  21.2 0.0 collective-permute-done.6
  21.2 0.6 fusion.20
  21.8 2.6 %collective-permute-done.2 = bf16[1,8,16,512]{3,2,1,0:T(8,128)(2,1)S(1)} collective-permute-done((bf16[1,8,16,512]{3,2,1,0:T(8,128)(2,1)S(1)}, bf16[1,8,16,512]{3,2,1,0:T(8,128)(2,1)S(1)}, u32[]{:S(2)}, u32[]{:S(2)}) %collective-permute-start.2) | collective-permute-done | bytes 131104 | tf_op jit(solution)/shard_map/ppermute | solution.py:23
  24.4 0.0 collective-permute-done.3
  24.4 0.1 fusion.13
  24.5 1.1 %fusion.21 = (bf16[1,8,128,256]{3,2,1,0:T(8,128)(2,1)}, bf16[1,8,128,256]{3,2,1,0:T(8,128)(2,1)}) fusion(bf16[1,8,128,512]{3,2,1,0:T(8,128)(2,1)S(1)} %fusion.13), kind=kLoop, calls=%fused_computation.44 | loop fusion | bytes 2097152 | tf_op jit(solution)/shard_map/slice | solution.py:153
  25.6 3.8 %shard_map.103 = bf16[1,4,64,2304]{3,2,1,0:T(8,128)(2,1)} custom-call(s32[1]{0:T(128)} %bitcast.first_ref, s32[16,12]{1,0:T(8,128)} %src_ref.5, s32[16,12]{1,0:T(8,128)} %start_ref.5, s32[16,12]{1,0:T(8,128)} %span_ref.5, s32[16,12]{1,0:T(8,128)} %basis_ref.5, f32[16,12]{1,0:T(8,128)} %rsqrt_multiply_fusion.scale_ref, ...), custom_call_target="tpu_custom_call" | custom-call | tf_op jit(solution)/shard_map/pallas_call | solution.py:123
  29.4 1.8 %convolution_bitcast_fusion = f32[9,256,256]{2,1,0:T(8,128)S(1)} fusion(bf16[4,8,9,8,256]{4,3,2,1,0:T(8,128)(2,1)} %bitcast.54, bf16[1,4,64,256]{3,2,1,0:T(8,128)(2,1)} %param.9), kind=kOutput, calls=%fused_computation.6 | convolution fusion | flops 301989888 | bytes 3670016 | tf_op jit(solution)/shard_map/brwq,brwo->qo/dot_general | solution.py:168
  31.2 1.5 %copy.32 = bf16[9,256,256]{1,2,0:T(8,128)(2,1)} copy(f32[9,256,256]{2,1,0:T(8,128)S(1)} %convolution_bitcast_fusion) | data formatting | bytes 3538944 | tf_op jit(solution)/shard_map/optimization_barrier | solution.py:183
  32.6 2.1 %dynamic-slice_convert_fusion.2 = (bf16[9,256,64]{1,2,0:T(8,128)(2,1)}, bf16[9,256,64]{1,2,0:T(8,128)(2,1)}, bf16[9,256,64]{1,2,0:T(8,128)(2,1)}) fusion(bf16[9,256,256]{1,2,0:T(8,128)(2,1)} %copy.32, s32[]{:T(128)S(6)} %select_n.53, s32[]{:T(128)S(6)} %select_n.57, s32[]{:T(128)S(6)} %select_n.55), kind=kLoop, calls=%fused_computation.23 | loop fusion | bytes 1769484 | tf_op jit(solution)/shard_map/convert_element_type | solution.py:55
  34.7 0.6 collective-permute-start.7
  35.3 0.9 %collective-permute-start.8 = (bf16[9,256,64]{1,2,0:T(8,128)(2,1)}, bf16[9,256,64]{1,2,0:T(8,128)(2,1)}, u32[]{:S(2)}, u32[]{:S(2)}) collective-permute-start(bf16[9,256,64]{1,2,0:T(8,128)(2,1)} %get-tuple-element.20), channel_id=1, source_target_pairs={{0,2},{1,3},{2,0},{3,1},{4,6},{5,7},{6,4},{7,5},{8,10},{9,11},{10,... | collective-permute-start | bytes 884744 | tf_op jit(solution)/shard_map/ppermute | solution.py:55
  36.2 0.4 collective-permute-start.9
  36.7 6.8 %shard_map.104 = bf16[1,2,64,2304]{3,2,1,0:T(8,128)(2,1)} custom-call(s32[1]{0:T(128)} %bitcast.first_ref, s32[16,12]{1,0:T(8,128)} %src_ref.5, s32[16,12]{1,0:T(8,128)} %start_ref.5, s32[16,12]{1,0:T(8,128)} %span_ref.5, s32[16,12]{1,0:T(8,128)} %basis_ref.5, f32[16,12]{1,0:T(8,128)} %rsqrt_multiply_fusion.scale_ref, ...), custom_call_target="tpu_custom_call" | custom-call | tf_op jit(solution)/shard_map/pallas_call | solution.py:123
  43.5 0.0 copy-start
  43.5 2.1 %convolution_bitcast_fusion.2 = f32[1,2,64,256]{3,2,1,0:T(8,128)} fusion(bf16[2304,256,1]{1,0,2:T(8,128)(2,1)S(1)} %bitcast.52, bf16[1,2,64,2304]{3,2,1,0:T(8,128)(2,1)} %shard_map.104), kind=kOutput, calls=%fused_computation.14 | convolution fusion | flops 150994944 | bytes 1900544 | tf_op jit(solution)/shard_map/bpwq,qc->bpwc/dot_general | solution.py:178
  45.6 0.0 copy-done
  45.6 2.5 %fusion.9 = f32[1,4,64,256]{3,2,1,0:T(8,128)} fusion(bf16[2304,256,1]{1,0,2:T(8,128)(2,1)} %bitcast.55, bf16[1,4,64,2304]{3,2,1,0:T(8,128)(2,1)S(1)} %copy-done), kind=kOutput, calls=%fused_computation.12 | convolution fusion | flops 301989888 | bytes 2621440 | tf_op jit(solution)/shard_map/brwq,qo->brwo/dot_general | solution.py:166
  48.1 0.0 collective-permute-done.7
  48.1 2.0 %copy.33 = bf16[9,256,64]{2,1,0:T(8,128)(2,1)} copy(bf16[9,256,64]{1,2,0:T(8,128)(2,1)} %collective-permute-done.7) | data formatting | bytes 589824 | tf_op jit(solution)/shard_map/ppermute | solution.py:55
  50.1 0.0 collective-permute-done.8
  50.1 2.0 %copy.35 = bf16[9,256,64]{2,1,0:T(8,128)(2,1)} copy(bf16[9,256,64]{1,2,0:T(8,128)(2,1)} %collective-permute-done.8) | data formatting | bytes 589824 | tf_op jit(solution)/shard_map/ppermute | solution.py:55
  52.1 0.0 collective-permute-done.9
  52.1 2.0 %copy.37 = bf16[9,256,64]{2,1,0:T(8,128)(2,1)} copy(bf16[9,256,64]{1,2,0:T(8,128)(2,1)} %collective-permute-done.9) | data formatting | bytes 589824 | tf_op jit(solution)/shard_map/ppermute | solution.py:55
  54.2 1.8 %convert_add_fusion = f32[9,256,64]{2,1,0:T(8,128)S(1)} fusion(bf16[9,256,64]{2,1,0:T(8,128)(2,1)} %copy.37, bf16[9,256,64]{2,1,0:T(8,128)(2,1)} %copy.35, bf16[9,256,64]{2,1,0:T(8,128)(2,1)} %copy.33, f32[9,256,256]{2,1,0:T(8,128)S(1)} %convolution_bitcast_fusion, s32[]{:T(128)S(6)} %select_n.51), kind=kLoop, calls=%fused_computation.11 | loop fusion | flops 884736 | bytes 2064388 | tf_op jit(solution)/shard_map/add | solution.py:56
  56.0 0.0 copy-start.2
  56.0 1.0 %copy-done.2 = f32[9,256,64]{2,1,0:T(8,128)} copy-done((f32[9,256,64]{2,1,0:T(8,128)}, f32[9,256,64]{2,1,0:T(8,128)S(1)}, u32[]{:S(2)}) %copy-start.2) | copy-done | bytes 589848
  57.0 0.1 dynamic-slice_convert_fusion.5
  57.1 0.9 %collective-permute-start.10 = (bf16[9,64,64]{2,1,0:T(8,128)(2,1)S(1)}, bf16[9,64,64]{2,1,0:T(8,128)(2,1)S(1)}, u32[]{:S(2)}, u32[]{:S(2)}) collective-permute-start(bf16[9,64,64]{2,1,0:T(8,128)(2,1)S(1)} %get-tuple-element.15), channel_id=1, source_target_pairs={{0,4},{4,8},{8,12},{12,0},{1,5},{5,9},{9,13},{13,1},{2,6},{6,10},{... | collective-permute-start | bytes 221192 | tf_op jit(solution)/shard_map/ppermute | solution.py:55
  58.0 2.3 %collective-permute-start.11 = (bf16[9,64,64]{2,1,0:T(8,128)(2,1)S(1)}, bf16[9,64,64]{2,1,0:T(8,128)(2,1)S(1)}, u32[]{:S(2)}, u32[]{:S(2)}) collective-permute-start(bf16[9,64,64]{2,1,0:T(8,128)(2,1)S(1)} %get-tuple-element.17), channel_id=1, source_target_pairs={{0,8},{4,12},{8,0},{12,4},{1,9},{5,13},{9,1},{13,5},{2,10},{6,14},... | collective-permute-start | bytes 221192 | tf_op jit(solution)/shard_map/ppermute | solution.py:55
  60.3 2.8 %collective-permute-start.12 = (bf16[9,64,64]{2,1,0:T(8,128)(2,1)S(1)}, bf16[9,64,64]{2,1,0:T(8,128)(2,1)S(1)}, u32[]{:S(2)}, u32[]{:S(2)}) collective-permute-start(bf16[9,64,64]{2,1,0:T(8,128)(2,1)S(1)} %get-tuple-element.16), channel_id=1, source_target_pairs={{0,12},{4,0},{8,4},{12,8},{1,13},{5,1},{9,5},{13,9},{2,14},{6,2},{... | collective-permute-start | bytes 221192 | tf_op jit(solution)/shard_map/ppermute | solution.py:55
  63.2 5.7 %shard_map.105 = bf16[1,2,64,2304]{3,2,1,0:T(8,128)(2,1)} custom-call(s32[1]{0:T(128)} %bitcast.first_ref, s32[16,12]{1,0:T(8,128)} %src_ref.5, s32[16,12]{1,0:T(8,128)} %start_ref.5, s32[16,12]{1,0:T(8,128)} %span_ref.5, s32[16,12]{1,0:T(8,128)} %basis_ref.5, f32[16,12]{1,0:T(8,128)} %rsqrt_multiply_fusion.scale_ref, ...), custom_call_target="tpu_custom_call" | custom-call | tf_op jit(solution)/shard_map/pallas_call | solution.py:123
  68.8 0.0 copy-start.3
  68.8 1.4 %convolution_bitcast_fusion.1 = f32[1,2,64,256]{3,2,1,0:T(8,128)S(1)} fusion(bf16[2304,256,1]{1,0,2:T(8,128)(2,1)S(1)} %bitcast.53, bf16[1,2,64,2304]{3,2,1,0:T(8,128)(2,1)} %shard_map.105), kind=kOutput, calls=%fused_computation.13 | convolution fusion | flops 150994944 | bytes 1900544 | tf_op jit(solution)/shard_map/bpwq,qc->bpwc/dot_general | solution.py:178
  70.3 0.0 copy-done.3
  70.3 0.7 pad_maximum_fusion
  71.0 0.0 collective-permute-done.10
  71.0 0.2 collective-permute-done.11
  71.2 0.0 collective-permute-done.12
  71.2 1.8 %add_multiply_fusion = f32[9,64,64]{2,1,0:T(8,128)} fusion(bf16[9,64,64]{2,1,0:T(8,128)(2,1)S(1)} %collective-permute-done.12, bf16[9,64,64]{2,1,0:T(8,128)(2,1)S(1)} %collective-permute-done.11, bf16[9,64,64]{2,1,0:T(8,128)(2,1)S(1)} %collective-permute-done.10, f32[9,256,64]{2,1,0:T(8,128)} %copy-done.2, s32[]{:T(128)S(6)} %select_n.58), kind=kLoop, calls=%fused_computation.24 | loop fusion | flops 258048 | bytes 516100 | tf_op jit(solution)/shard_map/div | solution.py:192
  (6 shorter events, 0.1 us)
Async XLA Ops:
  0.6 13.2 %copy-start.1 = (bf16[9,256,256]{2,1,0:T(8,128)(2,1)S(1)}, bf16[9,256,256]{2,1,0:T(8,128)(2,1)}, u32[]{:S(2)}) copy-start(bf16[9,256,256]{2,1,0:T(8,128)(2,1)} %param.10) | copy-start | bytes 3538948
  2.7 18.5 %collective-permute-start.4 = (f32[2,1,4,256]{3,0,2,1:T(2,128)S(1)}, f32[2,1,4,256]{3,0,2,1:T(2,128)S(1)}, u32[]{:S(2)}, u32[]{:S(2)}) collective-permute-start(f32[2,1,4,256]{3,0,2,1:T(2,128)S(1)} %pad_maximum_fusion.4), channel_id=1, source_target_pairs={{0,1},{1,2},{2,3},{3,0},{4,5},{5,6},{6,7},{7,4},{8,9},{9,10},{10,1... | collective-permute-start | bytes 24584 | tf_op jit(solution)/shard_map/ppermute | solution.py:43
  3.2 18.0 %collective-permute-start.5 = (f32[2,1,4,256]{3,0,2,1:T(2,128)S(1)}, f32[2,1,4,256]{3,0,2,1:T(2,128)S(1)}, u32[]{:S(2)}, u32[]{:S(2)}) collective-permute-start(f32[2,1,4,256]{3,0,2,1:T(2,128)S(1)} %pad_maximum_fusion.4), channel_id=1, source_target_pairs={{0,2},{1,3},{2,0},{3,1},{4,6},{5,7},{6,4},{7,5},{8,10},{9,11},{10,... | collective-permute-start | bytes 24584 | tf_op jit(solution)/shard_map/ppermute | solution.py:43
  5.7 15.4 %collective-permute-start.6 = (f32[2,1,4,256]{3,0,2,1:T(2,128)S(1)}, f32[2,1,4,256]{3,0,2,1:T(2,128)S(1)}, u32[]{:S(2)}, u32[]{:S(2)}) collective-permute-start(f32[2,1,4,256]{3,0,2,1:T(2,128)S(1)} %pad_maximum_fusion.4), channel_id=1, source_target_pairs={{0,3},{1,0},{2,1},{3,2},{4,7},{5,4},{6,5},{7,6},{8,11},{9,8},{10,9... | collective-permute-start | bytes 24584 | tf_op jit(solution)/shard_map/ppermute | solution.py:43
  9.0 6.3 %collective-permute-start = (bf16[1,2,64,512]{3,2,1,0:T(8,128)(2,1)S(1)}, bf16[1,2,64,512]{3,2,1,0:T(8,128)(2,1)S(1)}, u32[]{:S(2)}, u32[]{:S(2)}) collective-permute-start(bf16[1,2,64,512]{3,2,1,0:T(8,128)(2,1)S(1)} %get-tuple-element.25), channel_id=1, source_target_pairs={{0,4},{4,8},{8,12},{1,5},{5,9},{9,13},{2,6},{6,10},{10,14},{3,7},{... | collective-permute-start | bytes 393224 | tf_op jit(solution)/shard_map/ppermute | solution.py:23
  12.5 6.9 %collective-permute-start.1 = (bf16[1,2,64,512]{3,2,1,0:T(8,128)(2,1)S(1)}, bf16[1,2,64,512]{3,2,1,0:T(8,128)(2,1)S(1)}, u32[]{:S(2)}, u32[]{:S(2)}) collective-permute-start(bf16[1,2,64,512]{3,2,1,0:T(8,128)(2,1)S(1)} %get-tuple-element.26), channel_id=1, source_target_pairs={{4,0},{8,4},{12,8},{5,1},{9,5},{13,9},{6,2},{10,6},{14,10},{7,3},{... | collective-permute-start | bytes 393224 | tf_op jit(solution)/shard_map/ppermute | solution.py:26
  13.9 0.8 %copy-start.4 = (s32[16,12]{1,0:T(8,128)S(1)}, s32[16,12]{1,0:T(8,128)}, u32[]{:S(2)}) copy-start(s32[16,12]{1,0:T(8,128)} %span_ref.5) | copy-start | bytes 2308
  13.9 0.8 %copy-start.5 = (f32[16,12]{1,0:T(8,128)S(1)}, f32[16,12]{1,0:T(8,128)}, u32[]{:S(2)}) copy-start(f32[16,12]{1,0:T(8,128)} %param.15) | copy-start | bytes 2308
  19.4 5.0 %collective-permute-start.2 = (bf16[1,8,16,512]{3,2,1,0:T(8,128)(2,1)S(1)}, bf16[1,8,16,512]{3,2,1,0:T(8,128)(2,1)S(1)}, u32[]{:S(2)}, u32[]{:S(2)}) collective-permute-start(bf16[1,8,16,512]{3,2,1,0:T(8,128)(2,1)S(1)} %get-tuple-element.23), channel_id=1, source_target_pairs={{0,1},{1,2},{2,3},{3,0},{4,5},{5,6},{6,7},{7,4},{8,9},{9,10},{10,1... | collective-permute-start | bytes 393224 | tf_op jit(solution)/shard_map/ppermute | solution.py:23
  19.4 5.0 %collective-permute-start.3 = (bf16[1,8,16,512]{3,2,1,0:T(8,128)(2,1)S(1)}, bf16[1,8,16,512]{3,2,1,0:T(8,128)(2,1)S(1)}, u32[]{:S(2)}, u32[]{:S(2)}) collective-permute-start(bf16[1,8,16,512]{3,2,1,0:T(8,128)(2,1)S(1)} %get-tuple-element.24), channel_id=1, source_target_pairs={{1,0},{2,1},{3,2},{0,3},{5,4},{6,5},{7,6},{4,7},{9,8},{10,9},{11,1... | collective-permute-start | bytes 393224 | tf_op jit(solution)/shard_map/ppermute | solution.py:26
  34.7 13.4 %collective-permute-start.7 = (bf16[9,256,64]{1,2,0:T(8,128)(2,1)}, bf16[9,256,64]{1,2,0:T(8,128)(2,1)}, u32[]{:S(2)}, u32[]{:S(2)}) collective-permute-start(bf16[9,256,64]{1,2,0:T(8,128)(2,1)} %get-tuple-element.18), channel_id=1, source_target_pairs={{0,1},{1,2},{2,3},{3,0},{4,5},{5,6},{6,7},{7,4},{8,9},{9,10},{10,1... | collective-permute-start | bytes 884744 | tf_op jit(solution)/shard_map/ppermute | solution.py:55
  35.3 14.8 %collective-permute-start.8 = (bf16[9,256,64]{1,2,0:T(8,128)(2,1)}, bf16[9,256,64]{1,2,0:T(8,128)(2,1)}, u32[]{:S(2)}, u32[]{:S(2)}) collective-permute-start(bf16[9,256,64]{1,2,0:T(8,128)(2,1)} %get-tuple-element.20), channel_id=1, source_target_pairs={{0,2},{1,3},{2,0},{3,1},{4,6},{5,7},{6,4},{7,5},{8,10},{9,11},{10,... | collective-permute-start | bytes 884744 | tf_op jit(solution)/shard_map/ppermute | solution.py:55
  36.2 15.9 %collective-permute-start.9 = (bf16[9,256,64]{1,2,0:T(8,128)(2,1)}, bf16[9,256,64]{1,2,0:T(8,128)(2,1)}, u32[]{:S(2)}, u32[]{:S(2)}) collective-permute-start(bf16[9,256,64]{1,2,0:T(8,128)(2,1)} %get-tuple-element.19), channel_id=1, source_target_pairs={{0,3},{1,0},{2,1},{3,2},{4,7},{5,4},{6,5},{7,6},{8,11},{9,8},{10,9... | collective-permute-start | bytes 884744 | tf_op jit(solution)/shard_map/ppermute | solution.py:55
  43.5 2.1 %copy-start = (bf16[1,4,64,2304]{3,2,1,0:T(8,128)(2,1)S(1)}, bf16[1,4,64,2304]{3,2,1,0:T(8,128)(2,1)}, u32[]{:S(2)}) copy-start(bf16[1,4,64,2304]{3,2,1,0:T(8,128)(2,1)} %shard_map.103) | copy-start | bytes 3538948
  56.0 1.1 %copy-start.2 = (f32[9,256,64]{2,1,0:T(8,128)}, f32[9,256,64]{2,1,0:T(8,128)S(1)}, u32[]{:S(2)}) copy-start(f32[9,256,64]{2,1,0:T(8,128)S(1)} %convert_add_fusion) | copy-start | bytes 1769476
  57.1 13.9 %collective-permute-start.10 = (bf16[9,64,64]{2,1,0:T(8,128)(2,1)S(1)}, bf16[9,64,64]{2,1,0:T(8,128)(2,1)S(1)}, u32[]{:S(2)}, u32[]{:S(2)}) collective-permute-start(bf16[9,64,64]{2,1,0:T(8,128)(2,1)S(1)} %get-tuple-element.15), channel_id=1, source_target_pairs={{0,4},{4,8},{8,12},{12,0},{1,5},{5,9},{9,13},{13,1},{2,6},{6,10},{... | collective-permute-start | bytes 221192 | tf_op jit(solution)/shard_map/ppermute | solution.py:55
  58.0 13.2 %collective-permute-start.11 = (bf16[9,64,64]{2,1,0:T(8,128)(2,1)S(1)}, bf16[9,64,64]{2,1,0:T(8,128)(2,1)S(1)}, u32[]{:S(2)}, u32[]{:S(2)}) collective-permute-start(bf16[9,64,64]{2,1,0:T(8,128)(2,1)S(1)} %get-tuple-element.17), channel_id=1, source_target_pairs={{0,8},{4,12},{8,0},{12,4},{1,9},{5,13},{9,1},{13,5},{2,10},{6,14},... | collective-permute-start | bytes 221192 | tf_op jit(solution)/shard_map/ppermute | solution.py:55
  60.3 10.9 %collective-permute-start.12 = (bf16[9,64,64]{2,1,0:T(8,128)(2,1)S(1)}, bf16[9,64,64]{2,1,0:T(8,128)(2,1)S(1)}, u32[]{:S(2)}, u32[]{:S(2)}) collective-permute-start(bf16[9,64,64]{2,1,0:T(8,128)(2,1)S(1)} %get-tuple-element.16), channel_id=1, source_target_pairs={{0,12},{4,0},{8,4},{12,8},{1,13},{5,1},{9,5},{13,9},{2,14},{6,2},{... | collective-permute-start | bytes 221192 | tf_op jit(solution)/shard_map/ppermute | solution.py:55
  68.8 1.4 %copy-start.3 = (f32[1,2,64,256]{3,2,1,0:T(8,128)S(1)}, f32[1,2,64,256]{3,2,1,0:T(8,128)}, u32[]{:S(2)}) copy-start(f32[1,2,64,256]{3,2,1,0:T(8,128)} %convolution_bitcast_fusion.2) | copy-start | bytes 393220

commit v12 on v9

--- a/solution.py
+++ b/solution.py
@@ -105,6 +105,74 @@
         out_ref[0, 0, :, k * channels:(k + 1) * channels] = acc_ref[k].astype(jnp.bfloat16)
 
 
+def scatter_kernel(
+    first_ref, src_ref, start_ref, span_ref, basis_ref, scale_ref, field_ref, total_ref,
+    out_ref, acc_ref, *, slots, height, lon_count, lon_total,
+):
+    first_row = first_ref[0]
+    rows = out_ref.shape[1]
+    window = field_ref.shape[1]
+    padded = field_ref.shape[2]
+    channels = field_ref.shape[3]
+    acc_ref[...] = jnp.zeros(acc_ref.shape, jnp.float32)
+    out_col = lax.broadcasted_iota(jnp.int32, (lon_count, padded), 0)
+    in_col = lax.broadcasted_iota(jnp.int32, (lon_count, padded), 1) - RIM
+    offset = out_col - in_col
+    for row in range(window):
+        global_row = first_row + row - REACH
+        inside = (global_row >= 0) & (global_row < height)
+        table_row = jnp.clip(global_row, 0, height - 1)
+        for slot in range(slots):
+            target = src_ref[table_row, slot] - first_row
+            scale = scale_ref[table_row, slot]
+            hit = inside & (target >= 0) & (target < rows) & (scale != 0.0)
+
+            @pl.when(hit)
+            def _():
+                start = start_ref[table_row, slot]
+                span = span_ref[table_row, slot]
+                basis = basis_ref[table_row, slot]
+                narrow = span < lon_total
+                band = ((offset >= start) & (offset < start + span) & narrow).astype(
+                    jnp.bfloat16
+                )
+                boxed = jnp.dot(band, field_ref[0, row], preferred_element_type=jnp.float32)
+                full = jnp.where(narrow, 0.0, 1.0).astype(jnp.float32)
+                boxed = boxed + full * total_ref[0, row]
+                acc_ref[target, basis] = acc_ref[target, basis] + scale * boxed
+
+    for p in range(rows):
+        for k in range(BASIS):
+            out_ref[0, p, :, k * channels:(k + 1) * channels] = acc_ref[p, k].astype(
+                jnp.bfloat16
+            )
+
+
+def run_scatter(first, tables, field, totals, row_count, lon_count, lon_total):
+    members, window, padded, channels = field.shape
+    height, slots = tables[0].shape
+    smem = pl.BlockSpec(memory_space=pltpu.SMEM)
+    kernel = functools.partial(
+        scatter_kernel, slots=slots, height=height, lon_count=lon_count, lon_total=lon_total
+    )
+    return pl.pallas_call(
+        kernel,
+        grid=(members,),
+        in_specs=[smem] * 6
+        + [
+            pl.BlockSpec((1, window, padded, channels), lambda b: (b, 0, 0, 0)),
+            pl.BlockSpec((1, window, 1, channels), lambda b: (b, 0, 0, 0)),
+        ],
+        out_specs=pl.BlockSpec(
+            (1, row_count, lon_count, BASIS * channels), lambda b: (b, 0, 0, 0)
+        ),
+        out_shape=jax.ShapeDtypeStruct(
+            (members, row_count, lon_count, BASIS * channels), jnp.bfloat16
+        ),
+        scratch_shapes=[pltpu.VMEM((row_count, BASIS, lon_count, channels), jnp.float32)],
+    )(first, *tables, field, totals[:, :, None, :])
+
+
 def run_filter(first, tables, field, totals, row_count, lon_count, lon_total, backward):
     members, window, padded, channels = field.shape
     height, slots = tables[0].shape
@@ -169,8 +237,8 @@
     reduced = ring_scatter(partial_value, "lon", 2)
     grad_wide, grad_totals, reduced = lax.optimization_barrier((grad_wide, grad_totals, reduced))
     reduced = ring_scatter(reduced, "lat", 1)
-    back_filtered = run_filter(
-        first, tables, grad_wide, grad_totals, row_count, lon_count, lon_total, True
+    back_filtered = run_scatter(
+        first, tables, grad_wide, grad_totals, row_count, lon_count, lon_total
     )
     w_back = jnp.transpose(weight, (0, 2, 1)).reshape(BASIS * channels, channels)
     grad_input = jnp.einsum(

time: 68 us -> 67.5 us (level)
  Pallas kernels: 14.6 us -> 13.7 us
    pallas_call x2 -> x1, Pallas kernels: 14.6 us -> 3.93 us  [run_filter(): pl.pallas_call(kernel, grid=(members, row_count), in_specs=[smem] * 6 + [...]
    pallas_call x0 -> x1, Pallas kernels: none -> 9.8 us  [run_scatter(): pl.pallas_call(kernel, grid=(members,), in_specs=[smem] * 6 + [pl.BlockSp...]
  transfers between devices with their start and end apart: 13 -> 13, of which waited for: 6 -> 6; matrix products, arithmetic and copies ran while one was open for 16% -> 16% of each run, Pallas kernels for 16% -> 15%
where the time goes in v12:
time: 67.5 us; the launch traced here: 66.5 us
  starting transfers between devices  18.6 us (28%)
  waiting for transfers between devices  14.5 us (21%)
  Pallas kernels  13.7 us (20%)
  local copies, waits for them, and re-layouts  8.08 us (12%)
  matrix products  6.69 us (10%)
  other arithmetic  4.05 us (6%)
  between operations  0.84 us (1%)
    pallas_call x1, Pallas kernels, run_scatter(): pl.pallas_call(kernel, grid=(members,), in_specs=[smem] * 6 + [pl.BlockSp...  9.8 us
    ppermute x6, starting transfers between devices, ring_scatter(): sent = lax.ppermute(piece.astype(jnp.bfloat16), axis, pairs)  7.56 us
    ppermute x6, waiting for transfers between devices, ring_scatter(): sent = lax.ppermute(piece.astype(jnp.bfloat16), axis, pairs)  7.06 us
    ppermute x3, starting transfers between devices, ring_sum(): total = total + lax.ppermute(value, axis, pairs)  4.46 us
    ppermute x2, waiting for transfers between devices, with_halo(): lax.ppermute(lax.slice_in_dim(block, 0, width, axis=dim), axis, backward)  4.37 us
    unnamed x13, local copies, waits for them, and re-layouts  4.28 us
    pallas_call x1, Pallas kernels, run_filter(): pl.pallas_call(kernel, grid=(members, row_count), in_specs=[smem] * 6 + [...  3.93 us
    ppermute x2, starting transfers between devices, with_halo(): lax.ppermute(lax.slice_in_dim(block, block.shape[dim] - width, None, axis...  3.54 us
  transfers between devices with their start and end apart: 13, of which 6 were waited for; matrix products, arithmetic and copies ran while one was open for 16% of the time, Pallas kernels for 15%

profile of v12, /device:TPU:0, one launch (start us, length us, event | category | flops | bytes accessed | tf_op | source)
XLA Modules:
  0.0 66.5 jit_solution(9222748245130230571)
XLA Ops:
  0.6 0.0 copy-start.3
  0.6 0.0 copy-start.4
  0.7 0.9 %convert_reduce_fusion = f32[4,256]{1,0:T(4,128)S(1)} fusion(bf16[1,4,64,256]{3,2,1,0:T(8,128)(2,1)} %param.9), kind=kLoop, calls=%fused_computation.27 | loop fusion | flops 130048 | bytes 135168 | tf_op jit(solution)/shard_map/reduce_sum | solution.py:220
  1.6 0.9 %convert_reduce_fusion.1 = f32[4,256]{1,0:T(4,128)S(1)} fusion(bf16[1,4,64,256]{3,2,1,0:T(8,128)(2,1)} %param.8), kind=kLoop, calls=%fused_computation.28 | loop fusion | flops 130048 | bytes 135168 | tf_op jit(solution)/shard_map/reduce_sum | solution.py:220
  2.6 0.5 collective-permute-start.4
  3.1 2.6 %collective-permute-start.5 = (f32[2,1,4,256]{3,0,2,1:T(2,128)S(1)}, f32[2,1,4,256]{3,0,2,1:T(2,128)S(1)}, u32[]{:S(2)}, u32[]{:S(2)}) collective-permute-start(f32[2,1,4,256]{3,0,2,1:T(2,128)S(1)} %pad_maximum_fusion.3), channel_id=1, source_target_pairs={{0,2},{1,3},{2,0},{3,1},{4,6},{5,7},{6,4},{7,5},{8,10},{9,11},{10,... | collective-permute-start | bytes 24584 | tf_op jit(solution)/shard_map/ppermute | solution.py:43
  5.7 1.4 %collective-permute-start.6 = (f32[2,1,4,256]{3,0,2,1:T(2,128)S(1)}, f32[2,1,4,256]{3,0,2,1:T(2,128)S(1)}, u32[]{:S(2)}, u32[]{:S(2)}) collective-permute-start(f32[2,1,4,256]{3,0,2,1:T(2,128)S(1)} %pad_maximum_fusion.3), channel_id=1, source_target_pairs={{0,3},{1,0},{2,1},{3,2},{4,7},{5,4},{6,5},{7,6},{8,11},{9,8},{10,9... | collective-permute-start | bytes 24584 | tf_op jit(solution)/shard_map/ppermute | solution.py:43
  7.0 0.9 %constant_dynamic-update-slice_fusion.1 = bf16[1,4,64,512]{3,2,1,0:T(8,128)(2,1)S(1)} fusion(bf16[1,4,64,256]{3,2,1,0:T(8,128)(2,1)} %param.8), kind=kLoop, calls=%fused_computation.41 | loop fusion | bytes 262144
  8.0 0.9 %constant_dynamic-update-slice_fusion = bf16[1,4,64,512]{3,2,1,0:T(8,128)(2,1)S(1)} fusion(bf16[1,4,64,512]{3,2,1,0:T(8,128)(2,1)S(1)} %constant_dynamic-update-slice_fusion.1, bf16[1,4,64,256]{3,2,1,0:T(8,128)(2,1)} %param.9), kind=kLoop, calls=%fused_computation.40 | loop fusion | bytes 262144 | tf_op jit(solution)/shard_map/concatenate | solution.py:216
  8.9 3.5 %collective-permute-start = (bf16[1,2,64,512]{3,2,1,0:T(8,128)(2,1)S(1)}, bf16[1,2,64,512]{3,2,1,0:T(8,128)(2,1)S(1)}, u32[]{:S(2)}, u32[]{:S(2)}) collective-permute-start(bf16[1,2,64,512]{3,2,1,0:T(8,128)(2,1)S(1)} %get-tuple-element.25), channel_id=1, source_target_pairs={{0,4},{4,8},{8,12},{1,5},{5,9},{9,13},{2,6},{6,10},{10,14},{3,7},{... | collective-permute-start | bytes 393224 | tf_op jit(solution)/shard_map/ppermute | solution.py:23
  12.4 1.3 %collective-permute-start.1 = (bf16[1,2,64,512]{3,2,1,0:T(8,128)(2,1)S(1)}, bf16[1,2,64,512]{3,2,1,0:T(8,128)(2,1)S(1)}, u32[]{:S(2)}, u32[]{:S(2)}) collective-permute-start(bf16[1,2,64,512]{3,2,1,0:T(8,128)(2,1)S(1)} %get-tuple-element.26), channel_id=1, source_target_pairs={{4,0},{8,4},{12,8},{5,1},{9,5},{13,9},{6,2},{10,6},{14,10},{7,3},{... | collective-permute-start | bytes 393224 | tf_op jit(solution)/shard_map/ppermute | solution.py:26
  13.7 0.0 copy-done.3
  13.8 0.0 copy-done.4
  13.8 0.6 rsqrt_multiply_fusion.scale_ref
  14.4 0.5 collective-permute-done
  14.9 4.4 %collective-permute-done.1 = bf16[1,2,64,512]{3,2,1,0:T(8,128)(2,1)S(1)} collective-permute-done((bf16[1,2,64,512]{3,2,1,0:T(8,128)(2,1)S(1)}, bf16[1,2,64,512]{3,2,1,0:T(8,128)(2,1)S(1)}, u32[]{:S(2)}, u32[]{:S(2)}) %collective-permute-start.1) | collective-permute-done | bytes 131104 | tf_op jit(solution)/shard_map/ppermute | solution.py:26
  19.3 0.1 collective-permute-start.2
  19.3 1.7 %collective-permute-start.3 = (bf16[1,8,16,512]{3,2,1,0:T(8,128)(2,1)S(1)}, bf16[1,8,16,512]{3,2,1,0:T(8,128)(2,1)S(1)}, u32[]{:S(2)}, u32[]{:S(2)}) collective-permute-start(bf16[1,8,16,512]{3,2,1,0:T(8,128)(2,1)S(1)} %get-tuple-element.24), channel_id=1, source_target_pairs={{1,0},{2,1},{3,2},{0,3},{5,4},{6,5},{7,6},{4,7},{9,8},{10,9},{11,1... | collective-permute-start | bytes 393224 | tf_op jit(solution)/shard_map/ppermute | solution.py:26
  21.1 0.0 collective-permute-done.4
  21.1 0.0 collective-permute-done.5
  21.1 0.0 collective-permute-done.6
  21.1 0.6 fusion.23
  21.7 2.6 %collective-permute-done.2 = bf16[1,8,16,512]{3,2,1,0:T(8,128)(2,1)S(1)} collective-permute-done((bf16[1,8,16,512]{3,2,1,0:T(8,128)(2,1)S(1)}, bf16[1,8,16,512]{3,2,1,0:T(8,128)(2,1)S(1)}, u32[]{:S(2)}, u32[]{:S(2)}) %collective-permute-start.2) | collective-permute-done | bytes 131104 | tf_op jit(solution)/shard_map/ppermute | solution.py:23
  24.3 0.0 collective-permute-done.3
  24.3 0.1 fusion.18
  24.4 1.1 %fusion.24 = (bf16[1,8,128,256]{3,2,1,0:T(8,128)(2,1)}, bf16[1,8,128,256]{3,2,1,0:T(8,128)(2,1)}) fusion(bf16[1,8,128,512]{3,2,1,0:T(8,128)(2,1)S(1)} %fusion.18), kind=kLoop, calls=%fused_computation.42 | loop fusion | bytes 2097152 | tf_op jit(solution)/shard_map/slice | solution.py:218
  25.5 0.0 copy-start.2
  25.5 3.9 %shard_map.103 = bf16[1,4,64,2304]{3,2,1,0:T(8,128)(2,1)} custom-call(s32[1]{0:T(128)} %bitcast.first_ref, s32[16,12]{1,0:T(8,128)} %src_ref.3, s32[16,12]{1,0:T(8,128)} %start_ref.3, s32[16,12]{1,0:T(8,128)} %span_ref.3, s32[16,12]{1,0:T(8,128)} %basis_ref.3, f32[16,12]{1,0:T(8,128)} %rsqrt_multiply_fusion.scale_ref, ...), custom_call_target="tpu_custom_call" | custom-call | tf_op jit(solution)/shard_map/pallas_call | solution.py:188
  29.4 0.0 copy-done.2
  29.4 1.8 %convolution_bitcast_fusion = f32[9,256,256]{1,2,0:T(8,128)S(1)} fusion(bf16[4,8,9,8,256]{4,3,2,1,0:T(8,128)(2,1)} %bitcast.45, bf16[1,4,64,256]{3,2,1,0:T(8,128)(2,1)S(1)} %copy-done.2), kind=kOutput, calls=%fused_computation.6 | convolution fusion | flops 301989888 | bytes 3670016 | tf_op jit(solution)/shard_map/brwq,brwo->qo/dot_general | solution.py:233
  31.2 0.9 %dynamic-slice_convert_fusion.2 = (bf16[9,256,64]{1,2,0:T(8,128)(2,1)}, bf16[9,256,64]{1,2,0:T(8,128)(2,1)}, bf16[9,256,64]{1,2,0:T(8,128)(2,1)}) fusion(f32[9,256,256]{1,2,0:T(8,128)S(1)} %convolution_bitcast_fusion, s32[]{:T(128)S(6)} %select_n.53, s32[]{:T(128)S(6)} %select_n.57, s32[]{:T(128)S(6)} %select_n.55), kind=kLoop, calls=%fused_computation.22 | loop fusion | bytes 1769484 | tf_op jit(solution)/shard_map/convert_element_type | solution.py:55
  32.2 0.6 collective-permute-start.7
  32.8 0.9 %collective-permute-start.8 = (bf16[9,256,64]{1,2,0:T(8,128)(2,1)}, bf16[9,256,64]{1,2,0:T(8,128)(2,1)}, u32[]{:S(2)}, u32[]{:S(2)}) collective-permute-start(bf16[9,256,64]{1,2,0:T(8,128)(2,1)} %get-tuple-element.17), channel_id=1, source_target_pairs={{0,2},{1,3},{2,0},{3,1},{4,6},{5,7},{6,4},{7,5},{8,10},{9,11},{10,... | collective-permute-start | bytes 884744 | tf_op jit(solution)/shard_map/ppermute | solution.py:55
  33.7 0.4 collective-permute-start.9
  34.2 0.0 copy-start
  34.2 2.5 %copy.16 = bf16[9,256,256]{1,2,0:T(8,128)(2,1)} copy(bf16[9,256,256]{2,1,0:T(8,128)(2,1)} %param.10) | data formatting | bytes 2359296 | tf_op args[2]
  36.6 0.0 copy-done
  36.6 2.5 %fusion.11 = f32[1,4,64,256]{3,2,1,0:T(8,128)} fusion(bf16[2304,256,1]{1,0,2:T(8,128)(2,1)} %bitcast.46, bf16[1,4,64,2304]{3,2,1,0:T(8,128)(2,1)S(1)} %copy-done), kind=kOutput, calls=%fused_computation.13 | convolution fusion | flops 301989888 | bytes 2621440 | tf_op jit(solution)/shard_map/brwq,qo->brwo/dot_general | solution.py:231
  39.1 1.4 %collective-permute-done.7 = bf16[9,256,64]{1,2,0:T(8,128)(2,1)} collective-permute-done((bf16[9,256,64]{1,2,0:T(8,128)(2,1)}, bf16[9,256,64]{1,2,0:T(8,128)(2,1)}, u32[]{:S(2)}, u32[]{:S(2)}) %collective-permute-start.7) | collective-permute-done | bytes 294944 | tf_op jit(solution)/shard_map/ppermute | solution.py:55
  40.5 2.5 %collective-permute-done.8 = bf16[9,256,64]{1,2,0:T(8,128)(2,1)} collective-permute-done((bf16[9,256,64]{1,2,0:T(8,128)(2,1)}, bf16[9,256,64]{1,2,0:T(8,128)(2,1)}, u32[]{:S(2)}, u32[]{:S(2)}) %collective-permute-start.8) | collective-permute-done | bytes 294944 | tf_op jit(solution)/shard_map/ppermute | solution.py:55
  43.0 3.1 %collective-permute-done.9 = bf16[9,256,64]{1,2,0:T(8,128)(2,1)} collective-permute-done((bf16[9,256,64]{1,2,0:T(8,128)(2,1)}, bf16[9,256,64]{1,2,0:T(8,128)(2,1)}, u32[]{:S(2)}, u32[]{:S(2)}) %collective-permute-start.9) | collective-permute-done | bytes 294944 | tf_op jit(solution)/shard_map/ppermute | solution.py:55
  46.2 1.3 %convert_add_fusion = f32[9,256,64]{1,2,0:T(8,128)S(1)} fusion(bf16[9,256,64]{1,2,0:T(8,128)(2,1)} %collective-permute-done.9, bf16[9,256,64]{1,2,0:T(8,128)(2,1)} %collective-permute-done.8, bf16[9,256,64]{1,2,0:T(8,128)(2,1)} %collective-permute-done.7, f32[9,256,256]{1,2,0:T(8,128)S(1)} %convolution_bitcast_fusion, s32[]{:T(128)S(6)} %select_n.51), kind=kLoop, calls=%fused_computation.19 | loop fusion | flops 884736 | bytes 2064388 | tf_op jit(solution)/shard_map/add | solution.py:56
  47.4 0.0 copy-start.1
  47.4 0.2 dynamic-slice_convert_fusion.5
  47.6 1.6 %collective-permute-start.10 = (bf16[9,64,64]{1,2,0:T(8,128)(2,1)S(1)}, bf16[9,64,64]{1,2,0:T(8,128)(2,1)S(1)}, u32[]{:S(2)}, u32[]{:S(2)}) collective-permute-start(bf16[9,64,64]{1,2,0:T(8,128)(2,1)S(1)} %get-tuple-element.20), channel_id=1, source_target_pairs={{0,4},{4,8},{8,12},{12,0},{1,5},{5,9},{9,13},{13,1},{2,6},{6,10},{... | collective-permute-start | bytes 221192 | tf_op jit(solution)/shard_map/ppermute | solution.py:55
  49.3 1.1 %collective-permute-start.11 = (bf16[9,64,64]{1,2,0:T(8,128)(2,1)S(1)}, bf16[9,64,64]{1,2,0:T(8,128)(2,1)S(1)}, u32[]{:S(2)}, u32[]{:S(2)}) collective-permute-start(bf16[9,64,64]{1,2,0:T(8,128)(2,1)S(1)} %get-tuple-element.22), channel_id=1, source_target_pairs={{0,8},{4,12},{8,0},{12,4},{1,9},{5,13},{9,1},{13,5},{2,10},{6,14},... | collective-permute-start | bytes 221192 | tf_op jit(solution)/shard_map/ppermute | solution.py:55
  50.4 2.8 %collective-permute-start.12 = (bf16[9,64,64]{1,2,0:T(8,128)(2,1)S(1)}, bf16[9,64,64]{1,2,0:T(8,128)(2,1)S(1)}, u32[]{:S(2)}, u32[]{:S(2)}) collective-permute-start(bf16[9,64,64]{1,2,0:T(8,128)(2,1)S(1)} %get-tuple-element.21), channel_id=1, source_target_pairs={{0,12},{4,0},{8,4},{12,8},{1,13},{5,1},{9,5},{13,9},{2,14},{6,2},{... | collective-permute-start | bytes 221192 | tf_op jit(solution)/shard_map/ppermute | solution.py:55
  53.2 9.8 %shard_map.104 = bf16[1,4,64,2304]{3,2,1,0:T(8,128)(2,1)} custom-call(s32[1]{0:T(128)} %bitcast.first_ref, s32[16,12]{1,0:T(8,128)} %src_ref.3, s32[16,12]{1,0:T(8,128)} %start_ref.3, s32[16,12]{1,0:T(8,128)} %span_ref.3, s32[16,12]{1,0:T(8,128)} %basis_ref.3, f32[16,12]{1,0:T(8,128)} %rsqrt_multiply_fusion.scale_ref, ...), custom_call_target="tpu_custom_call" | custom-call | tf_op jit(solution)/shard_map/pallas_call | solution.py:158
  63.0 0.0 copy-done.1
  63.0 2.5 %fusion.14 = f32[1,4,64,256]{3,2,1,0:T(8,128)} fusion(bf16[2304,256,1]{1,0,2:T(8,128)(2,1)S(1)} %bitcast.47, bf16[1,4,64,2304]{3,2,1,0:T(8,128)(2,1)} %shard_map.104), kind=kOutput, calls=%fused_computation.14 | convolution fusion | flops 301989888 | bytes 2621440 | tf_op jit(solution)/shard_map/bpwq,qc->bpwc/dot_general | solution.py:244
  65.5 0.0 collective-permute-done.10
  65.5 0.0 collective-permute-done.11
  65.5 0.0 collective-permute-done.12
  65.5 0.2 add_multiply_fusion
  65.6 0.9 %copy.17 = f32[9,64,64]{2,1,0:T(8,128)} copy(f32[9,64,64]{1,2,0:T(8,128)S(1)} %add_multiply_fusion) | data formatting | bytes 294912
  (6 shorter events, 0.1 us)
Async XLA Ops:
  0.6 13.1 %copy-start.3 = (s32[16,12]{1,0:T(8,128)S(1)}, s32[16,12]{1,0:T(8,128)}, u32[]{:S(2)}) copy-start(s32[16,12]{1,0:T(8,128)} %span_ref.3) | copy-start | bytes 2308
  0.6 13.1 %copy-start.4 = (f32[16,12]{1,0:T(8,128)S(1)}, f32[16,12]{1,0:T(8,128)}, u32[]{:S(2)}) copy-start(f32[16,12]{1,0:T(8,128)} %param.15) | copy-start | bytes 2308
  2.6 18.5 %collective-permute-start.4 = (f32[2,1,4,256]{3,0,2,1:T(2,128)S(1)}, f32[2,1,4,256]{3,0,2,1:T(2,128)S(1)}, u32[]{:S(2)}, u32[]{:S(2)}) collective-permute-start(f32[2,1,4,256]{3,0,2,1:T(2,128)S(1)} %pad_maximum_fusion.3), channel_id=1, source_target_pairs={{0,1},{1,2},{2,3},{3,0},{4,5},{5,6},{6,7},{7,4},{8,9},{9,10},{10,1... | collective-permute-start | bytes 24584 | tf_op jit(solution)/shard_map/ppermute | solution.py:43
  3.1 18.0 %collective-permute-start.5 = (f32[2,1,4,256]{3,0,2,1:T(2,128)S(1)}, f32[2,1,4,256]{3,0,2,1:T(2,128)S(1)}, u32[]{:S(2)}, u32[]{:S(2)}) collective-permute-start(f32[2,1,4,256]{3,0,2,1:T(2,128)S(1)} %pad_maximum_fusion.3), channel_id=1, source_target_pairs={{0,2},{1,3},{2,0},{3,1},{4,6},{5,7},{6,4},{7,5},{8,10},{9,11},{10,... | collective-permute-start | bytes 24584 | tf_op jit(solution)/shard_map/ppermute | solution.py:43
  5.7 15.4 %collective-permute-start.6 = (f32[2,1,4,256]{3,0,2,1:T(2,128)S(1)}, f32[2,1,4,256]{3,0,2,1:T(2,128)S(1)}, u32[]{:S(2)}, u32[]{:S(2)}) collective-permute-start(f32[2,1,4,256]{3,0,2,1:T(2,128)S(1)} %pad_maximum_fusion.3), channel_id=1, source_target_pairs={{0,3},{1,0},{2,1},{3,2},{4,7},{5,4},{6,5},{7,6},{8,11},{9,8},{10,9... | collective-permute-start | bytes 24584 | tf_op jit(solution)/shard_map/ppermute | solution.py:43
  8.9 6.0 %collective-permute-start = (bf16[1,2,64,512]{3,2,1,0:T(8,128)(2,1)S(1)}, bf16[1,2,64,512]{3,2,1,0:T(8,128)(2,1)S(1)}, u32[]{:S(2)}, u32[]{:S(2)}) collective-permute-start(bf16[1,2,64,512]{3,2,1,0:T(8,128)(2,1)S(1)} %get-tuple-element.25), channel_id=1, source_target_pairs={{0,4},{4,8},{8,12},{1,5},{5,9},{9,13},{2,6},{6,10},{10,14},{3,7},{... | collective-permute-start | bytes 393224 | tf_op jit(solution)/shard_map/ppermute | solution.py:23
  12.4 6.9 %collective-permute-start.1 = (bf16[1,2,64,512]{3,2,1,0:T(8,128)(2,1)S(1)}, bf16[1,2,64,512]{3,2,1,0:T(8,128)(2,1)S(1)}, u32[]{:S(2)}, u32[]{:S(2)}) collective-permute-start(bf16[1,2,64,512]{3,2,1,0:T(8,128)(2,1)S(1)} %get-tuple-element.26), channel_id=1, source_target_pairs={{4,0},{8,4},{12,8},{5,1},{9,5},{13,9},{6,2},{10,6},{14,10},{7,3},{... | collective-permute-start | bytes 393224 | tf_op jit(solution)/shard_map/ppermute | solution.py:26
  19.3 5.0 %collective-permute-start.2 = (bf16[1,8,16,512]{3,2,1,0:T(8,128)(2,1)S(1)}, bf16[1,8,16,512]{3,2,1,0:T(8,128)(2,1)S(1)}, u32[]{:S(2)}, u32[]{:S(2)}) collective-permute-start(bf16[1,8,16,512]{3,2,1,0:T(8,128)(2,1)S(1)} %get-tuple-element.23), channel_id=1, source_target_pairs={{0,1},{1,2},{2,3},{3,0},{4,5},{5,6},{6,7},{7,4},{8,9},{9,10},{10,1... | collective-permute-start | bytes 393224 | tf_op jit(solution)/shard_map/ppermute | solution.py:23
  19.3 5.0 %collective-permute-start.3 = (bf16[1,8,16,512]{3,2,1,0:T(8,128)(2,1)S(1)}, bf16[1,8,16,512]{3,2,1,0:T(8,128)(2,1)S(1)}, u32[]{:S(2)}, u32[]{:S(2)}) collective-permute-start(bf16[1,8,16,512]{3,2,1,0:T(8,128)(2,1)S(1)} %get-tuple-element.24), channel_id=1, source_target_pairs={{1,0},{2,1},{3,2},{0,3},{5,4},{6,5},{7,6},{4,7},{9,8},{10,9},{11,1... | collective-permute-start | bytes 393224 | tf_op jit(solution)/shard_map/ppermute | solution.py:26
  25.5 3.9 %copy-start.2 = (bf16[1,4,64,256]{3,2,1,0:T(8,128)(2,1)S(1)}, bf16[1,4,64,256]{3,2,1,0:T(8,128)(2,1)}, u32[]{:S(2)}) copy-start(bf16[1,4,64,256]{3,2,1,0:T(8,128)(2,1)} %param.9) | copy-start | bytes 393220
  32.2 8.4 %collective-permute-start.7 = (bf16[9,256,64]{1,2,0:T(8,128)(2,1)}, bf16[9,256,64]{1,2,0:T(8,128)(2,1)}, u32[]{:S(2)}, u32[]{:S(2)}) collective-permute-start(bf16[9,256,64]{1,2,0:T(8,128)(2,1)} %get-tuple-element.15), channel_id=1, source_target_pairs={{0,1},{1,2},{2,3},{3,0},{4,5},{5,6},{6,7},{7,4},{8,9},{9,10},{10,1... | collective-permute-start | bytes 884744 | tf_op jit(solution)/shard_map/ppermute | solution.py:55
  32.8 10.2 %collective-permute-start.8 = (bf16[9,256,64]{1,2,0:T(8,128)(2,1)}, bf16[9,256,64]{1,2,0:T(8,128)(2,1)}, u32[]{:S(2)}, u32[]{:S(2)}) collective-permute-start(bf16[9,256,64]{1,2,0:T(8,128)(2,1)} %get-tuple-element.17), channel_id=1, source_target_pairs={{0,2},{1,3},{2,0},{3,1},{4,6},{5,7},{6,4},{7,5},{8,10},{9,11},{10,... | collective-permute-start | bytes 884744 | tf_op jit(solution)/shard_map/ppermute | solution.py:55
  33.7 12.4 %collective-permute-start.9 = (bf16[9,256,64]{1,2,0:T(8,128)(2,1)}, bf16[9,256,64]{1,2,0:T(8,128)(2,1)}, u32[]{:S(2)}, u32[]{:S(2)}) collective-permute-start(bf16[9,256,64]{1,2,0:T(8,128)(2,1)} %get-tuple-element.16), channel_id=1, source_target_pairs={{0,3},{1,0},{2,1},{3,2},{4,7},{5,4},{6,5},{7,6},{8,11},{9,8},{10,9... | collective-permute-start | bytes 884744 | tf_op jit(solution)/shard_map/ppermute | solution.py:55
  34.2 2.5 %copy-start = (bf16[1,4,64,2304]{3,2,1,0:T(8,128)(2,1)S(1)}, bf16[1,4,64,2304]{3,2,1,0:T(8,128)(2,1)}, u32[]{:S(2)}) copy-start(bf16[1,4,64,2304]{3,2,1,0:T(8,128)(2,1)} %shard_map.103) | copy-start | bytes 3538948
  47.4 15.6 %copy-start.1 = (bf16[9,256,256]{1,2,0:T(8,128)(2,1)S(1)}, bf16[9,256,256]{1,2,0:T(8,128)(2,1)}, u32[]{:S(2)}) copy-start(bf16[9,256,256]{1,2,0:T(8,128)(2,1)} %copy.16) | copy-start | bytes 3538948
  47.6 17.8 %collective-permute-start.10 = (bf16[9,64,64]{1,2,0:T(8,128)(2,1)S(1)}, bf16[9,64,64]{1,2,0:T(8,128)(2,1)S(1)}, u32[]{:S(2)}, u32[]{:S(2)}) collective-permute-start(bf16[9,64,64]{1,2,0:T(8,128)(2,1)S(1)} %get-tuple-element.20), channel_id=1, source_target_pairs={{0,4},{4,8},{8,12},{12,0},{1,5},{5,9},{9,13},{13,1},{2,6},{6,10},{... | collective-permute-start | bytes 221192 | tf_op jit(solution)/shard_map/ppermute | solution.py:55
  49.3 16.2 %collective-permute-start.11 = (bf16[9,64,64]{1,2,0:T(8,128)(2,1)S(1)}, bf16[9,64,64]{1,2,0:T(8,128)(2,1)S(1)}, u32[]{:S(2)}, u32[]{:S(2)}) collective-permute-start(bf16[9,64,64]{1,2,0:T(8,128)(2,1)S(1)} %get-tuple-element.22), channel_id=1, source_target_pairs={{0,8},{4,12},{8,0},{12,4},{1,9},{5,13},{9,1},{13,5},{2,10},{6,14},... | collective-permute-start | bytes 221192 | tf_op jit(solution)/shard_map/ppermute | solution.py:55
  50.4 15.1 %collective-permute-start.12 = (bf16[9,64,64]{1,2,0:T(8,128)(2,1)S(1)}, bf16[9,64,64]{1,2,0:T(8,128)(2,1)S(1)}, u32[]{:S(2)}, u32[]{:S(2)}) collective-permute-start(bf16[9,64,64]{1,2,0:T(8,128)(2,1)S(1)} %get-tuple-element.21), channel_id=1, source_target_pairs={{0,12},{4,0},{8,4},{12,8},{1,13},{5,1},{9,5},{13,9},{2,14},{6,2},{... | collective-permute-start | bytes 221192 | tf_op jit(solution)/shard_map/ppermute | solution.py:55

commit v13 on v12

--- a/solution.py
+++ b/solution.py
@@ -107,7 +107,7 @@
 
 def scatter_kernel(
     first_ref, src_ref, start_ref, span_ref, basis_ref, scale_ref, field_ref, total_ref,
-    out_ref, acc_ref, *, slots, height, lon_count, lon_total,
+    weight_ref, out_ref, acc_ref, *, slots, height, lon_count, lon_total,
 ):
     first_row = first_ref[0]
     rows = out_ref.shape[1]
@@ -142,14 +142,20 @@
                 acc_ref[target, basis] = acc_ref[target, basis] + scale * boxed
 
     for p in range(rows):
+        mixed = jnp.zeros((lon_count, weight_ref.shape[1]), jnp.float32)
         for k in range(BASIS):
-            out_ref[0, p, :, k * channels:(k + 1) * channels] = acc_ref[p, k].astype(
-                jnp.bfloat16
+            mixed = mixed + lax.dot_general(
+                acc_ref[p, k].astype(jnp.bfloat16),
+                weight_ref[k],
+                (((1,), (1,)), ((), ())),
+                preferred_element_type=jnp.float32,
             )
-
-
-def run_scatter(first, tables, field, totals, row_count, lon_count, lon_total):
+        out_ref[0, p] = mixed
+
+
+def run_scatter(first, tables, field, totals, weight, row_count, lon_count, lon_total):
     members, window, padded, channels = field.shape
+    basis, in_channels, out_channels = weight.shape
     height, slots = tables[0].shape
     smem = pl.BlockSpec(memory_space=pltpu.SMEM)
     kernel = functools.partial(
@@ -162,15 +168,16 @@
         + [
             pl.BlockSpec((1, window, padded, channels), lambda b: (b, 0, 0, 0)),
             pl.BlockSpec((1, window, 1, channels), lambda b: (b, 0, 0, 0)),
+            pl.BlockSpec((basis, in_channels, out_channels), lambda b: (0, 0, 0)),
         ],
         out_specs=pl.BlockSpec(
-            (1, row_count, lon_count, BASIS * channels), lambda b: (b, 0, 0, 0)
+            (1, row_count, lon_count, in_channels), lambda b: (b, 0, 0, 0)
         ),
         out_shape=jax.ShapeDtypeStruct(
-            (members, row_count, lon_count, BASIS * channels), jnp.bfloat16
+            (members, row_count, lon_count, in_channels), jnp.float32
         ),
         scratch_shapes=[pltpu.VMEM((row_count, BASIS, lon_count, channels), jnp.float32)],
-    )(first, *tables, field, totals[:, :, None, :])
+    )(first, *tables, field, totals[:, :, None, :], weight)
 
 
 def run_filter(first, tables, field, totals, row_count, lon_count, lon_total, backward):
@@ -237,12 +244,8 @@
     reduced = ring_scatter(partial_value, "lon", 2)
     grad_wide, grad_totals, reduced = lax.optimization_barrier((grad_wide, grad_totals, reduced))
     reduced = ring_scatter(reduced, "lat", 1)
-    back_filtered = run_scatter(
-        first, tables, grad_wide, grad_totals, row_count, lon_count, lon_total
-    )
-    w_back = jnp.transpose(weight, (0, 2, 1)).reshape(BASIS * channels, channels)
-    grad_input = jnp.einsum(
-        "bpwq,qc->bpwc", back_filtered, w_back, preferred_element_type=jnp.float32
+    grad_input = run_scatter(
+        first, tables, grad_wide, grad_totals, weight, row_count, lon_count, lon_total
     )
     grad_weight = reduced / jnp.sqrt(jnp.float32(members * height * lon_total))
     return (response, grad_input, grad_weight)

time: 67.5 us -> 67.9 us (level); the launches traced: 66.5 us -> 67.7 us
  waiting for transfers between devices: 14.5 us -> 21.2 us
  matrix products: 6.69 us -> 2.96 us
  local copies, waits for them, and re-layouts: 8.08 us -> 5.65 us
  starting transfers between devices: 18.6 us -> 17 us
  Pallas kernels: 13.7 us -> 15.2 us
  other arithmetic: 4.05 us -> 4.75 us
    ppermute x6, waiting for transfers between devices: 7.06 us -> 14.3 us  [ring_scatter(): sent = lax.ppermute(piece.astype(jnp.bfloat16), axis, pairs)]
    unnamed x13 -> x12, local copies, waits for them, and re-layouts: 4.28 us -> 1.8 us
    dot_general x1 -> x0, matrix products: 2.45 us -> none  [on_device(): jnp.einsum('bpwq,qc->bpwc', back_filtered, w_back, preferred_element_type...]
    ppermute x2, waiting for transfers between devices: 4.37 us -> 2.32 us  [with_halo(): lax.ppermute(lax.slice_in_dim(block, 0, width, axis=dim), axis, backward)]
    pallas_call x1, Pallas kernels: 9.8 us -> 11.4 us  [run_scatter(): pl.pallas_call(kernel, grid=(members,), in_specs=[smem] * 6 + [pl.BlockSp...]
    ppermute x2, starting transfers between devices: 3.02 us -> 1.45 us  [with_halo(): lax.ppermute(lax.slice_in_dim(block, 0, width, axis=dim), axis, backward)]
    ppermute x2, waiting for transfers between devices: 3.09 us -> 4.56 us  [with_halo(): lax.ppermute(lax.slice_in_dim(block, block.shape[dim] - width, None, axis...]
    ppermute x2, starting transfers between devices: 3.54 us -> 4.96 us  [with_halo(): lax.ppermute(lax.slice_in_dim(block, block.shape[dim] - width, None, axis...]
  transfers between devices with their start and end apart: 13 -> 13, of which waited for: 6 -> 6; matrix products, arithmetic and copies ran while one was open for 16% -> 7% of each run, Pallas kernels for 15% -> 17%
where the time goes in v13:
time: 67.9 us; the launch traced here: 67.7 us
  waiting for transfers between devices  21.2 us (31%)
  starting transfers between devices  17 us (25%)
  Pallas kernels  15.2 us (22%)
  local copies, waits for them, and re-layouts  5.65 us (8%)
  other arithmetic  4.75 us (7%)
  matrix products  2.96 us (4%)
  between operations  0.83 us (1%)
    ppermute x6, waiting for transfers between devices, ring_scatter(): sent = lax.ppermute(piece.astype(jnp.bfloat16), axis, pairs)  14.3 us
    pallas_call x1, Pallas kernels, run_scatter(): pl.pallas_call(kernel, grid=(members,), in_specs=[smem] * 6 + [pl.BlockSp...  11.4 us
    ppermute x6, starting transfers between devices, ring_scatter(): sent = lax.ppermute(piece.astype(jnp.bfloat16), axis, pairs)  7.39 us
    ppermute x2, starting transfers between devices, with_halo(): lax.ppermute(lax.slice_in_dim(block, block.shape[dim] - width, None, axis...  4.96 us
    ppermute x2, waiting for transfers between devices, with_halo(): lax.ppermute(lax.slice_in_dim(block, block.shape[dim] - width, None, axis...  4.56 us
    pallas_call x1, Pallas kernels, run_filter(): pl.pallas_call(kernel, grid=(members, row_count), in_specs=[smem] * 6 + [...  3.79 us
    ppermute x3, starting transfers between devices, ring_sum(): total = total + lax.ppermute(value, axis, pairs)  3.23 us
    ppermute x2, waiting for transfers between devices, with_halo(): lax.ppermute(lax.slice_in_dim(block, 0, width, axis=dim), axis, backward)  2.32 us
  transfers between devices with their start and end apart: 13, of which 6 were waited for; matrix products, arithmetic and copies ran while one was open for 7% of the time, Pallas kernels for 17%

profile of v13, /device:TPU:0, one launch (start us, length us, event | category | flops | bytes accessed | tf_op | source)
XLA Modules:
  0.0 67.7 jit_solution(16458645128188347808)
XLA Ops:
  0.6 0.9 %convert_reduce_fusion = f32[4,256]{1,0:T(4,128)S(1)} fusion(bf16[1,4,64,256]{3,2,1,0:T(8,128)(2,1)} %param.9), kind=kLoop, calls=%fused_computation.24 | loop fusion | flops 130048 | bytes 135168 | tf_op jit(solution)/shard_map/reduce_sum | solution.py:227
  1.6 0.9 %convert_reduce_fusion.1 = f32[4,256]{1,0:T(4,128)S(1)} fusion(bf16[1,4,64,256]{3,2,1,0:T(8,128)(2,1)} %param.8), kind=kLoop, calls=%fused_computation.25 | loop fusion | flops 130048 | bytes 135168 | tf_op jit(solution)/shard_map/reduce_sum | solution.py:227
  2.5 2.4 %collective-permute-start.6 = (f32[2,1,4,256]{3,0,2,1:T(2,128)S(1)}, f32[2,1,4,256]{3,0,2,1:T(2,128)S(1)}, u32[]{:S(2)}, u32[]{:S(2)}) collective-permute-start(f32[2,1,4,256]{3,0,2,1:T(2,128)S(1)} %pad_maximum_fusion.3), channel_id=1, source_target_pairs={{0,3},{1,0},{2,1},{3,2},{4,7},{5,4},{6,5},{7,6},{8,11},{9,8},{10,9... | collective-permute-start | bytes 24584 | tf_op jit(solution)/shard_map/ppermute | solution.py:43
  5.0 0.6 collective-permute-start.5
  5.6 0.2 collective-permute-start.4
  5.8 0.9 %constant_dynamic-update-slice_fusion.1 = bf16[1,4,64,512]{3,2,1,0:T(8,128)(2,1)S(1)} fusion(bf16[1,4,64,256]{3,2,1,0:T(8,128)(2,1)} %param.8), kind=kLoop, calls=%fused_computation.38 | loop fusion | bytes 262144
  6.7 0.9 %constant_dynamic-update-slice_fusion = bf16[1,4,64,512]{3,2,1,0:T(8,128)(2,1)S(1)} fusion(bf16[1,4,64,512]{3,2,1,0:T(8,128)(2,1)S(1)} %constant_dynamic-update-slice_fusion.1, bf16[1,4,64,256]{3,2,1,0:T(8,128)(2,1)} %param.9), kind=kLoop, calls=%fused_computation.37 | loop fusion | bytes 262144 | tf_op jit(solution)/shard_map/concatenate | solution.py:223
  7.6 1.3 %collective-permute-start.1 = (bf16[1,2,64,512]{3,2,1,0:T(8,128)(2,1)S(1)}, bf16[1,2,64,512]{3,2,1,0:T(8,128)(2,1)S(1)}, u32[]{:S(2)}, u32[]{:S(2)}) collective-permute-start(bf16[1,2,64,512]{3,2,1,0:T(8,128)(2,1)S(1)} %get-tuple-element.26), channel_id=1, source_target_pairs={{4,0},{8,4},{12,8},{5,1},{9,5},{13,9},{6,2},{10,6},{14,10},{7,3},{... | collective-permute-start | bytes 393224 | tf_op jit(solution)/shard_map/ppermute | solution.py:26
  8.9 4.6 %collective-permute-start = (bf16[1,2,64,512]{3,2,1,0:T(8,128)(2,1)S(1)}, bf16[1,2,64,512]{3,2,1,0:T(8,128)(2,1)S(1)}, u32[]{:S(2)}, u32[]{:S(2)}) collective-permute-start(bf16[1,2,64,512]{3,2,1,0:T(8,128)(2,1)S(1)} %get-tuple-element.25), channel_id=1, source_target_pairs={{0,4},{4,8},{8,12},{1,5},{5,9},{9,13},{2,6},{6,10},{10,14},{3,7},{... | collective-permute-start | bytes 393224 | tf_op jit(solution)/shard_map/ppermute | solution.py:23
  13.6 1.3 %rsqrt_multiply_fusion.scale_ref = f32[16,12]{1,0:T(8,128)} fusion(f32[16,12]{1,0:T(8,128)} %param.15, s32[16,12]{1,0:T(8,128)} %span_ref.3), kind=kLoop, calls=%fused_computation.36 | loop fusion | flops 384 | bytes 2304 | tf_op jit(solution)/shard_map/div | solution.py:219
  14.9 0.8 %collective-permute-done.1 = bf16[1,2,64,512]{3,2,1,0:T(8,128)(2,1)S(1)} collective-permute-done((bf16[1,2,64,512]{3,2,1,0:T(8,128)(2,1)S(1)}, bf16[1,2,64,512]{3,2,1,0:T(8,128)(2,1)S(1)}, u32[]{:S(2)}, u32[]{:S(2)}) %collective-permute-start.1) | collective-permute-done | bytes 131104 | tf_op jit(solution)/shard_map/ppermute | solution.py:26
  15.6 1.6 %collective-permute-done = bf16[1,2,64,512]{3,2,1,0:T(8,128)(2,1)S(1)} collective-permute-done((bf16[1,2,64,512]{3,2,1,0:T(8,128)(2,1)S(1)}, bf16[1,2,64,512]{3,2,1,0:T(8,128)(2,1)S(1)}, u32[]{:S(2)}, u32[]{:S(2)}) %collective-permute-start) | collective-permute-done | bytes 131104 | tf_op jit(solution)/shard_map/ppermute | solution.py:23
  17.3 0.2 collective-permute-start.3
  17.5 0.4 collective-permute-start.2
  17.9 0.0 collective-permute-done.6
  17.9 0.0 collective-permute-done.5
  17.9 0.0 collective-permute-done.4
  17.9 0.6 fusion.18
  18.5 1.6 %collective-permute-done.3 = bf16[1,8,16,512]{3,2,1,0:T(8,128)(2,1)S(1)} collective-permute-done((bf16[1,8,16,512]{3,2,1,0:T(8,128)(2,1)S(1)}, bf16[1,8,16,512]{3,2,1,0:T(8,128)(2,1)S(1)}, u32[]{:S(2)}, u32[]{:S(2)}) %collective-permute-start.3) | collective-permute-done | bytes 131104 | tf_op jit(solution)/shard_map/ppermute | solution.py:26
  20.1 2.9 %collective-permute-done.2 = bf16[1,8,16,512]{3,2,1,0:T(8,128)(2,1)S(1)} collective-permute-done((bf16[1,8,16,512]{3,2,1,0:T(8,128)(2,1)S(1)}, bf16[1,8,16,512]{3,2,1,0:T(8,128)(2,1)S(1)}, u32[]{:S(2)}, u32[]{:S(2)}) %collective-permute-start.2) | collective-permute-done | bytes 131104 | tf_op jit(solution)/shard_map/ppermute | solution.py:23
  23.0 0.1 fusion.13
  23.1 0.0 copy-start.4
  23.1 1.1 %fusion.19 = (bf16[1,8,128,256]{3,2,1,0:T(8,128)(2,1)}, bf16[1,8,128,256]{3,2,1,0:T(8,128)(2,1)}) fusion(bf16[1,8,128,512]{3,2,1,0:T(8,128)(2,1)S(1)} %fusion.13), kind=kLoop, calls=%fused_computation.39 | loop fusion | bytes 2097152 | tf_op jit(solution)/shard_map/slice | solution.py:225
  24.2 3.8 %shard_map.103 = bf16[1,4,64,2304]{3,2,1,0:T(8,128)(2,1)} custom-call(s32[1]{0:T(128)} %bitcast.first_ref, s32[16,12]{1,0:T(8,128)} %src_ref.3, s32[16,12]{1,0:T(8,128)} %start_ref.3, s32[16,12]{1,0:T(8,128)} %span_ref.3, s32[16,12]{1,0:T(8,128)} %basis_ref.3, f32[16,12]{1,0:T(8,128)} %rsqrt_multiply_fusion.scale_ref, ...), custom_call_target="tpu_custom_call" | custom-call | tf_op jit(solution)/shard_map/pallas_call | solution.py:195
  28.0 0.0 copy-done.4
  28.0 1.8 %convolution_bitcast_fusion = f32[9,256,256]{1,2,0:T(8,128)S(1)} fusion(bf16[4,8,9,8,256]{4,3,2,1,0:T(8,128)(2,1)} %bitcast.32, bf16[1,4,64,256]{3,2,1,0:T(8,128)(2,1)S(1)} %copy-done.4), kind=kOutput, calls=%fused_computation.6 | convolution fusion | flops 301989888 | bytes 3670016 | tf_op jit(solution)/shard_map/brwq,brwo->qo/dot_general | solution.py:240
  29.8 0.0 copy-start
  29.8 1.0 %dynamic-slice_convert_fusion.2 = (bf16[9,256,64]{1,2,0:T(8,128)(2,1)}, bf16[9,256,64]{1,2,0:T(8,128)(2,1)}, bf16[9,256,64]{1,2,0:T(8,128)(2,1)}) fusion(f32[9,256,256]{1,2,0:T(8,128)S(1)} %convolution_bitcast_fusion, s32[]{:T(128)S(6)} %select_n.53, s32[]{:T(128)S(6)} %select_n.57, s32[]{:T(128)S(6)} %select_n.55), kind=kLoop, calls=%fused_computation.19 | loop fusion | bytes 1769484 | tf_op jit(solution)/shard_map/convert_element_type | solution.py:55
  30.8 0.0 collective-permute-start.9
  30.8 1.7 %collective-permute-start.8 = (bf16[9,256,64]{1,2,0:T(8,128)(2,1)}, bf16[9,256,64]{1,2,0:T(8,128)(2,1)}, u32[]{:S(2)}, u32[]{:S(2)}) collective-permute-start(bf16[9,256,64]{1,2,0:T(8,128)(2,1)} %get-tuple-element.17), channel_id=1, source_target_pairs={{0,2},{1,3},{2,0},{3,1},{4,6},{5,7},{6,4},{7,5},{8,10},{9,11},{10,... | collective-permute-start | bytes 884744 | tf_op jit(solution)/shard_map/ppermute | solution.py:55
  32.5 0.0 collective-permute-start.7
  32.5 0.0 copy-start.1
  32.5 5.7 %collective-permute-done.9 = bf16[9,256,64]{1,2,0:T(8,128)(2,1)} collective-permute-done((bf16[9,256,64]{1,2,0:T(8,128)(2,1)}, bf16[9,256,64]{1,2,0:T(8,128)(2,1)}, u32[]{:S(2)}, u32[]{:S(2)}) %collective-permute-start.9) | collective-permute-done | bytes 294944 | tf_op jit(solution)/shard_map/ppermute | solution.py:55
  38.2 8.6 %collective-permute-done.8 = bf16[9,256,64]{1,2,0:T(8,128)(2,1)} collective-permute-done((bf16[9,256,64]{1,2,0:T(8,128)(2,1)}, bf16[9,256,64]{1,2,0:T(8,128)(2,1)}, u32[]{:S(2)}, u32[]{:S(2)}) %collective-permute-start.8) | collective-permute-done | bytes 294944 | tf_op jit(solution)/shard_map/ppermute | solution.py:55
  46.9 0.0 collective-permute-done.7
  46.9 1.3 %convert_add_fusion = f32[9,256,64]{1,2,0:T(8,128)S(1)} fusion(bf16[9,256,64]{1,2,0:T(8,128)(2,1)} %collective-permute-done.9, bf16[9,256,64]{1,2,0:T(8,128)(2,1)} %collective-permute-done.8, bf16[9,256,64]{1,2,0:T(8,128)(2,1)} %collective-permute-done.7, f32[9,256,256]{1,2,0:T(8,128)S(1)} %convolution_bitcast_fusion, s32[]{:T(128)S(6)} %select_n.51), kind=kLoop, calls=%fused_computation.16 | loop fusion | flops 884736 | bytes 2064388 | tf_op jit(solution)/shard_map/add | solution.py:56
  48.1 0.0 copy-start.2
  48.1 0.2 dynamic-slice_convert_fusion.5
  48.3 4.6 %collective-permute-start.12 = (bf16[9,64,64]{1,2,0:T(8,128)(2,1)S(1)}, bf16[9,64,64]{1,2,0:T(8,128)(2,1)S(1)}, u32[]{:S(2)}, u32[]{:S(2)}) collective-permute-start(bf16[9,64,64]{1,2,0:T(8,128)(2,1)S(1)} %get-tuple-element.21), channel_id=1, source_target_pairs={{0,12},{4,0},{8,4},{12,8},{1,13},{5,1},{9,5},{13,9},{2,14},{6,2},{... | collective-permute-start | bytes 221192 | tf_op jit(solution)/shard_map/ppermute | solution.py:55
  53.0 0.0 collective-permute-start.11
  53.0 1.0 %collective-permute-start.10 = (bf16[9,64,64]{1,2,0:T(8,128)(2,1)S(1)}, bf16[9,64,64]{1,2,0:T(8,128)(2,1)S(1)}, u32[]{:S(2)}, u32[]{:S(2)}) collective-permute-start(bf16[9,64,64]{1,2,0:T(8,128)(2,1)S(1)} %get-tuple-element.20), channel_id=1, source_target_pairs={{0,4},{4,8},{8,12},{12,0},{1,5},{5,9},{9,13},{13,1},{2,6},{6,10},{... | collective-permute-start | bytes 221192 | tf_op jit(solution)/shard_map/ppermute | solution.py:55
  54.0 0.0 copy-done
  54.0 0.0 copy-done.1
  54.0 1.2 %fusion.9 = f32[1,4,64,256]{3,2,1,0:T(8,128)} fusion(bf16[2304,256,1]{1,0,2:T(8,128)(2,1)S(1)} %bitcast.33, bf16[1,4,64,2304]{3,2,1,0:T(8,128)(2,1)S(1)} %copy-done), kind=kOutput, calls=%fused_computation.11 | convolution fusion | flops 301989888 | bytes 2621440 | tf_op jit(solution)/shard_map/brwq,qo->brwo/dot_general | solution.py:238
  55.2 0.0 copy-done.2
  55.2 0.0 copy-start.3
  55.2 11.4 %shard_map.104 = f32[1,4,64,256]{3,2,1,0:T(8,128)} custom-call(s32[1]{0:T(128)} %bitcast.first_ref, s32[16,12]{1,0:T(8,128)} %src_ref.3, s32[16,12]{1,0:T(8,128)} %start_ref.3, s32[16,12]{1,0:T(8,128)} %span_ref.3, s32[16,12]{1,0:T(8,128)} %basis_ref.3, f32[16,12]{1,0:T(8,128)} %rsqrt_multiply_fusion.scale_ref, ...), custom_call_target="tpu_custom_call" | custom-call | tf_op jit(solution)/shard_map/pallas_call | solution.py:164
  66.6 0.0 collective-permute-done.12
  66.6 0.0 collective-permute-done.11
  66.6 0.0 collective-permute-done.10
  66.6 0.0 copy-done.3
  66.7 0.2 add_multiply_fusion
  66.8 0.9 %copy.16 = f32[9,64,64]{2,1,0:T(8,128)} copy(f32[9,64,64]{1,2,0:T(8,128)S(1)} %add_multiply_fusion) | data formatting | bytes 294912
  (6 shorter events, 0.1 us)
Async XLA Ops:
  2.5 15.3 %collective-permute-start.6 = (f32[2,1,4,256]{3,0,2,1:T(2,128)S(1)}, f32[2,1,4,256]{3,0,2,1:T(2,128)S(1)}, u32[]{:S(2)}, u32[]{:S(2)}) collective-permute-start(f32[2,1,4,256]{3,0,2,1:T(2,128)S(1)} %pad_maximum_fusion.3), channel_id=1, source_target_pairs={{0,3},{1,0},{2,1},{3,2},{4,7},{5,4},{6,5},{7,6},{8,11},{9,8},{10,9... | collective-permute-start | bytes 24584 | tf_op jit(solution)/shard_map/ppermute | solution.py:43
  5.0 12.9 %collective-permute-start.5 = (f32[2,1,4,256]{3,0,2,1:T(2,128)S(1)}, f32[2,1,4,256]{3,0,2,1:T(2,128)S(1)}, u32[]{:S(2)}, u32[]{:S(2)}) collective-permute-start(f32[2,1,4,256]{3,0,2,1:T(2,128)S(1)} %pad_maximum_fusion.3), channel_id=1, source_target_pairs={{0,2},{1,3},{2,0},{3,1},{4,6},{5,7},{6,4},{7,5},{8,10},{9,11},{10,... | collective-permute-start | bytes 24584 | tf_op jit(solution)/shard_map/ppermute | solution.py:43
  5.6 12.3 %collective-permute-start.4 = (f32[2,1,4,256]{3,0,2,1:T(2,128)S(1)}, f32[2,1,4,256]{3,0,2,1:T(2,128)S(1)}, u32[]{:S(2)}, u32[]{:S(2)}) collective-permute-start(f32[2,1,4,256]{3,0,2,1:T(2,128)S(1)} %pad_maximum_fusion.3), channel_id=1, source_target_pairs={{0,1},{1,2},{2,3},{3,0},{4,5},{5,6},{6,7},{7,4},{8,9},{9,10},{10,1... | collective-permute-start | bytes 24584 | tf_op jit(solution)/shard_map/ppermute | solution.py:43
  7.6 8.0 %collective-permute-start.1 = (bf16[1,2,64,512]{3,2,1,0:T(8,128)(2,1)S(1)}, bf16[1,2,64,512]{3,2,1,0:T(8,128)(2,1)S(1)}, u32[]{:S(2)}, u32[]{:S(2)}) collective-permute-start(bf16[1,2,64,512]{3,2,1,0:T(8,128)(2,1)S(1)} %get-tuple-element.26), channel_id=1, source_target_pairs={{4,0},{8,4},{12,8},{5,1},{9,5},{13,9},{6,2},{10,6},{14,10},{7,3},{... | collective-permute-start | bytes 393224 | tf_op jit(solution)/shard_map/ppermute | solution.py:26
  8.9 8.3 %collective-permute-start = (bf16[1,2,64,512]{3,2,1,0:T(8,128)(2,1)S(1)}, bf16[1,2,64,512]{3,2,1,0:T(8,128)(2,1)S(1)}, u32[]{:S(2)}, u32[]{:S(2)}) collective-permute-start(bf16[1,2,64,512]{3,2,1,0:T(8,128)(2,1)S(1)} %get-tuple-element.25), channel_id=1, source_target_pairs={{0,4},{4,8},{8,12},{1,5},{5,9},{9,13},{2,6},{6,10},{10,14},{3,7},{... | collective-permute-start | bytes 393224 | tf_op jit(solution)/shard_map/ppermute | solution.py:23
  17.3 2.8 %collective-permute-start.3 = (bf16[1,8,16,512]{3,2,1,0:T(8,128)(2,1)S(1)}, bf16[1,8,16,512]{3,2,1,0:T(8,128)(2,1)S(1)}, u32[]{:S(2)}, u32[]{:S(2)}) collective-permute-start(bf16[1,8,16,512]{3,2,1,0:T(8,128)(2,1)S(1)} %get-tuple-element.24), channel_id=1, source_target_pairs={{1,0},{2,1},{3,2},{0,3},{5,4},{6,5},{7,6},{4,7},{9,8},{10,9},{11,1... | collective-permute-start | bytes 393224 | tf_op jit(solution)/shard_map/ppermute | solution.py:26
  17.5 5.5 %collective-permute-start.2 = (bf16[1,8,16,512]{3,2,1,0:T(8,128)(2,1)S(1)}, bf16[1,8,16,512]{3,2,1,0:T(8,128)(2,1)S(1)}, u32[]{:S(2)}, u32[]{:S(2)}) collective-permute-start(bf16[1,8,16,512]{3,2,1,0:T(8,128)(2,1)S(1)} %get-tuple-element.23), channel_id=1, source_target_pairs={{0,1},{1,2},{2,3},{3,0},{4,5},{5,6},{6,7},{7,4},{8,9},{9,10},{10,1... | collective-permute-start | bytes 393224 | tf_op jit(solution)/shard_map/ppermute | solution.py:23
  23.1 4.9 %copy-start.4 = (bf16[1,4,64,256]{3,2,1,0:T(8,128)(2,1)S(1)}, bf16[1,4,64,256]{3,2,1,0:T(8,128)(2,1)}, u32[]{:S(2)}) copy-start(bf16[1,4,64,256]{3,2,1,0:T(8,128)(2,1)} %param.9) | copy-start | bytes 393220
  29.8 24.2 %copy-start = (bf16[1,4,64,2304]{3,2,1,0:T(8,128)(2,1)S(1)}, bf16[1,4,64,2304]{3,2,1,0:T(8,128)(2,1)}, u32[]{:S(2)}) copy-start(bf16[1,4,64,2304]{3,2,1,0:T(8,128)(2,1)} %shard_map.103) | copy-start | bytes 3538948
  30.8 7.4 %collective-permute-start.9 = (bf16[9,256,64]{1,2,0:T(8,128)(2,1)}, bf16[9,256,64]{1,2,0:T(8,128)(2,1)}, u32[]{:S(2)}, u32[]{:S(2)}) collective-permute-start(bf16[9,256,64]{1,2,0:T(8,128)(2,1)} %get-tuple-element.16), channel_id=1, source_target_pairs={{0,3},{1,0},{2,1},{3,2},{4,7},{5,4},{6,5},{7,6},{8,11},{9,8},{10,9... | collective-permute-start | bytes 884744 | tf_op jit(solution)/shard_map/ppermute | solution.py:55
  30.8 16.1 %collective-permute-start.8 = (bf16[9,256,64]{1,2,0:T(8,128)(2,1)}, bf16[9,256,64]{1,2,0:T(8,128)(2,1)}, u32[]{:S(2)}, u32[]{:S(2)}) collective-permute-start(bf16[9,256,64]{1,2,0:T(8,128)(2,1)} %get-tuple-element.17), channel_id=1, source_target_pairs={{0,2},{1,3},{2,0},{3,1},{4,6},{5,7},{6,4},{7,5},{8,10},{9,11},{10,... | collective-permute-start | bytes 884744 | tf_op jit(solution)/shard_map/ppermute | solution.py:55
  32.5 14.3 %collective-permute-start.7 = (bf16[9,256,64]{1,2,0:T(8,128)(2,1)}, bf16[9,256,64]{1,2,0:T(8,128)(2,1)}, u32[]{:S(2)}, u32[]{:S(2)}) collective-permute-start(bf16[9,256,64]{1,2,0:T(8,128)(2,1)} %get-tuple-element.15), channel_id=1, source_target_pairs={{0,1},{1,2},{2,3},{3,0},{4,5},{5,6},{6,7},{7,4},{8,9},{9,10},{10,1... | collective-permute-start | bytes 884744 | tf_op jit(solution)/shard_map/ppermute | solution.py:55
  32.5 21.5 %copy-start.1 = (bf16[9,256,256]{2,1,0:T(8,128)(2,1)S(1)}, bf16[9,256,256]{2,1,0:T(8,128)(2,1)}, u32[]{:S(2)}) copy-start(bf16[9,256,256]{2,1,0:T(8,128)(2,1)} %weight_ref.1) | copy-start | bytes 3538948
  48.1 7.0 %copy-start.2 = (f32[9,256,64]{1,2,0:T(8,128)}, f32[9,256,64]{1,2,0:T(8,128)S(1)}, u32[]{:S(2)}) copy-start(f32[9,256,64]{1,2,0:T(8,128)S(1)} %convert_add_fusion) | copy-start | bytes 1769476
  48.3 18.3 %collective-permute-start.12 = (bf16[9,64,64]{1,2,0:T(8,128)(2,1)S(1)}, bf16[9,64,64]{1,2,0:T(8,128)(2,1)S(1)}, u32[]{:S(2)}, u32[]{:S(2)}) collective-permute-start(bf16[9,64,64]{1,2,0:T(8,128)(2,1)S(1)} %get-tuple-element.21), channel_id=1, source_target_pairs={{0,12},{4,0},{8,4},{12,8},{1,13},{5,1},{9,5},{13,9},{2,14},{6,2},{... | collective-permute-start | bytes 221192 | tf_op jit(solution)/shard_map/ppermute | solution.py:55
  53.0 13.6 %collective-permute-start.11 = (bf16[9,64,64]{1,2,0:T(8,128)(2,1)S(1)}, bf16[9,64,64]{1,2,0:T(8,128)(2,1)S(1)}, u32[]{:S(2)}, u32[]{:S(2)}) collective-permute-start(bf16[9,64,64]{1,2,0:T(8,128)(2,1)S(1)} %get-tuple-element.22), channel_id=1, source_target_pairs={{0,8},{4,12},{8,0},{12,4},{1,9},{5,13},{9,1},{13,5},{2,10},{6,14},... | collective-permute-start | bytes 221192 | tf_op jit(solution)/shard_map/ppermute | solution.py:55
  53.0 13.6 %collective-permute-start.10 = (bf16[9,64,64]{1,2,0:T(8,128)(2,1)S(1)}, bf16[9,64,64]{1,2,0:T(8,128)(2,1)S(1)}, u32[]{:S(2)}, u32[]{:S(2)}) collective-permute-start(bf16[9,64,64]{1,2,0:T(8,128)(2,1)S(1)} %get-tuple-element.20), channel_id=1, source_target_pairs={{0,4},{4,8},{8,12},{12,0},{1,5},{5,9},{9,13},{13,1},{2,6},{6,10},{... | collective-permute-start | bytes 221192 | tf_op jit(solution)/shard_map/ppermute | solution.py:55
  55.2 11.5 %copy-start.3 = (f32[9,256,64]{1,2,0:T(8,128)S(1)}, f32[9,256,64]{1,2,0:T(8,128)}, u32[]{:S(2)}) copy-start(f32[9,256,64]{1,2,0:T(8,128)} %copy-done.2) | copy-start | bytes 1769476

commit v14 on v12

--- a/solution.py
+++ b/solution.py
@@ -148,8 +148,9 @@
             )
 
 
-def run_scatter(first, tables, field, totals, row_count, lon_count, lon_total):
-    members, window, padded, channels = field.shape
+def run_scatter(first, tables, field, totals, row_count, lon_count, lon_total, part=0):
+    members, window, padded, combined = field.shape
+    channels = totals.shape[-1]
     height, slots = tables[0].shape
     smem = pl.BlockSpec(memory_space=pltpu.SMEM)
     kernel = functools.partial(
@@ -160,7 +161,7 @@
         grid=(members,),
         in_specs=[smem] * 6
         + [
-            pl.BlockSpec((1, window, padded, channels), lambda b: (b, 0, 0, 0)),
+            pl.BlockSpec((1, window, padded, channels), lambda b: (b, 0, 0, part)),
             pl.BlockSpec((1, window, 1, channels), lambda b: (b, 0, 0, 0)),
         ],
         out_specs=pl.BlockSpec(
@@ -173,8 +174,11 @@
     )(first, *tables, field, totals[:, :, None, :])
 
 
-def run_filter(first, tables, field, totals, row_count, lon_count, lon_total, backward):
-    members, window, padded, channels = field.shape
+def run_filter(
+    first, tables, field, totals, row_count, lon_count, lon_total, backward, part=0
+):
+    members, window, padded, combined = field.shape
+    channels = totals.shape[-1]
     height, slots = tables[0].shape
     smem = pl.BlockSpec(memory_space=pltpu.SMEM)
     kernel = functools.partial(
@@ -190,7 +194,7 @@
         grid=(members, row_count),
         in_specs=[smem] * 6
         + [
-            pl.BlockSpec((1, window, padded, channels), lambda b, r: (b, 0, 0, 0)),
+            pl.BlockSpec((1, window, padded, channels), lambda b, r: (b, 0, 0, part)),
             pl.BlockSpec((1, window, 1, channels), lambda b, r: (b, 0, 0, 0)),
         ],
         out_specs=pl.BlockSpec(
@@ -214,8 +218,6 @@
     tables = (src_rows, lon_start, lon_span, basis_idx, weighting)
 
     both = extend(jnp.concatenate([inputs, cotangent], axis=3), padded)
-    widened = both[..., :channels]
-    grad_wide = both[..., channels:]
     row_sums = jnp.stack(
         [jnp.sum(inputs, axis=2, dtype=jnp.float32), jnp.sum(cotangent, axis=2, dtype=jnp.float32)]
     )
@@ -226,7 +228,7 @@
         framed = with_halo(local_totals, (("lat", 2),), REACH, False)
     totals, grad_totals = framed[0], framed[1]
 
-    flattened = run_filter(first, tables, widened, totals, row_count, lon_count, lon_total, False)
+    flattened = run_filter(first, tables, both, totals, row_count, lon_count, lon_total, False, 0)
     w_fwd = weight.reshape(BASIS * channels, channels)
     response = jnp.einsum("brwq,qo->brwo", flattened, w_fwd, preferred_element_type=jnp.float32)
 
@@ -235,10 +237,10 @@
     )
     partial_value = partial_value.reshape(BASIS, channels, channels)
     reduced = ring_scatter(partial_value, "lon", 2)
-    grad_wide, grad_totals, reduced = lax.optimization_barrier((grad_wide, grad_totals, reduced))
+    both, grad_totals, reduced = lax.optimization_barrier((both, grad_totals, reduced))
     reduced = ring_scatter(reduced, "lat", 1)
     back_filtered = run_scatter(
-        first, tables, grad_wide, grad_totals, row_count, lon_count, lon_total
+        first, tables, both, grad_totals, row_count, lon_count, lon_total, 1
     )
     w_back = jnp.transpose(weight, (0, 2, 1)).reshape(BASIS * channels, channels)
     grad_input = jnp.einsum(

time: 67.5 us -> 67.4 us (level)
  local copies, waits for them, and re-layouts: 8.08 us -> 6.97 us
  other arithmetic: 4.05 us -> 5.03 us
    slice x1 -> x0, local copies, waits for them, and re-layouts: 1.1 us -> none  [on_device(): grad_wide = both[..., channels:]]
    concatenate x1, other arithmetic: 0.09 us -> 1.07 us  [with_halo(): block = jnp.concatenate([low, block, high], axis=dim)]
where the time goes in v14:
time: 67.4 us; the launch traced here: 66.8 us
  starting transfers between devices  18.6 us (28%)
  waiting for transfers between devices  14.5 us (22%)
  Pallas kernels  14.2 us (21%)
  local copies, waits for them, and re-layouts  6.97 us (10%)
  matrix products  6.69 us (10%)
  other arithmetic  5.03 us (7%)
  between operations  0.83 us (1%)
    pallas_call x1, Pallas kernels, run_scatter(): pl.pallas_call(kernel, grid=(members,), in_specs=[smem] * 6 + [pl.BlockSp...  10.2 us
    ppermute x6, starting transfers between devices, ring_scatter(): sent = lax.ppermute(piece.astype(jnp.bfloat16), axis, pairs)  7.57 us
    ppermute x6, waiting for transfers between devices, ring_scatter(): sent = lax.ppermute(piece.astype(jnp.bfloat16), axis, pairs)  7.08 us
    ppermute x3, starting transfers between devices, ring_sum(): total = total + lax.ppermute(value, axis, pairs)  4.46 us
    ppermute x2, waiting for transfers between devices, with_halo(): lax.ppermute(lax.slice_in_dim(block, 0, width, axis=dim), axis, backward)  4.37 us
    unnamed x13, local copies, waits for them, and re-layouts  4.26 us
    pallas_call x1, Pallas kernels, run_filter(): pl.pallas_call(kernel, grid=(members, row_count), in_specs=[smem] * 6 + [...  3.92 us
    ppermute x2, starting transfers between devices, with_halo(): lax.ppermute(lax.slice_in_dim(block, block.shape[dim] - width, None, axis...  3.54 us
  transfers between devices with their start and end apart: 13, of which 6 were waited for; matrix products, arithmetic and copies ran while one was open for 16% of the time, Pallas kernels for 15%

profile of v14, /device:TPU:0, one launch (start us, length us, event | category | flops | bytes accessed | tf_op | source)
XLA Modules:
  0.0 66.8 jit_solution(7454633792371590457)
XLA Ops:
  0.6 0.0 copy-start.3
  0.6 0.0 copy-start.4
  0.7 0.9 %convert_reduce_fusion = f32[4,256]{1,0:T(4,128)S(1)} fusion(bf16[1,4,64,256]{3,2,1,0:T(8,128)(2,1)} %param.9), kind=kLoop, calls=%fused_computation.27 | loop fusion | flops 130048 | bytes 135168 | tf_op jit(solution)/shard_map/reduce_sum | solution.py:222
  1.6 0.9 %convert_reduce_fusion.1 = f32[4,256]{1,0:T(4,128)S(1)} fusion(bf16[1,4,64,256]{3,2,1,0:T(8,128)(2,1)} %param.8), kind=kLoop, calls=%fused_computation.28 | loop fusion | flops 130048 | bytes 135168 | tf_op jit(solution)/shard_map/reduce_sum | solution.py:222
  2.6 0.5 collective-permute-start.4
  3.1 2.6 %collective-permute-start.5 = (f32[2,1,4,256]{3,0,2,1:T(2,128)S(1)}, f32[2,1,4,256]{3,0,2,1:T(2,128)S(1)}, u32[]{:S(2)}, u32[]{:S(2)}) collective-permute-start(f32[2,1,4,256]{3,0,2,1:T(2,128)S(1)} %pad_maximum_fusion.3), channel_id=1, source_target_pairs={{0,2},{1,3},{2,0},{3,1},{4,6},{5,7},{6,4},{7,5},{8,10},{9,11},{10,... | collective-permute-start | bytes 24584 | tf_op jit(solution)/shard_map/ppermute | solution.py:43
  5.7 1.4 %collective-permute-start.6 = (f32[2,1,4,256]{3,0,2,1:T(2,128)S(1)}, f32[2,1,4,256]{3,0,2,1:T(2,128)S(1)}, u32[]{:S(2)}, u32[]{:S(2)}) collective-permute-start(f32[2,1,4,256]{3,0,2,1:T(2,128)S(1)} %pad_maximum_fusion.3), channel_id=1, source_target_pairs={{0,3},{1,0},{2,1},{3,2},{4,7},{5,4},{6,5},{7,6},{8,11},{9,8},{10,9... | collective-permute-start | bytes 24584 | tf_op jit(solution)/shard_map/ppermute | solution.py:43
  7.0 0.9 %constant_dynamic-update-slice_fusion.1 = bf16[1,4,64,512]{3,2,1,0:T(8,128)(2,1)S(1)} fusion(bf16[1,4,64,256]{3,2,1,0:T(8,128)(2,1)} %param.8), kind=kLoop, calls=%fused_computation.41 | loop fusion | bytes 262144
  8.0 0.9 %constant_dynamic-update-slice_fusion = bf16[1,4,64,512]{3,2,1,0:T(8,128)(2,1)S(1)} fusion(bf16[1,4,64,512]{3,2,1,0:T(8,128)(2,1)S(1)} %constant_dynamic-update-slice_fusion.1, bf16[1,4,64,256]{3,2,1,0:T(8,128)(2,1)} %param.9), kind=kLoop, calls=%fused_computation.40 | loop fusion | bytes 262144 | tf_op jit(solution)/shard_map/concatenate | solution.py:220
  8.9 3.5 %collective-permute-start = (bf16[1,2,64,512]{3,2,1,0:T(8,128)(2,1)S(1)}, bf16[1,2,64,512]{3,2,1,0:T(8,128)(2,1)S(1)}, u32[]{:S(2)}, u32[]{:S(2)}) collective-permute-start(bf16[1,2,64,512]{3,2,1,0:T(8,128)(2,1)S(1)} %get-tuple-element.23), channel_id=1, source_target_pairs={{0,4},{4,8},{8,12},{1,5},{5,9},{9,13},{2,6},{6,10},{10,14},{3,7},{... | collective-permute-start | bytes 393224 | tf_op jit(solution)/shard_map/ppermute | solution.py:23
  12.4 1.3 %collective-permute-start.1 = (bf16[1,2,64,512]{3,2,1,0:T(8,128)(2,1)S(1)}, bf16[1,2,64,512]{3,2,1,0:T(8,128)(2,1)S(1)}, u32[]{:S(2)}, u32[]{:S(2)}) collective-permute-start(bf16[1,2,64,512]{3,2,1,0:T(8,128)(2,1)S(1)} %get-tuple-element.24), channel_id=1, source_target_pairs={{4,0},{8,4},{12,8},{5,1},{9,5},{13,9},{6,2},{10,6},{14,10},{7,3},{... | collective-permute-start | bytes 393224 | tf_op jit(solution)/shard_map/ppermute | solution.py:26
  13.7 0.0 copy-done.3
  13.8 0.0 copy-done.4
  13.8 0.6 rsqrt_multiply_fusion.scale_ref
  14.4 0.5 collective-permute-done
  14.9 4.4 %collective-permute-done.1 = bf16[1,2,64,512]{3,2,1,0:T(8,128)(2,1)S(1)} collective-permute-done((bf16[1,2,64,512]{3,2,1,0:T(8,128)(2,1)S(1)}, bf16[1,2,64,512]{3,2,1,0:T(8,128)(2,1)S(1)}, u32[]{:S(2)}, u32[]{:S(2)}) %collective-permute-start.1) | collective-permute-done | bytes 131104 | tf_op jit(solution)/shard_map/ppermute | solution.py:26
  19.3 0.1 collective-permute-start.2
  19.3 1.7 %collective-permute-start.3 = (bf16[1,8,16,512]{3,2,1,0:T(8,128)(2,1)S(1)}, bf16[1,8,16,512]{3,2,1,0:T(8,128)(2,1)S(1)}, u32[]{:S(2)}, u32[]{:S(2)}) collective-permute-start(bf16[1,8,16,512]{3,2,1,0:T(8,128)(2,1)S(1)} %get-tuple-element.22), channel_id=1, source_target_pairs={{1,0},{2,1},{3,2},{0,3},{5,4},{6,5},{7,6},{4,7},{9,8},{10,9},{11,1... | collective-permute-start | bytes 393224 | tf_op jit(solution)/shard_map/ppermute | solution.py:26
  21.1 0.0 collective-permute-done.4
  21.1 0.0 collective-permute-done.5
  21.1 0.0 collective-permute-done.6
  21.1 0.6 fusion.23
  21.7 2.6 %collective-permute-done.2 = bf16[1,8,16,512]{3,2,1,0:T(8,128)(2,1)S(1)} collective-permute-done((bf16[1,8,16,512]{3,2,1,0:T(8,128)(2,1)S(1)}, bf16[1,8,16,512]{3,2,1,0:T(8,128)(2,1)S(1)}, u32[]{:S(2)}, u32[]{:S(2)}) %collective-permute-start.2) | collective-permute-done | bytes 131104 | tf_op jit(solution)/shard_map/ppermute | solution.py:23
  24.3 0.0 collective-permute-done.3
  24.3 1.1 %fusion.18.field_ref = bf16[1,8,128,512]{3,2,1,0:T(8,128)(2,1)} fusion(bf16[1,8,16,512]{3,2,1,0:T(8,128)(2,1)S(1)} %collective-permute-done.3, bf16[1,8,16,512]{3,2,1,0:T(8,128)(2,1)S(1)} %collective-permute-done.2, bf16[1,2,64,512]{3,2,1,0:T(8,128)(2,1)S(1)} %collective-permute-done.1, bf16[1,4,64,512]{3,2,1,0:T(8,128)(2,1)S(1)} %constant_dynamic-update-slice_fusion, ...), kind=kLoop, calls=%fused_computation.16 | loop fusion | flops 8388608 | bytes 1835008 | tf_op jit(solution)/shard_map/concatenate | solution.py:27
  25.4 0.0 copy-start.2
  25.4 3.9 %shard_map.103 = bf16[1,4,64,2304]{3,2,1,0:T(8,128)(2,1)} custom-call(s32[1]{0:T(128)} %bitcast.first_ref, s32[16,12]{1,0:T(8,128)} %src_ref.3, s32[16,12]{1,0:T(8,128)} %start_ref.3, s32[16,12]{1,0:T(8,128)} %span_ref.3, s32[16,12]{1,0:T(8,128)} %basis_ref.3, f32[16,12]{1,0:T(8,128)} %rsqrt_multiply_fusion.scale_ref, ...), custom_call_target="tpu_custom_call" | custom-call | tf_op jit(solution)/shard_map/pallas_call | solution.py:192
  29.3 0.0 copy-done.2
  29.3 1.8 %convolution_bitcast_fusion = f32[9,256,256]{1,2,0:T(8,128)S(1)} fusion(bf16[4,8,9,8,256]{4,3,2,1,0:T(8,128)(2,1)} %bitcast.45, bf16[1,4,64,256]{3,2,1,0:T(8,128)(2,1)S(1)} %copy-done.2), kind=kOutput, calls=%fused_computation.6 | convolution fusion | flops 301989888 | bytes 3670016 | tf_op jit(solution)/shard_map/brwq,brwo->qo/dot_general | solution.py:235
  31.1 0.9 %dynamic-slice_convert_fusion.2 = (bf16[9,256,64]{1,2,0:T(8,128)(2,1)}, bf16[9,256,64]{1,2,0:T(8,128)(2,1)}, bf16[9,256,64]{1,2,0:T(8,128)(2,1)}) fusion(f32[9,256,256]{1,2,0:T(8,128)S(1)} %convolution_bitcast_fusion, s32[]{:T(128)S(6)} %select_n.53, s32[]{:T(128)S(6)} %select_n.57, s32[]{:T(128)S(6)} %select_n.55), kind=kLoop, calls=%fused_computation.22 | loop fusion | bytes 1769484 | tf_op jit(solution)/shard_map/convert_element_type | solution.py:55
  32.0 0.6 collective-permute-start.7
  32.7 0.9 %collective-permute-start.8 = (bf16[9,256,64]{1,2,0:T(8,128)(2,1)}, bf16[9,256,64]{1,2,0:T(8,128)(2,1)}, u32[]{:S(2)}, u32[]{:S(2)}) collective-permute-start(bf16[9,256,64]{1,2,0:T(8,128)(2,1)} %get-tuple-element.17), channel_id=1, source_target_pairs={{0,2},{1,3},{2,0},{3,1},{4,6},{5,7},{6,4},{7,5},{8,10},{9,11},{10,... | collective-permute-start | bytes 884744 | tf_op jit(solution)/shard_map/ppermute | solution.py:55
  33.6 0.4 collective-permute-start.9
  34.0 0.0 copy-start
  34.0 2.5 %copy.16 = bf16[9,256,256]{1,2,0:T(8,128)(2,1)} copy(bf16[9,256,256]{2,1,0:T(8,128)(2,1)} %param.10) | data formatting | bytes 2359296 | tf_op args[2]
  36.5 0.0 copy-done
  36.5 2.5 %fusion.11 = f32[1,4,64,256]{3,2,1,0:T(8,128)} fusion(bf16[2304,256,1]{1,0,2:T(8,128)(2,1)} %bitcast.46, bf16[1,4,64,2304]{3,2,1,0:T(8,128)(2,1)S(1)} %copy-done), kind=kOutput, calls=%fused_computation.13 | convolution fusion | flops 301989888 | bytes 2621440 | tf_op jit(solution)/shard_map/brwq,qo->brwo/dot_general | solution.py:233
  39.0 1.5 %collective-permute-done.7 = bf16[9,256,64]{1,2,0:T(8,128)(2,1)} collective-permute-done((bf16[9,256,64]{1,2,0:T(8,128)(2,1)}, bf16[9,256,64]{1,2,0:T(8,128)(2,1)}, u32[]{:S(2)}, u32[]{:S(2)}) %collective-permute-start.7) | collective-permute-done | bytes 294944 | tf_op jit(solution)/shard_map/ppermute | solution.py:55
  40.4 2.5 %collective-permute-done.8 = bf16[9,256,64]{1,2,0:T(8,128)(2,1)} collective-permute-done((bf16[9,256,64]{1,2,0:T(8,128)(2,1)}, bf16[9,256,64]{1,2,0:T(8,128)(2,1)}, u32[]{:S(2)}, u32[]{:S(2)}) %collective-permute-start.8) | collective-permute-done | bytes 294944 | tf_op jit(solution)/shard_map/ppermute | solution.py:55
  42.9 3.1 %collective-permute-done.9 = bf16[9,256,64]{1,2,0:T(8,128)(2,1)} collective-permute-done((bf16[9,256,64]{1,2,0:T(8,128)(2,1)}, bf16[9,256,64]{1,2,0:T(8,128)(2,1)}, u32[]{:S(2)}, u32[]{:S(2)}) %collective-permute-start.9) | collective-permute-done | bytes 294944 | tf_op jit(solution)/shard_map/ppermute | solution.py:55
  46.0 1.3 %convert_add_fusion = f32[9,256,64]{1,2,0:T(8,128)S(1)} fusion(bf16[9,256,64]{1,2,0:T(8,128)(2,1)} %collective-permute-done.9, bf16[9,256,64]{1,2,0:T(8,128)(2,1)} %collective-permute-done.8, bf16[9,256,64]{1,2,0:T(8,128)(2,1)} %collective-permute-done.7, f32[9,256,256]{1,2,0:T(8,128)S(1)} %convolution_bitcast_fusion, s32[]{:T(128)S(6)} %select_n.51), kind=kLoop, calls=%fused_computation.19 | loop fusion | flops 884736 | bytes 2064388 | tf_op jit(solution)/shard_map/add | solution.py:56
  47.3 0.2 dynamic-slice_convert_fusion.5
  47.5 0.0 copy-start.1
  47.5 1.6 %collective-permute-start.10 = (bf16[9,64,64]{1,2,0:T(8,128)(2,1)S(1)}, bf16[9,64,64]{1,2,0:T(8,128)(2,1)S(1)}, u32[]{:S(2)}, u32[]{:S(2)}) collective-permute-start(bf16[9,64,64]{1,2,0:T(8,128)(2,1)S(1)} %get-tuple-element.18), channel_id=1, source_target_pairs={{0,4},{4,8},{8,12},{12,0},{1,5},{5,9},{9,13},{13,1},{2,6},{6,10},{... | collective-permute-start | bytes 221192 | tf_op jit(solution)/shard_map/ppermute | solution.py:55
  49.1 1.1 %collective-permute-start.11 = (bf16[9,64,64]{1,2,0:T(8,128)(2,1)S(1)}, bf16[9,64,64]{1,2,0:T(8,128)(2,1)S(1)}, u32[]{:S(2)}, u32[]{:S(2)}) collective-permute-start(bf16[9,64,64]{1,2,0:T(8,128)(2,1)S(1)} %get-tuple-element.20), channel_id=1, source_target_pairs={{0,8},{4,12},{8,0},{12,4},{1,9},{5,13},{9,1},{13,5},{2,10},{6,14},... | collective-permute-start | bytes 221192 | tf_op jit(solution)/shard_map/ppermute | solution.py:55
  50.2 2.8 %collective-permute-start.12 = (bf16[9,64,64]{1,2,0:T(8,128)(2,1)S(1)}, bf16[9,64,64]{1,2,0:T(8,128)(2,1)S(1)}, u32[]{:S(2)}, u32[]{:S(2)}) collective-permute-start(bf16[9,64,64]{1,2,0:T(8,128)(2,1)S(1)} %get-tuple-element.19), channel_id=1, source_target_pairs={{0,12},{4,0},{8,4},{12,8},{1,13},{5,1},{9,5},{13,9},{2,14},{6,2},{... | collective-permute-start | bytes 221192 | tf_op jit(solution)/shard_map/ppermute | solution.py:55
  53.1 10.2 %shard_map.104 = bf16[1,4,64,2304]{3,2,1,0:T(8,128)(2,1)} custom-call(s32[1]{0:T(128)} %bitcast.first_ref, s32[16,12]{1,0:T(8,128)} %src_ref.3, s32[16,12]{1,0:T(8,128)} %start_ref.3, s32[16,12]{1,0:T(8,128)} %span_ref.3, s32[16,12]{1,0:T(8,128)} %basis_ref.3, f32[16,12]{1,0:T(8,128)} %rsqrt_multiply_fusion.scale_ref, ...), custom_call_target="tpu_custom_call" | custom-call | tf_op jit(solution)/shard_map/pallas_call | solution.py:159
  63.3 0.0 copy-done.1
  63.3 2.5 %fusion.14 = f32[1,4,64,256]{3,2,1,0:T(8,128)} fusion(bf16[2304,256,1]{1,0,2:T(8,128)(2,1)S(1)} %bitcast.47, bf16[1,4,64,2304]{3,2,1,0:T(8,128)(2,1)} %shard_map.104), kind=kOutput, calls=%fused_computation.14 | convolution fusion | flops 301989888 | bytes 2621440 | tf_op jit(solution)/shard_map/bpwq,qc->bpwc/dot_general | solution.py:246
  65.8 0.0 collective-permute-done.10
  65.8 0.0 collective-permute-done.11
  65.8 0.0 collective-permute-done.12
  65.8 0.2 add_multiply_fusion
  66.0 0.9 %copy.17 = f32[9,64,64]{2,1,0:T(8,128)} copy(f32[9,64,64]{1,2,0:T(8,128)S(1)} %add_multiply_fusion) | data formatting | bytes 294912
  (6 shorter events, 0.1 us)
Async XLA Ops:
  0.6 13.1 %copy-start.3 = (s32[16,12]{1,0:T(8,128)S(1)}, s32[16,12]{1,0:T(8,128)}, u32[]{:S(2)}) copy-start(s32[16,12]{1,0:T(8,128)} %span_ref.3) | copy-start | bytes 2308
  0.6 13.1 %copy-start.4 = (f32[16,12]{1,0:T(8,128)S(1)}, f32[16,12]{1,0:T(8,128)}, u32[]{:S(2)}) copy-start(f32[16,12]{1,0:T(8,128)} %param.15) | copy-start | bytes 2308
  2.6 18.5 %collective-permute-start.4 = (f32[2,1,4,256]{3,0,2,1:T(2,128)S(1)}, f32[2,1,4,256]{3,0,2,1:T(2,128)S(1)}, u32[]{:S(2)}, u32[]{:S(2)}) collective-permute-start(f32[2,1,4,256]{3,0,2,1:T(2,128)S(1)} %pad_maximum_fusion.3), channel_id=1, source_target_pairs={{0,1},{1,2},{2,3},{3,0},{4,5},{5,6},{6,7},{7,4},{8,9},{9,10},{10,1... | collective-permute-start | bytes 24584 | tf_op jit(solution)/shard_map/ppermute | solution.py:43
  3.1 18.0 %collective-permute-start.5 = (f32[2,1,4,256]{3,0,2,1:T(2,128)S(1)}, f32[2,1,4,256]{3,0,2,1:T(2,128)S(1)}, u32[]{:S(2)}, u32[]{:S(2)}) collective-permute-start(f32[2,1,4,256]{3,0,2,1:T(2,128)S(1)} %pad_maximum_fusion.3), channel_id=1, source_target_pairs={{0,2},{1,3},{2,0},{3,1},{4,6},{5,7},{6,4},{7,5},{8,10},{9,11},{10,... | collective-permute-start | bytes 24584 | tf_op jit(solution)/shard_map/ppermute | solution.py:43
  5.7 15.4 %collective-permute-start.6 = (f32[2,1,4,256]{3,0,2,1:T(2,128)S(1)}, f32[2,1,4,256]{3,0,2,1:T(2,128)S(1)}, u32[]{:S(2)}, u32[]{:S(2)}) collective-permute-start(f32[2,1,4,256]{3,0,2,1:T(2,128)S(1)} %pad_maximum_fusion.3), channel_id=1, source_target_pairs={{0,3},{1,0},{2,1},{3,2},{4,7},{5,4},{6,5},{7,6},{8,11},{9,8},{10,9... | collective-permute-start | bytes 24584 | tf_op jit(solution)/shard_map/ppermute | solution.py:43
  8.9 6.0 %collective-permute-start = (bf16[1,2,64,512]{3,2,1,0:T(8,128)(2,1)S(1)}, bf16[1,2,64,512]{3,2,1,0:T(8,128)(2,1)S(1)}, u32[]{:S(2)}, u32[]{:S(2)}) collective-permute-start(bf16[1,2,64,512]{3,2,1,0:T(8,128)(2,1)S(1)} %get-tuple-element.23), channel_id=1, source_target_pairs={{0,4},{4,8},{8,12},{1,5},{5,9},{9,13},{2,6},{6,10},{10,14},{3,7},{... | collective-permute-start | bytes 393224 | tf_op jit(solution)/shard_map/ppermute | solution.py:23
  12.4 6.9 %collective-permute-start.1 = (bf16[1,2,64,512]{3,2,1,0:T(8,128)(2,1)S(1)}, bf16[1,2,64,512]{3,2,1,0:T(8,128)(2,1)S(1)}, u32[]{:S(2)}, u32[]{:S(2)}) collective-permute-start(bf16[1,2,64,512]{3,2,1,0:T(8,128)(2,1)S(1)} %get-tuple-element.24), channel_id=1, source_target_pairs={{4,0},{8,4},{12,8},{5,1},{9,5},{13,9},{6,2},{10,6},{14,10},{7,3},{... | collective-permute-start | bytes 393224 | tf_op jit(solution)/shard_map/ppermute | solution.py:26
  19.3 5.0 %collective-permute-start.2 = (bf16[1,8,16,512]{3,2,1,0:T(8,128)(2,1)S(1)}, bf16[1,8,16,512]{3,2,1,0:T(8,128)(2,1)S(1)}, u32[]{:S(2)}, u32[]{:S(2)}) collective-permute-start(bf16[1,8,16,512]{3,2,1,0:T(8,128)(2,1)S(1)} %get-tuple-element.21), channel_id=1, source_target_pairs={{0,1},{1,2},{2,3},{3,0},{4,5},{5,6},{6,7},{7,4},{8,9},{9,10},{10,1... | collective-permute-start | bytes 393224 | tf_op jit(solution)/shard_map/ppermute | solution.py:23
  19.3 5.0 %collective-permute-start.3 = (bf16[1,8,16,512]{3,2,1,0:T(8,128)(2,1)S(1)}, bf16[1,8,16,512]{3,2,1,0:T(8,128)(2,1)S(1)}, u32[]{:S(2)}, u32[]{:S(2)}) collective-permute-start(bf16[1,8,16,512]{3,2,1,0:T(8,128)(2,1)S(1)} %get-tuple-element.22), channel_id=1, source_target_pairs={{1,0},{2,1},{3,2},{0,3},{5,4},{6,5},{7,6},{4,7},{9,8},{10,9},{11,1... | collective-permute-start | bytes 393224 | tf_op jit(solution)/shard_map/ppermute | solution.py:26
  25.4 3.9 %copy-start.2 = (bf16[1,4,64,256]{3,2,1,0:T(8,128)(2,1)S(1)}, bf16[1,4,64,256]{3,2,1,0:T(8,128)(2,1)}, u32[]{:S(2)}) copy-start(bf16[1,4,64,256]{3,2,1,0:T(8,128)(2,1)} %param.9) | copy-start | bytes 393220
  32.0 8.4 %collective-permute-start.7 = (bf16[9,256,64]{1,2,0:T(8,128)(2,1)}, bf16[9,256,64]{1,2,0:T(8,128)(2,1)}, u32[]{:S(2)}, u32[]{:S(2)}) collective-permute-start(bf16[9,256,64]{1,2,0:T(8,128)(2,1)} %get-tuple-element.15), channel_id=1, source_target_pairs={{0,1},{1,2},{2,3},{3,0},{4,5},{5,6},{6,7},{7,4},{8,9},{9,10},{10,1... | collective-permute-start | bytes 884744 | tf_op jit(solution)/shard_map/ppermute | solution.py:55
  32.7 10.2 %collective-permute-start.8 = (bf16[9,256,64]{1,2,0:T(8,128)(2,1)}, bf16[9,256,64]{1,2,0:T(8,128)(2,1)}, u32[]{:S(2)}, u32[]{:S(2)}) collective-permute-start(bf16[9,256,64]{1,2,0:T(8,128)(2,1)} %get-tuple-element.17), channel_id=1, source_target_pairs={{0,2},{1,3},{2,0},{3,1},{4,6},{5,7},{6,4},{7,5},{8,10},{9,11},{10,... | collective-permute-start | bytes 884744 | tf_op jit(solution)/shard_map/ppermute | solution.py:55
  33.6 12.4 %collective-permute-start.9 = (bf16[9,256,64]{1,2,0:T(8,128)(2,1)}, bf16[9,256,64]{1,2,0:T(8,128)(2,1)}, u32[]{:S(2)}, u32[]{:S(2)}) collective-permute-start(bf16[9,256,64]{1,2,0:T(8,128)(2,1)} %get-tuple-element.16), channel_id=1, source_target_pairs={{0,3},{1,0},{2,1},{3,2},{4,7},{5,4},{6,5},{7,6},{8,11},{9,8},{10,9... | collective-permute-start | bytes 884744 | tf_op jit(solution)/shard_map/ppermute | solution.py:55
  34.0 2.5 %copy-start = (bf16[1,4,64,2304]{3,2,1,0:T(8,128)(2,1)S(1)}, bf16[1,4,64,2304]{3,2,1,0:T(8,128)(2,1)}, u32[]{:S(2)}) copy-start(bf16[1,4,64,2304]{3,2,1,0:T(8,128)(2,1)} %shard_map.103) | copy-start | bytes 3538948
  47.5 15.8 %copy-start.1 = (bf16[9,256,256]{1,2,0:T(8,128)(2,1)S(1)}, bf16[9,256,256]{1,2,0:T(8,128)(2,1)}, u32[]{:S(2)}) copy-start(bf16[9,256,256]{1,2,0:T(8,128)(2,1)} %copy.16) | copy-start | bytes 3538948
  47.5 18.3 %collective-permute-start.10 = (bf16[9,64,64]{1,2,0:T(8,128)(2,1)S(1)}, bf16[9,64,64]{1,2,0:T(8,128)(2,1)S(1)}, u32[]{:S(2)}, u32[]{:S(2)}) collective-permute-start(bf16[9,64,64]{1,2,0:T(8,128)(2,1)S(1)} %get-tuple-element.18), channel_id=1, source_target_pairs={{0,4},{4,8},{8,12},{12,0},{1,5},{5,9},{9,13},{13,1},{2,6},{6,10},{... | collective-permute-start | bytes 221192 | tf_op jit(solution)/shard_map/ppermute | solution.py:55
  49.1 16.6 %collective-permute-start.11 = (bf16[9,64,64]{1,2,0:T(8,128)(2,1)S(1)}, bf16[9,64,64]{1,2,0:T(8,128)(2,1)S(1)}, u32[]{:S(2)}, u32[]{:S(2)}) collective-permute-start(bf16[9,64,64]{1,2,0:T(8,128)(2,1)S(1)} %get-tuple-element.20), channel_id=1, source_target_pairs={{0,8},{4,12},{8,0},{12,4},{1,9},{5,13},{9,1},{13,5},{2,10},{6,14},... | collective-permute-start | bytes 221192 | tf_op jit(solution)/shard_map/ppermute | solution.py:55
  50.2 15.6 %collective-permute-start.12 = (bf16[9,64,64]{1,2,0:T(8,128)(2,1)S(1)}, bf16[9,64,64]{1,2,0:T(8,128)(2,1)S(1)}, u32[]{:S(2)}, u32[]{:S(2)}) collective-permute-start(bf16[9,64,64]{1,2,0:T(8,128)(2,1)S(1)} %get-tuple-element.19), channel_id=1, source_target_pairs={{0,12},{4,0},{8,4},{12,8},{1,13},{5,1},{9,5},{13,9},{2,14},{6,2},{... | collective-permute-start | bytes 221192 | tf_op jit(solution)/shard_map/ppermute | solution.py:55

commit v15 on v14

--- a/solution.py
+++ b/solution.py
@@ -26,13 +26,6 @@
         high = lax.ppermute(lax.slice_in_dim(block, 0, width, axis=dim), axis, backward)
         block = jnp.concatenate([low, block, high], axis=dim)
     return block
-
-
-def extend(grid_field, padded):
-    grid_field = with_halo(grid_field, (("lat", 1),), REACH, False)
-    grid_field = with_halo(grid_field, (("lon", 2),), RIM, True)
-    extra = padded - grid_field.shape[2]
-    return jnp.pad(grid_field, ((0, 0), (0, 0), (0, extra), (0, 0)))
 
 
 def ring_sum(value, axis):
@@ -217,10 +210,13 @@
     first = jnp.reshape(first_row, (1,)).astype(jnp.int32)
     tables = (src_rows, lon_start, lon_span, basis_idx, weighting)
 
-    both = extend(jnp.concatenate([inputs, cotangent], axis=3), padded)
-    row_sums = jnp.stack(
-        [jnp.sum(inputs, axis=2, dtype=jnp.float32), jnp.sum(cotangent, axis=2, dtype=jnp.float32)]
-    )
+    joined = jnp.concatenate([inputs, cotangent], axis=3)
+    banded = with_halo(joined, (("lat", 1),), REACH, False)
+    banded, source = lax.optimization_barrier((banded, joined))
+    both = with_halo(banded, (("lon", 2),), RIM, True)
+    both = jnp.pad(both, ((0, 0), (0, 0), (0, padded - both.shape[2]), (0, 0)))
+    sums = jnp.sum(source, axis=2, dtype=jnp.float32)
+    row_sums = jnp.stack([sums[..., :channels], sums[..., channels:]])
     local_totals = ring_sum(row_sums, "lon")
     if row_count >= POLAR + REACH:
         framed = jnp.pad(local_totals, ((0, 0), (0, 0), (REACH, REACH), (0, 0)))

time: 67.4 us -> 65.6 us (0.973)
  other arithmetic: 5.03 us -> 3.98 us
    reduce_sum x2 -> x1, other arithmetic: 1.88 us -> 0.06 us  [on_device(): sums = jnp.sum(source, axis=2, dtype=jnp.float32)]
    ppermute x3, starting transfers between devices: 4.46 us -> 3 us  [ring_sum(): total = total + lax.ppermute(value, axis, pairs)]
    ppermute x2, starting transfers between devices: 3.54 us -> 4.99 us  [with_halo(): lax.ppermute(lax.slice_in_dim(block, block.shape[dim] - width, None, axis...]
    div x1, other arithmetic: 0.61 us -> 1.32 us  [on_device(): weighting = quad_weight / jnp.sqrt(lon_span.astype(jnp.float32))]
    unnamed x13 -> x9, local copies, waits for them, and re-layouts: 4.26 us -> 4.27 us
  transfers between devices with their start and end apart: 13 -> 13, of which waited for: 6 -> 6; matrix products, arithmetic and copies ran while one was open for 16% -> 14% of each run, Pallas kernels for 15% -> 16%
where the time goes in v15:
time: 65.6 us; the launch traced here: 65.1 us
  starting transfers between devices  18.6 us (28%)
  Pallas kernels  14.2 us (22%)
  waiting for transfers between devices  13.9 us (21%)
  local copies, waits for them, and re-layouts  6.99 us (11%)
  matrix products  6.68 us (10%)
  other arithmetic  3.98 us (6%)
  between operations  0.82 us (1%)
    pallas_call x1, Pallas kernels, run_scatter(): pl.pallas_call(kernel, grid=(members,), in_specs=[smem] * 6 + [pl.BlockSp...  10.3 us
    ppermute x6, starting transfers between devices, ring_scatter(): sent = lax.ppermute(piece.astype(jnp.bfloat16), axis, pairs)  7.54 us
    ppermute x6, waiting for transfers between devices, ring_scatter(): sent = lax.ppermute(piece.astype(jnp.bfloat16), axis, pairs)  7.06 us
    ppermute x2, starting transfers between devices, with_halo(): lax.ppermute(lax.slice_in_dim(block, block.shape[dim] - width, None, axis...  4.99 us
    unnamed x9, local copies, waits for them, and re-layouts  4.27 us
    ppermute x2, waiting for transfers between devices, with_halo(): lax.ppermute(lax.slice_in_dim(block, 0, width, axis=dim), axis, backward)  4.13 us
    pallas_call x1, Pallas kernels, run_filter(): pl.pallas_call(kernel, grid=(members, row_count), in_specs=[smem] * 6 + [...  3.92 us
    ppermute x2, starting transfers between devices, with_halo(): lax.ppermute(lax.slice_in_dim(block, 0, width, axis=dim), axis, backward)  3.02 us
  transfers between devices with their start and end apart: 13, of which 6 were waited for; matrix products, arithmetic and copies ran while one was open for 14% of the time, Pallas kernels for 16%

profile of v15, /device:TPU:0, one launch (start us, length us, event | category | flops | bytes accessed | tf_op | source)
XLA Modules:
  0.0 65.1 jit_solution(15464855971918785628)
XLA Ops:
  0.6 0.9 %constant_dynamic-update-slice_fusion.1 = bf16[1,4,64,512]{3,2,1,0:T(8,128)(2,1)S(1)} fusion(bf16[1,4,64,256]{3,2,1,0:T(8,128)(2,1)} %param.8), kind=kLoop, calls=%fused_computation.34 | loop fusion | bytes 262144
  1.5 0.9 %constant_dynamic-update-slice_fusion = bf16[1,4,64,512]{3,2,1,0:T(8,128)(2,1)S(1)} fusion(bf16[1,4,64,512]{3,2,1,0:T(8,128)(2,1)S(1)} %constant_dynamic-update-slice_fusion.1, bf16[1,4,64,256]{3,2,1,0:T(8,128)(2,1)} %param.9), kind=kLoop, calls=%fused_computation.33 | loop fusion | bytes 262144 | tf_op jit(solution)/shard_map/concatenate | solution.py:213
  2.5 4.9 %collective-permute-start = (bf16[1,2,64,512]{3,2,1,0:T(8,128)(2,1)S(1)}, bf16[1,2,64,512]{3,2,1,0:T(8,128)(2,1)S(1)}, u32[]{:S(2)}, u32[]{:S(2)}) collective-permute-start(bf16[1,2,64,512]{3,2,1,0:T(8,128)(2,1)S(1)} %get-tuple-element.27), channel_id=1, source_target_pairs={{0,4},{4,8},{8,12},{1,5},{5,9},{9,13},{2,6},{6,10},{10,14},{3,7},{... | collective-permute-start | bytes 393224 | tf_op jit(solution)/shard_map/ppermute | solution.py:23
  7.4 1.3 %collective-permute-start.1 = (bf16[1,2,64,512]{3,2,1,0:T(8,128)(2,1)S(1)}, bf16[1,2,64,512]{3,2,1,0:T(8,128)(2,1)S(1)}, u32[]{:S(2)}, u32[]{:S(2)}) collective-permute-start(bf16[1,2,64,512]{3,2,1,0:T(8,128)(2,1)S(1)} %get-tuple-element.28), channel_id=1, source_target_pairs={{4,0},{8,4},{12,8},{5,1},{9,5},{13,9},{6,2},{10,6},{14,10},{7,3},{... | collective-permute-start | bytes 393224 | tf_op jit(solution)/shard_map/ppermute | solution.py:26
  8.8 1.3 %rsqrt_multiply_fusion.scale_ref = f32[16,12]{1,0:T(8,128)} fusion(f32[16,12]{1,0:T(8,128)} %param.15, s32[16,12]{1,0:T(8,128)} %span_ref.3), kind=kLoop, calls=%fused_computation.32 | loop fusion | flops 384 | bytes 2304 | tf_op jit(solution)/shard_map/div | solution.py:209
  10.1 0.1 collective-permute-done
  10.2 4.1 %collective-permute-done.1 = bf16[1,2,64,512]{3,2,1,0:T(8,128)(2,1)S(1)} collective-permute-done((bf16[1,2,64,512]{3,2,1,0:T(8,128)(2,1)S(1)}, bf16[1,2,64,512]{3,2,1,0:T(8,128)(2,1)S(1)}, u32[]{:S(2)}, u32[]{:S(2)}) %collective-permute-start.1) | collective-permute-done | bytes 131104 | tf_op jit(solution)/shard_map/ppermute | solution.py:26
  14.3 0.1 pad_maximum_fusion
  14.4 0.1 convert_reduce_fusion
  14.5 0.1 collective-permute-start.4
  14.5 1.6 %collective-permute-start.5 = (f32[2,1,4,256]{3,0,2,1:T(2,128)S(1)}, f32[2,1,4,256]{3,0,2,1:T(2,128)S(1)}, u32[]{:S(2)}, u32[]{:S(2)}) collective-permute-start(f32[2,1,4,256]{3,0,2,1:T(2,128)S(1)} %pad_maximum_fusion.1), channel_id=1, source_target_pairs={{0,2},{1,3},{2,0},{3,1},{4,6},{5,7},{6,4},{7,5},{8,10},{9,11},{10,... | collective-permute-start | bytes 24584 | tf_op jit(solution)/shard_map/ppermute | solution.py:36
  16.1 1.4 %collective-permute-start.6 = (f32[2,1,4,256]{3,0,2,1:T(2,128)S(1)}, f32[2,1,4,256]{3,0,2,1:T(2,128)S(1)}, u32[]{:S(2)}, u32[]{:S(2)}) collective-permute-start(f32[2,1,4,256]{3,0,2,1:T(2,128)S(1)} %pad_maximum_fusion.1), channel_id=1, source_target_pairs={{0,3},{1,0},{2,1},{3,2},{4,7},{5,4},{6,5},{7,6},{8,11},{9,8},{10,9... | collective-permute-start | bytes 24584 | tf_op jit(solution)/shard_map/ppermute | solution.py:36
  17.5 0.1 collective-permute-start.2
  17.6 1.7 %collective-permute-start.3 = (bf16[1,8,16,512]{3,2,1,0:T(8,128)(2,1)S(1)}, bf16[1,8,16,512]{3,2,1,0:T(8,128)(2,1)S(1)}, u32[]{:S(2)}, u32[]{:S(2)}) collective-permute-start(bf16[1,8,16,512]{3,2,1,0:T(8,128)(2,1)S(1)} %get-tuple-element.26), channel_id=1, source_target_pairs={{1,0},{2,1},{3,2},{0,3},{5,4},{6,5},{7,6},{4,7},{9,8},{10,9},{11,1... | collective-permute-start | bytes 393224 | tf_op jit(solution)/shard_map/ppermute | solution.py:26
  19.3 0.0 collective-permute-done.4
  19.3 0.0 collective-permute-done.5
  19.3 0.0 collective-permute-done.6
  19.3 0.6 fusion.19
  20.0 2.6 %collective-permute-done.2 = bf16[1,8,16,512]{3,2,1,0:T(8,128)(2,1)S(1)} collective-permute-done((bf16[1,8,16,512]{3,2,1,0:T(8,128)(2,1)S(1)}, bf16[1,8,16,512]{3,2,1,0:T(8,128)(2,1)S(1)}, u32[]{:S(2)}, u32[]{:S(2)}) %collective-permute-start.2) | collective-permute-done | bytes 131104 | tf_op jit(solution)/shard_map/ppermute | solution.py:23
  22.5 0.0 collective-permute-done.3
  22.5 1.1 %fusion.16.field_ref = bf16[1,8,128,512]{3,2,1,0:T(8,128)(2,1)} fusion(bf16[1,8,16,512]{3,2,1,0:T(8,128)(2,1)S(1)} %collective-permute-done.3, bf16[1,8,64,512]{3,2,1,0:T(8,128)(2,1)S(1)} %pad_maximum_fusion, bf16[1,8,16,512]{3,2,1,0:T(8,128)(2,1)S(1)} %collective-permute-done.2), kind=kLoop, calls=%fused_computation.14 | loop fusion | flops 5242880 | bytes 1835008 | tf_op jit(solution)/shard_map/concatenate | solution.py:27
  23.6 0.0 copy-start.2
  23.6 3.9 %shard_map.103 = bf16[1,4,64,2304]{3,2,1,0:T(8,128)(2,1)} custom-call(s32[1]{0:T(128)} %bitcast.first_ref, s32[16,12]{1,0:T(8,128)} %src_ref.3, s32[16,12]{1,0:T(8,128)} %start_ref.3, s32[16,12]{1,0:T(8,128)} %span_ref.3, s32[16,12]{1,0:T(8,128)} %basis_ref.3, f32[16,12]{1,0:T(8,128)} %rsqrt_multiply_fusion.scale_ref, ...), custom_call_target="tpu_custom_call" | custom-call | tf_op jit(solution)/shard_map/pallas_call | solution.py:185
  27.6 0.0 copy-done.2
  27.6 1.8 %convolution_bitcast_fusion = f32[9,256,256]{1,2,0:T(8,128)S(1)} fusion(bf16[4,8,9,8,256]{4,3,2,1,0:T(8,128)(2,1)} %bitcast.49, bf16[1,4,64,256]{3,2,1,0:T(8,128)(2,1)S(1)} %copy-done.2), kind=kOutput, calls=%fused_computation.4 | convolution fusion | flops 301989888 | bytes 3670016 | tf_op jit(solution)/shard_map/brwq,brwo->qo/dot_general | solution.py:231
  29.3 0.9 %dynamic-slice_convert_fusion.2 = (bf16[9,256,64]{1,2,0:T(8,128)(2,1)}, bf16[9,256,64]{1,2,0:T(8,128)(2,1)}, bf16[9,256,64]{1,2,0:T(8,128)(2,1)}) fusion(f32[9,256,256]{1,2,0:T(8,128)S(1)} %convolution_bitcast_fusion, s32[]{:T(128)S(6)} %select_n.53, s32[]{:T(128)S(6)} %select_n.57, s32[]{:T(128)S(6)} %select_n.55), kind=kLoop, calls=%fused_computation.18 | loop fusion | bytes 1769484 | tf_op jit(solution)/shard_map/convert_element_type | solution.py:48
  30.3 0.6 collective-permute-start.7
  30.9 0.9 %collective-permute-start.8 = (bf16[9,256,64]{1,2,0:T(8,128)(2,1)}, bf16[9,256,64]{1,2,0:T(8,128)(2,1)}, u32[]{:S(2)}, u32[]{:S(2)}) collective-permute-start(bf16[9,256,64]{1,2,0:T(8,128)(2,1)} %get-tuple-element.21), channel_id=1, source_target_pairs={{0,2},{1,3},{2,0},{3,1},{4,6},{5,7},{6,4},{7,5},{8,10},{9,11},{10,... | collective-permute-start | bytes 884744 | tf_op jit(solution)/shard_map/ppermute | solution.py:48
  31.8 0.4 collective-permute-start.9
  32.3 0.0 copy-start
  32.3 2.5 %copy.16 = bf16[9,256,256]{1,2,0:T(8,128)(2,1)} copy(bf16[9,256,256]{2,1,0:T(8,128)(2,1)} %param.10) | data formatting | bytes 2359296 | tf_op args[2]
  34.7 0.0 copy-done
  34.7 2.5 %fusion.9 = f32[1,4,64,256]{3,2,1,0:T(8,128)} fusion(bf16[2304,256,1]{1,0,2:T(8,128)(2,1)} %bitcast.50, bf16[1,4,64,2304]{3,2,1,0:T(8,128)(2,1)S(1)} %copy-done), kind=kOutput, calls=%fused_computation.11 | convolution fusion | flops 301989888 | bytes 2621440 | tf_op jit(solution)/shard_map/brwq,qo->brwo/dot_general | solution.py:229
  37.2 1.5 %collective-permute-done.7 = bf16[9,256,64]{1,2,0:T(8,128)(2,1)} collective-permute-done((bf16[9,256,64]{1,2,0:T(8,128)(2,1)}, bf16[9,256,64]{1,2,0:T(8,128)(2,1)}, u32[]{:S(2)}, u32[]{:S(2)}) %collective-permute-start.7) | collective-permute-done | bytes 294944 | tf_op jit(solution)/shard_map/ppermute | solution.py:48
  38.7 2.4 %collective-permute-done.8 = bf16[9,256,64]{1,2,0:T(8,128)(2,1)} collective-permute-done((bf16[9,256,64]{1,2,0:T(8,128)(2,1)}, bf16[9,256,64]{1,2,0:T(8,128)(2,1)}, u32[]{:S(2)}, u32[]{:S(2)}) %collective-permute-start.8) | collective-permute-done | bytes 294944 | tf_op jit(solution)/shard_map/ppermute | solution.py:48
  41.1 3.1 %collective-permute-done.9 = bf16[9,256,64]{1,2,0:T(8,128)(2,1)} collective-permute-done((bf16[9,256,64]{1,2,0:T(8,128)(2,1)}, bf16[9,256,64]{1,2,0:T(8,128)(2,1)}, u32[]{:S(2)}, u32[]{:S(2)}) %collective-permute-start.9) | collective-permute-done | bytes 294944 | tf_op jit(solution)/shard_map/ppermute | solution.py:48
  44.3 1.3 %convert_add_fusion = f32[9,256,64]{1,2,0:T(8,128)S(1)} fusion(bf16[9,256,64]{1,2,0:T(8,128)(2,1)} %collective-permute-done.9, bf16[9,256,64]{1,2,0:T(8,128)(2,1)} %collective-permute-done.8, bf16[9,256,64]{1,2,0:T(8,128)(2,1)} %collective-permute-done.7, f32[9,256,256]{1,2,0:T(8,128)S(1)} %convolution_bitcast_fusion, s32[]{:T(128)S(6)} %select_n.51), kind=kLoop, calls=%fused_computation.15 | loop fusion | flops 884736 | bytes 2064388 | tf_op jit(solution)/shard_map/add | solution.py:49
  45.5 0.2 dynamic-slice_convert_fusion.5
  45.7 0.0 copy-start.1
  45.7 1.6 %collective-permute-start.10 = (bf16[9,64,64]{1,2,0:T(8,128)(2,1)S(1)}, bf16[9,64,64]{1,2,0:T(8,128)(2,1)S(1)}, u32[]{:S(2)}, u32[]{:S(2)}) collective-permute-start(bf16[9,64,64]{1,2,0:T(8,128)(2,1)S(1)} %get-tuple-element.22), channel_id=1, source_target_pairs={{0,4},{4,8},{8,12},{12,0},{1,5},{5,9},{9,13},{13,1},{2,6},{6,10},{... | collective-permute-start | bytes 221192 | tf_op jit(solution)/shard_map/ppermute | solution.py:48
  47.4 1.1 %collective-permute-start.11 = (bf16[9,64,64]{1,2,0:T(8,128)(2,1)S(1)}, bf16[9,64,64]{1,2,0:T(8,128)(2,1)S(1)}, u32[]{:S(2)}, u32[]{:S(2)}) collective-permute-start(bf16[9,64,64]{1,2,0:T(8,128)(2,1)S(1)} %get-tuple-element.24), channel_id=1, source_target_pairs={{0,8},{4,12},{8,0},{12,4},{1,9},{5,13},{9,1},{13,5},{2,10},{6,14},... | collective-permute-start | bytes 221192 | tf_op jit(solution)/shard_map/ppermute | solution.py:48
  48.5 2.8 %collective-permute-start.12 = (bf16[9,64,64]{1,2,0:T(8,128)(2,1)S(1)}, bf16[9,64,64]{1,2,0:T(8,128)(2,1)S(1)}, u32[]{:S(2)}, u32[]{:S(2)}) collective-permute-start(bf16[9,64,64]{1,2,0:T(8,128)(2,1)S(1)} %get-tuple-element.23), channel_id=1, source_target_pairs={{0,12},{4,0},{8,4},{12,8},{1,13},{5,1},{9,5},{13,9},{2,14},{6,2},{... | collective-permute-start | bytes 221192 | tf_op jit(solution)/shard_map/ppermute | solution.py:48
  51.3 10.3 %shard_map.104 = bf16[1,4,64,2304]{3,2,1,0:T(8,128)(2,1)} custom-call(s32[1]{0:T(128)} %bitcast.first_ref, s32[16,12]{1,0:T(8,128)} %src_ref.3, s32[16,12]{1,0:T(8,128)} %start_ref.3, s32[16,12]{1,0:T(8,128)} %span_ref.3, s32[16,12]{1,0:T(8,128)} %basis_ref.3, f32[16,12]{1,0:T(8,128)} %rsqrt_multiply_fusion.scale_ref, ...), custom_call_target="tpu_custom_call" | custom-call | tf_op jit(solution)/shard_map/pallas_call | solution.py:152
  61.6 0.0 copy-done.1
  61.6 2.4 %fusion.12 = f32[1,4,64,256]{3,2,1,0:T(8,128)} fusion(bf16[2304,256,1]{1,0,2:T(8,128)(2,1)S(1)} %bitcast.51, bf16[1,4,64,2304]{3,2,1,0:T(8,128)(2,1)} %shard_map.104), kind=kOutput, calls=%fused_computation.12 | convolution fusion | flops 301989888 | bytes 2621440 | tf_op jit(solution)/shard_map/bpwq,qc->bpwc/dot_general | solution.py:242
  64.1 0.0 collective-permute-done.10
  64.1 0.0 collective-permute-done.11
  64.1 0.0 collective-permute-done.12
  64.1 0.2 add_multiply_fusion
  64.3 0.9 %copy.17 = f32[9,64,64]{2,1,0:T(8,128)} copy(f32[9,64,64]{1,2,0:T(8,128)S(1)} %add_multiply_fusion) | data formatting | bytes 294912
  (6 shorter events, 0.1 us)
Async XLA Ops:
  2.5 7.7 %collective-permute-start = (bf16[1,2,64,512]{3,2,1,0:T(8,128)(2,1)S(1)}, bf16[1,2,64,512]{3,2,1,0:T(8,128)(2,1)S(1)}, u32[]{:S(2)}, u32[]{:S(2)}) collective-permute-start(bf16[1,2,64,512]{3,2,1,0:T(8,128)(2,1)S(1)} %get-tuple-element.27), channel_id=1, source_target_pairs={{0,4},{4,8},{8,12},{1,5},{5,9},{9,13},{2,6},{6,10},{10,14},{3,7},{... | collective-permute-start | bytes 393224 | tf_op jit(solution)/shard_map/ppermute | solution.py:23
  7.4 6.9 %collective-permute-start.1 = (bf16[1,2,64,512]{3,2,1,0:T(8,128)(2,1)S(1)}, bf16[1,2,64,512]{3,2,1,0:T(8,128)(2,1)S(1)}, u32[]{:S(2)}, u32[]{:S(2)}) collective-permute-start(bf16[1,2,64,512]{3,2,1,0:T(8,128)(2,1)S(1)} %get-tuple-element.28), channel_id=1, source_target_pairs={{4,0},{8,4},{12,8},{5,1},{9,5},{13,9},{6,2},{10,6},{14,10},{7,3},{... | collective-permute-start | bytes 393224 | tf_op jit(solution)/shard_map/ppermute | solution.py:26
  14.5 4.8 %collective-permute-start.4 = (f32[2,1,4,256]{3,0,2,1:T(2,128)S(1)}, f32[2,1,4,256]{3,0,2,1:T(2,128)S(1)}, u32[]{:S(2)}, u32[]{:S(2)}) collective-permute-start(f32[2,1,4,256]{3,0,2,1:T(2,128)S(1)} %pad_maximum_fusion.1), channel_id=1, source_target_pairs={{0,1},{1,2},{2,3},{3,0},{4,5},{5,6},{6,7},{7,4},{8,9},{9,10},{10,1... | collective-permute-start | bytes 24584 | tf_op jit(solution)/shard_map/ppermute | solution.py:36
  14.5 4.8 %collective-permute-start.5 = (f32[2,1,4,256]{3,0,2,1:T(2,128)S(1)}, f32[2,1,4,256]{3,0,2,1:T(2,128)S(1)}, u32[]{:S(2)}, u32[]{:S(2)}) collective-permute-start(f32[2,1,4,256]{3,0,2,1:T(2,128)S(1)} %pad_maximum_fusion.1), channel_id=1, source_target_pairs={{0,2},{1,3},{2,0},{3,1},{4,6},{5,7},{6,4},{7,5},{8,10},{9,11},{10,... | collective-permute-start | bytes 24584 | tf_op jit(solution)/shard_map/ppermute | solution.py:36
  16.1 3.2 %collective-permute-start.6 = (f32[2,1,4,256]{3,0,2,1:T(2,128)S(1)}, f32[2,1,4,256]{3,0,2,1:T(2,128)S(1)}, u32[]{:S(2)}, u32[]{:S(2)}) collective-permute-start(f32[2,1,4,256]{3,0,2,1:T(2,128)S(1)} %pad_maximum_fusion.1), channel_id=1, source_target_pairs={{0,3},{1,0},{2,1},{3,2},{4,7},{5,4},{6,5},{7,6},{8,11},{9,8},{10,9... | collective-permute-start | bytes 24584 | tf_op jit(solution)/shard_map/ppermute | solution.py:36
  17.5 5.0 %collective-permute-start.2 = (bf16[1,8,16,512]{3,2,1,0:T(8,128)(2,1)S(1)}, bf16[1,8,16,512]{3,2,1,0:T(8,128)(2,1)S(1)}, u32[]{:S(2)}, u32[]{:S(2)}) collective-permute-start(bf16[1,8,16,512]{3,2,1,0:T(8,128)(2,1)S(1)} %get-tuple-element.25), channel_id=1, source_target_pairs={{0,1},{1,2},{2,3},{3,0},{4,5},{5,6},{6,7},{7,4},{8,9},{9,10},{10,1... | collective-permute-start | bytes 393224 | tf_op jit(solution)/shard_map/ppermute | solution.py:23
  17.6 5.0 %collective-permute-start.3 = (bf16[1,8,16,512]{3,2,1,0:T(8,128)(2,1)S(1)}, bf16[1,8,16,512]{3,2,1,0:T(8,128)(2,1)S(1)}, u32[]{:S(2)}, u32[]{:S(2)}) collective-permute-start(bf16[1,8,16,512]{3,2,1,0:T(8,128)(2,1)S(1)} %get-tuple-element.26), channel_id=1, source_target_pairs={{1,0},{2,1},{3,2},{0,3},{5,4},{6,5},{7,6},{4,7},{9,8},{10,9},{11,1... | collective-permute-start | bytes 393224 | tf_op jit(solution)/shard_map/ppermute | solution.py:26
  23.6 3.9 %copy-start.2 = (bf16[1,4,64,256]{3,2,1,0:T(8,128)(2,1)S(1)}, bf16[1,4,64,256]{3,2,1,0:T(8,128)(2,1)}, u32[]{:S(2)}) copy-start(bf16[1,4,64,256]{3,2,1,0:T(8,128)(2,1)} %param.9) | copy-start | bytes 393220
  30.3 8.4 %collective-permute-start.7 = (bf16[9,256,64]{1,2,0:T(8,128)(2,1)}, bf16[9,256,64]{1,2,0:T(8,128)(2,1)}, u32[]{:S(2)}, u32[]{:S(2)}) collective-permute-start(bf16[9,256,64]{1,2,0:T(8,128)(2,1)} %get-tuple-element.19), channel_id=1, source_target_pairs={{0,1},{1,2},{2,3},{3,0},{4,5},{5,6},{6,7},{7,4},{8,9},{9,10},{10,1... | collective-permute-start | bytes 884744 | tf_op jit(solution)/shard_map/ppermute | solution.py:48
  30.9 10.2 %collective-permute-start.8 = (bf16[9,256,64]{1,2,0:T(8,128)(2,1)}, bf16[9,256,64]{1,2,0:T(8,128)(2,1)}, u32[]{:S(2)}, u32[]{:S(2)}) collective-permute-start(bf16[9,256,64]{1,2,0:T(8,128)(2,1)} %get-tuple-element.21), channel_id=1, source_target_pairs={{0,2},{1,3},{2,0},{3,1},{4,6},{5,7},{6,4},{7,5},{8,10},{9,11},{10,... | collective-permute-start | bytes 884744 | tf_op jit(solution)/shard_map/ppermute | solution.py:48
  31.8 12.4 %collective-permute-start.9 = (bf16[9,256,64]{1,2,0:T(8,128)(2,1)}, bf16[9,256,64]{1,2,0:T(8,128)(2,1)}, u32[]{:S(2)}, u32[]{:S(2)}) collective-permute-start(bf16[9,256,64]{1,2,0:T(8,128)(2,1)} %get-tuple-element.20), channel_id=1, source_target_pairs={{0,3},{1,0},{2,1},{3,2},{4,7},{5,4},{6,5},{7,6},{8,11},{9,8},{10,9... | collective-permute-start | bytes 884744 | tf_op jit(solution)/shard_map/ppermute | solution.py:48
  32.3 2.5 %copy-start = (bf16[1,4,64,2304]{3,2,1,0:T(8,128)(2,1)S(1)}, bf16[1,4,64,2304]{3,2,1,0:T(8,128)(2,1)}, u32[]{:S(2)}) copy-start(bf16[1,4,64,2304]{3,2,1,0:T(8,128)(2,1)} %shard_map.103) | copy-start | bytes 3538948
  45.7 15.9 %copy-start.1 = (bf16[9,256,256]{1,2,0:T(8,128)(2,1)S(1)}, bf16[9,256,256]{1,2,0:T(8,128)(2,1)}, u32[]{:S(2)}) copy-start(bf16[9,256,256]{1,2,0:T(8,128)(2,1)} %copy.16) | copy-start | bytes 3538948
  45.7 18.3 %collective-permute-start.10 = (bf16[9,64,64]{1,2,0:T(8,128)(2,1)S(1)}, bf16[9,64,64]{1,2,0:T(8,128)(2,1)S(1)}, u32[]{:S(2)}, u32[]{:S(2)}) collective-permute-start(bf16[9,64,64]{1,2,0:T(8,128)(2,1)S(1)} %get-tuple-element.22), channel_id=1, source_target_pairs={{0,4},{4,8},{8,12},{12,0},{1,5},{5,9},{9,13},{13,1},{2,6},{6,10},{... | collective-permute-start | bytes 221192 | tf_op jit(solution)/shard_map/ppermute | solution.py:48
  47.4 16.7 %collective-permute-start.11 = (bf16[9,64,64]{1,2,0:T(8,128)(2,1)S(1)}, bf16[9,64,64]{1,2,0:T(8,128)(2,1)S(1)}, u32[]{:S(2)}, u32[]{:S(2)}) collective-permute-start(bf16[9,64,64]{1,2,0:T(8,128)(2,1)S(1)} %get-tuple-element.24), channel_id=1, source_target_pairs={{0,8},{4,12},{8,0},{12,4},{1,9},{5,13},{9,1},{13,5},{2,10},{6,14},... | collective-permute-start | bytes 221192 | tf_op jit(solution)/shard_map/ppermute | solution.py:48
  48.5 15.6 %collective-permute-start.12 = (bf16[9,64,64]{1,2,0:T(8,128)(2,1)S(1)}, bf16[9,64,64]{1,2,0:T(8,128)(2,1)S(1)}, u32[]{:S(2)}, u32[]{:S(2)}) collective-permute-start(bf16[9,64,64]{1,2,0:T(8,128)(2,1)S(1)} %get-tuple-element.23), channel_id=1, source_target_pairs={{0,12},{4,0},{8,4},{12,8},{1,13},{5,1},{9,5},{13,9},{2,14},{6,2},{... | collective-permute-start | bytes 221192 | tf_op jit(solution)/shard_map/ppermute | solution.py:48

commit v16 on v15

--- a/solution.py
+++ b/solution.py
@@ -47,6 +47,21 @@
         piece = lax.dynamic_slice_in_dim(value, ((own + shift) % count) * block, block, dim)
         sent = lax.ppermute(piece.astype(jnp.bfloat16), axis, pairs)
         total = total + sent.astype(jnp.float32)
+    return total
+
+
+def exchange_scatter(value, axis, dim):
+    count = lax.axis_size(axis)
+    own = lax.axis_index(axis)
+    block = value.shape[dim] // count
+    pieces = jnp.stack(jnp.split(value, count, axis=dim))
+    mine = lax.dynamic_index_in_dim(pieces, own, 0, keepdims=False)
+    moved = lax.all_to_all(pieces.astype(jnp.bfloat16), axis, 0, 0, tiled=True)
+    others = moved.astype(jnp.float32)
+    total = mine
+    for source in range(count):
+        other = lax.dynamic_index_in_dim(others, (own + source + 1) % count, 0, keepdims=False)
+        total = total + jnp.where(source + 1 < count, other, 0.0)
     return total
 
 
@@ -234,7 +249,7 @@
     partial_value = partial_value.reshape(BASIS, channels, channels)
     reduced = ring_scatter(partial_value, "lon", 2)
     both, grad_totals, reduced = lax.optimization_barrier((both, grad_totals, reduced))
-    reduced = ring_scatter(reduced, "lat", 1)
+    reduced = exchange_scatter(reduced, "lat", 1)
     back_filtered = run_scatter(
         first, tables, both, grad_totals, row_count, lon_count, lon_total, 1
     )

time: 65.6 us -> 71.3 us (1.087)
  the two profiles are of different devices: /device:TPU:0 before, /device:TPU:1 now
where the time goes in v16:
time: 71.3 us; the launch traced here: 70.2 us
  waiting for transfers between devices  19.6 us (27%)
  starting transfers between devices  16.2 us (23%)
  Pallas kernels  13.2 us (19%)
  local copies, waits for them, and re-layouts  11.3 us (16%)
  other arithmetic  5.08 us (7%)
  matrix products  4.15 us (6%)
  between operations  0.83 us (1%)
    ppermute x3, waiting for transfers between devices, ring_scatter(): sent = lax.ppermute(piece.astype(jnp.bfloat16), axis, pairs)  12.2 us
    pallas_call x1, Pallas kernels, run_scatter(): pl.pallas_call(kernel, grid=(members,), in_specs=[smem] * 6 + [pl.BlockSp...  9.28 us
    unnamed x15, local copies, waits for them, and re-layouts  8.51 us
    ppermute x2, waiting for transfers between devices, with_halo(): lax.ppermute(lax.slice_in_dim(block, 0, width, axis=dim), axis, backward)  6.04 us
    ppermute x2, starting transfers between devices, with_halo(): lax.ppermute(lax.slice_in_dim(block, block.shape[dim] - width, None, axis...  5.62 us
    all_to_all x1, starting transfers between devices, exchange_scatter(): moved = lax.all_to_all(pieces.astype(jnp.bfloat16), axis, 0, 0, tiled=True)  4.09 us
    pallas_call x1, Pallas kernels, run_filter(): pl.pallas_call(kernel, grid=(members, row_count), in_specs=[smem] * 6 + [...  3.94 us
    ppermute x3, starting transfers between devices, ring_sum(): total = total + lax.ppermute(value, axis, pairs)  3.73 us
  transfers between devices with their start and end apart: 11, of which 8 were waited for; matrix products, arithmetic and copies ran while one was open for 9% of the time, Pallas kernels for 13%

profile of v16, /device:TPU:1, one launch (start us, length us, event | category | flops | bytes accessed | tf_op | source)
XLA Modules:
  0.0 70.2 jit_solution(6573161537791201434)
XLA Ops:
  0.6 0.9 %constant_dynamic-update-slice_fusion.1 = bf16[1,4,64,512]{3,2,1,0:T(8,128)(2,1)S(1)} fusion(bf16[1,4,64,256]{3,2,1,0:T(8,128)(2,1)} %param.8), kind=kLoop, calls=%fused_computation.36 | loop fusion | bytes 262144
  1.5 0.9 %constant_dynamic-update-slice_fusion = bf16[1,4,64,512]{3,2,1,0:T(8,128)(2,1)S(1)} fusion(bf16[1,4,64,512]{3,2,1,0:T(8,128)(2,1)S(1)} %constant_dynamic-update-slice_fusion.1, bf16[1,4,64,256]{3,2,1,0:T(8,128)(2,1)} %param.9), kind=kLoop, calls=%fused_computation.35 | loop fusion | bytes 262144 | tf_op jit(solution)/shard_map/concatenate | solution.py:228
  2.5 4.0 %collective-permute-start = (bf16[1,2,64,512]{3,2,1,0:T(8,128)(2,1)S(1)}, bf16[1,2,64,512]{3,2,1,0:T(8,128)(2,1)S(1)}, u32[]{:S(2)}, u32[]{:S(2)}) collective-permute-start(bf16[1,2,64,512]{3,2,1,0:T(8,128)(2,1)S(1)} %get-tuple-element.28), channel_id=1, source_target_pairs={{0,4},{4,8},{8,12},{1,5},{5,9},{9,13},{2,6},{6,10},{10,14},{3,7},{... | collective-permute-start | bytes 393224 | tf_op jit(solution)/shard_map/ppermute | solution.py:23
  6.5 1.3 %collective-permute-start.1 = (bf16[1,2,64,512]{3,2,1,0:T(8,128)(2,1)S(1)}, bf16[1,2,64,512]{3,2,1,0:T(8,128)(2,1)S(1)}, u32[]{:S(2)}, u32[]{:S(2)}) collective-permute-start(bf16[1,2,64,512]{3,2,1,0:T(8,128)(2,1)S(1)} %get-tuple-element.29), channel_id=1, source_target_pairs={{4,0},{8,4},{12,8},{5,1},{9,5},{13,9},{6,2},{10,6},{14,10},{7,3},{... | collective-permute-start | bytes 393224 | tf_op jit(solution)/shard_map/ppermute | solution.py:26
  7.9 1.3 %rsqrt_multiply_fusion.scale_ref = f32[16,12]{1,0:T(8,128)} fusion(f32[16,12]{1,0:T(8,128)} %param.15, s32[16,12]{1,0:T(8,128)} %span_ref.3), kind=kLoop, calls=%fused_computation.34 | loop fusion | flops 384 | bytes 2304 | tf_op jit(solution)/shard_map/div | solution.py:224
  9.2 0.0 collective-permute-done
  9.2 3.0 %collective-permute-done.1 = bf16[1,2,64,512]{3,2,1,0:T(8,128)(2,1)S(1)} collective-permute-done((bf16[1,2,64,512]{3,2,1,0:T(8,128)(2,1)S(1)}, bf16[1,2,64,512]{3,2,1,0:T(8,128)(2,1)S(1)}, u32[]{:S(2)}, u32[]{:S(2)}) %collective-permute-start.1) | collective-permute-done | bytes 131104 | tf_op jit(solution)/shard_map/ppermute | solution.py:26
  12.3 0.1 pad_maximum_fusion.1
  12.3 0.1 convert_reduce_fusion
  12.4 3.3 %collective-permute-start.4 = (f32[2,1,4,256]{3,0,2,1:T(2,128)S(1)}, f32[2,1,4,256]{3,0,2,1:T(2,128)S(1)}, u32[]{:S(2)}, u32[]{:S(2)}) collective-permute-start(f32[2,1,4,256]{3,0,2,1:T(2,128)S(1)} %pad_maximum_fusion.2), channel_id=1, source_target_pairs={{0,1},{1,2},{2,3},{3,0},{4,5},{5,6},{6,7},{7,4},{8,9},{9,10},{10,1... | collective-permute-start | bytes 24584 | tf_op jit(solution)/shard_map/ppermute | solution.py:36
  15.7 0.3 collective-permute-start.5
  15.9 0.2 collective-permute-start.6
  16.2 1.6 %collective-permute-start.2 = (bf16[1,8,16,512]{3,2,1,0:T(8,128)(2,1)S(1)}, bf16[1,8,16,512]{3,2,1,0:T(8,128)(2,1)S(1)}, u32[]{:S(2)}, u32[]{:S(2)}) collective-permute-start(bf16[1,8,16,512]{3,2,1,0:T(8,128)(2,1)S(1)} %get-tuple-element.26), channel_id=1, source_target_pairs={{0,1},{1,2},{2,3},{3,0},{4,5},{5,6},{6,7},{7,4},{8,9},{9,10},{10,1... | collective-permute-start | bytes 393224 | tf_op jit(solution)/shard_map/ppermute | solution.py:23
  17.8 0.0 collective-permute-start.3
  17.8 0.0 collective-permute-done.4
  17.8 0.4 collective-permute-done.5
  18.2 0.8 %collective-permute-done.6 = f32[2,1,4,256]{3,0,2,1:T(2,128)S(1)} collective-permute-done((f32[2,1,4,256]{3,0,2,1:T(2,128)S(1)}, f32[2,1,4,256]{3,0,2,1:T(2,128)S(1)}, u32[]{:S(2)}, u32[]{:S(2)}) %collective-permute-start.6) | collective-permute-done | bytes 8224 | tf_op jit(solution)/shard_map/ppermute | solution.py:36
  19.0 0.6 fusion.19
  19.6 0.1 collective-permute-done.2
  19.7 3.0 %collective-permute-done.3 = bf16[1,8,16,512]{3,2,1,0:T(8,128)(2,1)S(1)} collective-permute-done((bf16[1,8,16,512]{3,2,1,0:T(8,128)(2,1)S(1)}, bf16[1,8,16,512]{3,2,1,0:T(8,128)(2,1)S(1)}, u32[]{:S(2)}, u32[]{:S(2)}) %collective-permute-start.3) | collective-permute-done | bytes 131104 | tf_op jit(solution)/shard_map/ppermute | solution.py:26
  22.7 1.1 %fusion.16.field_ref = bf16[1,8,128,512]{3,2,1,0:T(8,128)(2,1)} fusion(bf16[1,8,16,512]{3,2,1,0:T(8,128)(2,1)S(1)} %collective-permute-done.3, bf16[1,8,64,512]{3,2,1,0:T(8,128)(2,1)S(1)} %pad_maximum_fusion.1, bf16[1,8,16,512]{3,2,1,0:T(8,128)(2,1)S(1)} %collective-permute-done.2), kind=kLoop, calls=%fused_computation.15 | loop fusion | flops 5242880 | bytes 1835008 | tf_op jit(solution)/shard_map/concatenate | solution.py:27
  23.8 0.0 copy-start.4
  23.8 3.9 %shard_map.103 = bf16[1,4,64,2304]{3,2,1,0:T(8,128)(2,1)} custom-call(s32[1]{0:T(128)} %bitcast.first_ref, s32[16,12]{1,0:T(8,128)} %src_ref.3, s32[16,12]{1,0:T(8,128)} %start_ref.3, s32[16,12]{1,0:T(8,128)} %span_ref.3, s32[16,12]{1,0:T(8,128)} %basis_ref.3, f32[16,12]{1,0:T(8,128)} %rsqrt_multiply_fusion.scale_ref, ...), custom_call_target="tpu_custom_call" | custom-call | tf_op jit(solution)/shard_map/pallas_call | solution.py:200
  27.7 0.0 copy-done.4
  27.7 1.8 %convolution_bitcast_fusion = f32[9,256,256]{1,2,0:T(8,128)S(1)} fusion(bf16[4,8,9,8,256]{4,3,2,1,0:T(8,128)(2,1)} %bitcast.63, bf16[1,4,64,256]{3,2,1,0:T(8,128)(2,1)S(1)} %copy-done.4), kind=kOutput, calls=%fused_computation.4 | convolution fusion | flops 301989888 | bytes 3670016 | tf_op jit(solution)/shard_map/brwq,brwo->qo/dot_general | solution.py:246
  29.5 0.0 copy-start.2
  29.5 0.9 %dynamic-slice_convert_fusion.2 = (bf16[9,256,64]{1,2,0:T(8,128)(2,1)}, bf16[9,256,64]{1,2,0:T(8,128)(2,1)}, bf16[9,256,64]{1,2,0:T(8,128)(2,1)}) fusion(f32[9,256,256]{1,2,0:T(8,128)S(1)} %convolution_bitcast_fusion, s32[]{:T(128)S(6)} %select_n.67, s32[]{:T(128)S(6)} %select_n.71, s32[]{:T(128)S(6)} %select_n.69), kind=kLoop, calls=%fused_computation.19 | loop fusion | bytes 1769484 | tf_op jit(solution)/shard_map/convert_element_type | solution.py:48
  30.5 0.0 collective-permute-start.7
  30.5 1.2 %collective-permute-start.8 = (bf16[9,256,64]{1,2,0:T(8,128)(2,1)}, bf16[9,256,64]{1,2,0:T(8,128)(2,1)}, u32[]{:S(2)}, u32[]{:S(2)}) collective-permute-start(bf16[9,256,64]{1,2,0:T(8,128)(2,1)} %get-tuple-element.21), channel_id=1, source_target_pairs={{0,2},{1,3},{2,0},{3,1},{4,6},{5,7},{6,4},{7,5},{8,10},{9,11},{10,... | collective-permute-start | bytes 884744 | tf_op jit(solution)/shard_map/ppermute | solution.py:48
  31.7 0.2 collective-permute-start.9
  31.9 0.0 copy-done.2
  31.9 1.5 %copy.16 = bf16[9,256,256]{1,2,0:T(8,128)(2,1)} copy(bf16[9,256,256]{2,1,0:T(8,128)(2,1)S(1)} %copy-done.2) | data formatting | bytes 2359296 | tf_op args[2]
  33.4 2.5 %collective-permute-done.7 = bf16[9,256,64]{1,2,0:T(8,128)(2,1)} collective-permute-done((bf16[9,256,64]{1,2,0:T(8,128)(2,1)}, bf16[9,256,64]{1,2,0:T(8,128)(2,1)}, u32[]{:S(2)}, u32[]{:S(2)}) %collective-permute-start.7) | collective-permute-done | bytes 294944 | tf_op jit(solution)/shard_map/ppermute | solution.py:48
  36.0 8.4 %collective-permute-done.8 = bf16[9,256,64]{1,2,0:T(8,128)(2,1)} collective-permute-done((bf16[9,256,64]{1,2,0:T(8,128)(2,1)}, bf16[9,256,64]{1,2,0:T(8,128)(2,1)}, u32[]{:S(2)}, u32[]{:S(2)}) %collective-permute-start.8) | collective-permute-done | bytes 294944 | tf_op jit(solution)/shard_map/ppermute | solution.py:48
  44.4 1.2 %collective-permute-done.9 = bf16[9,256,64]{1,2,0:T(8,128)(2,1)} collective-permute-done((bf16[9,256,64]{1,2,0:T(8,128)(2,1)}, bf16[9,256,64]{1,2,0:T(8,128)(2,1)}, u32[]{:S(2)}, u32[]{:S(2)}) %collective-permute-start.9) | collective-permute-done | bytes 294944 | tf_op jit(solution)/shard_map/ppermute | solution.py:48
  45.6 1.3 %convert_add_fusion = f32[9,256,64]{1,2,0:T(8,128)S(1)} fusion(bf16[9,256,64]{1,2,0:T(8,128)(2,1)} %collective-permute-done.9, bf16[9,256,64]{1,2,0:T(8,128)(2,1)} %collective-permute-done.8, bf16[9,256,64]{1,2,0:T(8,128)(2,1)} %collective-permute-done.7, f32[9,256,256]{1,2,0:T(8,128)S(1)} %convolution_bitcast_fusion, s32[]{:T(128)S(6)} %select_n.65), kind=kLoop, calls=%fused_computation.16 | loop fusion | flops 884736 | bytes 2064388 | tf_op jit(solution)/shard_map/add | solution.py:49
  46.9 0.2 slice_bitcast_fusion.3
  47.1 0.9 %fusion.23 = bf16[4,9,64,64]{3,2,1,0:T(8,128)(2,1)} fusion(f32[1,9,64,64]{2,3,1,0:T(8,128)S(1)} %get-tuple-element.23, f32[1,9,64,64]{2,3,1,0:T(8,128)S(1)} %get-tuple-element.24, f32[1,9,64,64]{2,3,1,0:T(8,128)S(1)} %get-tuple-element.25, f32[1,9,64,64]{2,3,1,0:T(8,128)S(1)} %get-tuple-element.22), kind=kLoop, calls=%fused_computation.43 | loop fusion | flops 442368 | bytes 884736
  48.1 0.0 copy-start
  48.1 2.3 %reshape.45 = bf16[4,2,18432]{2,1,0:T(2,128)(2,1)} reshape(bf16[4,9,64,64]{3,2,1,0:T(8,128)(2,1)} %fusion.23) | data formatting | bytes 589824
  50.4 4.1 %all-to-all-start = ((bf16[4,2,18432]{2,1,0:T(2,128)(2,1)}), bf16[4,2,18432]{2,1,0:T(2,128)(2,1)}, u32[]{:S(2)}, u32[]{:S(2)}) async-start(bf16[4,2,18432]{2,1,0:T(2,128)(2,1)} %reshape.45), calls=%async_computation | async-start | bytes 589824 | tf_op jit(solution)/shard_map/all_to_all | solution.py:59
  54.5 0.0 copy-done
  54.5 1.2 %fusion.9 = f32[1,4,64,256]{3,2,1,0:T(8,128)} fusion(bf16[2304,256,1]{1,0,2:T(8,128)(2,1)S(1)} %bitcast.64, bf16[1,4,64,2304]{3,2,1,0:T(8,128)(2,1)S(1)} %copy-done), kind=kOutput, calls=%fused_computation.12 | convolution fusion | flops 301989888 | bytes 2621440 | tf_op jit(solution)/shard_map/brwq,qo->brwo/dot_general | solution.py:244
  55.7 9.3 %shard_map.104 = bf16[1,4,64,2304]{3,2,1,0:T(8,128)(2,1)} custom-call(s32[1]{0:T(128)} %bitcast.first_ref, s32[16,12]{1,0:T(8,128)} %src_ref.3, s32[16,12]{1,0:T(8,128)} %start_ref.3, s32[16,12]{1,0:T(8,128)} %span_ref.3, s32[16,12]{1,0:T(8,128)} %basis_ref.3, f32[16,12]{1,0:T(8,128)} %rsqrt_multiply_fusion.scale_ref, ...), custom_call_target="tpu_custom_call" | custom-call | tf_op jit(solution)/shard_map/pallas_call | solution.py:167
  64.9 0.0 copy-start.1
  64.9 0.0 copy-start.3
  64.9 0.1 pad_maximum_fusion
  65.1 1.1 %copy-done.1 = bf16[1,4,64,2304]{3,2,1,0:T(8,128)(2,1)S(1)} copy-done((bf16[1,4,64,2304]{3,2,1,0:T(8,128)(2,1)S(1)}, bf16[1,4,64,2304]{3,2,1,0:T(8,128)(2,1)}, u32[]{:S(2)}) %copy-start.1) | copy-done | bytes 1179672
  66.2 0.4 copy-done.3
  66.6 1.2 %fusion.12 = f32[1,4,64,256]{3,2,1,0:T(8,128)} fusion(bf16[2304,256,1]{1,0,2:T(8,128)(2,1)S(1)} %bitcast.65, bf16[1,4,64,2304]{3,2,1,0:T(8,128)(2,1)S(1)} %copy-done.1), kind=kOutput, calls=%fused_computation.13 | convolution fusion | flops 301989888 | bytes 2621440 | tf_op jit(solution)/shard_map/bpwq,qc->bpwc/dot_general | solution.py:257
  67.8 0.0 all-to-all-done
  67.8 1.4 %reshape.46 = bf16[4,9,64,64]{3,2,1,0:T(8,128)(2,1)S(1)} reshape(bf16[4,2,18432]{2,1,0:T(2,128)(2,1)} %all-to-all-done) | data formatting | bytes 589824
  69.1 0.1 bitcast_convert_fusion
  69.3 0.1 multiply_bitcast_fusion
  69.4 0.9 %copy.17 = f32[9,64,64]{2,1,0:T(8,128)} copy(f32[9,64,64]{1,2,0:T(8,128)S(1)} %multiply_bitcast_fusion) | data formatting | bytes 294912
  (6 shorter events, 0.1 us)
Async XLA Ops:
  2.5 6.7 %collective-permute-start = (bf16[1,2,64,512]{3,2,1,0:T(8,128)(2,1)S(1)}, bf16[1,2,64,512]{3,2,1,0:T(8,128)(2,1)S(1)}, u32[]{:S(2)}, u32[]{:S(2)}) collective-permute-start(bf16[1,2,64,512]{3,2,1,0:T(8,128)(2,1)S(1)} %get-tuple-element.28), channel_id=1, source_target_pairs={{0,4},{4,8},{8,12},{1,5},{5,9},{9,13},{2,6},{6,10},{10,14},{3,7},{... | collective-permute-start | bytes 393224 | tf_op jit(solution)/shard_map/ppermute | solution.py:23
  6.5 5.7 %collective-permute-start.1 = (bf16[1,2,64,512]{3,2,1,0:T(8,128)(2,1)S(1)}, bf16[1,2,64,512]{3,2,1,0:T(8,128)(2,1)S(1)}, u32[]{:S(2)}, u32[]{:S(2)}) collective-permute-start(bf16[1,2,64,512]{3,2,1,0:T(8,128)(2,1)S(1)} %get-tuple-element.29), channel_id=1, source_target_pairs={{4,0},{8,4},{12,8},{5,1},{9,5},{13,9},{6,2},{10,6},{14,10},{7,3},{... | collective-permute-start | bytes 393224 | tf_op jit(solution)/shard_map/ppermute | solution.py:26
  12.4 5.3 %collective-permute-start.4 = (f32[2,1,4,256]{3,0,2,1:T(2,128)S(1)}, f32[2,1,4,256]{3,0,2,1:T(2,128)S(1)}, u32[]{:S(2)}, u32[]{:S(2)}) collective-permute-start(f32[2,1,4,256]{3,0,2,1:T(2,128)S(1)} %pad_maximum_fusion.2), channel_id=1, source_target_pairs={{0,1},{1,2},{2,3},{3,0},{4,5},{5,6},{6,7},{7,4},{8,9},{9,10},{10,1... | collective-permute-start | bytes 24584 | tf_op jit(solution)/shard_map/ppermute | solution.py:36
  15.7 2.5 %collective-permute-start.5 = (f32[2,1,4,256]{3,0,2,1:T(2,128)S(1)}, f32[2,1,4,256]{3,0,2,1:T(2,128)S(1)}, u32[]{:S(2)}, u32[]{:S(2)}) collective-permute-start(f32[2,1,4,256]{3,0,2,1:T(2,128)S(1)} %pad_maximum_fusion.2), channel_id=1, source_target_pairs={{0,2},{1,3},{2,0},{3,1},{4,6},{5,7},{6,4},{7,5},{8,10},{9,11},{10,... | collective-permute-start | bytes 24584 | tf_op jit(solution)/shard_map/ppermute | solution.py:36
  15.9 3.1 %collective-permute-start.6 = (f32[2,1,4,256]{3,0,2,1:T(2,128)S(1)}, f32[2,1,4,256]{3,0,2,1:T(2,128)S(1)}, u32[]{:S(2)}, u32[]{:S(2)}) collective-permute-start(f32[2,1,4,256]{3,0,2,1:T(2,128)S(1)} %pad_maximum_fusion.2), channel_id=1, source_target_pairs={{0,3},{1,0},{2,1},{3,2},{4,7},{5,4},{6,5},{7,6},{8,11},{9,8},{10,9... | collective-permute-start | bytes 24584 | tf_op jit(solution)/shard_map/ppermute | solution.py:36
  16.2 3.5 %collective-permute-start.2 = (bf16[1,8,16,512]{3,2,1,0:T(8,128)(2,1)S(1)}, bf16[1,8,16,512]{3,2,1,0:T(8,128)(2,1)S(1)}, u32[]{:S(2)}, u32[]{:S(2)}) collective-permute-start(bf16[1,8,16,512]{3,2,1,0:T(8,128)(2,1)S(1)} %get-tuple-element.26), channel_id=1, source_target_pairs={{0,1},{1,2},{2,3},{3,0},{4,5},{5,6},{6,7},{7,4},{8,9},{9,10},{10,1... | collective-permute-start | bytes 393224 | tf_op jit(solution)/shard_map/ppermute | solution.py:23
  17.8 5.0 %collective-permute-start.3 = (bf16[1,8,16,512]{3,2,1,0:T(8,128)(2,1)S(1)}, bf16[1,8,16,512]{3,2,1,0:T(8,128)(2,1)S(1)}, u32[]{:S(2)}, u32[]{:S(2)}) collective-permute-start(bf16[1,8,16,512]{3,2,1,0:T(8,128)(2,1)S(1)} %get-tuple-element.27), channel_id=1, source_target_pairs={{1,0},{2,1},{3,2},{0,3},{5,4},{6,5},{7,6},{4,7},{9,8},{10,9},{11,1... | collective-permute-start | bytes 393224 | tf_op jit(solution)/shard_map/ppermute | solution.py:26
  23.8 3.9 %copy-start.4 = (bf16[1,4,64,256]{3,2,1,0:T(8,128)(2,1)S(1)}, bf16[1,4,64,256]{3,2,1,0:T(8,128)(2,1)}, u32[]{:S(2)}) copy-start(bf16[1,4,64,256]{3,2,1,0:T(8,128)(2,1)} %param.9) | copy-start | bytes 393220
  29.5 2.4 %copy-start.2 = (bf16[9,256,256]{2,1,0:T(8,128)(2,1)S(1)}, bf16[9,256,256]{2,1,0:T(8,128)(2,1)}, u32[]{:S(2)}) copy-start(bf16[9,256,256]{2,1,0:T(8,128)(2,1)} %param.10) | copy-start | bytes 3538948
  30.5 5.5 %collective-permute-start.7 = (bf16[9,256,64]{1,2,0:T(8,128)(2,1)}, bf16[9,256,64]{1,2,0:T(8,128)(2,1)}, u32[]{:S(2)}, u32[]{:S(2)}) collective-permute-start(bf16[9,256,64]{1,2,0:T(8,128)(2,1)} %get-tuple-element.19), channel_id=1, source_target_pairs={{0,1},{1,2},{2,3},{3,0},{4,5},{5,6},{6,7},{7,4},{8,9},{9,10},{10,1... | collective-permute-start | bytes 884744 | tf_op jit(solution)/shard_map/ppermute | solution.py:48
  30.5 13.9 %collective-permute-start.8 = (bf16[9,256,64]{1,2,0:T(8,128)(2,1)}, bf16[9,256,64]{1,2,0:T(8,128)(2,1)}, u32[]{:S(2)}, u32[]{:S(2)}) collective-permute-start(bf16[9,256,64]{1,2,0:T(8,128)(2,1)} %get-tuple-element.21), channel_id=1, source_target_pairs={{0,2},{1,3},{2,0},{3,1},{4,6},{5,7},{6,4},{7,5},{8,10},{9,11},{10,... | collective-permute-start | bytes 884744 | tf_op jit(solution)/shard_map/ppermute | solution.py:48
  31.7 13.9 %collective-permute-start.9 = (bf16[9,256,64]{1,2,0:T(8,128)(2,1)}, bf16[9,256,64]{1,2,0:T(8,128)(2,1)}, u32[]{:S(2)}, u32[]{:S(2)}) collective-permute-start(bf16[9,256,64]{1,2,0:T(8,128)(2,1)} %get-tuple-element.20), channel_id=1, source_target_pairs={{0,3},{1,0},{2,1},{3,2},{4,7},{5,4},{6,5},{7,6},{8,11},{9,8},{10,9... | collective-permute-start | bytes 884744 | tf_op jit(solution)/shard_map/ppermute | solution.py:48
  48.1 6.4 %copy-start = (bf16[1,4,64,2304]{3,2,1,0:T(8,128)(2,1)S(1)}, bf16[1,4,64,2304]{3,2,1,0:T(8,128)(2,1)}, u32[]{:S(2)}) copy-start(bf16[1,4,64,2304]{3,2,1,0:T(8,128)(2,1)} %shard_map.103) | copy-start | bytes 3538948
  50.4 17.4 %all-to-all-start = ((bf16[4,2,18432]{2,1,0:T(2,128)(2,1)}), bf16[4,2,18432]{2,1,0:T(2,128)(2,1)}, u32[]{:S(2)}, u32[]{:S(2)}) async-start(bf16[4,2,18432]{2,1,0:T(2,128)(2,1)} %reshape.45), calls=%async_computation | async-start | bytes 589824 | tf_op jit(solution)/shard_map/all_to_all | solution.py:59
  64.9 1.3 %copy-start.1 = (bf16[1,4,64,2304]{3,2,1,0:T(8,128)(2,1)S(1)}, bf16[1,4,64,2304]{3,2,1,0:T(8,128)(2,1)}, u32[]{:S(2)}) copy-start(bf16[1,4,64,2304]{3,2,1,0:T(8,128)(2,1)} %shard_map.104) | copy-start | bytes 3538948
  64.9 1.6 %copy-start.3 = (bf16[9,256,256]{1,2,0:T(8,128)(2,1)S(1)}, bf16[9,256,256]{1,2,0:T(8,128)(2,1)}, u32[]{:S(2)}) copy-start(bf16[9,256,256]{1,2,0:T(8,128)(2,1)} %copy.16) | copy-start | bytes 3538948

commit v17 on v15

--- a/solution.py
+++ b/solution.py
@@ -100,9 +100,9 @@
 
 def scatter_kernel(
     first_ref, src_ref, start_ref, span_ref, basis_ref, scale_ref, field_ref, total_ref,
-    out_ref, acc_ref, *, slots, height, lon_count, lon_total,
-):
-    first_row = first_ref[0]
+    out_ref, acc_ref, *, slots, height, lon_count, lon_total, lowest,
+):
+    first_row = first_ref[0] + lowest
     rows = out_ref.shape[1]
     window = field_ref.shape[1]
     padded = field_ref.shape[2]
@@ -111,8 +111,8 @@
     out_col = lax.broadcasted_iota(jnp.int32, (lon_count, padded), 0)
     in_col = lax.broadcasted_iota(jnp.int32, (lon_count, padded), 1) - RIM
     offset = out_col - in_col
-    for row in range(window):
-        global_row = first_row + row - REACH
+    for row in range(lowest, lowest + rows + 2 * REACH):
+        global_row = first_ref[0] + row - REACH
         inside = (global_row >= 0) & (global_row < height)
         table_row = jnp.clip(global_row, 0, height - 1)
         for slot in range(slots):
@@ -141,13 +141,20 @@
             )
 
 
-def run_scatter(first, tables, field, totals, row_count, lon_count, lon_total, part=0):
+def run_scatter(
+    first, tables, field, totals, row_count, lon_count, lon_total, part=0, lowest=0
+):
     members, window, padded, combined = field.shape
     channels = totals.shape[-1]
     height, slots = tables[0].shape
     smem = pl.BlockSpec(memory_space=pltpu.SMEM)
     kernel = functools.partial(
-        scatter_kernel, slots=slots, height=height, lon_count=lon_count, lon_total=lon_total
+        scatter_kernel,
+        slots=slots,
+        height=height,
+        lon_count=lon_count,
+        lon_total=lon_total,
+        lowest=lowest,
     )
     return pl.pallas_call(
         kernel,
@@ -233,14 +240,26 @@
     )
     partial_value = partial_value.reshape(BASIS, channels, channels)
     reduced = ring_scatter(partial_value, "lon", 2)
+    w_back = jnp.transpose(weight, (0, 2, 1)).reshape(BASIS * channels, channels)
+
+    def backward_rows(field, field_totals, lowest, count):
+        back_filtered = run_scatter(
+            first, tables, field, field_totals, count, lon_count, lon_total, 1, lowest
+        )
+        return jnp.einsum(
+            "bpwq,qc->bpwc", back_filtered, w_back, preferred_element_type=jnp.float32
+        )
+
+    early_rows = row_count // 2
+    early_input = backward_rows(both, grad_totals, 0, early_rows)
     both, grad_totals, reduced = lax.optimization_barrier((both, grad_totals, reduced))
     reduced = ring_scatter(reduced, "lat", 1)
-    back_filtered = run_scatter(
-        first, tables, both, grad_totals, row_count, lon_count, lon_total, 1
-    )
-    w_back = jnp.transpose(weight, (0, 2, 1)).reshape(BASIS * channels, channels)
-    grad_input = jnp.einsum(
-        "bpwq,qc->bpwc", back_filtered, w_back, preferred_element_type=jnp.float32
+    grad_input = jnp.concatenate(
+        [
+            early_input,
+            backward_rows(both, grad_totals, early_rows, row_count - early_rows),
+        ],
+        axis=1,
     )
     grad_weight = reduced / jnp.sqrt(jnp.float32(members * height * lon_total))
     return (response, grad_input, grad_weight)

time: 65.6 us -> 63.8 us (0.973)
  the two profiles are of different devices: /device:TPU:0 before, /device:TPU:9 now
where the time goes in v17:
time: 63.8 us; the launch traced here: 63.4 us
  Pallas kernels  16 us (25%)
  starting transfers between devices  14.6 us (23%)
  waiting for transfers between devices  13.9 us (22%)
  matrix products  7.84 us (12%)
  local copies, waits for them, and re-layouts  6.18 us (10%)
  other arithmetic  3.96 us (6%)
  between operations  0.94 us (1%)
    pallas_call x2, Pallas kernels, run_scatter(): pl.pallas_call(kernel, grid=(members,), in_specs=[smem] * 6 + [pl.BlockSp...  12.2 us
    ppermute x6, waiting for transfers between devices, ring_scatter(): sent = lax.ppermute(piece.astype(jnp.bfloat16), axis, pairs)  7.46 us
    ppermute x2, waiting for transfers between devices, with_halo(): lax.ppermute(lax.slice_in_dim(block, 0, width, axis=dim), axis, backward)  5.1 us
    ppermute x2, starting transfers between devices, with_halo(): lax.ppermute(lax.slice_in_dim(block, block.shape[dim] - width, None, axis...  4.78 us
    ppermute x6, starting transfers between devices, ring_scatter(): sent = lax.ppermute(piece.astype(jnp.bfloat16), axis, pairs)  4.04 us
    pallas_call x1, Pallas kernels, run_filter(): pl.pallas_call(kernel, grid=(members, row_count), in_specs=[smem] * 6 + [...  3.8 us
    ppermute x3, starting transfers between devices, ring_sum(): total = total + lax.ppermute(value, axis, pairs)  3.73 us
    dot_general x2, matrix products, backward_rows(): jnp.einsum('bpwq,qc->bpwc', back_filtered, w_back, preferred_element_type...  3.6 us
  transfers between devices with their start and end apart: 13, of which 10 were waited for; matrix products, arithmetic and copies ran while one was open for 14% of the time, Pallas kernels for 19%

profile of v17, /device:TPU:9, one launch (start us, length us, event | category | flops | bytes accessed | tf_op | source)
XLA Modules:
  0.0 63.4 jit_solution(7979425449004295340)
XLA Ops:
  0.6 0.0 copy-start.1
  0.6 1.0 %constant_dynamic-update-slice_fusion.1 = bf16[1,4,64,512]{3,2,1,0:T(8,128)(2,1)S(1)} fusion(bf16[1,4,64,256]{3,2,1,0:T(8,128)(2,1)} %param.8), kind=kLoop, calls=%fused_computation.35 | loop fusion | bytes 262144
  1.7 0.9 %constant_dynamic-update-slice_fusion = bf16[1,4,64,512]{3,2,1,0:T(8,128)(2,1)S(1)} fusion(bf16[1,4,64,512]{3,2,1,0:T(8,128)(2,1)S(1)} %constant_dynamic-update-slice_fusion.1, bf16[1,4,64,256]{3,2,1,0:T(8,128)(2,1)} %param.9), kind=kLoop, calls=%fused_computation.34 | loop fusion | bytes 262144 | tf_op jit(solution)/shard_map/concatenate | solution.py:220
  2.6 3.2 %collective-permute-start = (bf16[1,2,64,512]{3,2,1,0:T(8,128)(2,1)S(1)}, bf16[1,2,64,512]{3,2,1,0:T(8,128)(2,1)S(1)}, u32[]{:S(2)}, u32[]{:S(2)}) collective-permute-start(bf16[1,2,64,512]{3,2,1,0:T(8,128)(2,1)S(1)} %get-tuple-element.27), channel_id=1, source_target_pairs={{0,4},{4,8},{8,12},{1,5},{5,9},{9,13},{2,6},{6,10},{10,14},{3,7},{... | collective-permute-start | bytes 393224 | tf_op jit(solution)/shard_map/ppermute | solution.py:23
  5.8 2.1 %collective-permute-start.1 = (bf16[1,2,64,512]{3,2,1,0:T(8,128)(2,1)S(1)}, bf16[1,2,64,512]{3,2,1,0:T(8,128)(2,1)S(1)}, u32[]{:S(2)}, u32[]{:S(2)}) collective-permute-start(bf16[1,2,64,512]{3,2,1,0:T(8,128)(2,1)S(1)} %get-tuple-element.28), channel_id=1, source_target_pairs={{4,0},{8,4},{12,8},{5,1},{9,5},{13,9},{6,2},{10,6},{14,10},{7,3},{... | collective-permute-start | bytes 393224 | tf_op jit(solution)/shard_map/ppermute | solution.py:26
  8.0 0.0 copy-done.1
  8.0 0.0 copy-start.5
  8.0 0.0 copy-start.6
  8.0 0.7 %copy.17 = bf16[9,256,256]{1,2,0:T(8,128)(2,1)S(1)} copy(bf16[9,256,256]{2,1,0:T(8,128)(2,1)S(1)} %copy-done.1) | data formatting | bytes 2359296 | tf_op args[2]
  8.8 0.0 copy-done.5
  8.8 0.0 copy-done.6
  8.8 0.6 rsqrt_multiply_fusion.scale_ref
  9.4 0.0 collective-permute-done
  9.4 2.1 %collective-permute-done.1 = bf16[1,2,64,512]{3,2,1,0:T(8,128)(2,1)S(1)} collective-permute-done((bf16[1,2,64,512]{3,2,1,0:T(8,128)(2,1)S(1)}, bf16[1,2,64,512]{3,2,1,0:T(8,128)(2,1)S(1)}, u32[]{:S(2)}, u32[]{:S(2)}) %collective-permute-start.1) | collective-permute-done | bytes 131104 | tf_op jit(solution)/shard_map/ppermute | solution.py:26
  11.5 0.1 pad_maximum_fusion
  11.6 0.1 convert_reduce_fusion
  11.7 3.3 %collective-permute-start.4 = (f32[2,1,4,256]{3,0,2,1:T(2,128)S(1)}, f32[2,1,4,256]{3,0,2,1:T(2,128)S(1)}, u32[]{:S(2)}, u32[]{:S(2)}) collective-permute-start(f32[2,1,4,256]{3,0,2,1:T(2,128)S(1)} %pad_maximum_fusion.2), channel_id=1, source_target_pairs={{0,1},{1,2},{2,3},{3,0},{4,5},{5,6},{6,7},{7,4},{8,9},{9,10},{10,1... | collective-permute-start | bytes 24584 | tf_op jit(solution)/shard_map/ppermute | solution.py:36
  15.0 0.3 collective-permute-start.5
  15.2 0.2 collective-permute-start.6
  15.4 1.6 %collective-permute-start.2 = (bf16[1,8,16,512]{3,2,1,0:T(8,128)(2,1)S(1)}, bf16[1,8,16,512]{3,2,1,0:T(8,128)(2,1)S(1)}, u32[]{:S(2)}, u32[]{:S(2)}) collective-permute-start(bf16[1,8,16,512]{3,2,1,0:T(8,128)(2,1)S(1)} %get-tuple-element.25), channel_id=1, source_target_pairs={{0,1},{1,2},{2,3},{3,0},{4,5},{5,6},{6,7},{7,4},{8,9},{9,10},{10,1... | collective-permute-start | bytes 393224 | tf_op jit(solution)/shard_map/ppermute | solution.py:23
  17.0 0.0 collective-permute-start.3
  17.0 0.0 collective-permute-done.4
  17.0 0.4 collective-permute-done.5
  17.5 0.8 %collective-permute-done.6 = f32[2,1,4,256]{3,0,2,1:T(2,128)S(1)} collective-permute-done((f32[2,1,4,256]{3,0,2,1:T(2,128)S(1)}, f32[2,1,4,256]{3,0,2,1:T(2,128)S(1)}, u32[]{:S(2)}, u32[]{:S(2)}) %collective-permute-start.6) | collective-permute-done | bytes 8224 | tf_op jit(solution)/shard_map/ppermute | solution.py:36
  18.3 0.6 fusion.17
  18.9 0.1 collective-permute-done.2
  19.0 3.0 %collective-permute-done.3 = bf16[1,8,16,512]{3,2,1,0:T(8,128)(2,1)S(1)} collective-permute-done((bf16[1,8,16,512]{3,2,1,0:T(8,128)(2,1)S(1)}, bf16[1,8,16,512]{3,2,1,0:T(8,128)(2,1)S(1)}, u32[]{:S(2)}, u32[]{:S(2)}) %collective-permute-start.3) | collective-permute-done | bytes 131104 | tf_op jit(solution)/shard_map/ppermute | solution.py:26
  22.0 1.1 %fusion.11.field_ref = bf16[1,8,128,512]{3,2,1,0:T(8,128)(2,1)} fusion(bf16[1,8,16,512]{3,2,1,0:T(8,128)(2,1)S(1)} %collective-permute-done.3, bf16[1,8,64,512]{3,2,1,0:T(8,128)(2,1)S(1)} %pad_maximum_fusion, bf16[1,8,16,512]{3,2,1,0:T(8,128)(2,1)S(1)} %collective-permute-done.2), kind=kLoop, calls=%fused_computation.13 | loop fusion | flops 5242880 | bytes 1835008 | tf_op jit(solution)/shard_map/concatenate | solution.py:27
  23.1 3.8 %shard_map.103 = bf16[1,4,64,2304]{3,2,1,0:T(8,128)(2,1)} custom-call(s32[1]{0:T(128)} %bitcast.first_ref, s32[16,12]{1,0:T(8,128)} %src_ref.5, s32[16,12]{1,0:T(8,128)} %start_ref.5, s32[16,12]{1,0:T(8,128)} %span_ref.5, s32[16,12]{1,0:T(8,128)} %basis_ref.5, f32[16,12]{1,0:T(8,128)} %rsqrt_multiply_fusion.scale_ref, ...), custom_call_target="tpu_custom_call" | custom-call | tf_op jit(solution)/shard_map/pallas_call | solution.py:192
  26.9 1.8 %convolution_bitcast_fusion = f32[9,256,256]{1,2,0:T(8,128)S(1)} fusion(bf16[4,8,9,8,256]{4,3,2,1,0:T(8,128)(2,1)} %bitcast.57, bf16[1,4,64,256]{3,2,1,0:T(8,128)(2,1)} %param.9), kind=kOutput, calls=%fused_computation.4 | convolution fusion | flops 301989888 | bytes 3670016 | tf_op jit(solution)/shard_map/brwq,brwo->qo/dot_general | solution.py:238
  28.6 0.9 %dynamic-slice_convert_fusion.2 = (bf16[9,256,64]{1,2,0:T(8,128)(2,1)}, bf16[9,256,64]{1,2,0:T(8,128)(2,1)}, bf16[9,256,64]{1,2,0:T(8,128)(2,1)}) fusion(f32[9,256,256]{1,2,0:T(8,128)S(1)} %convolution_bitcast_fusion, s32[]{:T(128)S(6)} %select_n.53, s32[]{:T(128)S(6)} %select_n.57, s32[]{:T(128)S(6)} %select_n.55), kind=kLoop, calls=%fused_computation.19 | loop fusion | bytes 1769484 | tf_op jit(solution)/shard_map/convert_element_type | solution.py:48
  29.6 0.0 collective-permute-start.7
  29.6 1.2 %collective-permute-start.8 = (bf16[9,256,64]{1,2,0:T(8,128)(2,1)}, bf16[9,256,64]{1,2,0:T(8,128)(2,1)}, u32[]{:S(2)}, u32[]{:S(2)}) collective-permute-start(bf16[9,256,64]{1,2,0:T(8,128)(2,1)} %get-tuple-element.21), channel_id=1, source_target_pairs={{0,2},{1,3},{2,0},{3,1},{4,6},{5,7},{6,4},{7,5},{8,10},{9,11},{10,... | collective-permute-start | bytes 884744 | tf_op jit(solution)/shard_map/ppermute | solution.py:48
  30.8 0.2 collective-permute-start.9
  31.0 6.3 %shard_map.104 = bf16[1,2,64,2304]{3,2,1,0:T(8,128)(2,1)} custom-call(s32[1]{0:T(128)} %bitcast.first_ref, s32[16,12]{1,0:T(8,128)} %src_ref.5, s32[16,12]{1,0:T(8,128)} %start_ref.5, s32[16,12]{1,0:T(8,128)} %span_ref.5, s32[16,12]{1,0:T(8,128)} %basis_ref.5, f32[16,12]{1,0:T(8,128)} %rsqrt_multiply_fusion.scale_ref, ...), custom_call_target="tpu_custom_call" | custom-call | tf_op jit(solution)/shard_map/pallas_call | solution.py:159
  37.3 0.0 copy-start
  37.3 2.1 %convolution_bitcast_fusion.2 = f32[1,2,64,256]{3,2,1,0:T(8,128)} fusion(bf16[2304,256,1]{1,0,2:T(8,128)(2,1)S(1)} %bitcast.58, bf16[1,2,64,2304]{3,2,1,0:T(8,128)(2,1)} %shard_map.104), kind=kOutput, calls=%fused_computation.11 | convolution fusion | flops 150994944 | bytes 1900544 | tf_op jit(solution)/shard_map/bpwq,qc->bpwc/dot_general | solution.py:249
  39.4 0.0 copy-done
  39.4 2.5 %fusion.7 = f32[1,4,64,256]{3,2,1,0:T(8,128)} fusion(bf16[2304,256,1]{1,0,2:T(8,128)(2,1)} %bitcast.60, bf16[1,4,64,2304]{3,2,1,0:T(8,128)(2,1)S(1)} %copy-done), kind=kOutput, calls=%fused_computation.9 | convolution fusion | flops 301989888 | bytes 2621440 | tf_op jit(solution)/shard_map/brwq,qo->brwo/dot_general | solution.py:236
  41.9 0.0 collective-permute-done.7
  41.9 1.6 %collective-permute-done.8 = bf16[9,256,64]{1,2,0:T(8,128)(2,1)} collective-permute-done((bf16[9,256,64]{1,2,0:T(8,128)(2,1)}, bf16[9,256,64]{1,2,0:T(8,128)(2,1)}, u32[]{:S(2)}, u32[]{:S(2)}) %collective-permute-start.8) | collective-permute-done | bytes 294944 | tf_op jit(solution)/shard_map/ppermute | solution.py:48
  43.5 1.2 %collective-permute-done.9 = bf16[9,256,64]{1,2,0:T(8,128)(2,1)} collective-permute-done((bf16[9,256,64]{1,2,0:T(8,128)(2,1)}, bf16[9,256,64]{1,2,0:T(8,128)(2,1)}, u32[]{:S(2)}, u32[]{:S(2)}) %collective-permute-start.9) | collective-permute-done | bytes 294944 | tf_op jit(solution)/shard_map/ppermute | solution.py:48
  44.7 1.3 %convert_add_fusion = f32[9,256,64]{1,2,0:T(8,128)S(1)} fusion(bf16[9,256,64]{1,2,0:T(8,128)(2,1)} %collective-permute-done.9, bf16[9,256,64]{1,2,0:T(8,128)(2,1)} %collective-permute-done.8, bf16[9,256,64]{1,2,0:T(8,128)(2,1)} %collective-permute-done.7, f32[9,256,256]{1,2,0:T(8,128)S(1)} %convolution_bitcast_fusion, s32[]{:T(128)S(6)} %select_n.51), kind=kLoop, calls=%fused_computation.16 | loop fusion | flops 884736 | bytes 2064388 | tf_op jit(solution)/shard_map/add | solution.py:49
  46.0 0.0 copy-start.2
  46.0 0.8 %copy-done.2 = f32[9,256,64]{1,2,0:T(8,128)} copy-done((f32[9,256,64]{1,2,0:T(8,128)}, f32[9,256,64]{1,2,0:T(8,128)S(1)}, u32[]{:S(2)}) %copy-start.2) | copy-done | bytes 589848
  46.8 0.2 dynamic-slice_convert_fusion.5
  47.0 1.4 %collective-permute-start.10 = (bf16[9,64,64]{1,2,0:T(8,128)(2,1)S(1)}, bf16[9,64,64]{1,2,0:T(8,128)(2,1)S(1)}, u32[]{:S(2)}, u32[]{:S(2)}) collective-permute-start(bf16[9,64,64]{1,2,0:T(8,128)(2,1)S(1)} %get-tuple-element.22), channel_id=1, source_target_pairs={{0,4},{4,8},{8,12},{12,0},{1,5},{5,9},{9,13},{13,1},{2,6},{6,10},{... | collective-permute-start | bytes 221192 | tf_op jit(solution)/shard_map/ppermute | solution.py:48
  48.4 0.9 %collective-permute-start.11 = (bf16[9,64,64]{1,2,0:T(8,128)(2,1)S(1)}, bf16[9,64,64]{1,2,0:T(8,128)(2,1)S(1)}, u32[]{:S(2)}, u32[]{:S(2)}) collective-permute-start(bf16[9,64,64]{1,2,0:T(8,128)(2,1)S(1)} %get-tuple-element.24), channel_id=1, source_target_pairs={{0,8},{4,12},{8,0},{12,4},{1,9},{5,13},{9,1},{13,5},{2,10},{6,14},... | collective-permute-start | bytes 221192 | tf_op jit(solution)/shard_map/ppermute | solution.py:48
  49.3 0.3 collective-permute-start.12
  49.7 5.9 %shard_map.105 = bf16[1,2,64,2304]{3,2,1,0:T(8,128)(2,1)} custom-call(s32[1]{0:T(128)} %bitcast.first_ref, s32[16,12]{1,0:T(8,128)} %src_ref.5, s32[16,12]{1,0:T(8,128)} %start_ref.5, s32[16,12]{1,0:T(8,128)} %span_ref.5, s32[16,12]{1,0:T(8,128)} %basis_ref.5, f32[16,12]{1,0:T(8,128)} %rsqrt_multiply_fusion.scale_ref, ...), custom_call_target="tpu_custom_call" | custom-call | tf_op jit(solution)/shard_map/pallas_call | solution.py:159
  55.5 0.0 copy-start.4
  55.6 0.0 copy-start.3
  55.6 1.5 %convolution_bitcast_fusion.1 = f32[1,2,64,256]{3,2,1,0:T(8,128)S(1)} fusion(bf16[2304,256,1]{1,0,2:T(8,128)(2,1)S(1)} %bitcast.59, bf16[1,2,64,2304]{3,2,1,0:T(8,128)(2,1)} %shard_map.105), kind=kOutput, calls=%fused_computation.10 | convolution fusion | flops 150994944 | bytes 1900544 | tf_op jit(solution)/shard_map/bpwq,qc->bpwc/dot_general | solution.py:249
  57.0 0.0 copy-done.4
  57.0 0.7 %pad_maximum_fusion.1 = f32[1,4,64,256]{3,2,1,0:T(8,128)} fusion(f32[1,2,64,256]{3,2,1,0:T(8,128)S(1)} %convolution_bitcast_fusion.1, f32[1,2,64,256]{3,2,1,0:T(8,128)S(1)} %copy-done.4), kind=kLoop, calls=%fused_computation.26 | loop fusion | flops 65536 | bytes 524288 | tf_op jit(solution)/shard_map/concatenate | solution.py:257
  57.8 0.6 collective-permute-done.10
  58.3 2.4 %collective-permute-done.11 = bf16[9,64,64]{1,2,0:T(8,128)(2,1)S(1)} collective-permute-done((bf16[9,64,64]{1,2,0:T(8,128)(2,1)S(1)}, bf16[9,64,64]{1,2,0:T(8,128)(2,1)S(1)}, u32[]{:S(2)}, u32[]{:S(2)}) %collective-permute-start.11) | collective-permute-done | bytes 73760 | tf_op jit(solution)/shard_map/ppermute | solution.py:48
  60.7 1.6 %collective-permute-done.12 = bf16[9,64,64]{1,2,0:T(8,128)(2,1)S(1)} collective-permute-done((bf16[9,64,64]{1,2,0:T(8,128)(2,1)S(1)}, bf16[9,64,64]{1,2,0:T(8,128)(2,1)S(1)}, u32[]{:S(2)}, u32[]{:S(2)}) %collective-permute-start.12) | collective-permute-done | bytes 73760 | tf_op jit(solution)/shard_map/ppermute | solution.py:48
  62.4 0.0 copy-done.3
  62.4 0.1 add_multiply_fusion
  62.5 0.9 %copy.19 = f32[9,64,64]{2,1,0:T(8,128)} copy(f32[9,64,64]{1,2,0:T(8,128)S(1)} %add_multiply_fusion) | data formatting | bytes 294912
  (6 shorter events, 0.1 us)
Async XLA Ops:
  0.6 7.4 %copy-start.1 = (bf16[9,256,256]{2,1,0:T(8,128)(2,1)S(1)}, bf16[9,256,256]{2,1,0:T(8,128)(2,1)}, u32[]{:S(2)}) copy-start(bf16[9,256,256]{2,1,0:T(8,128)(2,1)} %param.10) | copy-start | bytes 3538948
  2.6 6.8 %collective-permute-start = (bf16[1,2,64,512]{3,2,1,0:T(8,128)(2,1)S(1)}, bf16[1,2,64,512]{3,2,1,0:T(8,128)(2,1)S(1)}, u32[]{:S(2)}, u32[]{:S(2)}) collective-permute-start(bf16[1,2,64,512]{3,2,1,0:T(8,128)(2,1)S(1)} %get-tuple-element.27), channel_id=1, source_target_pairs={{0,4},{4,8},{8,12},{1,5},{5,9},{9,13},{2,6},{6,10},{10,14},{3,7},{... | collective-permute-start | bytes 393224 | tf_op jit(solution)/shard_map/ppermute | solution.py:23
  5.8 5.7 %collective-permute-start.1 = (bf16[1,2,64,512]{3,2,1,0:T(8,128)(2,1)S(1)}, bf16[1,2,64,512]{3,2,1,0:T(8,128)(2,1)S(1)}, u32[]{:S(2)}, u32[]{:S(2)}) collective-permute-start(bf16[1,2,64,512]{3,2,1,0:T(8,128)(2,1)S(1)} %get-tuple-element.28), channel_id=1, source_target_pairs={{4,0},{8,4},{12,8},{5,1},{9,5},{13,9},{6,2},{10,6},{14,10},{7,3},{... | collective-permute-start | bytes 393224 | tf_op jit(solution)/shard_map/ppermute | solution.py:26
  8.0 0.8 %copy-start.5 = (s32[16,12]{1,0:T(8,128)S(1)}, s32[16,12]{1,0:T(8,128)}, u32[]{:S(2)}) copy-start(s32[16,12]{1,0:T(8,128)} %span_ref.5) | copy-start | bytes 2308
  8.0 0.8 %copy-start.6 = (f32[16,12]{1,0:T(8,128)S(1)}, f32[16,12]{1,0:T(8,128)}, u32[]{:S(2)}) copy-start(f32[16,12]{1,0:T(8,128)} %param.15) | copy-start | bytes 2308
  11.7 5.3 %collective-permute-start.4 = (f32[2,1,4,256]{3,0,2,1:T(2,128)S(1)}, f32[2,1,4,256]{3,0,2,1:T(2,128)S(1)}, u32[]{:S(2)}, u32[]{:S(2)}) collective-permute-start(f32[2,1,4,256]{3,0,2,1:T(2,128)S(1)} %pad_maximum_fusion.2), channel_id=1, source_target_pairs={{0,1},{1,2},{2,3},{3,0},{4,5},{5,6},{6,7},{7,4},{8,9},{9,10},{10,1... | collective-permute-start | bytes 24584 | tf_op jit(solution)/shard_map/ppermute | solution.py:36
  15.0 2.5 %collective-permute-start.5 = (f32[2,1,4,256]{3,0,2,1:T(2,128)S(1)}, f32[2,1,4,256]{3,0,2,1:T(2,128)S(1)}, u32[]{:S(2)}, u32[]{:S(2)}) collective-permute-start(f32[2,1,4,256]{3,0,2,1:T(2,128)S(1)} %pad_maximum_fusion.2), channel_id=1, source_target_pairs={{0,2},{1,3},{2,0},{3,1},{4,6},{5,7},{6,4},{7,5},{8,10},{9,11},{10,... | collective-permute-start | bytes 24584 | tf_op jit(solution)/shard_map/ppermute | solution.py:36
  15.2 3.1 %collective-permute-start.6 = (f32[2,1,4,256]{3,0,2,1:T(2,128)S(1)}, f32[2,1,4,256]{3,0,2,1:T(2,128)S(1)}, u32[]{:S(2)}, u32[]{:S(2)}) collective-permute-start(f32[2,1,4,256]{3,0,2,1:T(2,128)S(1)} %pad_maximum_fusion.2), channel_id=1, source_target_pairs={{0,3},{1,0},{2,1},{3,2},{4,7},{5,4},{6,5},{7,6},{8,11},{9,8},{10,9... | collective-permute-start | bytes 24584 | tf_op jit(solution)/shard_map/ppermute | solution.py:36
  15.4 3.5 %collective-permute-start.2 = (bf16[1,8,16,512]{3,2,1,0:T(8,128)(2,1)S(1)}, bf16[1,8,16,512]{3,2,1,0:T(8,128)(2,1)S(1)}, u32[]{:S(2)}, u32[]{:S(2)}) collective-permute-start(bf16[1,8,16,512]{3,2,1,0:T(8,128)(2,1)S(1)} %get-tuple-element.25), channel_id=1, source_target_pairs={{0,1},{1,2},{2,3},{3,0},{4,5},{5,6},{6,7},{7,4},{8,9},{9,10},{10,1... | collective-permute-start | bytes 393224 | tf_op jit(solution)/shard_map/ppermute | solution.py:23
  17.0 5.0 %collective-permute-start.3 = (bf16[1,8,16,512]{3,2,1,0:T(8,128)(2,1)S(1)}, bf16[1,8,16,512]{3,2,1,0:T(8,128)(2,1)S(1)}, u32[]{:S(2)}, u32[]{:S(2)}) collective-permute-start(bf16[1,8,16,512]{3,2,1,0:T(8,128)(2,1)S(1)} %get-tuple-element.26), channel_id=1, source_target_pairs={{1,0},{2,1},{3,2},{0,3},{5,4},{6,5},{7,6},{4,7},{9,8},{10,9},{11,1... | collective-permute-start | bytes 393224 | tf_op jit(solution)/shard_map/ppermute | solution.py:26
  29.6 12.3 %collective-permute-start.7 = (bf16[9,256,64]{1,2,0:T(8,128)(2,1)}, bf16[9,256,64]{1,2,0:T(8,128)(2,1)}, u32[]{:S(2)}, u32[]{:S(2)}) collective-permute-start(bf16[9,256,64]{1,2,0:T(8,128)(2,1)} %get-tuple-element.19), channel_id=1, source_target_pairs={{0,1},{1,2},{2,3},{3,0},{4,5},{5,6},{6,7},{7,4},{8,9},{9,10},{10,1... | collective-permute-start | bytes 884744 | tf_op jit(solution)/shard_map/ppermute | solution.py:48
  29.6 13.9 %collective-permute-start.8 = (bf16[9,256,64]{1,2,0:T(8,128)(2,1)}, bf16[9,256,64]{1,2,0:T(8,128)(2,1)}, u32[]{:S(2)}, u32[]{:S(2)}) collective-permute-start(bf16[9,256,64]{1,2,0:T(8,128)(2,1)} %get-tuple-element.21), channel_id=1, source_target_pairs={{0,2},{1,3},{2,0},{3,1},{4,6},{5,7},{6,4},{7,5},{8,10},{9,11},{10,... | collective-permute-start | bytes 884744 | tf_op jit(solution)/shard_map/ppermute | solution.py:48
  30.8 13.9 %collective-permute-start.9 = (bf16[9,256,64]{1,2,0:T(8,128)(2,1)}, bf16[9,256,64]{1,2,0:T(8,128)(2,1)}, u32[]{:S(2)}, u32[]{:S(2)}) collective-permute-start(bf16[9,256,64]{1,2,0:T(8,128)(2,1)} %get-tuple-element.20), channel_id=1, source_target_pairs={{0,3},{1,0},{2,1},{3,2},{4,7},{5,4},{6,5},{7,6},{8,11},{9,8},{10,9... | collective-permute-start | bytes 884744 | tf_op jit(solution)/shard_map/ppermute | solution.py:48
  37.3 2.1 %copy-start = (bf16[1,4,64,2304]{3,2,1,0:T(8,128)(2,1)S(1)}, bf16[1,4,64,2304]{3,2,1,0:T(8,128)(2,1)}, u32[]{:S(2)}) copy-start(bf16[1,4,64,2304]{3,2,1,0:T(8,128)(2,1)} %shard_map.103) | copy-start | bytes 3538948
  46.0 0.8 %copy-start.2 = (f32[9,256,64]{1,2,0:T(8,128)}, f32[9,256,64]{1,2,0:T(8,128)S(1)}, u32[]{:S(2)}) copy-start(f32[9,256,64]{1,2,0:T(8,128)S(1)} %convert_add_fusion) | copy-start | bytes 1769476
  47.0 11.3 %collective-permute-start.10 = (bf16[9,64,64]{1,2,0:T(8,128)(2,1)S(1)}, bf16[9,64,64]{1,2,0:T(8,128)(2,1)S(1)}, u32[]{:S(2)}, u32[]{:S(2)}) collective-permute-start(bf16[9,64,64]{1,2,0:T(8,128)(2,1)S(1)} %get-tuple-element.22), channel_id=1, source_target_pairs={{0,4},{4,8},{8,12},{12,0},{1,5},{5,9},{9,13},{13,1},{2,6},{6,10},{... | collective-permute-start | bytes 221192 | tf_op jit(solution)/shard_map/ppermute | solution.py:48
  48.4 12.3 %collective-permute-start.11 = (bf16[9,64,64]{1,2,0:T(8,128)(2,1)S(1)}, bf16[9,64,64]{1,2,0:T(8,128)(2,1)S(1)}, u32[]{:S(2)}, u32[]{:S(2)}) collective-permute-start(bf16[9,64,64]{1,2,0:T(8,128)(2,1)S(1)} %get-tuple-element.24), channel_id=1, source_target_pairs={{0,8},{4,12},{8,0},{12,4},{1,9},{5,13},{9,1},{13,5},{2,10},{6,14},... | collective-permute-start | bytes 221192 | tf_op jit(solution)/shard_map/ppermute | solution.py:48
  49.3 13.0 %collective-permute-start.12 = (bf16[9,64,64]{1,2,0:T(8,128)(2,1)S(1)}, bf16[9,64,64]{1,2,0:T(8,128)(2,1)S(1)}, u32[]{:S(2)}, u32[]{:S(2)}) collective-permute-start(bf16[9,64,64]{1,2,0:T(8,128)(2,1)S(1)} %get-tuple-element.23), channel_id=1, source_target_pairs={{0,12},{4,0},{8,4},{12,8},{1,13},{5,1},{9,5},{13,9},{2,14},{6,2},{... | collective-permute-start | bytes 221192 | tf_op jit(solution)/shard_map/ppermute | solution.py:48
  55.5 1.5 %copy-start.4 = (f32[1,2,64,256]{3,2,1,0:T(8,128)S(1)}, f32[1,2,64,256]{3,2,1,0:T(8,128)}, u32[]{:S(2)}) copy-start(f32[1,2,64,256]{3,2,1,0:T(8,128)} %convolution_bitcast_fusion.2) | copy-start | bytes 393220
  55.6 6.8 %copy-start.3 = (f32[9,256,64]{1,2,0:T(8,128)S(1)}, f32[9,256,64]{1,2,0:T(8,128)}, u32[]{:S(2)}) copy-start(f32[9,256,64]{1,2,0:T(8,128)} %copy-done.2) | copy-start | bytes 1769476

commit v18 on v17

--- a/solution.py
+++ b/solution.py
@@ -52,7 +52,7 @@
 
 def filter_kernel(
     first_ref, src_ref, start_ref, span_ref, basis_ref, scale_ref, field_ref, total_ref,
-    out_ref, acc_ref, *, slots, height, lon_count, lon_total, backward,
+    cot_ref, out_ref, part_ref, acc_ref, *, slots, height, lon_count, lon_total, backward,
 ):
     r = pl.program_id(1)
     first_row = first_ref[0]
@@ -94,8 +94,17 @@
             row = src_ref[table_row, slot] - first_row + REACH
             add_slot(row, table_row, slot, scale_ref[table_row, slot])
 
+    @pl.when((pl.program_id(0) == 0) & (pl.program_id(1) == 0))
+    def _():
+        part_ref[...] = jnp.zeros(part_ref.shape, jnp.float32)
+
+    cot = cot_ref[0, 0]
     for k in range(BASIS):
-        out_ref[0, 0, :, k * channels:(k + 1) * channels] = acc_ref[k].astype(jnp.bfloat16)
+        rounded = acc_ref[k].astype(jnp.bfloat16)
+        out_ref[0, 0, :, k * channels:(k + 1) * channels] = rounded
+        part_ref[k] = part_ref[k] + lax.dot_general(
+            rounded, cot, (((0,), (0,)), ((), ())), preferred_element_type=jnp.float32
+        )
 
 
 def scatter_kernel(
@@ -175,10 +184,11 @@
 
 
 def run_filter(
-    first, tables, field, totals, row_count, lon_count, lon_total, backward, part=0
+    first, tables, field, totals, cot, row_count, lon_count, lon_total, backward, part=0
 ):
     members, window, padded, combined = field.shape
     channels = totals.shape[-1]
+    out_channels = cot.shape[-1]
     height, slots = tables[0].shape
     smem = pl.BlockSpec(memory_space=pltpu.SMEM)
     kernel = functools.partial(
@@ -196,15 +206,18 @@
         + [
             pl.BlockSpec((1, window, padded, channels), lambda b, r: (b, 0, 0, part)),
             pl.BlockSpec((1, window, 1, channels), lambda b, r: (b, 0, 0, 0)),
-        ],
-        out_specs=pl.BlockSpec(
-            (1, 1, lon_count, BASIS * channels), lambda b, r: (b, r, 0, 0)
-        ),
-        out_shape=jax.ShapeDtypeStruct(
-            (members, row_count, lon_count, BASIS * channels), jnp.bfloat16
-        ),
+            pl.BlockSpec((1, 1, lon_count, out_channels), lambda b, r: (b, r, 0, 0)),
+        ],
+        out_specs=[
+            pl.BlockSpec((1, 1, lon_count, BASIS * channels), lambda b, r: (b, r, 0, 0)),
+            pl.BlockSpec((BASIS, channels, out_channels), lambda b, r: (0, 0, 0)),
+        ],
+        out_shape=[
+            jax.ShapeDtypeStruct((members, row_count, lon_count, BASIS * channels), jnp.bfloat16),
+            jax.ShapeDtypeStruct((BASIS, channels, out_channels), jnp.float32),
+        ],
         scratch_shapes=[pltpu.VMEM((BASIS, lon_count, channels), jnp.float32)],
-    )(first, *tables, field, totals[:, :, None, :])
+    )(first, *tables, field, totals[:, :, None, :], cot)
 
 
 def on_device(inputs, cotangent, weight, src_rows, lon_start, lon_span, basis_idx, quad_weight):
@@ -231,14 +244,12 @@
         framed = with_halo(local_totals, (("lat", 2),), REACH, False)
     totals, grad_totals = framed[0], framed[1]
 
-    flattened = run_filter(first, tables, both, totals, row_count, lon_count, lon_total, False, 0)
+    flattened, partial_value = run_filter(
+        first, tables, both, totals, cotangent, row_count, lon_count, lon_total, False, 0
+    )
     w_fwd = weight.reshape(BASIS * channels, channels)
     response = jnp.einsum("brwq,qo->brwo", flattened, w_fwd, preferred_element_type=jnp.float32)
 
-    partial_value = jnp.einsum(
-        "brwq,brwo->qo", flattened, cotangent, preferred_element_type=jnp.float32
-    )
-    partial_value = partial_value.reshape(BASIS, channels, channels)
     reduced = ring_scatter(partial_value, "lon", 2)
     w_back = jnp.transpose(weight, (0, 2, 1)).reshape(BASIS * channels, channels)
 

time: 63.8 us -> 74.8 us (1.17)
  the two profiles are of different devices: /device:TPU:9 before, /device:TPU:0 now
where the time goes in v18:
time: 74.8 us; the launch traced here: 73.9 us
  Pallas kernels  19.2 us (26%)
  starting transfers between devices  18.3 us (24%)
  local copies, waits for them, and re-layouts  17.9 us (24%)
  waiting for transfers between devices  6.65 us (9%)
  other arithmetic  6.11 us (8%)
  matrix products  4.74 us (6%)
  between operations  0.96 us (1%)
    pallas_call x2, Pallas kernels, run_scatter(): pl.pallas_call(kernel, grid=(members,), in_specs=[smem] * 6 + [pl.BlockSp...  12.8 us
    ppermute x6, starting transfers between devices, ring_scatter(): sent = lax.ppermute(piece.astype(jnp.bfloat16), axis, pairs)  7.32 us
    convert_element_type x5, local copies, waits for them, and re-layouts, ring_scatter(): sent = lax.ppermute(piece.astype(jnp.bfloat16), axis, pairs)  7.32 us
    pallas_call x1, Pallas kernels, run_filter(): pl.pallas_call(kernel, grid=(members, row_count), in_specs=[smem] * 6 + [...  6.4 us
    ppermute x3, local copies, waits for them, and re-layouts, ring_scatter(): sent = lax.ppermute(piece.astype(jnp.bfloat16), axis, pairs)  6.23 us
    ppermute x2, starting transfers between devices, with_halo(): lax.ppermute(lax.slice_in_dim(block, block.shape[dim] - width, None, axis...  4.99 us
    ppermute x2, waiting for transfers between devices, with_halo(): lax.ppermute(lax.slice_in_dim(block, 0, width, axis=dim), axis, backward)  4.04 us
    dot_general x2, matrix products, backward_rows(): jnp.einsum('bpwq,qc->bpwc', back_filtered, w_back, preferred_element_type...  3.56 us
  transfers between devices with their start and end apart: 13, of which 2 were waited for; matrix products, arithmetic and copies ran while one was open for 18% of the time, Pallas kernels for 17%

profile of v18, /device:TPU:0, one launch (start us, length us, event | category | flops | bytes accessed | tf_op | source)
XLA Modules:
  0.0 73.9 jit_solution(4962082738964358119)
XLA Ops:
  0.6 0.0 copy-start
  0.6 1.0 %constant_dynamic-update-slice_fusion.1 = bf16[1,4,64,512]{3,2,1,0:T(8,128)(2,1)S(1)} fusion(bf16[1,4,64,256]{3,2,1,0:T(8,128)(2,1)} %param.8), kind=kLoop, calls=%fused_computation.31 | loop fusion | bytes 262144
  1.7 0.9 %constant_dynamic-update-slice_fusion = bf16[1,4,64,512]{3,2,1,0:T(8,128)(2,1)S(1)} fusion(bf16[1,4,64,512]{3,2,1,0:T(8,128)(2,1)S(1)} %constant_dynamic-update-slice_fusion.1, bf16[1,4,64,256]{3,2,1,0:T(8,128)(2,1)} %cot_ref.1), kind=kLoop, calls=%fused_computation.30 | loop fusion | bytes 262144 | tf_op jit(solution)/shard_map/concatenate | solution.py:233
  2.6 4.9 %collective-permute-start = (bf16[1,2,64,512]{3,2,1,0:T(8,128)(2,1)S(1)}, bf16[1,2,64,512]{3,2,1,0:T(8,128)(2,1)S(1)}, u32[]{:S(2)}, u32[]{:S(2)}) collective-permute-start(bf16[1,2,64,512]{3,2,1,0:T(8,128)(2,1)S(1)} %get-tuple-element.25), channel_id=1, source_target_pairs={{0,4},{4,8},{8,12},{1,5},{5,9},{9,13},{2,6},{6,10},{10,14},{3,7},{... | collective-permute-start | bytes 393224 | tf_op jit(solution)/shard_map/ppermute | solution.py:23
  7.5 1.3 %collective-permute-start.1 = (bf16[1,2,64,512]{3,2,1,0:T(8,128)(2,1)S(1)}, bf16[1,2,64,512]{3,2,1,0:T(8,128)(2,1)S(1)}, u32[]{:S(2)}, u32[]{:S(2)}) collective-permute-start(bf16[1,2,64,512]{3,2,1,0:T(8,128)(2,1)S(1)} %get-tuple-element.26), channel_id=1, source_target_pairs={{4,0},{8,4},{12,8},{5,1},{9,5},{13,9},{6,2},{10,6},{14,10},{7,3},{... | collective-permute-start | bytes 393224 | tf_op jit(solution)/shard_map/ppermute | solution.py:26
  8.9 0.0 copy-done
  8.9 0.0 copy-start.5
  8.9 0.0 copy-start.6
  9.0 0.7 copy.27
  9.7 0.0 copy-done.5
  9.7 0.0 copy-done.6
  9.7 0.6 rsqrt_multiply_fusion.scale_ref
  10.4 0.0 collective-permute-done
  10.4 4.0 %collective-permute-done.1 = bf16[1,2,64,512]{3,2,1,0:T(8,128)(2,1)S(1)} collective-permute-done((bf16[1,2,64,512]{3,2,1,0:T(8,128)(2,1)S(1)}, bf16[1,2,64,512]{3,2,1,0:T(8,128)(2,1)S(1)}, u32[]{:S(2)}, u32[]{:S(2)}) %collective-permute-start.1) | collective-permute-done | bytes 131104 | tf_op jit(solution)/shard_map/ppermute | solution.py:26
  14.4 0.1 pad_maximum_fusion
  14.5 0.1 convert_reduce_fusion
  14.6 0.1 collective-permute-start.4
  14.6 1.6 %collective-permute-start.5 = (f32[2,1,4,256]{3,0,2,1:T(2,128)S(1)}, f32[2,1,4,256]{3,0,2,1:T(2,128)S(1)}, u32[]{:S(2)}, u32[]{:S(2)}) collective-permute-start(f32[2,1,4,256]{3,0,2,1:T(2,128)S(1)} %pad_maximum_fusion.2), channel_id=1, source_target_pairs={{0,2},{1,3},{2,0},{3,1},{4,6},{5,7},{6,4},{7,5},{8,10},{9,11},{10,... | collective-permute-start | bytes 24584 | tf_op jit(solution)/shard_map/ppermute | solution.py:36
  16.2 1.4 %collective-permute-start.6 = (f32[2,1,4,256]{3,0,2,1:T(2,128)S(1)}, f32[2,1,4,256]{3,0,2,1:T(2,128)S(1)}, u32[]{:S(2)}, u32[]{:S(2)}) collective-permute-start(f32[2,1,4,256]{3,0,2,1:T(2,128)S(1)} %pad_maximum_fusion.2), channel_id=1, source_target_pairs={{0,3},{1,0},{2,1},{3,2},{4,7},{5,4},{6,5},{7,6},{8,11},{9,8},{10,9... | collective-permute-start | bytes 24584 | tf_op jit(solution)/shard_map/ppermute | solution.py:36
  17.6 0.1 collective-permute-start.2
  17.7 1.7 %collective-permute-start.3 = (bf16[1,8,16,512]{3,2,1,0:T(8,128)(2,1)S(1)}, bf16[1,8,16,512]{3,2,1,0:T(8,128)(2,1)S(1)}, u32[]{:S(2)}, u32[]{:S(2)}) collective-permute-start(bf16[1,8,16,512]{3,2,1,0:T(8,128)(2,1)S(1)} %get-tuple-element.24), channel_id=1, source_target_pairs={{1,0},{2,1},{3,2},{0,3},{5,4},{6,5},{7,6},{4,7},{9,8},{10,9},{11,1... | collective-permute-start | bytes 393224 | tf_op jit(solution)/shard_map/ppermute | solution.py:26
  19.4 0.0 collective-permute-done.4
  19.4 0.0 collective-permute-done.5
  19.4 0.0 collective-permute-done.6
  19.4 0.6 fusion.14
  20.1 2.6 %collective-permute-done.2 = bf16[1,8,16,512]{3,2,1,0:T(8,128)(2,1)S(1)} collective-permute-done((bf16[1,8,16,512]{3,2,1,0:T(8,128)(2,1)S(1)}, bf16[1,8,16,512]{3,2,1,0:T(8,128)(2,1)S(1)}, u32[]{:S(2)}, u32[]{:S(2)}) %collective-permute-start.2) | collective-permute-done | bytes 131104 | tf_op jit(solution)/shard_map/ppermute | solution.py:23
  22.7 0.0 collective-permute-done.3
  22.7 1.1 %fusion.9.field_ref = bf16[1,8,128,512]{3,2,1,0:T(8,128)(2,1)} fusion(bf16[1,8,16,512]{3,2,1,0:T(8,128)(2,1)S(1)} %collective-permute-done.3, bf16[1,8,64,512]{3,2,1,0:T(8,128)(2,1)S(1)} %pad_maximum_fusion, bf16[1,8,16,512]{3,2,1,0:T(8,128)(2,1)S(1)} %collective-permute-done.2), kind=kLoop, calls=%fused_computation.14 | loop fusion | flops 5242880 | bytes 1835008 | tf_op jit(solution)/shard_map/concatenate | solution.py:27
  23.7 6.4 %shard_map.103 = (bf16[1,4,64,2304]{3,2,1,0:T(8,128)(2,1)}, f32[9,256,256]{2,1,0:T(8,128)}) custom-call(s32[1]{0:T(128)} %bitcast.first_ref, s32[16,12]{1,0:T(8,128)} %src_ref.5, s32[16,12]{1,0:T(8,128)} %start_ref.5, s32[16,12]{1,0:T(8,128)} %span_ref.5, s32[16,12]{1,0:T(8,128)} %basis_ref.5, f32[16,12]{1,0:T(8,128)} %rsqrt_multiply_fusion.scale_ref, ...), custom_call_target="tpu_custom_call" | custom-call | tf_op jit(solution)/shard_map/pallas_call | solution.py:202
  30.1 3.4 %dynamic-slice_convert_fusion.2 = (bf16[9,256,64]{2,1,0:T(8,128)(2,1)}, bf16[9,256,64]{2,1,0:T(8,128)(2,1)S(1)}, bf16[9,256,64]{2,1,0:T(8,128)(2,1)S(1)}) fusion(f32[9,256,256]{2,1,0:T(8,128)} %get-tuple-element.13, s32[]{:T(128)S(6)} %select_n.53, s32[]{:T(128)S(6)} %select_n.57, s32[]{:T(128)S(6)} %select_n.55), kind=kLoop, calls=%fused_computation.9 | loop fusion | bytes 1769484 | tf_op jit(solution)/shard_map/convert_element_type | solution.py:48
  33.5 2.0 %copy.28 = bf16[9,256,64]{1,2,0:T(8,128)(2,1)} copy(bf16[9,256,64]{2,1,0:T(8,128)(2,1)} %get-tuple-element.17) | data formatting | bytes 589824 | tf_op jit(solution)/shard_map/convert_element_type | solution.py:48
  35.5 0.6 collective-permute-start.7
  36.1 0.9 %copy.30 = bf16[9,256,64]{1,2,0:T(8,128)(2,1)} copy(bf16[9,256,64]{2,1,0:T(8,128)(2,1)S(1)} %get-tuple-element.19) | data formatting | bytes 589824 | tf_op jit(solution)/shard_map/convert_element_type | solution.py:48
  37.0 0.9 %collective-permute-start.8 = (bf16[9,256,64]{1,2,0:T(8,128)(2,1)}, bf16[9,256,64]{1,2,0:T(8,128)(2,1)}, u32[]{:S(2)}, u32[]{:S(2)}) collective-permute-start(bf16[9,256,64]{1,2,0:T(8,128)(2,1)} %copy.30), channel_id=1, source_target_pairs={{0,2},{1,3},{2,0},{3,1},{4,6},{5,7},{6,4},{7,5},{8,10},{9,11},{10,... | collective-permute-start | bytes 884744 | tf_op jit(solution)/shard_map/ppermute | solution.py:48
  38.0 0.9 %copy.32 = bf16[9,256,64]{1,2,0:T(8,128)(2,1)} copy(bf16[9,256,64]{2,1,0:T(8,128)(2,1)S(1)} %get-tuple-element.18) | data formatting | bytes 589824 | tf_op jit(solution)/shard_map/convert_element_type | solution.py:48
  38.9 0.4 collective-permute-start.9
  39.4 6.1 %shard_map.104 = bf16[1,2,64,2304]{3,2,1,0:T(8,128)(2,1)} custom-call(s32[1]{0:T(128)} %bitcast.first_ref, s32[16,12]{1,0:T(8,128)} %src_ref.5, s32[16,12]{1,0:T(8,128)} %start_ref.5, s32[16,12]{1,0:T(8,128)} %span_ref.5, s32[16,12]{1,0:T(8,128)} %basis_ref.5, f32[16,12]{1,0:T(8,128)} %rsqrt_multiply_fusion.scale_ref, ...), custom_call_target="tpu_custom_call" | custom-call | tf_op jit(solution)/shard_map/pallas_call | solution.py:168
  45.5 0.0 copy-start.3
  45.5 2.1 %convolution_bitcast_fusion.1 = f32[1,2,64,256]{3,2,1,0:T(8,128)} fusion(bf16[2304,256,1]{1,0,2:T(8,128)(2,1)S(1)} %bitcast.44, bf16[1,2,64,2304]{3,2,1,0:T(8,128)(2,1)} %shard_map.104), kind=kOutput, calls=%fused_computation.12 | convolution fusion | flops 150994944 | bytes 1900544 | tf_op jit(solution)/shard_map/bpwq,qc->bpwc/dot_general | solution.py:260
  47.6 0.0 copy-done.3
  47.6 1.2 %fusion.5 = f32[1,4,64,256]{3,2,1,0:T(8,128)} fusion(bf16[2304,256,1]{1,0,2:T(8,128)(2,1)S(1)} %bitcast.46, bf16[1,4,64,2304]{3,2,1,0:T(8,128)(2,1)S(1)} %copy-done.3), kind=kOutput, calls=%fused_computation.10 | convolution fusion | flops 301989888 | bytes 2621440 | tf_op jit(solution)/shard_map/brwq,qo->brwo/dot_general | solution.py:251
  48.8 0.0 copy-start.1
  48.8 0.0 collective-permute-done.7
  48.8 2.2 %copy.29 = bf16[9,256,64]{2,1,0:T(8,128)(2,1)} copy(bf16[9,256,64]{1,2,0:T(8,128)(2,1)} %collective-permute-done.7) | data formatting | bytes 589824 | tf_op jit(solution)/shard_map/ppermute | solution.py:48
  51.0 0.0 collective-permute-done.8
  51.0 2.0 %copy.31 = bf16[9,256,64]{2,1,0:T(8,128)(2,1)} copy(bf16[9,256,64]{1,2,0:T(8,128)(2,1)} %collective-permute-done.8) | data formatting | bytes 589824 | tf_op jit(solution)/shard_map/ppermute | solution.py:48
  53.0 0.0 collective-permute-done.9
  53.0 2.0 %copy.33 = bf16[9,256,64]{2,1,0:T(8,128)(2,1)} copy(bf16[9,256,64]{1,2,0:T(8,128)(2,1)} %collective-permute-done.9) | data formatting | bytes 589824 | tf_op jit(solution)/shard_map/ppermute | solution.py:48
  55.0 0.0 copy-done.1
  55.0 1.8 %convert_add_fusion = f32[9,256,64]{2,1,0:T(8,128)S(1)} fusion(bf16[9,256,64]{2,1,0:T(8,128)(2,1)} %copy.33, bf16[9,256,64]{2,1,0:T(8,128)(2,1)} %copy.31, bf16[9,256,64]{2,1,0:T(8,128)(2,1)} %copy.29, f32[9,256,256]{2,1,0:T(8,128)S(1)} %copy-done.1, s32[]{:T(128)S(6)} %select_n.51), kind=kLoop, calls=%fused_computation.6 | loop fusion | flops 884736 | bytes 2064388 | tf_op jit(solution)/shard_map/add | solution.py:49
  56.8 0.0 copy-start.2
  56.8 1.0 %copy-done.2 = f32[9,256,64]{2,1,0:T(8,128)} copy-done((f32[9,256,64]{2,1,0:T(8,128)}, f32[9,256,64]{2,1,0:T(8,128)S(1)}, u32[]{:S(2)}) %copy-start.2) | copy-done | bytes 589848
  57.9 0.1 dynamic-slice_convert_fusion.5
  57.9 0.8 %collective-permute-start.10 = (bf16[9,64,64]{2,1,0:T(8,128)(2,1)S(1)}, bf16[9,64,64]{2,1,0:T(8,128)(2,1)S(1)}, u32[]{:S(2)}, u32[]{:S(2)}) collective-permute-start(bf16[9,64,64]{2,1,0:T(8,128)(2,1)S(1)} %get-tuple-element.20), channel_id=1, source_target_pairs={{0,4},{4,8},{8,12},{12,0},{1,5},{5,9},{9,13},{13,1},{2,6},{6,10},{... | collective-permute-start | bytes 221192 | tf_op jit(solution)/shard_map/ppermute | solution.py:48
  58.8 1.7 %collective-permute-start.11 = (bf16[9,64,64]{2,1,0:T(8,128)(2,1)S(1)}, bf16[9,64,64]{2,1,0:T(8,128)(2,1)S(1)}, u32[]{:S(2)}, u32[]{:S(2)}) collective-permute-start(bf16[9,64,64]{2,1,0:T(8,128)(2,1)S(1)} %get-tuple-element.22), channel_id=1, source_target_pairs={{0,8},{4,12},{8,0},{12,4},{1,9},{5,13},{9,1},{13,5},{2,10},{6,14},... | collective-permute-start | bytes 221192 | tf_op jit(solution)/shard_map/ppermute | solution.py:48
  60.5 2.8 %collective-permute-start.12 = (bf16[9,64,64]{2,1,0:T(8,128)(2,1)S(1)}, bf16[9,64,64]{2,1,0:T(8,128)(2,1)S(1)}, u32[]{:S(2)}, u32[]{:S(2)}) collective-permute-start(bf16[9,64,64]{2,1,0:T(8,128)(2,1)S(1)} %get-tuple-element.21), channel_id=1, source_target_pairs={{0,12},{4,0},{8,4},{12,8},{1,13},{5,1},{9,5},{13,9},{2,14},{6,2},{... | collective-permute-start | bytes 221192 | tf_op jit(solution)/shard_map/ppermute | solution.py:48
  63.3 6.7 %shard_map.105 = bf16[1,2,64,2304]{3,2,1,0:T(8,128)(2,1)} custom-call(s32[1]{0:T(128)} %bitcast.first_ref, s32[16,12]{1,0:T(8,128)} %src_ref.5, s32[16,12]{1,0:T(8,128)} %start_ref.5, s32[16,12]{1,0:T(8,128)} %span_ref.5, s32[16,12]{1,0:T(8,128)} %basis_ref.5, f32[16,12]{1,0:T(8,128)} %rsqrt_multiply_fusion.scale_ref, ...), custom_call_target="tpu_custom_call" | custom-call | tf_op jit(solution)/shard_map/pallas_call | solution.py:168
  70.0 1.4 %convolution_bitcast_fusion = f32[1,2,64,256]{3,2,1,0:T(8,128)S(1)} fusion(bf16[2304,256,1]{1,0,2:T(8,128)(2,1)S(1)} %bitcast.45, bf16[1,2,64,2304]{3,2,1,0:T(8,128)(2,1)} %shard_map.105), kind=kOutput, calls=%fused_computation.11 | convolution fusion | flops 150994944 | bytes 1900544 | tf_op jit(solution)/shard_map/bpwq,qc->bpwc/dot_general | solution.py:260
  71.4 0.0 copy-done.4
  71.4 0.7 pad_maximum_fusion.1
  72.1 0.0 collective-permute-done.10
  72.1 0.0 collective-permute-done.11
  72.1 0.0 collective-permute-done.12
  72.1 1.8 %add_multiply_fusion = f32[9,64,64]{2,1,0:T(8,128)} fusion(bf16[9,64,64]{2,1,0:T(8,128)(2,1)S(1)} %collective-permute-done.12, bf16[9,64,64]{2,1,0:T(8,128)(2,1)S(1)} %collective-permute-done.11, bf16[9,64,64]{2,1,0:T(8,128)(2,1)S(1)} %collective-permute-done.10, f32[9,256,64]{2,1,0:T(8,128)} %copy-done.2, s32[]{:T(128)S(6)} %select_n.58), kind=kLoop, calls=%fused_computation.19 | loop fusion | flops 258048 | bytes 516100 | tf_op jit(solution)/shard_map/div | solution.py:275
  (7 shorter events, 0.1 us)
Async XLA Ops:
  0.6 8.3 %copy-start = (bf16[9,256,256]{2,1,0:T(8,128)(2,1)S(1)}, bf16[9,256,256]{2,1,0:T(8,128)(2,1)}, u32[]{:S(2)}) copy-start(bf16[9,256,256]{2,1,0:T(8,128)(2,1)} %param.10) | copy-start | bytes 3538948
  2.6 7.8 %collective-permute-start = (bf16[1,2,64,512]{3,2,1,0:T(8,128)(2,1)S(1)}, bf16[1,2,64,512]{3,2,1,0:T(8,128)(2,1)S(1)}, u32[]{:S(2)}, u32[]{:S(2)}) collective-permute-start(bf16[1,2,64,512]{3,2,1,0:T(8,128)(2,1)S(1)} %get-tuple-element.25), channel_id=1, source_target_pairs={{0,4},{4,8},{8,12},{1,5},{5,9},{9,13},{2,6},{6,10},{10,14},{3,7},{... | collective-permute-start | bytes 393224 | tf_op jit(solution)/shard_map/ppermute | solution.py:23
  7.5 6.9 %collective-permute-start.1 = (bf16[1,2,64,512]{3,2,1,0:T(8,128)(2,1)S(1)}, bf16[1,2,64,512]{3,2,1,0:T(8,128)(2,1)S(1)}, u32[]{:S(2)}, u32[]{:S(2)}) collective-permute-start(bf16[1,2,64,512]{3,2,1,0:T(8,128)(2,1)S(1)} %get-tuple-element.26), channel_id=1, source_target_pairs={{4,0},{8,4},{12,8},{5,1},{9,5},{13,9},{6,2},{10,6},{14,10},{7,3},{... | collective-permute-start | bytes 393224 | tf_op jit(solution)/shard_map/ppermute | solution.py:26
  8.9 0.8 %copy-start.5 = (s32[16,12]{1,0:T(8,128)S(1)}, s32[16,12]{1,0:T(8,128)}, u32[]{:S(2)}) copy-start(s32[16,12]{1,0:T(8,128)} %span_ref.5) | copy-start | bytes 2308
  8.9 0.8 %copy-start.6 = (f32[16,12]{1,0:T(8,128)S(1)}, f32[16,12]{1,0:T(8,128)}, u32[]{:S(2)}) copy-start(f32[16,12]{1,0:T(8,128)} %param.15) | copy-start | bytes 2308
  14.6 4.8 %collective-permute-start.4 = (f32[2,1,4,256]{3,0,2,1:T(2,128)S(1)}, f32[2,1,4,256]{3,0,2,1:T(2,128)S(1)}, u32[]{:S(2)}, u32[]{:S(2)}) collective-permute-start(f32[2,1,4,256]{3,0,2,1:T(2,128)S(1)} %pad_maximum_fusion.2), channel_id=1, source_target_pairs={{0,1},{1,2},{2,3},{3,0},{4,5},{5,6},{6,7},{7,4},{8,9},{9,10},{10,1... | collective-permute-start | bytes 24584 | tf_op jit(solution)/shard_map/ppermute | solution.py:36
  14.6 4.8 %collective-permute-start.5 = (f32[2,1,4,256]{3,0,2,1:T(2,128)S(1)}, f32[2,1,4,256]{3,0,2,1:T(2,128)S(1)}, u32[]{:S(2)}, u32[]{:S(2)}) collective-permute-start(f32[2,1,4,256]{3,0,2,1:T(2,128)S(1)} %pad_maximum_fusion.2), channel_id=1, source_target_pairs={{0,2},{1,3},{2,0},{3,1},{4,6},{5,7},{6,4},{7,5},{8,10},{9,11},{10,... | collective-permute-start | bytes 24584 | tf_op jit(solution)/shard_map/ppermute | solution.py:36
  16.2 3.2 %collective-permute-start.6 = (f32[2,1,4,256]{3,0,2,1:T(2,128)S(1)}, f32[2,1,4,256]{3,0,2,1:T(2,128)S(1)}, u32[]{:S(2)}, u32[]{:S(2)}) collective-permute-start(f32[2,1,4,256]{3,0,2,1:T(2,128)S(1)} %pad_maximum_fusion.2), channel_id=1, source_target_pairs={{0,3},{1,0},{2,1},{3,2},{4,7},{5,4},{6,5},{7,6},{8,11},{9,8},{10,9... | collective-permute-start | bytes 24584 | tf_op jit(solution)/shard_map/ppermute | solution.py:36
  17.6 5.0 %collective-permute-start.2 = (bf16[1,8,16,512]{3,2,1,0:T(8,128)(2,1)S(1)}, bf16[1,8,16,512]{3,2,1,0:T(8,128)(2,1)S(1)}, u32[]{:S(2)}, u32[]{:S(2)}) collective-permute-start(bf16[1,8,16,512]{3,2,1,0:T(8,128)(2,1)S(1)} %get-tuple-element.23), channel_id=1, source_target_pairs={{0,1},{1,2},{2,3},{3,0},{4,5},{5,6},{6,7},{7,4},{8,9},{9,10},{10,1... | collective-permute-start | bytes 393224 | tf_op jit(solution)/shard_map/ppermute | solution.py:23
  17.7 5.0 %collective-permute-start.3 = (bf16[1,8,16,512]{3,2,1,0:T(8,128)(2,1)S(1)}, bf16[1,8,16,512]{3,2,1,0:T(8,128)(2,1)S(1)}, u32[]{:S(2)}, u32[]{:S(2)}) collective-permute-start(bf16[1,8,16,512]{3,2,1,0:T(8,128)(2,1)S(1)} %get-tuple-element.24), channel_id=1, source_target_pairs={{1,0},{2,1},{3,2},{0,3},{5,4},{6,5},{7,6},{4,7},{9,8},{10,9},{11,1... | collective-permute-start | bytes 393224 | tf_op jit(solution)/shard_map/ppermute | solution.py:26
  35.5 13.3 %collective-permute-start.7 = (bf16[9,256,64]{1,2,0:T(8,128)(2,1)}, bf16[9,256,64]{1,2,0:T(8,128)(2,1)}, u32[]{:S(2)}, u32[]{:S(2)}) collective-permute-start(bf16[9,256,64]{1,2,0:T(8,128)(2,1)} %copy.28), channel_id=1, source_target_pairs={{0,1},{1,2},{2,3},{3,0},{4,5},{5,6},{6,7},{7,4},{8,9},{9,10},{10,1... | collective-permute-start | bytes 884744 | tf_op jit(solution)/shard_map/ppermute | solution.py:48
  37.0 13.9 %collective-permute-start.8 = (bf16[9,256,64]{1,2,0:T(8,128)(2,1)}, bf16[9,256,64]{1,2,0:T(8,128)(2,1)}, u32[]{:S(2)}, u32[]{:S(2)}) collective-permute-start(bf16[9,256,64]{1,2,0:T(8,128)(2,1)} %copy.30), channel_id=1, source_target_pairs={{0,2},{1,3},{2,0},{3,1},{4,6},{5,7},{6,4},{7,5},{8,10},{9,11},{10,... | collective-permute-start | bytes 884744 | tf_op jit(solution)/shard_map/ppermute | solution.py:48
  38.9 14.1 %collective-permute-start.9 = (bf16[9,256,64]{1,2,0:T(8,128)(2,1)}, bf16[9,256,64]{1,2,0:T(8,128)(2,1)}, u32[]{:S(2)}, u32[]{:S(2)}) collective-permute-start(bf16[9,256,64]{1,2,0:T(8,128)(2,1)} %copy.32), channel_id=1, source_target_pairs={{0,3},{1,0},{2,1},{3,2},{4,7},{5,4},{6,5},{7,6},{8,11},{9,8},{10,9... | collective-permute-start | bytes 884744 | tf_op jit(solution)/shard_map/ppermute | solution.py:48
  45.5 2.1 %copy-start.3 = (bf16[1,4,64,2304]{3,2,1,0:T(8,128)(2,1)S(1)}, bf16[1,4,64,2304]{3,2,1,0:T(8,128)(2,1)}, u32[]{:S(2)}) copy-start(bf16[1,4,64,2304]{3,2,1,0:T(8,128)(2,1)} %get-tuple-element.12) | copy-start | bytes 3538948
  48.8 6.2 %copy-start.1 = (f32[9,256,256]{2,1,0:T(8,128)S(1)}, f32[9,256,256]{2,1,0:T(8,128)}, u32[]{:S(2)}) copy-start(f32[9,256,256]{2,1,0:T(8,128)} %get-tuple-element.13) | copy-start | bytes 7077892
  56.8 1.0 %copy-start.2 = (f32[9,256,64]{2,1,0:T(8,128)}, f32[9,256,64]{2,1,0:T(8,128)S(1)}, u32[]{:S(2)}) copy-start(f32[9,256,64]{2,1,0:T(8,128)S(1)} %convert_add_fusion) | copy-start | bytes 1769476
  57.9 14.2 %collective-permute-start.10 = (bf16[9,64,64]{2,1,0:T(8,128)(2,1)S(1)}, bf16[9,64,64]{2,1,0:T(8,128)(2,1)S(1)}, u32[]{:S(2)}, u32[]{:S(2)}) collective-permute-start(bf16[9,64,64]{2,1,0:T(8,128)(2,1)S(1)} %get-tuple-element.20), channel_id=1, source_target_pairs={{0,4},{4,8},{8,12},{12,0},{1,5},{5,9},{9,13},{13,1},{2,6},{6,10},{... | collective-permute-start | bytes 221192 | tf_op jit(solution)/shard_map/ppermute | solution.py:48
  58.8 13.4 %collective-permute-start.11 = (bf16[9,64,64]{2,1,0:T(8,128)(2,1)S(1)}, bf16[9,64,64]{2,1,0:T(8,128)(2,1)S(1)}, u32[]{:S(2)}, u32[]{:S(2)}) collective-permute-start(bf16[9,64,64]{2,1,0:T(8,128)(2,1)S(1)} %get-tuple-element.22), channel_id=1, source_target_pairs={{0,8},{4,12},{8,0},{12,4},{1,9},{5,13},{9,1},{13,5},{2,10},{6,14},... | collective-permute-start | bytes 221192 | tf_op jit(solution)/shard_map/ppermute | solution.py:48
  60.5 11.7 %collective-permute-start.12 = (bf16[9,64,64]{2,1,0:T(8,128)(2,1)S(1)}, bf16[9,64,64]{2,1,0:T(8,128)(2,1)S(1)}, u32[]{:S(2)}, u32[]{:S(2)}) collective-permute-start(bf16[9,64,64]{2,1,0:T(8,128)(2,1)S(1)} %get-tuple-element.21), channel_id=1, source_target_pairs={{0,12},{4,0},{8,4},{12,8},{1,13},{5,1},{9,5},{13,9},{2,14},{6,2},{... | collective-permute-start | bytes 221192 | tf_op jit(solution)/shard_map/ppermute | solution.py:48
  70.0 1.4 %copy-start.4 = (f32[1,2,64,256]{3,2,1,0:T(8,128)S(1)}, f32[1,2,64,256]{3,2,1,0:T(8,128)}, u32[]{:S(2)}) copy-start(f32[1,2,64,256]{3,2,1,0:T(8,128)} %convolution_bitcast_fusion.1) | copy-start | bytes 393220

commit v19 on v17

--- a/solution.py
+++ b/solution.py
@@ -42,7 +42,7 @@
     own = lax.axis_index(axis)
     block = value.shape[dim] // count
     total = lax.dynamic_slice_in_dim(value, own * block, block, dim)
-    for shift in range(1, count):
+    for shift in [count // 2] + [t for t in range(1, count) if t != count // 2]:
         pairs = [(i, (i + shift) % count) for i in range(count)]
         piece = lax.dynamic_slice_in_dim(value, ((own + shift) % count) * block, block, dim)
         sent = lax.ppermute(piece.astype(jnp.bfloat16), axis, pairs)

time: 63.8 us -> 64.5 us (1.011)
  the two profiles are of different devices: /device:TPU:9 before, /device:TPU:0 now
where the time goes in v19:
time: 64.5 us; the launch traced here: 64.6 us
  starting transfers between devices  19.6 us (30%)
  Pallas kernels  15.8 us (24%)
  waiting for transfers between devices  10.2 us (16%)
  matrix products  7.84 us (12%)
  local copies, waits for them, and re-layouts  6.18 us (10%)
  other arithmetic  3.97 us (6%)
  between operations  0.97 us (2%)
    pallas_call x2, Pallas kernels, run_scatter(): pl.pallas_call(kernel, grid=(members,), in_specs=[smem] * 6 + [pl.BlockSp...  12 us
    ppermute x6, starting transfers between devices, ring_scatter(): sent = lax.ppermute(piece.astype(jnp.bfloat16), axis, pairs)  8.58 us
    ppermute x2, starting transfers between devices, with_halo(): lax.ppermute(lax.slice_in_dim(block, block.shape[dim] - width, None, axis...  4.99 us
    ppermute x2, waiting for transfers between devices, with_halo(): lax.ppermute(lax.slice_in_dim(block, 0, width, axis=dim), axis, backward)  4.04 us
    pallas_call x1, Pallas kernels, run_filter(): pl.pallas_call(kernel, grid=(members, row_count), in_specs=[smem] * 6 + [...  3.81 us
    dot_general x2, matrix products, backward_rows(): jnp.einsum('bpwq,qc->bpwc', back_filtered, w_back, preferred_element_type...  3.6 us
    ppermute x6, waiting for transfers between devices, ring_scatter(): sent = lax.ppermute(piece.astype(jnp.bfloat16), axis, pairs)  3.54 us
    unnamed x17, local copies, waits for them, and re-layouts  3.46 us
  transfers between devices with their start and end apart: 13, of which 3 were waited for; matrix products, arithmetic and copies ran while one was open for 14% of the time, Pallas kernels for 19%

profile of v19, /device:TPU:0, one launch (start us, length us, event | category | flops | bytes accessed | tf_op | source)
XLA Modules:
  0.0 64.6 jit_solution(16967672398100273101)
XLA Ops:
  0.6 0.0 copy-start.1
  0.6 1.0 %constant_dynamic-update-slice_fusion.1 = bf16[1,4,64,512]{3,2,1,0:T(8,128)(2,1)S(1)} fusion(bf16[1,4,64,256]{3,2,1,0:T(8,128)(2,1)} %param.8), kind=kLoop, calls=%fused_computation.35 | loop fusion | bytes 262144
  1.7 0.9 %constant_dynamic-update-slice_fusion = bf16[1,4,64,512]{3,2,1,0:T(8,128)(2,1)S(1)} fusion(bf16[1,4,64,512]{3,2,1,0:T(8,128)(2,1)S(1)} %constant_dynamic-update-slice_fusion.1, bf16[1,4,64,256]{3,2,1,0:T(8,128)(2,1)} %param.9), kind=kLoop, calls=%fused_computation.34 | loop fusion | bytes 262144 | tf_op jit(solution)/shard_map/concatenate | solution.py:220
  2.6 4.9 %collective-permute-start = (bf16[1,2,64,512]{3,2,1,0:T(8,128)(2,1)S(1)}, bf16[1,2,64,512]{3,2,1,0:T(8,128)(2,1)S(1)}, u32[]{:S(2)}, u32[]{:S(2)}) collective-permute-start(bf16[1,2,64,512]{3,2,1,0:T(8,128)(2,1)S(1)} %get-tuple-element.27), channel_id=1, source_target_pairs={{0,4},{4,8},{8,12},{1,5},{5,9},{9,13},{2,6},{6,10},{10,14},{3,7},{... | collective-permute-start | bytes 393224 | tf_op jit(solution)/shard_map/ppermute | solution.py:23
  7.5 1.3 %collective-permute-start.1 = (bf16[1,2,64,512]{3,2,1,0:T(8,128)(2,1)S(1)}, bf16[1,2,64,512]{3,2,1,0:T(8,128)(2,1)S(1)}, u32[]{:S(2)}, u32[]{:S(2)}) collective-permute-start(bf16[1,2,64,512]{3,2,1,0:T(8,128)(2,1)S(1)} %get-tuple-element.28), channel_id=1, source_target_pairs={{4,0},{8,4},{12,8},{5,1},{9,5},{13,9},{6,2},{10,6},{14,10},{7,3},{... | collective-permute-start | bytes 393224 | tf_op jit(solution)/shard_map/ppermute | solution.py:26
  8.9 0.0 copy-done.1
  8.9 0.0 copy-start.5
  8.9 0.0 copy-start.6
  9.0 0.7 %copy.17 = bf16[9,256,256]{1,2,0:T(8,128)(2,1)S(1)} copy(bf16[9,256,256]{2,1,0:T(8,128)(2,1)S(1)} %copy-done.1) | data formatting | bytes 2359296 | tf_op args[2]
  9.7 0.0 copy-done.5
  9.7 0.0 copy-done.6
  9.7 0.6 rsqrt_multiply_fusion.scale_ref
  10.4 0.0 collective-permute-done
  10.4 4.0 %collective-permute-done.1 = bf16[1,2,64,512]{3,2,1,0:T(8,128)(2,1)S(1)} collective-permute-done((bf16[1,2,64,512]{3,2,1,0:T(8,128)(2,1)S(1)}, bf16[1,2,64,512]{3,2,1,0:T(8,128)(2,1)S(1)}, u32[]{:S(2)}, u32[]{:S(2)}) %collective-permute-start.1) | collective-permute-done | bytes 131104 | tf_op jit(solution)/shard_map/ppermute | solution.py:26
  14.4 0.1 pad_maximum_fusion
  14.5 0.1 convert_reduce_fusion
  14.6 0.1 collective-permute-start.4
  14.6 1.6 %collective-permute-start.5 = (f32[2,1,4,256]{3,0,2,1:T(2,128)S(1)}, f32[2,1,4,256]{3,0,2,1:T(2,128)S(1)}, u32[]{:S(2)}, u32[]{:S(2)}) collective-permute-start(f32[2,1,4,256]{3,0,2,1:T(2,128)S(1)} %pad_maximum_fusion.2), channel_id=1, source_target_pairs={{0,2},{1,3},{2,0},{3,1},{4,6},{5,7},{6,4},{7,5},{8,10},{9,11},{10,... | collective-permute-start | bytes 24584 | tf_op jit(solution)/shard_map/ppermute | solution.py:36
  16.2 1.4 %collective-permute-start.6 = (f32[2,1,4,256]{3,0,2,1:T(2,128)S(1)}, f32[2,1,4,256]{3,0,2,1:T(2,128)S(1)}, u32[]{:S(2)}, u32[]{:S(2)}) collective-permute-start(f32[2,1,4,256]{3,0,2,1:T(2,128)S(1)} %pad_maximum_fusion.2), channel_id=1, source_target_pairs={{0,3},{1,0},{2,1},{3,2},{4,7},{5,4},{6,5},{7,6},{8,11},{9,8},{10,9... | collective-permute-start | bytes 24584 | tf_op jit(solution)/shard_map/ppermute | solution.py:36
  17.6 0.1 collective-permute-start.2
  17.7 1.7 %collective-permute-start.3 = (bf16[1,8,16,512]{3,2,1,0:T(8,128)(2,1)S(1)}, bf16[1,8,16,512]{3,2,1,0:T(8,128)(2,1)S(1)}, u32[]{:S(2)}, u32[]{:S(2)}) collective-permute-start(bf16[1,8,16,512]{3,2,1,0:T(8,128)(2,1)S(1)} %get-tuple-element.26), channel_id=1, source_target_pairs={{1,0},{2,1},{3,2},{0,3},{5,4},{6,5},{7,6},{4,7},{9,8},{10,9},{11,1... | collective-permute-start | bytes 393224 | tf_op jit(solution)/shard_map/ppermute | solution.py:26
  19.4 0.0 collective-permute-done.4
  19.4 0.0 collective-permute-done.5
  19.4 0.0 collective-permute-done.6
  19.4 0.6 fusion.17
  20.1 2.6 %collective-permute-done.2 = bf16[1,8,16,512]{3,2,1,0:T(8,128)(2,1)S(1)} collective-permute-done((bf16[1,8,16,512]{3,2,1,0:T(8,128)(2,1)S(1)}, bf16[1,8,16,512]{3,2,1,0:T(8,128)(2,1)S(1)}, u32[]{:S(2)}, u32[]{:S(2)}) %collective-permute-start.2) | collective-permute-done | bytes 131104 | tf_op jit(solution)/shard_map/ppermute | solution.py:23
  22.7 0.0 collective-permute-done.3
  22.7 1.1 %fusion.11.field_ref = bf16[1,8,128,512]{3,2,1,0:T(8,128)(2,1)} fusion(bf16[1,8,16,512]{3,2,1,0:T(8,128)(2,1)S(1)} %collective-permute-done.3, bf16[1,8,64,512]{3,2,1,0:T(8,128)(2,1)S(1)} %pad_maximum_fusion, bf16[1,8,16,512]{3,2,1,0:T(8,128)(2,1)S(1)} %collective-permute-done.2), kind=kLoop, calls=%fused_computation.13 | loop fusion | flops 5242880 | bytes 1835008 | tf_op jit(solution)/shard_map/concatenate | solution.py:27
  23.7 3.8 %shard_map.103 = bf16[1,4,64,2304]{3,2,1,0:T(8,128)(2,1)} custom-call(s32[1]{0:T(128)} %bitcast.first_ref, s32[16,12]{1,0:T(8,128)} %src_ref.5, s32[16,12]{1,0:T(8,128)} %start_ref.5, s32[16,12]{1,0:T(8,128)} %span_ref.5, s32[16,12]{1,0:T(8,128)} %basis_ref.5, f32[16,12]{1,0:T(8,128)} %rsqrt_multiply_fusion.scale_ref, ...), custom_call_target="tpu_custom_call" | custom-call | tf_op jit(solution)/shard_map/pallas_call | solution.py:192
  27.5 1.8 %convolution_bitcast_fusion = f32[9,256,256]{1,2,0:T(8,128)S(1)} fusion(bf16[4,8,9,8,256]{4,3,2,1,0:T(8,128)(2,1)} %bitcast.57, bf16[1,4,64,256]{3,2,1,0:T(8,128)(2,1)} %param.9), kind=kOutput, calls=%fused_computation.4 | convolution fusion | flops 301989888 | bytes 3670016 | tf_op jit(solution)/shard_map/brwq,brwo->qo/dot_general | solution.py:238
  29.3 0.9 %dynamic-slice_convert_fusion.2 = (bf16[9,256,64]{1,2,0:T(8,128)(2,1)}, bf16[9,256,64]{1,2,0:T(8,128)(2,1)}, bf16[9,256,64]{1,2,0:T(8,128)(2,1)}) fusion(f32[9,256,256]{1,2,0:T(8,128)S(1)} %convolution_bitcast_fusion, s32[]{:T(128)S(6)} %select_n.53, s32[]{:T(128)S(6)} %select_n.57, s32[]{:T(128)S(6)} %select_n.55), kind=kLoop, calls=%fused_computation.19 | loop fusion | bytes 1769484 | tf_op jit(solution)/shard_map/convert_element_type | solution.py:48
  30.3 0.3 collective-permute-start.7
  30.6 0.9 %collective-permute-start.8 = (bf16[9,256,64]{1,2,0:T(8,128)(2,1)}, bf16[9,256,64]{1,2,0:T(8,128)(2,1)}, u32[]{:S(2)}, u32[]{:S(2)}) collective-permute-start(bf16[9,256,64]{1,2,0:T(8,128)(2,1)} %get-tuple-element.21), channel_id=1, source_target_pairs={{0,1},{1,2},{2,3},{3,0},{4,5},{5,6},{6,7},{7,4},{8,9},{9,10},{10,1... | collective-permute-start | bytes 884744 | tf_op jit(solution)/shard_map/ppermute | solution.py:48
  31.5 0.8 %collective-permute-start.9 = (bf16[9,256,64]{1,2,0:T(8,128)(2,1)}, bf16[9,256,64]{1,2,0:T(8,128)(2,1)}, u32[]{:S(2)}, u32[]{:S(2)}) collective-permute-start(bf16[9,256,64]{1,2,0:T(8,128)(2,1)} %get-tuple-element.20), channel_id=1, source_target_pairs={{0,3},{1,0},{2,1},{3,2},{4,7},{5,4},{6,5},{7,6},{8,11},{9,8},{10,9... | collective-permute-start | bytes 884744 | tf_op jit(solution)/shard_map/ppermute | solution.py:48
  32.3 5.7 %shard_map.104 = bf16[1,2,64,2304]{3,2,1,0:T(8,128)(2,1)} custom-call(s32[1]{0:T(128)} %bitcast.first_ref, s32[16,12]{1,0:T(8,128)} %src_ref.5, s32[16,12]{1,0:T(8,128)} %start_ref.5, s32[16,12]{1,0:T(8,128)} %span_ref.5, s32[16,12]{1,0:T(8,128)} %basis_ref.5, f32[16,12]{1,0:T(8,128)} %rsqrt_multiply_fusion.scale_ref, ...), custom_call_target="tpu_custom_call" | custom-call | tf_op jit(solution)/shard_map/pallas_call | solution.py:159
  38.0 0.0 copy-start
  38.0 2.1 %convolution_bitcast_fusion.2 = f32[1,2,64,256]{3,2,1,0:T(8,128)} fusion(bf16[2304,256,1]{1,0,2:T(8,128)(2,1)S(1)} %bitcast.58, bf16[1,2,64,2304]{3,2,1,0:T(8,128)(2,1)} %shard_map.104), kind=kOutput, calls=%fused_computation.11 | convolution fusion | flops 150994944 | bytes 1900544 | tf_op jit(solution)/shard_map/bpwq,qc->bpwc/dot_general | solution.py:249
  40.2 0.0 copy-done
  40.2 2.5 %fusion.7 = f32[1,4,64,256]{3,2,1,0:T(8,128)} fusion(bf16[2304,256,1]{1,0,2:T(8,128)(2,1)} %bitcast.60, bf16[1,4,64,2304]{3,2,1,0:T(8,128)(2,1)S(1)} %copy-done), kind=kOutput, calls=%fused_computation.9 | convolution fusion | flops 301989888 | bytes 2621440 | tf_op jit(solution)/shard_map/brwq,qo->brwo/dot_general | solution.py:236
  42.6 0.0 collective-permute-done.7
  42.6 3.5 %collective-permute-done.8 = bf16[9,256,64]{1,2,0:T(8,128)(2,1)} collective-permute-done((bf16[9,256,64]{1,2,0:T(8,128)(2,1)}, bf16[9,256,64]{1,2,0:T(8,128)(2,1)}, u32[]{:S(2)}, u32[]{:S(2)}) %collective-permute-start.8) | collective-permute-done | bytes 294944 | tf_op jit(solution)/shard_map/ppermute | solution.py:48
  46.1 0.0 collective-permute-done.9
  46.2 1.3 %convert_add_fusion = f32[9,256,64]{1,2,0:T(8,128)S(1)} fusion(bf16[9,256,64]{1,2,0:T(8,128)(2,1)} %collective-permute-done.9, bf16[9,256,64]{1,2,0:T(8,128)(2,1)} %collective-permute-done.8, bf16[9,256,64]{1,2,0:T(8,128)(2,1)} %collective-permute-done.7, f32[9,256,256]{1,2,0:T(8,128)S(1)} %convolution_bitcast_fusion, s32[]{:T(128)S(6)} %select_n.51), kind=kLoop, calls=%fused_computation.16 | loop fusion | flops 884736 | bytes 2064388 | tf_op jit(solution)/shard_map/add | solution.py:49
  47.4 0.0 copy-start.2
  47.4 0.8 %copy-done.2 = f32[9,256,64]{1,2,0:T(8,128)} copy-done((f32[9,256,64]{1,2,0:T(8,128)}, f32[9,256,64]{1,2,0:T(8,128)S(1)}, u32[]{:S(2)}) %copy-start.2) | copy-done | bytes 589848
  48.3 0.2 dynamic-slice_convert_fusion.5
  48.5 2.7 %collective-permute-start.10 = (bf16[9,64,64]{1,2,0:T(8,128)(2,1)S(1)}, bf16[9,64,64]{1,2,0:T(8,128)(2,1)S(1)}, u32[]{:S(2)}, u32[]{:S(2)}) collective-permute-start(bf16[9,64,64]{1,2,0:T(8,128)(2,1)S(1)} %get-tuple-element.22), channel_id=1, source_target_pairs={{0,8},{4,12},{8,0},{12,4},{1,9},{5,13},{9,1},{13,5},{2,10},{6,14},... | collective-permute-start | bytes 221192 | tf_op jit(solution)/shard_map/ppermute | solution.py:48
  51.1 0.0 collective-permute-start.11
  51.1 3.8 %collective-permute-start.12 = (bf16[9,64,64]{1,2,0:T(8,128)(2,1)S(1)}, bf16[9,64,64]{1,2,0:T(8,128)(2,1)S(1)}, u32[]{:S(2)}, u32[]{:S(2)}) collective-permute-start(bf16[9,64,64]{1,2,0:T(8,128)(2,1)S(1)} %get-tuple-element.23), channel_id=1, source_target_pairs={{0,12},{4,0},{8,4},{12,8},{1,13},{5,1},{9,5},{13,9},{2,14},{6,2},{... | collective-permute-start | bytes 221192 | tf_op jit(solution)/shard_map/ppermute | solution.py:48
  55.0 6.3 %shard_map.105 = bf16[1,2,64,2304]{3,2,1,0:T(8,128)(2,1)} custom-call(s32[1]{0:T(128)} %bitcast.first_ref, s32[16,12]{1,0:T(8,128)} %src_ref.5, s32[16,12]{1,0:T(8,128)} %start_ref.5, s32[16,12]{1,0:T(8,128)} %span_ref.5, s32[16,12]{1,0:T(8,128)} %basis_ref.5, f32[16,12]{1,0:T(8,128)} %rsqrt_multiply_fusion.scale_ref, ...), custom_call_target="tpu_custom_call" | custom-call | tf_op jit(solution)/shard_map/pallas_call | solution.py:159
  61.3 0.0 copy-start.4
  61.3 0.0 copy-start.3
  61.3 1.5 %convolution_bitcast_fusion.1 = f32[1,2,64,256]{3,2,1,0:T(8,128)S(1)} fusion(bf16[2304,256,1]{1,0,2:T(8,128)(2,1)S(1)} %bitcast.59, bf16[1,2,64,2304]{3,2,1,0:T(8,128)(2,1)} %shard_map.105), kind=kOutput, calls=%fused_computation.10 | convolution fusion | flops 150994944 | bytes 1900544 | tf_op jit(solution)/shard_map/bpwq,qc->bpwc/dot_general | solution.py:249
  62.8 0.0 copy-done.4
  62.8 0.7 %pad_maximum_fusion.1 = f32[1,4,64,256]{3,2,1,0:T(8,128)} fusion(f32[1,2,64,256]{3,2,1,0:T(8,128)S(1)} %convolution_bitcast_fusion.1, f32[1,2,64,256]{3,2,1,0:T(8,128)S(1)} %copy-done.4), kind=kLoop, calls=%fused_computation.26 | loop fusion | flops 65536 | bytes 524288 | tf_op jit(solution)/shard_map/concatenate | solution.py:257
  63.5 0.0 collective-permute-done.10
  63.5 0.0 collective-permute-done.11
  63.5 0.0 collective-permute-done.12
  63.5 0.0 copy-done.3
  63.5 0.2 add_multiply_fusion
  63.7 0.9 %copy.19 = f32[9,64,64]{2,1,0:T(8,128)} copy(f32[9,64,64]{1,2,0:T(8,128)S(1)} %add_multiply_fusion) | data formatting | bytes 294912
  (6 shorter events, 0.1 us)
Async XLA Ops:
  0.6 8.3 %copy-start.1 = (bf16[9,256,256]{2,1,0:T(8,128)(2,1)S(1)}, bf16[9,256,256]{2,1,0:T(8,128)(2,1)}, u32[]{:S(2)}) copy-start(bf16[9,256,256]{2,1,0:T(8,128)(2,1)} %param.10) | copy-start | bytes 3538948
  2.6 7.8 %collective-permute-start = (bf16[1,2,64,512]{3,2,1,0:T(8,128)(2,1)S(1)}, bf16[1,2,64,512]{3,2,1,0:T(8,128)(2,1)S(1)}, u32[]{:S(2)}, u32[]{:S(2)}) collective-permute-start(bf16[1,2,64,512]{3,2,1,0:T(8,128)(2,1)S(1)} %get-tuple-element.27), channel_id=1, source_target_pairs={{0,4},{4,8},{8,12},{1,5},{5,9},{9,13},{2,6},{6,10},{10,14},{3,7},{... | collective-permute-start | bytes 393224 | tf_op jit(solution)/shard_map/ppermute | solution.py:23
  7.5 6.9 %collective-permute-start.1 = (bf16[1,2,64,512]{3,2,1,0:T(8,128)(2,1)S(1)}, bf16[1,2,64,512]{3,2,1,0:T(8,128)(2,1)S(1)}, u32[]{:S(2)}, u32[]{:S(2)}) collective-permute-start(bf16[1,2,64,512]{3,2,1,0:T(8,128)(2,1)S(1)} %get-tuple-element.28), channel_id=1, source_target_pairs={{4,0},{8,4},{12,8},{5,1},{9,5},{13,9},{6,2},{10,6},{14,10},{7,3},{... | collective-permute-start | bytes 393224 | tf_op jit(solution)/shard_map/ppermute | solution.py:26
  8.9 0.8 %copy-start.5 = (s32[16,12]{1,0:T(8,128)S(1)}, s32[16,12]{1,0:T(8,128)}, u32[]{:S(2)}) copy-start(s32[16,12]{1,0:T(8,128)} %span_ref.5) | copy-start | bytes 2308
  8.9 0.8 %copy-start.6 = (f32[16,12]{1,0:T(8,128)S(1)}, f32[16,12]{1,0:T(8,128)}, u32[]{:S(2)}) copy-start(f32[16,12]{1,0:T(8,128)} %param.15) | copy-start | bytes 2308
  14.6 4.8 %collective-permute-start.4 = (f32[2,1,4,256]{3,0,2,1:T(2,128)S(1)}, f32[2,1,4,256]{3,0,2,1:T(2,128)S(1)}, u32[]{:S(2)}, u32[]{:S(2)}) collective-permute-start(f32[2,1,4,256]{3,0,2,1:T(2,128)S(1)} %pad_maximum_fusion.2), channel_id=1, source_target_pairs={{0,1},{1,2},{2,3},{3,0},{4,5},{5,6},{6,7},{7,4},{8,9},{9,10},{10,1... | collective-permute-start | bytes 24584 | tf_op jit(solution)/shard_map/ppermute | solution.py:36
  14.6 4.8 %collective-permute-start.5 = (f32[2,1,4,256]{3,0,2,1:T(2,128)S(1)}, f32[2,1,4,256]{3,0,2,1:T(2,128)S(1)}, u32[]{:S(2)}, u32[]{:S(2)}) collective-permute-start(f32[2,1,4,256]{3,0,2,1:T(2,128)S(1)} %pad_maximum_fusion.2), channel_id=1, source_target_pairs={{0,2},{1,3},{2,0},{3,1},{4,6},{5,7},{6,4},{7,5},{8,10},{9,11},{10,... | collective-permute-start | bytes 24584 | tf_op jit(solution)/shard_map/ppermute | solution.py:36
  16.2 3.2 %collective-permute-start.6 = (f32[2,1,4,256]{3,0,2,1:T(2,128)S(1)}, f32[2,1,4,256]{3,0,2,1:T(2,128)S(1)}, u32[]{:S(2)}, u32[]{:S(2)}) collective-permute-start(f32[2,1,4,256]{3,0,2,1:T(2,128)S(1)} %pad_maximum_fusion.2), channel_id=1, source_target_pairs={{0,3},{1,0},{2,1},{3,2},{4,7},{5,4},{6,5},{7,6},{8,11},{9,8},{10,9... | collective-permute-start | bytes 24584 | tf_op jit(solution)/shard_map/ppermute | solution.py:36
  17.6 5.0 %collective-permute-start.2 = (bf16[1,8,16,512]{3,2,1,0:T(8,128)(2,1)S(1)}, bf16[1,8,16,512]{3,2,1,0:T(8,128)(2,1)S(1)}, u32[]{:S(2)}, u32[]{:S(2)}) collective-permute-start(bf16[1,8,16,512]{3,2,1,0:T(8,128)(2,1)S(1)} %get-tuple-element.25), channel_id=1, source_target_pairs={{0,1},{1,2},{2,3},{3,0},{4,5},{5,6},{6,7},{7,4},{8,9},{9,10},{10,1... | collective-permute-start | bytes 393224 | tf_op jit(solution)/shard_map/ppermute | solution.py:23
  17.7 5.0 %collective-permute-start.3 = (bf16[1,8,16,512]{3,2,1,0:T(8,128)(2,1)S(1)}, bf16[1,8,16,512]{3,2,1,0:T(8,128)(2,1)S(1)}, u32[]{:S(2)}, u32[]{:S(2)}) collective-permute-start(bf16[1,8,16,512]{3,2,1,0:T(8,128)(2,1)S(1)} %get-tuple-element.26), channel_id=1, source_target_pairs={{1,0},{2,1},{3,2},{0,3},{5,4},{6,5},{7,6},{4,7},{9,8},{10,9},{11,1... | collective-permute-start | bytes 393224 | tf_op jit(solution)/shard_map/ppermute | solution.py:26
  30.3 12.4 %collective-permute-start.7 = (bf16[9,256,64]{1,2,0:T(8,128)(2,1)}, bf16[9,256,64]{1,2,0:T(8,128)(2,1)}, u32[]{:S(2)}, u32[]{:S(2)}) collective-permute-start(bf16[9,256,64]{1,2,0:T(8,128)(2,1)} %get-tuple-element.19), channel_id=1, source_target_pairs={{0,2},{1,3},{2,0},{3,1},{4,6},{5,7},{6,4},{7,5},{8,10},{9,11},{10,... | collective-permute-start | bytes 884744 | tf_op jit(solution)/shard_map/ppermute | solution.py:48
  30.6 15.5 %collective-permute-start.8 = (bf16[9,256,64]{1,2,0:T(8,128)(2,1)}, bf16[9,256,64]{1,2,0:T(8,128)(2,1)}, u32[]{:S(2)}, u32[]{:S(2)}) collective-permute-start(bf16[9,256,64]{1,2,0:T(8,128)(2,1)} %get-tuple-element.21), channel_id=1, source_target_pairs={{0,1},{1,2},{2,3},{3,0},{4,5},{5,6},{6,7},{7,4},{8,9},{9,10},{10,1... | collective-permute-start | bytes 884744 | tf_op jit(solution)/shard_map/ppermute | solution.py:48
  31.5 14.6 %collective-permute-start.9 = (bf16[9,256,64]{1,2,0:T(8,128)(2,1)}, bf16[9,256,64]{1,2,0:T(8,128)(2,1)}, u32[]{:S(2)}, u32[]{:S(2)}) collective-permute-start(bf16[9,256,64]{1,2,0:T(8,128)(2,1)} %get-tuple-element.20), channel_id=1, source_target_pairs={{0,3},{1,0},{2,1},{3,2},{4,7},{5,4},{6,5},{7,6},{8,11},{9,8},{10,9... | collective-permute-start | bytes 884744 | tf_op jit(solution)/shard_map/ppermute | solution.py:48
  38.0 2.1 %copy-start = (bf16[1,4,64,2304]{3,2,1,0:T(8,128)(2,1)S(1)}, bf16[1,4,64,2304]{3,2,1,0:T(8,128)(2,1)}, u32[]{:S(2)}) copy-start(bf16[1,4,64,2304]{3,2,1,0:T(8,128)(2,1)} %shard_map.103) | copy-start | bytes 3538948
  47.4 0.8 %copy-start.2 = (f32[9,256,64]{1,2,0:T(8,128)}, f32[9,256,64]{1,2,0:T(8,128)S(1)}, u32[]{:S(2)}) copy-start(f32[9,256,64]{1,2,0:T(8,128)S(1)} %convert_add_fusion) | copy-start | bytes 1769476
  48.5 15.1 %collective-permute-start.10 = (bf16[9,64,64]{1,2,0:T(8,128)(2,1)S(1)}, bf16[9,64,64]{1,2,0:T(8,128)(2,1)S(1)}, u32[]{:S(2)}, u32[]{:S(2)}) collective-permute-start(bf16[9,64,64]{1,2,0:T(8,128)(2,1)S(1)} %get-tuple-element.22), channel_id=1, source_target_pairs={{0,8},{4,12},{8,0},{12,4},{1,9},{5,13},{9,1},{13,5},{2,10},{6,14},... | collective-permute-start | bytes 221192 | tf_op jit(solution)/shard_map/ppermute | solution.py:48
  51.1 12.4 %collective-permute-start.11 = (bf16[9,64,64]{1,2,0:T(8,128)(2,1)S(1)}, bf16[9,64,64]{1,2,0:T(8,128)(2,1)S(1)}, u32[]{:S(2)}, u32[]{:S(2)}) collective-permute-start(bf16[9,64,64]{1,2,0:T(8,128)(2,1)S(1)} %get-tuple-element.24), channel_id=1, source_target_pairs={{0,4},{4,8},{8,12},{12,0},{1,5},{5,9},{9,13},{13,1},{2,6},{6,10},{... | collective-permute-start | bytes 221192 | tf_op jit(solution)/shard_map/ppermute | solution.py:48
  51.1 12.4 %collective-permute-start.12 = (bf16[9,64,64]{1,2,0:T(8,128)(2,1)S(1)}, bf16[9,64,64]{1,2,0:T(8,128)(2,1)S(1)}, u32[]{:S(2)}, u32[]{:S(2)}) collective-permute-start(bf16[9,64,64]{1,2,0:T(8,128)(2,1)S(1)} %get-tuple-element.23), channel_id=1, source_target_pairs={{0,12},{4,0},{8,4},{12,8},{1,13},{5,1},{9,5},{13,9},{2,14},{6,2},{... | collective-permute-start | bytes 221192 | tf_op jit(solution)/shard_map/ppermute | solution.py:48
  61.3 1.5 %copy-start.4 = (f32[1,2,64,256]{3,2,1,0:T(8,128)S(1)}, f32[1,2,64,256]{3,2,1,0:T(8,128)}, u32[]{:S(2)}) copy-start(f32[1,2,64,256]{3,2,1,0:T(8,128)} %convolution_bitcast_fusion.2) | copy-start | bytes 393220
  61.3 2.2 %copy-start.3 = (f32[9,256,64]{1,2,0:T(8,128)S(1)}, f32[9,256,64]{1,2,0:T(8,128)}, u32[]{:S(2)}) copy-start(f32[9,256,64]{1,2,0:T(8,128)} %copy-done.2) | copy-start | bytes 1769476

commit v20 on v17

--- a/solution.py
+++ b/solution.py
@@ -52,9 +52,10 @@
 
 def filter_kernel(
     first_ref, src_ref, start_ref, span_ref, basis_ref, scale_ref, field_ref, total_ref,
-    out_ref, acc_ref, *, slots, height, lon_count, lon_total, backward,
+    out_ref, acc_ref, ring_ref, *, slots, height, lon_count, lon_total, backward,
 ):
     r = pl.program_id(1)
+    ring_ref[...] = jnp.zeros(ring_ref.shape, jnp.float32)
     first_row = first_ref[0]
     padded = field_ref.shape[2]
     channels = field_ref.shape[3]
@@ -71,7 +72,7 @@
         band = ((offset >= start) & (offset < start + span) & narrow).astype(jnp.bfloat16)
         boxed = jnp.dot(band, field_ref[0, row], preferred_element_type=jnp.float32)
         full = jnp.where(narrow, 0.0, 1.0).astype(jnp.float32)
-        boxed = boxed + full * total_ref[0, row]
+        ring_ref[basis] = ring_ref[basis] + (scale * full) * total_ref[0, row]
         acc_ref[basis] = acc_ref[basis] + scale * boxed
 
     if backward:
@@ -95,7 +96,9 @@
             add_slot(row, table_row, slot, scale_ref[table_row, slot])
 
     for k in range(BASIS):
-        out_ref[0, 0, :, k * channels:(k + 1) * channels] = acc_ref[k].astype(jnp.bfloat16)
+        out_ref[0, 0, :, k * channels:(k + 1) * channels] = (acc_ref[k] + ring_ref[k]).astype(
+            jnp.bfloat16
+        )
 
 
 def scatter_kernel(
@@ -203,7 +206,10 @@
         out_shape=jax.ShapeDtypeStruct(
             (members, row_count, lon_count, BASIS * channels), jnp.bfloat16
         ),
-        scratch_shapes=[pltpu.VMEM((BASIS, lon_count, channels), jnp.float32)],
+        scratch_shapes=[
+            pltpu.VMEM((BASIS, lon_count, channels), jnp.float32),
+            pltpu.VMEM((BASIS, 1, channels), jnp.float32),
+        ],
     )(first, *tables, field, totals[:, :, None, :])
 
 

time: 63.8 us -> 63.9 us (level)
  the two profiles are of different devices: /device:TPU:9 before, /device:TPU:13 now
where the time goes in v20:
time: 63.9 us; the launch traced here: 63.5 us
  Pallas kernels  16.3 us (26%)
  starting transfers between devices  14.6 us (23%)
  waiting for transfers between devices  13.6 us (21%)
  matrix products  7.83 us (12%)
  local copies, waits for them, and re-layouts  6.18 us (10%)
  other arithmetic  3.96 us (6%)
  between operations  0.94 us (1%)
    pallas_call x2, Pallas kernels, run_scatter(): pl.pallas_call(kernel, grid=(members,), in_specs=[smem] * 6 + [pl.BlockSp...  12.4 us
    ppermute x6, waiting for transfers between devices, ring_scatter(): sent = lax.ppermute(piece.astype(jnp.bfloat16), axis, pairs)  7.2 us
    ppermute x2, waiting for transfers between devices, with_halo(): lax.ppermute(lax.slice_in_dim(block, 0, width, axis=dim), axis, backward)  5.1 us
    ppermute x2, starting transfers between devices, with_halo(): lax.ppermute(lax.slice_in_dim(block, block.shape[dim] - width, None, axis...  4.78 us
    ppermute x6, starting transfers between devices, ring_scatter(): sent = lax.ppermute(piece.astype(jnp.bfloat16), axis, pairs)  4.04 us
    pallas_call x1, Pallas kernels, run_filter(): pl.pallas_call(kernel, grid=(members, row_count), in_specs=[smem] * 6 + [...  3.92 us
    ppermute x3, starting transfers between devices, ring_sum(): total = total + lax.ppermute(value, axis, pairs)  3.73 us
    dot_general x2, matrix products, backward_rows(): jnp.einsum('bpwq,qc->bpwc', back_filtered, w_back, preferred_element_type...  3.6 us
  transfers between devices with their start and end apart: 13, of which 9 were waited for; matrix products, arithmetic and copies ran while one was open for 14% of the time, Pallas kernels for 20%

profile of v20, /device:TPU:13, one launch (start us, length us, event | category | flops | bytes accessed | tf_op | source)
XLA Modules:
  0.0 63.5 jit_solution(3935790088808567024)
XLA Ops:
  0.6 0.0 copy-start.1
  0.6 1.0 %constant_dynamic-update-slice_fusion.1 = bf16[1,4,64,512]{3,2,1,0:T(8,128)(2,1)S(1)} fusion(bf16[1,4,64,256]{3,2,1,0:T(8,128)(2,1)} %param.8), kind=kLoop, calls=%fused_computation.35 | loop fusion | bytes 262144
  1.7 0.9 %constant_dynamic-update-slice_fusion = bf16[1,4,64,512]{3,2,1,0:T(8,128)(2,1)S(1)} fusion(bf16[1,4,64,512]{3,2,1,0:T(8,128)(2,1)S(1)} %constant_dynamic-update-slice_fusion.1, bf16[1,4,64,256]{3,2,1,0:T(8,128)(2,1)} %param.9), kind=kLoop, calls=%fused_computation.34 | loop fusion | bytes 262144 | tf_op jit(solution)/shard_map/concatenate | solution.py:226
  2.6 3.2 %collective-permute-start = (bf16[1,2,64,512]{3,2,1,0:T(8,128)(2,1)S(1)}, bf16[1,2,64,512]{3,2,1,0:T(8,128)(2,1)S(1)}, u32[]{:S(2)}, u32[]{:S(2)}) collective-permute-start(bf16[1,2,64,512]{3,2,1,0:T(8,128)(2,1)S(1)} %get-tuple-element.27), channel_id=1, source_target_pairs={{0,4},{4,8},{8,12},{1,5},{5,9},{9,13},{2,6},{6,10},{10,14},{3,7},{... | collective-permute-start | bytes 393224 | tf_op jit(solution)/shard_map/ppermute | solution.py:23
  5.8 2.1 %collective-permute-start.1 = (bf16[1,2,64,512]{3,2,1,0:T(8,128)(2,1)S(1)}, bf16[1,2,64,512]{3,2,1,0:T(8,128)(2,1)S(1)}, u32[]{:S(2)}, u32[]{:S(2)}) collective-permute-start(bf16[1,2,64,512]{3,2,1,0:T(8,128)(2,1)S(1)} %get-tuple-element.28), channel_id=1, source_target_pairs={{4,0},{8,4},{12,8},{5,1},{9,5},{13,9},{6,2},{10,6},{14,10},{7,3},{... | collective-permute-start | bytes 393224 | tf_op jit(solution)/shard_map/ppermute | solution.py:26
  8.0 0.0 copy-done.1
  8.0 0.0 copy-start.5
  8.0 0.0 copy-start.6
  8.0 0.7 %copy.17 = bf16[9,256,256]{1,2,0:T(8,128)(2,1)S(1)} copy(bf16[9,256,256]{2,1,0:T(8,128)(2,1)S(1)} %copy-done.1) | data formatting | bytes 2359296 | tf_op args[2]
  8.8 0.0 copy-done.5
  8.8 0.0 copy-done.6
  8.8 0.6 rsqrt_multiply_fusion.scale_ref
  9.4 0.0 collective-permute-done
  9.4 2.1 %collective-permute-done.1 = bf16[1,2,64,512]{3,2,1,0:T(8,128)(2,1)S(1)} collective-permute-done((bf16[1,2,64,512]{3,2,1,0:T(8,128)(2,1)S(1)}, bf16[1,2,64,512]{3,2,1,0:T(8,128)(2,1)S(1)}, u32[]{:S(2)}, u32[]{:S(2)}) %collective-permute-start.1) | collective-permute-done | bytes 131104 | tf_op jit(solution)/shard_map/ppermute | solution.py:26
  11.5 0.1 pad_maximum_fusion
  11.6 0.1 convert_reduce_fusion
  11.7 3.3 %collective-permute-start.4 = (f32[2,1,4,256]{3,0,2,1:T(2,128)S(1)}, f32[2,1,4,256]{3,0,2,1:T(2,128)S(1)}, u32[]{:S(2)}, u32[]{:S(2)}) collective-permute-start(f32[2,1,4,256]{3,0,2,1:T(2,128)S(1)} %pad_maximum_fusion.2), channel_id=1, source_target_pairs={{0,1},{1,2},{2,3},{3,0},{4,5},{5,6},{6,7},{7,4},{8,9},{9,10},{10,1... | collective-permute-start | bytes 24584 | tf_op jit(solution)/shard_map/ppermute | solution.py:36
  15.0 0.3 collective-permute-start.5
  15.2 0.2 collective-permute-start.6
  15.4 1.6 %collective-permute-start.2 = (bf16[1,8,16,512]{3,2,1,0:T(8,128)(2,1)S(1)}, bf16[1,8,16,512]{3,2,1,0:T(8,128)(2,1)S(1)}, u32[]{:S(2)}, u32[]{:S(2)}) collective-permute-start(bf16[1,8,16,512]{3,2,1,0:T(8,128)(2,1)S(1)} %get-tuple-element.25), channel_id=1, source_target_pairs={{0,1},{1,2},{2,3},{3,0},{4,5},{5,6},{6,7},{7,4},{8,9},{9,10},{10,1... | collective-permute-start | bytes 393224 | tf_op jit(solution)/shard_map/ppermute | solution.py:23
  17.0 0.0 collective-permute-start.3
  17.0 0.0 collective-permute-done.4
  17.0 0.4 collective-permute-done.5
  17.5 0.8 %collective-permute-done.6 = f32[2,1,4,256]{3,0,2,1:T(2,128)S(1)} collective-permute-done((f32[2,1,4,256]{3,0,2,1:T(2,128)S(1)}, f32[2,1,4,256]{3,0,2,1:T(2,128)S(1)}, u32[]{:S(2)}, u32[]{:S(2)}) %collective-permute-start.6) | collective-permute-done | bytes 8224 | tf_op jit(solution)/shard_map/ppermute | solution.py:36
  18.3 0.6 fusion.17
  18.9 0.1 collective-permute-done.2
  19.0 3.0 %collective-permute-done.3 = bf16[1,8,16,512]{3,2,1,0:T(8,128)(2,1)S(1)} collective-permute-done((bf16[1,8,16,512]{3,2,1,0:T(8,128)(2,1)S(1)}, bf16[1,8,16,512]{3,2,1,0:T(8,128)(2,1)S(1)}, u32[]{:S(2)}, u32[]{:S(2)}) %collective-permute-start.3) | collective-permute-done | bytes 131104 | tf_op jit(solution)/shard_map/ppermute | solution.py:26
  22.0 1.1 %fusion.11.field_ref = bf16[1,8,128,512]{3,2,1,0:T(8,128)(2,1)} fusion(bf16[1,8,16,512]{3,2,1,0:T(8,128)(2,1)S(1)} %collective-permute-done.3, bf16[1,8,64,512]{3,2,1,0:T(8,128)(2,1)S(1)} %pad_maximum_fusion, bf16[1,8,16,512]{3,2,1,0:T(8,128)(2,1)S(1)} %collective-permute-done.2), kind=kLoop, calls=%fused_computation.13 | loop fusion | flops 5242880 | bytes 1835008 | tf_op jit(solution)/shard_map/concatenate | solution.py:27
  23.1 3.9 %shard_map.103 = bf16[1,4,64,2304]{3,2,1,0:T(8,128)(2,1)} custom-call(s32[1]{0:T(128)} %bitcast.first_ref, s32[16,12]{1,0:T(8,128)} %src_ref.5, s32[16,12]{1,0:T(8,128)} %start_ref.5, s32[16,12]{1,0:T(8,128)} %span_ref.5, s32[16,12]{1,0:T(8,128)} %basis_ref.5, f32[16,12]{1,0:T(8,128)} %rsqrt_multiply_fusion.scale_ref, ...), custom_call_target="tpu_custom_call" | custom-call | tf_op jit(solution)/shard_map/pallas_call | solution.py:195
  27.0 1.8 %convolution_bitcast_fusion = f32[9,256,256]{1,2,0:T(8,128)S(1)} fusion(bf16[4,8,9,8,256]{4,3,2,1,0:T(8,128)(2,1)} %bitcast.57, bf16[1,4,64,256]{3,2,1,0:T(8,128)(2,1)} %param.9), kind=kOutput, calls=%fused_computation.4 | convolution fusion | flops 301989888 | bytes 3670016 | tf_op jit(solution)/shard_map/brwq,brwo->qo/dot_general | solution.py:244
  28.8 0.9 %dynamic-slice_convert_fusion.2 = (bf16[9,256,64]{1,2,0:T(8,128)(2,1)}, bf16[9,256,64]{1,2,0:T(8,128)(2,1)}, bf16[9,256,64]{1,2,0:T(8,128)(2,1)}) fusion(f32[9,256,256]{1,2,0:T(8,128)S(1)} %convolution_bitcast_fusion, s32[]{:T(128)S(6)} %select_n.53, s32[]{:T(128)S(6)} %select_n.57, s32[]{:T(128)S(6)} %select_n.55), kind=kLoop, calls=%fused_computation.19 | loop fusion | bytes 1769484 | tf_op jit(solution)/shard_map/convert_element_type | solution.py:48
  29.7 0.0 collective-permute-start.7
  29.7 1.2 %collective-permute-start.8 = (bf16[9,256,64]{1,2,0:T(8,128)(2,1)}, bf16[9,256,64]{1,2,0:T(8,128)(2,1)}, u32[]{:S(2)}, u32[]{:S(2)}) collective-permute-start(bf16[9,256,64]{1,2,0:T(8,128)(2,1)} %get-tuple-element.21), channel_id=1, source_target_pairs={{0,2},{1,3},{2,0},{3,1},{4,6},{5,7},{6,4},{7,5},{8,10},{9,11},{10,... | collective-permute-start | bytes 884744 | tf_op jit(solution)/shard_map/ppermute | solution.py:48
  30.9 0.2 collective-permute-start.9
  31.1 5.8 %shard_map.104 = bf16[1,2,64,2304]{3,2,1,0:T(8,128)(2,1)} custom-call(s32[1]{0:T(128)} %bitcast.first_ref, s32[16,12]{1,0:T(8,128)} %src_ref.5, s32[16,12]{1,0:T(8,128)} %start_ref.5, s32[16,12]{1,0:T(8,128)} %span_ref.5, s32[16,12]{1,0:T(8,128)} %basis_ref.5, f32[16,12]{1,0:T(8,128)} %rsqrt_multiply_fusion.scale_ref, ...), custom_call_target="tpu_custom_call" | custom-call | tf_op jit(solution)/shard_map/pallas_call | solution.py:162
  36.9 0.0 copy-start
  36.9 2.1 %convolution_bitcast_fusion.2 = f32[1,2,64,256]{3,2,1,0:T(8,128)} fusion(bf16[2304,256,1]{1,0,2:T(8,128)(2,1)S(1)} %bitcast.58, bf16[1,2,64,2304]{3,2,1,0:T(8,128)(2,1)} %shard_map.104), kind=kOutput, calls=%fused_computation.11 | convolution fusion | flops 150994944 | bytes 1900544 | tf_op jit(solution)/shard_map/bpwq,qc->bpwc/dot_general | solution.py:255
  39.0 0.0 copy-done
  39.0 2.5 %fusion.7 = f32[1,4,64,256]{3,2,1,0:T(8,128)} fusion(bf16[2304,256,1]{1,0,2:T(8,128)(2,1)} %bitcast.60, bf16[1,4,64,2304]{3,2,1,0:T(8,128)(2,1)S(1)} %copy-done), kind=kOutput, calls=%fused_computation.9 | convolution fusion | flops 301989888 | bytes 2621440 | tf_op jit(solution)/shard_map/brwq,qo->brwo/dot_general | solution.py:242
  41.5 0.0 collective-permute-done.7
  41.5 2.1 %collective-permute-done.8 = bf16[9,256,64]{1,2,0:T(8,128)(2,1)} collective-permute-done((bf16[9,256,64]{1,2,0:T(8,128)(2,1)}, bf16[9,256,64]{1,2,0:T(8,128)(2,1)}, u32[]{:S(2)}, u32[]{:S(2)}) %collective-permute-start.8) | collective-permute-done | bytes 294944 | tf_op jit(solution)/shard_map/ppermute | solution.py:48
  43.6 1.2 %collective-permute-done.9 = bf16[9,256,64]{1,2,0:T(8,128)(2,1)} collective-permute-done((bf16[9,256,64]{1,2,0:T(8,128)(2,1)}, bf16[9,256,64]{1,2,0:T(8,128)(2,1)}, u32[]{:S(2)}, u32[]{:S(2)}) %collective-permute-start.9) | collective-permute-done | bytes 294944 | tf_op jit(solution)/shard_map/ppermute | solution.py:48
  44.8 1.3 %convert_add_fusion = f32[9,256,64]{1,2,0:T(8,128)S(1)} fusion(bf16[9,256,64]{1,2,0:T(8,128)(2,1)} %collective-permute-done.9, bf16[9,256,64]{1,2,0:T(8,128)(2,1)} %collective-permute-done.8, bf16[9,256,64]{1,2,0:T(8,128)(2,1)} %collective-permute-done.7, f32[9,256,256]{1,2,0:T(8,128)S(1)} %convolution_bitcast_fusion, s32[]{:T(128)S(6)} %select_n.51), kind=kLoop, calls=%fused_computation.16 | loop fusion | flops 884736 | bytes 2064388 | tf_op jit(solution)/shard_map/add | solution.py:49
  46.1 0.0 copy-start.2
  46.1 0.8 %copy-done.2 = f32[9,256,64]{1,2,0:T(8,128)} copy-done((f32[9,256,64]{1,2,0:T(8,128)}, f32[9,256,64]{1,2,0:T(8,128)S(1)}, u32[]{:S(2)}) %copy-start.2) | copy-done | bytes 589848
  47.0 0.2 dynamic-slice_convert_fusion.5
  47.1 1.4 %collective-permute-start.10 = (bf16[9,64,64]{1,2,0:T(8,128)(2,1)S(1)}, bf16[9,64,64]{1,2,0:T(8,128)(2,1)S(1)}, u32[]{:S(2)}, u32[]{:S(2)}) collective-permute-start(bf16[9,64,64]{1,2,0:T(8,128)(2,1)S(1)} %get-tuple-element.22), channel_id=1, source_target_pairs={{0,4},{4,8},{8,12},{12,0},{1,5},{5,9},{9,13},{13,1},{2,6},{6,10},{... | collective-permute-start | bytes 221192 | tf_op jit(solution)/shard_map/ppermute | solution.py:48
  48.5 1.0 %collective-permute-start.11 = (bf16[9,64,64]{1,2,0:T(8,128)(2,1)S(1)}, bf16[9,64,64]{1,2,0:T(8,128)(2,1)S(1)}, u32[]{:S(2)}, u32[]{:S(2)}) collective-permute-start(bf16[9,64,64]{1,2,0:T(8,128)(2,1)S(1)} %get-tuple-element.24), channel_id=1, source_target_pairs={{0,8},{4,12},{8,0},{12,4},{1,9},{5,13},{9,1},{13,5},{2,10},{6,14},... | collective-permute-start | bytes 221192 | tf_op jit(solution)/shard_map/ppermute | solution.py:48
  49.5 0.3 collective-permute-start.12
  49.8 6.7 %shard_map.105 = bf16[1,2,64,2304]{3,2,1,0:T(8,128)(2,1)} custom-call(s32[1]{0:T(128)} %bitcast.first_ref, s32[16,12]{1,0:T(8,128)} %src_ref.5, s32[16,12]{1,0:T(8,128)} %start_ref.5, s32[16,12]{1,0:T(8,128)} %span_ref.5, s32[16,12]{1,0:T(8,128)} %basis_ref.5, f32[16,12]{1,0:T(8,128)} %rsqrt_multiply_fusion.scale_ref, ...), custom_call_target="tpu_custom_call" | custom-call | tf_op jit(solution)/shard_map/pallas_call | solution.py:162
  56.4 0.0 copy-start.4
  56.4 0.0 copy-start.3
  56.4 1.5 %convolution_bitcast_fusion.1 = f32[1,2,64,256]{3,2,1,0:T(8,128)S(1)} fusion(bf16[2304,256,1]{1,0,2:T(8,128)(2,1)S(1)} %bitcast.59, bf16[1,2,64,2304]{3,2,1,0:T(8,128)(2,1)} %shard_map.105), kind=kOutput, calls=%fused_computation.10 | convolution fusion | flops 150994944 | bytes 1900544 | tf_op jit(solution)/shard_map/bpwq,qc->bpwc/dot_general | solution.py:255
  57.9 0.0 copy-done.4
  57.9 0.7 %pad_maximum_fusion.1 = f32[1,4,64,256]{3,2,1,0:T(8,128)} fusion(f32[1,2,64,256]{3,2,1,0:T(8,128)S(1)} %convolution_bitcast_fusion.1, f32[1,2,64,256]{3,2,1,0:T(8,128)S(1)} %copy-done.4), kind=kLoop, calls=%fused_computation.26 | loop fusion | flops 65536 | bytes 524288 | tf_op jit(solution)/shard_map/concatenate | solution.py:263
  58.6 0.0 collective-permute-done.10
  58.6 2.2 %collective-permute-done.11 = bf16[9,64,64]{1,2,0:T(8,128)(2,1)S(1)} collective-permute-done((bf16[9,64,64]{1,2,0:T(8,128)(2,1)S(1)}, bf16[9,64,64]{1,2,0:T(8,128)(2,1)S(1)}, u32[]{:S(2)}, u32[]{:S(2)}) %collective-permute-start.11) | collective-permute-done | bytes 73760 | tf_op jit(solution)/shard_map/ppermute | solution.py:48
  60.8 1.7 %collective-permute-done.12 = bf16[9,64,64]{1,2,0:T(8,128)(2,1)S(1)} collective-permute-done((bf16[9,64,64]{1,2,0:T(8,128)(2,1)S(1)}, bf16[9,64,64]{1,2,0:T(8,128)(2,1)S(1)}, u32[]{:S(2)}, u32[]{:S(2)}) %collective-permute-start.12) | collective-permute-done | bytes 73760 | tf_op jit(solution)/shard_map/ppermute | solution.py:48
  62.5 0.0 copy-done.3
  62.5 0.1 add_multiply_fusion
  62.6 0.9 %copy.19 = f32[9,64,64]{2,1,0:T(8,128)} copy(f32[9,64,64]{1,2,0:T(8,128)S(1)} %add_multiply_fusion) | data formatting | bytes 294912
  (6 shorter events, 0.1 us)
Async XLA Ops:
  0.6 7.4 %copy-start.1 = (bf16[9,256,256]{2,1,0:T(8,128)(2,1)S(1)}, bf16[9,256,256]{2,1,0:T(8,128)(2,1)}, u32[]{:S(2)}) copy-start(bf16[9,256,256]{2,1,0:T(8,128)(2,1)} %param.10) | copy-start | bytes 3538948
  2.6 6.8 %collective-permute-start = (bf16[1,2,64,512]{3,2,1,0:T(8,128)(2,1)S(1)}, bf16[1,2,64,512]{3,2,1,0:T(8,128)(2,1)S(1)}, u32[]{:S(2)}, u32[]{:S(2)}) collective-permute-start(bf16[1,2,64,512]{3,2,1,0:T(8,128)(2,1)S(1)} %get-tuple-element.27), channel_id=1, source_target_pairs={{0,4},{4,8},{8,12},{1,5},{5,9},{9,13},{2,6},{6,10},{10,14},{3,7},{... | collective-permute-start | bytes 393224 | tf_op jit(solution)/shard_map/ppermute | solution.py:23
  5.8 5.7 %collective-permute-start.1 = (bf16[1,2,64,512]{3,2,1,0:T(8,128)(2,1)S(1)}, bf16[1,2,64,512]{3,2,1,0:T(8,128)(2,1)S(1)}, u32[]{:S(2)}, u32[]{:S(2)}) collective-permute-start(bf16[1,2,64,512]{3,2,1,0:T(8,128)(2,1)S(1)} %get-tuple-element.28), channel_id=1, source_target_pairs={{4,0},{8,4},{12,8},{5,1},{9,5},{13,9},{6,2},{10,6},{14,10},{7,3},{... | collective-permute-start | bytes 393224 | tf_op jit(solution)/shard_map/ppermute | solution.py:26
  8.0 0.8 %copy-start.5 = (s32[16,12]{1,0:T(8,128)S(1)}, s32[16,12]{1,0:T(8,128)}, u32[]{:S(2)}) copy-start(s32[16,12]{1,0:T(8,128)} %span_ref.5) | copy-start | bytes 2308
  8.0 0.8 %copy-start.6 = (f32[16,12]{1,0:T(8,128)S(1)}, f32[16,12]{1,0:T(8,128)}, u32[]{:S(2)}) copy-start(f32[16,12]{1,0:T(8,128)} %param.15) | copy-start | bytes 2308
  11.7 5.3 %collective-permute-start.4 = (f32[2,1,4,256]{3,0,2,1:T(2,128)S(1)}, f32[2,1,4,256]{3,0,2,1:T(2,128)S(1)}, u32[]{:S(2)}, u32[]{:S(2)}) collective-permute-start(f32[2,1,4,256]{3,0,2,1:T(2,128)S(1)} %pad_maximum_fusion.2), channel_id=1, source_target_pairs={{0,1},{1,2},{2,3},{3,0},{4,5},{5,6},{6,7},{7,4},{8,9},{9,10},{10,1... | collective-permute-start | bytes 24584 | tf_op jit(solution)/shard_map/ppermute | solution.py:36
  15.0 2.5 %collective-permute-start.5 = (f32[2,1,4,256]{3,0,2,1:T(2,128)S(1)}, f32[2,1,4,256]{3,0,2,1:T(2,128)S(1)}, u32[]{:S(2)}, u32[]{:S(2)}) collective-permute-start(f32[2,1,4,256]{3,0,2,1:T(2,128)S(1)} %pad_maximum_fusion.2), channel_id=1, source_target_pairs={{0,2},{1,3},{2,0},{3,1},{4,6},{5,7},{6,4},{7,5},{8,10},{9,11},{10,... | collective-permute-start | bytes 24584 | tf_op jit(solution)/shard_map/ppermute | solution.py:36
  15.2 3.1 %collective-permute-start.6 = (f32[2,1,4,256]{3,0,2,1:T(2,128)S(1)}, f32[2,1,4,256]{3,0,2,1:T(2,128)S(1)}, u32[]{:S(2)}, u32[]{:S(2)}) collective-permute-start(f32[2,1,4,256]{3,0,2,1:T(2,128)S(1)} %pad_maximum_fusion.2), channel_id=1, source_target_pairs={{0,3},{1,0},{2,1},{3,2},{4,7},{5,4},{6,5},{7,6},{8,11},{9,8},{10,9... | collective-permute-start | bytes 24584 | tf_op jit(solution)/shard_map/ppermute | solution.py:36
  15.4 3.5 %collective-permute-start.2 = (bf16[1,8,16,512]{3,2,1,0:T(8,128)(2,1)S(1)}, bf16[1,8,16,512]{3,2,1,0:T(8,128)(2,1)S(1)}, u32[]{:S(2)}, u32[]{:S(2)}) collective-permute-start(bf16[1,8,16,512]{3,2,1,0:T(8,128)(2,1)S(1)} %get-tuple-element.25), channel_id=1, source_target_pairs={{0,1},{1,2},{2,3},{3,0},{4,5},{5,6},{6,7},{7,4},{8,9},{9,10},{10,1... | collective-permute-start | bytes 393224 | tf_op jit(solution)/shard_map/ppermute | solution.py:23
  17.0 5.0 %collective-permute-start.3 = (bf16[1,8,16,512]{3,2,1,0:T(8,128)(2,1)S(1)}, bf16[1,8,16,512]{3,2,1,0:T(8,128)(2,1)S(1)}, u32[]{:S(2)}, u32[]{:S(2)}) collective-permute-start(bf16[1,8,16,512]{3,2,1,0:T(8,128)(2,1)S(1)} %get-tuple-element.26), channel_id=1, source_target_pairs={{1,0},{2,1},{3,2},{0,3},{5,4},{6,5},{7,6},{4,7},{9,8},{10,9},{11,1... | collective-permute-start | bytes 393224 | tf_op jit(solution)/shard_map/ppermute | solution.py:26
  29.7 11.8 %collective-permute-start.7 = (bf16[9,256,64]{1,2,0:T(8,128)(2,1)}, bf16[9,256,64]{1,2,0:T(8,128)(2,1)}, u32[]{:S(2)}, u32[]{:S(2)}) collective-permute-start(bf16[9,256,64]{1,2,0:T(8,128)(2,1)} %get-tuple-element.19), channel_id=1, source_target_pairs={{0,1},{1,2},{2,3},{3,0},{4,5},{5,6},{6,7},{7,4},{8,9},{9,10},{10,1... | collective-permute-start | bytes 884744 | tf_op jit(solution)/shard_map/ppermute | solution.py:48
  29.7 13.9 %collective-permute-start.8 = (bf16[9,256,64]{1,2,0:T(8,128)(2,1)}, bf16[9,256,64]{1,2,0:T(8,128)(2,1)}, u32[]{:S(2)}, u32[]{:S(2)}) collective-permute-start(bf16[9,256,64]{1,2,0:T(8,128)(2,1)} %get-tuple-element.21), channel_id=1, source_target_pairs={{0,2},{1,3},{2,0},{3,1},{4,6},{5,7},{6,4},{7,5},{8,10},{9,11},{10,... | collective-permute-start | bytes 884744 | tf_op jit(solution)/shard_map/ppermute | solution.py:48
  30.9 13.9 %collective-permute-start.9 = (bf16[9,256,64]{1,2,0:T(8,128)(2,1)}, bf16[9,256,64]{1,2,0:T(8,128)(2,1)}, u32[]{:S(2)}, u32[]{:S(2)}) collective-permute-start(bf16[9,256,64]{1,2,0:T(8,128)(2,1)} %get-tuple-element.20), channel_id=1, source_target_pairs={{0,3},{1,0},{2,1},{3,2},{4,7},{5,4},{6,5},{7,6},{8,11},{9,8},{10,9... | collective-permute-start | bytes 884744 | tf_op jit(solution)/shard_map/ppermute | solution.py:48
  36.9 2.1 %copy-start = (bf16[1,4,64,2304]{3,2,1,0:T(8,128)(2,1)S(1)}, bf16[1,4,64,2304]{3,2,1,0:T(8,128)(2,1)}, u32[]{:S(2)}) copy-start(bf16[1,4,64,2304]{3,2,1,0:T(8,128)(2,1)} %shard_map.103) | copy-start | bytes 3538948
  46.1 0.8 %copy-start.2 = (f32[9,256,64]{1,2,0:T(8,128)}, f32[9,256,64]{1,2,0:T(8,128)S(1)}, u32[]{:S(2)}) copy-start(f32[9,256,64]{1,2,0:T(8,128)S(1)} %convert_add_fusion) | copy-start | bytes 1769476
  47.1 11.5 %collective-permute-start.10 = (bf16[9,64,64]{1,2,0:T(8,128)(2,1)S(1)}, bf16[9,64,64]{1,2,0:T(8,128)(2,1)S(1)}, u32[]{:S(2)}, u32[]{:S(2)}) collective-permute-start(bf16[9,64,64]{1,2,0:T(8,128)(2,1)S(1)} %get-tuple-element.22), channel_id=1, source_target_pairs={{0,4},{4,8},{8,12},{12,0},{1,5},{5,9},{9,13},{13,1},{2,6},{6,10},{... | collective-permute-start | bytes 221192 | tf_op jit(solution)/shard_map/ppermute | solution.py:48
  48.5 12.3 %collective-permute-start.11 = (bf16[9,64,64]{1,2,0:T(8,128)(2,1)S(1)}, bf16[9,64,64]{1,2,0:T(8,128)(2,1)S(1)}, u32[]{:S(2)}, u32[]{:S(2)}) collective-permute-start(bf16[9,64,64]{1,2,0:T(8,128)(2,1)S(1)} %get-tuple-element.24), channel_id=1, source_target_pairs={{0,8},{4,12},{8,0},{12,4},{1,9},{5,13},{9,1},{13,5},{2,10},{6,14},... | collective-permute-start | bytes 221192 | tf_op jit(solution)/shard_map/ppermute | solution.py:48
  49.5 13.0 %collective-permute-start.12 = (bf16[9,64,64]{1,2,0:T(8,128)(2,1)S(1)}, bf16[9,64,64]{1,2,0:T(8,128)(2,1)S(1)}, u32[]{:S(2)}, u32[]{:S(2)}) collective-permute-start(bf16[9,64,64]{1,2,0:T(8,128)(2,1)S(1)} %get-tuple-element.23), channel_id=1, source_target_pairs={{0,12},{4,0},{8,4},{12,8},{1,13},{5,1},{9,5},{13,9},{2,14},{6,2},{... | collective-permute-start | bytes 221192 | tf_op jit(solution)/shard_map/ppermute | solution.py:48
  56.4 1.5 %copy-start.4 = (f32[1,2,64,256]{3,2,1,0:T(8,128)S(1)}, f32[1,2,64,256]{3,2,1,0:T(8,128)}, u32[]{:S(2)}) copy-start(f32[1,2,64,256]{3,2,1,0:T(8,128)} %convolution_bitcast_fusion.2) | copy-start | bytes 393220
  56.4 6.1 %copy-start.3 = (f32[9,256,64]{1,2,0:T(8,128)S(1)}, f32[9,256,64]{1,2,0:T(8,128)}, u32[]{:S(2)}) copy-start(f32[9,256,64]{1,2,0:T(8,128)} %copy-done.2) | copy-start | bytes 1769476

commit v21 on v17

--- a/solution.py
+++ b/solution.py
@@ -45,6 +45,18 @@
     for shift in range(1, count):
         pairs = [(i, (i + shift) % count) for i in range(count)]
         piece = lax.dynamic_slice_in_dim(value, ((own + shift) % count) * block, block, dim)
+        sent = lax.ppermute(piece.astype(jnp.bfloat16), axis, pairs)
+        total = total + sent.astype(jnp.float32)
+    return total
+
+
+def rolled_scatter(value, axis, dim):
+    count = lax.axis_size(axis)
+    block = value.shape[dim] // count
+    total = lax.slice_in_dim(value, 0, block, axis=dim)
+    for shift in range(1, count):
+        pairs = [(i, (i + shift) % count) for i in range(count)]
+        piece = lax.slice_in_dim(value, shift * block, (shift + 1) * block, axis=dim)
         sent = lax.ppermute(piece.astype(jnp.bfloat16), axis, pairs)
         total = total + sent.astype(jnp.float32)
     return total
@@ -235,11 +247,13 @@
     w_fwd = weight.reshape(BASIS * channels, channels)
     response = jnp.einsum("brwq,qo->brwo", flattened, w_fwd, preferred_element_type=jnp.float32)
 
+    o_block = channels // lax.axis_size("lon")
+    rolled = jnp.roll(cotangent, -lax.axis_index("lon") * o_block, axis=3)
     partial_value = jnp.einsum(
-        "brwq,brwo->qo", flattened, cotangent, preferred_element_type=jnp.float32
+        "brwq,brwo->qo", flattened, rolled, preferred_element_type=jnp.float32
     )
     partial_value = partial_value.reshape(BASIS, channels, channels)
-    reduced = ring_scatter(partial_value, "lon", 2)
+    reduced = rolled_scatter(partial_value, "lon", 2)
     w_back = jnp.transpose(weight, (0, 2, 1)).reshape(BASIS * channels, channels)
 
     def backward_rows(field, field_totals, lowest, count):

time: 63.8 us -> 63.7 us (level)
  the two profiles are of different devices: /device:TPU:9 before, /device:TPU:15 now
where the time goes in v21:
time: 63.7 us; the launch traced here: 63.3 us
  Pallas kernels  16.3 us (26%)
  waiting for transfers between devices  15.2 us (24%)
  starting transfers between devices  14.9 us (23%)
  matrix products  7.43 us (12%)
  local copies, waits for them, and re-layouts  4.47 us (7%)
  other arithmetic  4.15 us (7%)
  between operations  0.91 us (1%)
    pallas_call x2, Pallas kernels, run_scatter(): pl.pallas_call(kernel, grid=(members,), in_specs=[smem] * 6 + [pl.BlockSp...  12.4 us
    ppermute x3, waiting for transfers between devices, ring_scatter(): sent = lax.ppermute(piece.astype(jnp.bfloat16), axis, pairs)  5.96 us
    ppermute x2, starting transfers between devices, with_halo(): lax.ppermute(lax.slice_in_dim(block, block.shape[dim] - width, None, axis...  5 us
    ppermute x2, waiting for transfers between devices, with_halo(): lax.ppermute(lax.slice_in_dim(block, 0, width, axis=dim), axis, backward)  4.01 us
    pallas_call x1, Pallas kernels, run_filter(): pl.pallas_call(kernel, grid=(members, row_count), in_specs=[smem] * 6 + [...  3.91 us
    ppermute x3, starting transfers between devices, ring_sum(): total = total + lax.ppermute(value, axis, pairs)  3.51 us
    dot_general x1, matrix products, on_device(): jnp.einsum('brwq,brwo->qo', flattened, rolled, preferred_element_type=jnp...  3.38 us
    ppermute x3, waiting for transfers between devices, rolled_scatter(): sent = lax.ppermute(piece.astype(jnp.bfloat16), axis, pairs)  3.36 us
  transfers between devices with their start and end apart: 13, of which 8 were waited for; matrix products, arithmetic and copies ran while one was open for 11% of the time, Pallas kernels for 20%

profile of v21, /device:TPU:15, one launch (start us, length us, event | category | flops | bytes accessed | tf_op | source)
XLA Modules:
  0.0 63.3 jit_solution(16902309187143877244)
XLA Ops:
  0.6 0.0 copy-start.1
  0.6 1.0 %constant_dynamic-update-slice_fusion.1 = bf16[1,4,64,512]{3,2,1,0:T(8,128)(2,1)S(1)} fusion(bf16[1,4,64,256]{3,2,1,0:T(8,128)(2,1)} %param.8), kind=kLoop, calls=%fused_computation.37 | loop fusion | bytes 262144
  1.7 0.9 %constant_dynamic-update-slice_fusion = bf16[1,4,64,512]{3,2,1,0:T(8,128)(2,1)S(1)} fusion(bf16[1,4,64,512]{3,2,1,0:T(8,128)(2,1)S(1)} %constant_dynamic-update-slice_fusion.1, bf16[1,4,64,256]{3,2,1,0:T(8,128)(2,1)} %param.9), kind=kLoop, calls=%fused_computation.36 | loop fusion | bytes 262144 | tf_op jit(solution)/shard_map/concatenate | solution.py:232
  2.6 3.2 %collective-permute-start = (bf16[1,2,64,512]{3,2,1,0:T(8,128)(2,1)S(1)}, bf16[1,2,64,512]{3,2,1,0:T(8,128)(2,1)S(1)}, u32[]{:S(2)}, u32[]{:S(2)}) collective-permute-start(bf16[1,2,64,512]{3,2,1,0:T(8,128)(2,1)S(1)} %get-tuple-element.27), channel_id=1, source_target_pairs={{0,4},{4,8},{8,12},{1,5},{5,9},{9,13},{2,6},{6,10},{10,14},{3,7},{... | collective-permute-start | bytes 393224 | tf_op jit(solution)/shard_map/ppermute | solution.py:23
  5.8 2.1 %collective-permute-start.1 = (bf16[1,2,64,512]{3,2,1,0:T(8,128)(2,1)S(1)}, bf16[1,2,64,512]{3,2,1,0:T(8,128)(2,1)S(1)}, u32[]{:S(2)}, u32[]{:S(2)}) collective-permute-start(bf16[1,2,64,512]{3,2,1,0:T(8,128)(2,1)S(1)} %get-tuple-element.28), channel_id=1, source_target_pairs={{4,0},{8,4},{12,8},{5,1},{9,5},{13,9},{6,2},{10,6},{14,10},{7,3},{... | collective-permute-start | bytes 393224 | tf_op jit(solution)/shard_map/ppermute | solution.py:26
  8.0 0.0 copy-done.1
  8.0 0.0 copy-start.3
  8.0 0.0 copy-start.4
  8.0 0.7 %copy.17 = bf16[9,256,256]{1,2,0:T(8,128)(2,1)S(1)} copy(bf16[9,256,256]{2,1,0:T(8,128)(2,1)S(1)} %copy-done.1) | data formatting | bytes 2359296 | tf_op args[2]
  8.8 0.0 copy-done.3
  8.8 0.0 copy-done.4
  8.8 0.6 rsqrt_multiply_fusion.scale_ref
  9.4 0.0 collective-permute-done
  9.4 2.1 %collective-permute-done.1 = bf16[1,2,64,512]{3,2,1,0:T(8,128)(2,1)S(1)} collective-permute-done((bf16[1,2,64,512]{3,2,1,0:T(8,128)(2,1)S(1)}, bf16[1,2,64,512]{3,2,1,0:T(8,128)(2,1)S(1)}, u32[]{:S(2)}, u32[]{:S(2)}) %collective-permute-start.1) | collective-permute-done | bytes 131104 | tf_op jit(solution)/shard_map/ppermute | solution.py:26
  11.5 0.1 pad_maximum_fusion
  11.6 0.1 convert_reduce_fusion
  11.7 2.3 %collective-permute-start.4 = (f32[2,1,4,256]{3,0,2,1:T(2,128)S(1)}, f32[2,1,4,256]{3,0,2,1:T(2,128)S(1)}, u32[]{:S(2)}, u32[]{:S(2)}) collective-permute-start(f32[2,1,4,256]{3,0,2,1:T(2,128)S(1)} %pad_maximum_fusion.2), channel_id=1, source_target_pairs={{0,1},{1,2},{2,3},{3,0},{4,5},{5,6},{6,7},{7,4},{8,9},{9,10},{10,1... | collective-permute-start | bytes 24584 | tf_op jit(solution)/shard_map/ppermute | solution.py:36
  14.0 1.2 %collective-permute-start.5 = (f32[2,1,4,256]{3,0,2,1:T(2,128)S(1)}, f32[2,1,4,256]{3,0,2,1:T(2,128)S(1)}, u32[]{:S(2)}, u32[]{:S(2)}) collective-permute-start(f32[2,1,4,256]{3,0,2,1:T(2,128)S(1)} %pad_maximum_fusion.2), channel_id=1, source_target_pairs={{0,2},{1,3},{2,0},{3,1},{4,6},{5,7},{6,4},{7,5},{8,10},{9,11},{10,... | collective-permute-start | bytes 24584 | tf_op jit(solution)/shard_map/ppermute | solution.py:36
  15.2 0.0 collective-permute-start.6
  15.2 1.8 %collective-permute-start.2 = (bf16[1,8,16,512]{3,2,1,0:T(8,128)(2,1)S(1)}, bf16[1,8,16,512]{3,2,1,0:T(8,128)(2,1)S(1)}, u32[]{:S(2)}, u32[]{:S(2)}) collective-permute-start(bf16[1,8,16,512]{3,2,1,0:T(8,128)(2,1)S(1)} %get-tuple-element.25), channel_id=1, source_target_pairs={{0,1},{1,2},{2,3},{3,0},{4,5},{5,6},{6,7},{7,4},{8,9},{9,10},{10,1... | collective-permute-start | bytes 393224 | tf_op jit(solution)/shard_map/ppermute | solution.py:23
  17.0 0.0 collective-permute-start.3
  17.0 0.0 collective-permute-done.4
  17.0 0.0 collective-permute-done.5
  17.0 1.6 %collective-permute-done.6 = f32[2,1,4,256]{3,0,2,1:T(2,128)S(1)} collective-permute-done((f32[2,1,4,256]{3,0,2,1:T(2,128)S(1)}, f32[2,1,4,256]{3,0,2,1:T(2,128)S(1)}, u32[]{:S(2)}, u32[]{:S(2)}) %collective-permute-start.6) | collective-permute-done | bytes 8224 | tf_op jit(solution)/shard_map/ppermute | solution.py:36
  18.7 0.6 fusion.22
  19.3 0.3 collective-permute-done.2
  19.5 1.9 %collective-permute-done.3 = bf16[1,8,16,512]{3,2,1,0:T(8,128)(2,1)S(1)} collective-permute-done((bf16[1,8,16,512]{3,2,1,0:T(8,128)(2,1)S(1)}, bf16[1,8,16,512]{3,2,1,0:T(8,128)(2,1)S(1)}, u32[]{:S(2)}, u32[]{:S(2)}) %collective-permute-start.3) | collective-permute-done | bytes 131104 | tf_op jit(solution)/shard_map/ppermute | solution.py:26
  21.4 1.1 %fusion.11.field_ref = bf16[1,8,128,512]{3,2,1,0:T(8,128)(2,1)} fusion(bf16[1,8,16,512]{3,2,1,0:T(8,128)(2,1)S(1)} %collective-permute-done.3, bf16[1,8,64,512]{3,2,1,0:T(8,128)(2,1)S(1)} %pad_maximum_fusion, bf16[1,8,16,512]{3,2,1,0:T(8,128)(2,1)S(1)} %collective-permute-done.2), kind=kLoop, calls=%fused_computation.13 | loop fusion | flops 5242880 | bytes 1835008 | tf_op jit(solution)/shard_map/concatenate | solution.py:27
  22.5 0.0 copy-start.2
  22.5 3.9 %shard_map.103 = bf16[1,4,64,2304]{3,2,1,0:T(8,128)(2,1)} custom-call(s32[1]{0:T(128)} %bitcast.first_ref, s32[16,12]{1,0:T(8,128)} %src_ref.5, s32[16,12]{1,0:T(8,128)} %start_ref.5, s32[16,12]{1,0:T(8,128)} %span_ref.5, s32[16,12]{1,0:T(8,128)} %basis_ref.5, f32[16,12]{1,0:T(8,128)} %rsqrt_multiply_fusion.scale_ref, ...), custom_call_target="tpu_custom_call" | custom-call | tf_op jit(solution)/shard_map/pallas_call | solution.py:204
  26.4 0.0 copy-done.2
  26.4 3.4 %fusion.27 = (bf16[9,256,256]{1,2,0:T(8,128)(2,1)S(1)}, f32[9,256,256]{1,2,0:T(8,128)}) fusion(s32[]{:T(128)S(6)} %select_n.40, bf16[1,4,64,256]{3,2,1,0:T(8,128)(2,1)S(1)} %copy-done.2, bf16[4,8,9,8,256]{4,3,2,1,0:T(8,128)(2,1)} %bitcast.61), kind=kOutput, calls=%fused_computation.47 | convolution fusion | flops 302841856 | bytes 4849668 | tf_op jit(solution)/shard_map/brwq,brwo->qo/dot_general | solution.py:252
  29.8 0.1 fusion.24
  29.9 0.6 %collective-permute-start.7 = (bf16[9,256,64]{1,2,0:T(8,128)(2,1)S(1)}, bf16[9,256,64]{1,2,0:T(8,128)(2,1)}, u32[]{:S(2)}, u32[]{:S(2)}) collective-permute-start(bf16[9,256,64]{1,2,0:T(8,128)(2,1)S(1)} %get-tuple-element.19), channel_id=1, source_target_pairs={{0,1},{1,2},{2,3},{3,0},{4,5},{5,6},{6,7},{7,4},{8,9},{9,10},{10,1... | collective-permute-start | bytes 884744 | tf_op jit(solution)/shard_map/ppermute | solution.py:60
  30.5 0.3 collective-permute-start.8
  30.8 0.7 %collective-permute-start.9 = (bf16[9,256,64]{1,2,0:T(8,128)(2,1)S(1)}, bf16[9,256,64]{1,2,0:T(8,128)(2,1)}, u32[]{:S(2)}, u32[]{:S(2)}) collective-permute-start(bf16[9,256,64]{1,2,0:T(8,128)(2,1)S(1)} %get-tuple-element.20), channel_id=1, source_target_pairs={{0,3},{1,0},{2,1},{3,2},{4,7},{5,4},{6,5},{7,6},{8,11},{9,8},{10,9... | collective-permute-start | bytes 884744 | tf_op jit(solution)/shard_map/ppermute | solution.py:60
  31.5 6.9 %shard_map.104 = bf16[1,2,64,2304]{3,2,1,0:T(8,128)(2,1)} custom-call(s32[1]{0:T(128)} %bitcast.first_ref, s32[16,12]{1,0:T(8,128)} %src_ref.5, s32[16,12]{1,0:T(8,128)} %start_ref.5, s32[16,12]{1,0:T(8,128)} %span_ref.5, s32[16,12]{1,0:T(8,128)} %basis_ref.5, f32[16,12]{1,0:T(8,128)} %rsqrt_multiply_fusion.scale_ref, ...), custom_call_target="tpu_custom_call" | custom-call | tf_op jit(solution)/shard_map/pallas_call | solution.py:171
  38.4 0.0 copy-start
  38.4 1.5 %convolution_bitcast_fusion.2 = f32[1,2,64,256]{3,2,1,0:T(8,128)S(1)} fusion(bf16[2304,256,1]{1,0,2:T(8,128)(2,1)S(1)} %bitcast.62, bf16[1,2,64,2304]{3,2,1,0:T(8,128)(2,1)} %shard_map.104), kind=kOutput, calls=%fused_computation.11 | convolution fusion | flops 150994944 | bytes 1900544 | tf_op jit(solution)/shard_map/bpwq,qc->bpwc/dot_general | solution.py:263
  39.9 0.0 copy-done
  39.9 1.2 %fusion.7 = f32[1,4,64,256]{3,2,1,0:T(8,128)} fusion(bf16[2304,256,1]{1,0,2:T(8,128)(2,1)S(1)} %bitcast.64, bf16[1,4,64,2304]{3,2,1,0:T(8,128)(2,1)S(1)} %copy-done), kind=kOutput, calls=%fused_computation.9 | convolution fusion | flops 301989888 | bytes 2621440 | tf_op jit(solution)/shard_map/brwq,qo->brwo/dot_general | solution.py:248
  41.1 0.0 collective-permute-done.7
  41.1 1.7 %collective-permute-done.8 = bf16[9,256,64]{1,2,0:T(8,128)(2,1)} collective-permute-done((bf16[9,256,64]{1,2,0:T(8,128)(2,1)S(1)}, bf16[9,256,64]{1,2,0:T(8,128)(2,1)}, u32[]{:S(2)}, u32[]{:S(2)}) %collective-permute-start.8) | collective-permute-done | bytes 294944 | tf_op jit(solution)/shard_map/ppermute | solution.py:60
  42.8 1.7 %collective-permute-done.9 = bf16[9,256,64]{1,2,0:T(8,128)(2,1)} collective-permute-done((bf16[9,256,64]{1,2,0:T(8,128)(2,1)S(1)}, bf16[9,256,64]{1,2,0:T(8,128)(2,1)}, u32[]{:S(2)}, u32[]{:S(2)}) %collective-permute-start.9) | collective-permute-done | bytes 294944 | tf_op jit(solution)/shard_map/ppermute | solution.py:60
  44.4 1.4 %fusion.13 = f32[9,256,64]{1,2,0:T(8,128)S(1)} fusion(f32[9,256,256]{1,2,0:T(8,128)} %get-tuple-element.35, bf16[9,256,64]{1,2,0:T(8,128)(2,1)} %collective-permute-done.9, bf16[9,256,64]{1,2,0:T(8,128)(2,1)} %collective-permute-done.8, bf16[9,256,64]{1,2,0:T(8,128)(2,1)} %collective-permute-done.7), kind=kLoop, calls=%fused_computation.16 | loop fusion | flops 884736 | bytes 2064384 | tf_op jit(solution)/shard_map/add | solution.py:61
  45.9 0.2 dynamic-slice_convert_fusion.2
  46.1 1.3 %collective-permute-start.10 = (bf16[9,64,64]{1,2,0:T(8,128)(2,1)S(1)}, bf16[9,64,64]{1,2,0:T(8,128)(2,1)S(1)}, u32[]{:S(2)}, u32[]{:S(2)}) collective-permute-start(bf16[9,64,64]{1,2,0:T(8,128)(2,1)S(1)} %get-tuple-element.22), channel_id=1, source_target_pairs={{0,4},{4,8},{8,12},{12,0},{1,5},{5,9},{9,13},{13,1},{2,6},{6,10},{... | collective-permute-start | bytes 221192 | tf_op jit(solution)/shard_map/ppermute | solution.py:48
  47.4 1.0 %collective-permute-start.11 = (bf16[9,64,64]{1,2,0:T(8,128)(2,1)S(1)}, bf16[9,64,64]{1,2,0:T(8,128)(2,1)S(1)}, u32[]{:S(2)}, u32[]{:S(2)}) collective-permute-start(bf16[9,64,64]{1,2,0:T(8,128)(2,1)S(1)} %get-tuple-element.24), channel_id=1, source_target_pairs={{0,8},{4,12},{8,0},{12,4},{1,9},{5,13},{9,1},{13,5},{2,10},{6,14},... | collective-permute-start | bytes 221192 | tf_op jit(solution)/shard_map/ppermute | solution.py:48
  48.4 0.3 collective-permute-start.12
  48.7 5.5 %shard_map.105 = bf16[1,2,64,2304]{3,2,1,0:T(8,128)(2,1)} custom-call(s32[1]{0:T(128)} %bitcast.first_ref, s32[16,12]{1,0:T(8,128)} %src_ref.5, s32[16,12]{1,0:T(8,128)} %start_ref.5, s32[16,12]{1,0:T(8,128)} %span_ref.5, s32[16,12]{1,0:T(8,128)} %basis_ref.5, f32[16,12]{1,0:T(8,128)} %rsqrt_multiply_fusion.scale_ref, ...), custom_call_target="tpu_custom_call" | custom-call | tf_op jit(solution)/shard_map/pallas_call | solution.py:171
  54.2 1.4 %convolution_bitcast_fusion.1 = f32[1,2,64,256]{3,2,1,0:T(8,128)S(1)} fusion(bf16[2304,256,1]{1,0,2:T(8,128)(2,1)S(1)} %bitcast.63, bf16[1,2,64,2304]{3,2,1,0:T(8,128)(2,1)} %shard_map.105), kind=kOutput, calls=%fused_computation.10 | convolution fusion | flops 150994944 | bytes 1900544 | tf_op jit(solution)/shard_map/bpwq,qc->bpwc/dot_general | solution.py:263
  55.6 0.7 %pad_maximum_fusion.1 = f32[1,4,64,256]{3,2,1,0:T(8,128)} fusion(f32[1,2,64,256]{3,2,1,0:T(8,128)S(1)} %convolution_bitcast_fusion.1, f32[1,2,64,256]{3,2,1,0:T(8,128)S(1)} %convolution_bitcast_fusion.2), kind=kLoop, calls=%fused_computation.27 | loop fusion | flops 65536 | bytes 524288 | tf_op jit(solution)/shard_map/concatenate | solution.py:271
  56.3 0.0 collective-permute-done.10
  56.3 4.2 %collective-permute-done.11 = bf16[9,64,64]{1,2,0:T(8,128)(2,1)S(1)} collective-permute-done((bf16[9,64,64]{1,2,0:T(8,128)(2,1)S(1)}, bf16[9,64,64]{1,2,0:T(8,128)(2,1)S(1)}, u32[]{:S(2)}, u32[]{:S(2)}) %collective-permute-start.11) | collective-permute-done | bytes 73760 | tf_op jit(solution)/shard_map/ppermute | solution.py:48
  60.5 1.8 %collective-permute-done.12 = bf16[9,64,64]{1,2,0:T(8,128)(2,1)S(1)} collective-permute-done((bf16[9,64,64]{1,2,0:T(8,128)(2,1)S(1)}, bf16[9,64,64]{1,2,0:T(8,128)(2,1)S(1)}, u32[]{:S(2)}, u32[]{:S(2)}) %collective-permute-start.12) | collective-permute-done | bytes 73760 | tf_op jit(solution)/shard_map/ppermute | solution.py:48
  62.3 0.1 add_multiply_fusion
  62.4 0.9 %copy.19 = f32[9,64,64]{2,1,0:T(8,128)} copy(f32[9,64,64]{1,2,0:T(8,128)S(1)} %add_multiply_fusion) | data formatting | bytes 294912
  (6 shorter events, 0.1 us)
Async XLA Ops:
  0.6 7.3 %copy-start.1 = (bf16[9,256,256]{2,1,0:T(8,128)(2,1)S(1)}, bf16[9,256,256]{2,1,0:T(8,128)(2,1)}, u32[]{:S(2)}) copy-start(bf16[9,256,256]{2,1,0:T(8,128)(2,1)} %param.10) | copy-start | bytes 3538948
  2.6 6.8 %collective-permute-start = (bf16[1,2,64,512]{3,2,1,0:T(8,128)(2,1)S(1)}, bf16[1,2,64,512]{3,2,1,0:T(8,128)(2,1)S(1)}, u32[]{:S(2)}, u32[]{:S(2)}) collective-permute-start(bf16[1,2,64,512]{3,2,1,0:T(8,128)(2,1)S(1)} %get-tuple-element.27), channel_id=1, source_target_pairs={{0,4},{4,8},{8,12},{1,5},{5,9},{9,13},{2,6},{6,10},{10,14},{3,7},{... | collective-permute-start | bytes 393224 | tf_op jit(solution)/shard_map/ppermute | solution.py:23
  5.8 5.7 %collective-permute-start.1 = (bf16[1,2,64,512]{3,2,1,0:T(8,128)(2,1)S(1)}, bf16[1,2,64,512]{3,2,1,0:T(8,128)(2,1)S(1)}, u32[]{:S(2)}, u32[]{:S(2)}) collective-permute-start(bf16[1,2,64,512]{3,2,1,0:T(8,128)(2,1)S(1)} %get-tuple-element.28), channel_id=1, source_target_pairs={{4,0},{8,4},{12,8},{5,1},{9,5},{13,9},{6,2},{10,6},{14,10},{7,3},{... | collective-permute-start | bytes 393224 | tf_op jit(solution)/shard_map/ppermute | solution.py:26
  8.0 0.8 %copy-start.3 = (s32[16,12]{1,0:T(8,128)S(1)}, s32[16,12]{1,0:T(8,128)}, u32[]{:S(2)}) copy-start(s32[16,12]{1,0:T(8,128)} %span_ref.5) | copy-start | bytes 2308
  8.0 0.8 %copy-start.4 = (f32[16,12]{1,0:T(8,128)S(1)}, f32[16,12]{1,0:T(8,128)}, u32[]{:S(2)}) copy-start(f32[16,12]{1,0:T(8,128)} %param.15) | copy-start | bytes 2308
  11.7 5.3 %collective-permute-start.4 = (f32[2,1,4,256]{3,0,2,1:T(2,128)S(1)}, f32[2,1,4,256]{3,0,2,1:T(2,128)S(1)}, u32[]{:S(2)}, u32[]{:S(2)}) collective-permute-start(f32[2,1,4,256]{3,0,2,1:T(2,128)S(1)} %pad_maximum_fusion.2), channel_id=1, source_target_pairs={{0,1},{1,2},{2,3},{3,0},{4,5},{5,6},{6,7},{7,4},{8,9},{9,10},{10,1... | collective-permute-start | bytes 24584 | tf_op jit(solution)/shard_map/ppermute | solution.py:36
  14.0 3.0 %collective-permute-start.5 = (f32[2,1,4,256]{3,0,2,1:T(2,128)S(1)}, f32[2,1,4,256]{3,0,2,1:T(2,128)S(1)}, u32[]{:S(2)}, u32[]{:S(2)}) collective-permute-start(f32[2,1,4,256]{3,0,2,1:T(2,128)S(1)} %pad_maximum_fusion.2), channel_id=1, source_target_pairs={{0,2},{1,3},{2,0},{3,1},{4,6},{5,7},{6,4},{7,5},{8,10},{9,11},{10,... | collective-permute-start | bytes 24584 | tf_op jit(solution)/shard_map/ppermute | solution.py:36
  15.2 3.4 %collective-permute-start.6 = (f32[2,1,4,256]{3,0,2,1:T(2,128)S(1)}, f32[2,1,4,256]{3,0,2,1:T(2,128)S(1)}, u32[]{:S(2)}, u32[]{:S(2)}) collective-permute-start(f32[2,1,4,256]{3,0,2,1:T(2,128)S(1)} %pad_maximum_fusion.2), channel_id=1, source_target_pairs={{0,3},{1,0},{2,1},{3,2},{4,7},{5,4},{6,5},{7,6},{8,11},{9,8},{10,9... | collective-permute-start | bytes 24584 | tf_op jit(solution)/shard_map/ppermute | solution.py:36
  15.2 4.3 %collective-permute-start.2 = (bf16[1,8,16,512]{3,2,1,0:T(8,128)(2,1)S(1)}, bf16[1,8,16,512]{3,2,1,0:T(8,128)(2,1)S(1)}, u32[]{:S(2)}, u32[]{:S(2)}) collective-permute-start(bf16[1,8,16,512]{3,2,1,0:T(8,128)(2,1)S(1)} %get-tuple-element.25), channel_id=1, source_target_pairs={{0,1},{1,2},{2,3},{3,0},{4,5},{5,6},{6,7},{7,4},{8,9},{9,10},{10,1... | collective-permute-start | bytes 393224 | tf_op jit(solution)/shard_map/ppermute | solution.py:23
  17.0 4.4 %collective-permute-start.3 = (bf16[1,8,16,512]{3,2,1,0:T(8,128)(2,1)S(1)}, bf16[1,8,16,512]{3,2,1,0:T(8,128)(2,1)S(1)}, u32[]{:S(2)}, u32[]{:S(2)}) collective-permute-start(bf16[1,8,16,512]{3,2,1,0:T(8,128)(2,1)S(1)} %get-tuple-element.26), channel_id=1, source_target_pairs={{1,0},{2,1},{3,2},{0,3},{5,4},{6,5},{7,6},{4,7},{9,8},{10,9},{11,1... | collective-permute-start | bytes 393224 | tf_op jit(solution)/shard_map/ppermute | solution.py:26
  22.5 3.9 %copy-start.2 = (bf16[1,4,64,256]{3,2,1,0:T(8,128)(2,1)S(1)}, bf16[1,4,64,256]{3,2,1,0:T(8,128)(2,1)}, u32[]{:S(2)}) copy-start(bf16[1,4,64,256]{3,2,1,0:T(8,128)(2,1)} %param.9) | copy-start | bytes 393220
  29.9 11.2 %collective-permute-start.7 = (bf16[9,256,64]{1,2,0:T(8,128)(2,1)S(1)}, bf16[9,256,64]{1,2,0:T(8,128)(2,1)}, u32[]{:S(2)}, u32[]{:S(2)}) collective-permute-start(bf16[9,256,64]{1,2,0:T(8,128)(2,1)S(1)} %get-tuple-element.19), channel_id=1, source_target_pairs={{0,1},{1,2},{2,3},{3,0},{4,5},{5,6},{6,7},{7,4},{8,9},{9,10},{10,1... | collective-permute-start | bytes 884744 | tf_op jit(solution)/shard_map/ppermute | solution.py:60
  30.5 12.3 %collective-permute-start.8 = (bf16[9,256,64]{1,2,0:T(8,128)(2,1)S(1)}, bf16[9,256,64]{1,2,0:T(8,128)(2,1)}, u32[]{:S(2)}, u32[]{:S(2)}) collective-permute-start(bf16[9,256,64]{1,2,0:T(8,128)(2,1)S(1)} %get-tuple-element.21), channel_id=1, source_target_pairs={{0,2},{1,3},{2,0},{3,1},{4,6},{5,7},{6,4},{7,5},{8,10},{9,11},{10,... | collective-permute-start | bytes 884744 | tf_op jit(solution)/shard_map/ppermute | solution.py:60
  30.8 13.6 %collective-permute-start.9 = (bf16[9,256,64]{1,2,0:T(8,128)(2,1)S(1)}, bf16[9,256,64]{1,2,0:T(8,128)(2,1)}, u32[]{:S(2)}, u32[]{:S(2)}) collective-permute-start(bf16[9,256,64]{1,2,0:T(8,128)(2,1)S(1)} %get-tuple-element.20), channel_id=1, source_target_pairs={{0,3},{1,0},{2,1},{3,2},{4,7},{5,4},{6,5},{7,6},{8,11},{9,8},{10,9... | collective-permute-start | bytes 884744 | tf_op jit(solution)/shard_map/ppermute | solution.py:60
  38.4 1.5 %copy-start = (bf16[1,4,64,2304]{3,2,1,0:T(8,128)(2,1)S(1)}, bf16[1,4,64,2304]{3,2,1,0:T(8,128)(2,1)}, u32[]{:S(2)}) copy-start(bf16[1,4,64,2304]{3,2,1,0:T(8,128)(2,1)} %shard_map.103) | copy-start | bytes 3538948
  46.1 10.2 %collective-permute-start.10 = (bf16[9,64,64]{1,2,0:T(8,128)(2,1)S(1)}, bf16[9,64,64]{1,2,0:T(8,128)(2,1)S(1)}, u32[]{:S(2)}, u32[]{:S(2)}) collective-permute-start(bf16[9,64,64]{1,2,0:T(8,128)(2,1)S(1)} %get-tuple-element.22), channel_id=1, source_target_pairs={{0,4},{4,8},{8,12},{12,0},{1,5},{5,9},{9,13},{13,1},{2,6},{6,10},{... | collective-permute-start | bytes 221192 | tf_op jit(solution)/shard_map/ppermute | solution.py:48
  47.4 13.1 %collective-permute-start.11 = (bf16[9,64,64]{1,2,0:T(8,128)(2,1)S(1)}, bf16[9,64,64]{1,2,0:T(8,128)(2,1)S(1)}, u32[]{:S(2)}, u32[]{:S(2)}) collective-permute-start(bf16[9,64,64]{1,2,0:T(8,128)(2,1)S(1)} %get-tuple-element.24), channel_id=1, source_target_pairs={{0,8},{4,12},{8,0},{12,4},{1,9},{5,13},{9,1},{13,5},{2,10},{6,14},... | collective-permute-start | bytes 221192 | tf_op jit(solution)/shard_map/ppermute | solution.py:48
  48.4 13.9 %collective-permute-start.12 = (bf16[9,64,64]{1,2,0:T(8,128)(2,1)S(1)}, bf16[9,64,64]{1,2,0:T(8,128)(2,1)S(1)}, u32[]{:S(2)}, u32[]{:S(2)}) collective-permute-start(bf16[9,64,64]{1,2,0:T(8,128)(2,1)S(1)} %get-tuple-element.23), channel_id=1, source_target_pairs={{0,12},{4,0},{8,4},{12,8},{1,13},{5,1},{9,5},{13,9},{2,14},{6,2},{... | collective-permute-start | bytes 221192 | tf_op jit(solution)/shard_map/ppermute | solution.py:48

commit v22 on v21

--- a/solution.py
+++ b/solution.py
@@ -63,7 +63,7 @@
 
 
 def filter_kernel(
-    first_ref, src_ref, start_ref, span_ref, basis_ref, scale_ref, field_ref, total_ref,
+    twist_ref, first_ref, src_ref, start_ref, span_ref, basis_ref, scale_ref, field_ref, total_ref,
     out_ref, acc_ref, *, slots, height, lon_count, lon_total, backward,
 ):
     r = pl.program_id(1)
@@ -106,8 +106,11 @@
             row = src_ref[table_row, slot] - first_row + REACH
             add_slot(row, table_row, slot, scale_ref[table_row, slot])
 
+    twist = (channels - twist_ref[0]) % channels
     for k in range(BASIS):
-        out_ref[0, 0, :, k * channels:(k + 1) * channels] = acc_ref[k].astype(jnp.bfloat16)
+        out_ref[0, 0, :, k * channels:(k + 1) * channels] = pltpu.roll(
+            acc_ref[k], twist, 1
+        ).astype(jnp.bfloat16)
 
 
 def scatter_kernel(
@@ -187,7 +190,7 @@
 
 
 def run_filter(
-    first, tables, field, totals, row_count, lon_count, lon_total, backward, part=0
+    twist, first, tables, field, totals, row_count, lon_count, lon_total, backward, part=0
 ):
     members, window, padded, combined = field.shape
     channels = totals.shape[-1]
@@ -204,7 +207,7 @@
     return pl.pallas_call(
         kernel,
         grid=(members, row_count),
-        in_specs=[smem] * 6
+        in_specs=[smem] * 7
         + [
             pl.BlockSpec((1, window, padded, channels), lambda b, r: (b, 0, 0, part)),
             pl.BlockSpec((1, window, 1, channels), lambda b, r: (b, 0, 0, 0)),
@@ -216,7 +219,7 @@
             (members, row_count, lon_count, BASIS * channels), jnp.bfloat16
         ),
         scratch_shapes=[pltpu.VMEM((BASIS, lon_count, channels), jnp.float32)],
-    )(first, *tables, field, totals[:, :, None, :])
+    )(twist, first, *tables, field, totals[:, :, None, :])
 
 
 def on_device(inputs, cotangent, weight, src_rows, lon_start, lon_span, basis_idx, quad_weight):
@@ -243,8 +246,13 @@
         framed = with_halo(local_totals, (("lat", 2),), REACH, False)
     totals, grad_totals = framed[0], framed[1]
 
-    flattened = run_filter(first, tables, both, totals, row_count, lon_count, lon_total, False, 0)
-    w_fwd = weight.reshape(BASIS * channels, channels)
+    c_block = channels // lax.axis_size("lat")
+    offset = lax.axis_index("lat") * c_block
+    twist = jnp.reshape(offset, (1,)).astype(jnp.int32)
+    flattened = run_filter(
+        twist, first, tables, both, totals, row_count, lon_count, lon_total, False, 0
+    )
+    w_fwd = jnp.roll(weight, -offset, axis=1).reshape(BASIS * channels, channels)
     response = jnp.einsum("brwq,qo->brwo", flattened, w_fwd, preferred_element_type=jnp.float32)
 
     o_block = channels // lax.axis_size("lon")
@@ -267,7 +275,7 @@
     early_rows = row_count // 2
     early_input = backward_rows(both, grad_totals, 0, early_rows)
     both, grad_totals, reduced = lax.optimization_barrier((both, grad_totals, reduced))
-    reduced = ring_scatter(reduced, "lat", 1)
+    reduced = rolled_scatter(reduced, "lat", 1)
     grad_input = jnp.concatenate(
         [
             early_input,

time: 63.7 us -> 67.3 us (1.057)
  the two profiles are of different devices: /device:TPU:15 before, /device:TPU:13 now
where the time goes in v22:
time: 67.3 us; the launch traced here: 66.8 us
  Pallas kernels  15.8 us (23%)
  starting transfers between devices  15.6 us (23%)
  waiting for transfers between devices  14.7 us (22%)
  matrix products  7.42 us (11%)
  local copies, waits for them, and re-layouts  6.7 us (10%)
  other arithmetic  5.7 us (8%)
  between operations  0.88 us (1%)
    pallas_call x2, Pallas kernels, run_scatter(): pl.pallas_call(kernel, grid=(members,), in_specs=[smem] * 6 + [pl.BlockSp...  11.5 us
    ppermute x6, waiting for transfers between devices, rolled_scatter(): sent = lax.ppermute(piece.astype(jnp.bfloat16), axis, pairs)  10.1 us
    ppermute x2, starting transfers between devices, with_halo(): lax.ppermute(lax.slice_in_dim(block, block.shape[dim] - width, None, axis...  4.77 us
    ppermute x6, starting transfers between devices, rolled_scatter(): sent = lax.ppermute(piece.astype(jnp.bfloat16), axis, pairs)  4.4 us
    pallas_call x1, Pallas kernels, run_filter(): pl.pallas_call(kernel, grid=(members, row_count), in_specs=[smem] * 7 + [...  4.3 us
    unnamed x17, local copies, waits for them, and re-layouts  4.21 us
    ppermute x3, starting transfers between devices, ring_sum(): total = total + lax.ppermute(value, axis, pairs)  3.69 us
    dot_general x1, matrix products, on_device(): jnp.einsum('brwq,brwo->qo', flattened, rolled, preferred_element_type=jnp...  3.37 us
  transfers between devices with their start and end apart: 13, of which 10 were waited for; matrix products, arithmetic and copies ran while one was open for 12% of the time, Pallas kernels for 17%

profile of v22, /device:TPU:13, one launch (start us, length us, event | category | flops | bytes accessed | tf_op | source)
XLA Modules:
  0.0 66.8 jit_solution(6820174829551447171)
XLA Ops:
  0.6 0.9 %constant_dynamic-update-slice_fusion.1 = bf16[1,4,64,512]{3,2,1,0:T(8,128)(2,1)S(1)} fusion(bf16[1,4,64,256]{3,2,1,0:T(8,128)(2,1)} %param.8), kind=kLoop, calls=%fused_computation.37 | loop fusion | bytes 262144
  1.5 0.9 %constant_dynamic-update-slice_fusion = bf16[1,4,64,512]{3,2,1,0:T(8,128)(2,1)S(1)} fusion(bf16[1,4,64,512]{3,2,1,0:T(8,128)(2,1)S(1)} %constant_dynamic-update-slice_fusion.1, bf16[1,4,64,256]{3,2,1,0:T(8,128)(2,1)} %param.9), kind=kLoop, calls=%fused_computation.36 | loop fusion | bytes 262144 | tf_op jit(solution)/shard_map/concatenate | solution.py:235
  2.5 0.0 copy-start.2
  2.5 0.7 %copy-done.2 = bf16[1,4,64,512]{3,2,1,0:T(8,128)(2,1)} copy-done((bf16[1,4,64,512]{3,2,1,0:T(8,128)(2,1)}, bf16[1,4,64,512]{3,2,1,0:T(8,128)(2,1)S(1)}, u32[]{:S(2)}) %copy-start.2) | copy-done | bytes 262168
  3.2 0.7 %fusion.28 = (bf16[1,2,64,512]{3,2,1,0:T(8,128)(2,1)}, bf16[1,2,64,512]{3,2,1,0:T(8,128)(2,1)}) fusion(bf16[1,4,64,512]{3,2,1,0:T(8,128)(2,1)S(1)} %constant_dynamic-update-slice_fusion), kind=kLoop, calls=%fused_computation.47 | loop fusion | bytes 524288 | tf_op jit(solution)/shard_map/slice | solution.py:24
  3.9 3.2 %collective-permute-start = (bf16[1,2,64,512]{3,2,1,0:T(8,128)(2,1)}, bf16[1,2,64,512]{3,2,1,0:T(8,128)(2,1)}, u32[]{:S(2)}, u32[]{:S(2)}) collective-permute-start(bf16[1,2,64,512]{3,2,1,0:T(8,128)(2,1)} %get-tuple-element.27), channel_id=1, source_target_pairs={{0,4},{4,8},{8,12},{1,5},{5,9},{9,13},{2,6},{6,10},{10,14},{3,7},{... | collective-permute-start | bytes 393224 | tf_op jit(solution)/shard_map/ppermute | solution.py:23
  7.1 2.7 %collective-permute-start.1 = (bf16[1,2,64,512]{3,2,1,0:T(8,128)(2,1)}, bf16[1,2,64,512]{3,2,1,0:T(8,128)(2,1)}, u32[]{:S(2)}, u32[]{:S(2)}) collective-permute-start(bf16[1,2,64,512]{3,2,1,0:T(8,128)(2,1)} %get-tuple-element.28), channel_id=1, source_target_pairs={{4,0},{8,4},{12,8},{5,1},{9,5},{13,9},{6,2},{10,6},{14,10},{7,3},{... | collective-permute-start | bytes 393224 | tf_op jit(solution)/shard_map/ppermute | solution.py:26
  9.9 0.0 copy-start.5
  9.9 0.0 copy-start.6
  9.9 0.0 copy-start.1
  9.9 1.7 %copy.17 = bf16[9,256,256]{1,2,0:T(8,128)(2,1)S(1)} copy(bf16[9,256,256]{2,1,0:T(8,128)(2,1)} %param.10) | data formatting | bytes 2359296 | tf_op args[2]
  11.6 0.0 copy-done.5
  11.6 0.0 copy-done.6
  11.6 0.6 rsqrt_multiply_fusion.scale_ref
  12.2 0.0 copy-done.1
  12.2 0.0 copy-start.3
  12.2 0.6 fusion.3
  12.8 0.0 collective-permute-done
  12.9 0.3 collective-permute-done.1
  13.1 0.0 copy-done.3
  13.2 1.0 %pad_maximum_fusion = bf16[1,8,64,512]{3,2,1,0:T(8,128)(2,1)S(1)} fusion(bf16[1,2,64,512]{3,2,1,0:T(8,128)(2,1)} %collective-permute-done.1, bf16[1,4,64,512]{3,2,1,0:T(8,128)(2,1)S(1)} %copy-done.3, bf16[1,2,64,512]{3,2,1,0:T(8,128)(2,1)} %collective-permute-done), kind=kLoop, calls=%fused_computation.22 | loop fusion | flops 524288 | bytes 1048576 | tf_op jit(solution)/shard_map/concatenate | solution.py:27
  14.2 0.1 convert_reduce_fusion
  14.3 3.2 %collective-permute-start.4 = (f32[2,1,4,256]{3,0,2,1:T(2,128)S(1)}, f32[2,1,4,256]{3,0,2,1:T(2,128)S(1)}, u32[]{:S(2)}, u32[]{:S(2)}) collective-permute-start(f32[2,1,4,256]{3,0,2,1:T(2,128)S(1)} %pad_maximum_fusion.2), channel_id=1, source_target_pairs={{0,1},{1,2},{2,3},{3,0},{4,5},{5,6},{6,7},{7,4},{8,9},{9,10},{10,1... | collective-permute-start | bytes 24584 | tf_op jit(solution)/shard_map/ppermute | solution.py:36
  17.5 0.3 collective-permute-start.5
  17.8 0.2 collective-permute-start.6
  18.0 1.6 %collective-permute-start.2 = (bf16[1,8,16,512]{3,2,1,0:T(8,128)(2,1)S(1)}, bf16[1,8,16,512]{3,2,1,0:T(8,128)(2,1)S(1)}, u32[]{:S(2)}, u32[]{:S(2)}) collective-permute-start(bf16[1,8,16,512]{3,2,1,0:T(8,128)(2,1)S(1)} %get-tuple-element.22), channel_id=1, source_target_pairs={{0,1},{1,2},{2,3},{3,0},{4,5},{5,6},{6,7},{7,4},{8,9},{9,10},{10,1... | collective-permute-start | bytes 393224 | tf_op jit(solution)/shard_map/ppermute | solution.py:23
  19.6 0.0 collective-permute-start.3
  19.6 0.0 collective-permute-done.4
  19.6 0.4 collective-permute-done.5
  20.0 0.8 %collective-permute-done.6 = f32[2,1,4,256]{3,0,2,1:T(2,128)S(1)} collective-permute-done((f32[2,1,4,256]{3,0,2,1:T(2,128)S(1)}, f32[2,1,4,256]{3,0,2,1:T(2,128)S(1)}, u32[]{:S(2)}, u32[]{:S(2)}) %collective-permute-start.6) | collective-permute-done | bytes 8224 | tf_op jit(solution)/shard_map/ppermute | solution.py:36
  20.9 0.6 fusion.23
  21.5 0.1 collective-permute-done.2
  21.6 3.0 %collective-permute-done.3 = bf16[1,8,16,512]{3,2,1,0:T(8,128)(2,1)S(1)} collective-permute-done((bf16[1,8,16,512]{3,2,1,0:T(8,128)(2,1)S(1)}, bf16[1,8,16,512]{3,2,1,0:T(8,128)(2,1)S(1)}, u32[]{:S(2)}, u32[]{:S(2)}) %collective-permute-start.3) | collective-permute-done | bytes 131104 | tf_op jit(solution)/shard_map/ppermute | solution.py:26
  24.6 1.1 %fusion.12.field_ref = bf16[1,8,128,512]{3,2,1,0:T(8,128)(2,1)} fusion(bf16[1,8,16,512]{3,2,1,0:T(8,128)(2,1)S(1)} %collective-permute-done.3, bf16[1,8,64,512]{3,2,1,0:T(8,128)(2,1)S(1)} %pad_maximum_fusion, bf16[1,8,16,512]{3,2,1,0:T(8,128)(2,1)S(1)} %collective-permute-done.2), kind=kLoop, calls=%fused_computation.16 | loop fusion | flops 5242880 | bytes 1835008 | tf_op jit(solution)/shard_map/concatenate | solution.py:27
  25.6 0.0 copy-start.4
  25.6 4.3 %shard_map.103 = bf16[1,4,64,2304]{3,2,1,0:T(8,128)(2,1)} custom-call(s32[1]{0:T(128)} %bitcast.twist_ref, s32[1]{0:T(128)} %bitcast.1.first_ref, s32[16,12]{1,0:T(8,128)} %src_ref.5, s32[16,12]{1,0:T(8,128)} %start_ref.5, s32[16,12]{1,0:T(8,128)} %span_ref.5, s32[16,12]{1,0:T(8,128)} %basis_ref.5, f32[16,12]{1,0:T(8,128)} %rsqrt_multiply_fusion.scale_ref, ...), custom_call_target="tpu_custom_call" | custom-call | tf_op jit(solution)/shard_map/pallas_call | solution.py:207
  29.9 0.0 copy-done.4
  29.9 3.4 %fusion.29 = (bf16[9,256,256]{1,2,0:T(8,128)(2,1)S(1)}, f32[9,256,256]{1,2,0:T(8,128)}) fusion(s32[]{:T(128)S(6)} %select_n.26, bf16[1,4,64,256]{3,2,1,0:T(8,128)(2,1)S(1)} %copy-done.4, bf16[4,8,9,8,256]{4,3,2,1,0:T(8,128)(2,1)} %bitcast.62), kind=kOutput, calls=%fused_computation.48 | convolution fusion | flops 302841856 | bytes 4849668 | tf_op jit(solution)/shard_map/brwq,brwo->qo/dot_general | solution.py:260
  33.3 0.1 fusion.25
  33.4 0.1 collective-permute-start.7
  33.4 1.2 %collective-permute-start.8 = (bf16[9,256,64]{1,2,0:T(8,128)(2,1)S(1)}, bf16[9,256,64]{1,2,0:T(8,128)(2,1)}, u32[]{:S(2)}, u32[]{:S(2)}) collective-permute-start(bf16[9,256,64]{1,2,0:T(8,128)(2,1)S(1)} %get-tuple-element.21), channel_id=1, source_target_pairs={{0,2},{1,3},{2,0},{3,1},{4,6},{5,7},{6,4},{7,5},{8,10},{9,11},{10,... | collective-permute-start | bytes 884744 | tf_op jit(solution)/shard_map/ppermute | solution.py:60
  34.7 0.2 collective-permute-start.9
  34.8 5.4 %shard_map.104 = bf16[1,2,64,2304]{3,2,1,0:T(8,128)(2,1)} custom-call(s32[1]{0:T(128)} %bitcast.1.first_ref, s32[16,12]{1,0:T(8,128)} %src_ref.5, s32[16,12]{1,0:T(8,128)} %start_ref.5, s32[16,12]{1,0:T(8,128)} %span_ref.5, s32[16,12]{1,0:T(8,128)} %basis_ref.5, f32[16,12]{1,0:T(8,128)} %rsqrt_multiply_fusion.scale_ref, ...), custom_call_target="tpu_custom_call" | custom-call | tf_op jit(solution)/shard_map/pallas_call | solution.py:174
  40.2 0.0 copy-start
  40.2 1.5 %convolution_bitcast_fusion.2 = f32[1,2,64,256]{3,2,1,0:T(8,128)S(1)} fusion(bf16[2304,256,1]{1,0,2:T(8,128)(2,1)S(1)} %bitcast.63, bf16[1,2,64,2304]{3,2,1,0:T(8,128)(2,1)} %shard_map.104), kind=kOutput, calls=%fused_computation.14 | convolution fusion | flops 150994944 | bytes 1900544 | tf_op jit(solution)/shard_map/bpwq,qc->bpwc/dot_general | solution.py:271
  41.7 0.0 copy-done
  41.7 1.2 %fusion.8 = f32[1,4,64,256]{3,2,1,0:T(8,128)} fusion(bf16[2304,256,1]{1,0,2:T(8,128)(2,1)S(1)} %bitcast.65, bf16[1,4,64,2304]{3,2,1,0:T(8,128)(2,1)S(1)} %copy-done), kind=kOutput, calls=%fused_computation.12 | convolution fusion | flops 301989888 | bytes 2621440 | tf_op jit(solution)/shard_map/brwq,qo->brwo/dot_general | solution.py:256
  42.9 0.0 collective-permute-done.7
  42.9 4.2 %collective-permute-done.8 = bf16[9,256,64]{1,2,0:T(8,128)(2,1)} collective-permute-done((bf16[9,256,64]{1,2,0:T(8,128)(2,1)S(1)}, bf16[9,256,64]{1,2,0:T(8,128)(2,1)}, u32[]{:S(2)}, u32[]{:S(2)}) %collective-permute-start.8) | collective-permute-done | bytes 294944 | tf_op jit(solution)/shard_map/ppermute | solution.py:60
  47.1 1.2 %collective-permute-done.9 = bf16[9,256,64]{1,2,0:T(8,128)(2,1)} collective-permute-done((bf16[9,256,64]{1,2,0:T(8,128)(2,1)S(1)}, bf16[9,256,64]{1,2,0:T(8,128)(2,1)}, u32[]{:S(2)}, u32[]{:S(2)}) %collective-permute-start.9) | collective-permute-done | bytes 294944 | tf_op jit(solution)/shard_map/ppermute | solution.py:60
  48.3 1.4 %fusion.14 = f32[9,256,64]{1,2,0:T(8,128)S(1)} fusion(f32[9,256,256]{1,2,0:T(8,128)} %get-tuple-element.35, bf16[9,256,64]{1,2,0:T(8,128)(2,1)} %collective-permute-done.9, bf16[9,256,64]{1,2,0:T(8,128)(2,1)} %collective-permute-done.8, bf16[9,256,64]{1,2,0:T(8,128)(2,1)} %collective-permute-done.7), kind=kLoop, calls=%fused_computation.19 | loop fusion | flops 884736 | bytes 2064384 | tf_op jit(solution)/shard_map/add | solution.py:61
  49.8 0.1 fusion.27
  50.0 1.3 %collective-permute-start.10 = (bf16[9,64,64]{1,2,0:T(8,128)(2,1)S(1)}, bf16[9,64,64]{1,2,0:T(8,128)(2,1)S(1)}, u32[]{:S(2)}, u32[]{:S(2)}) collective-permute-start(bf16[9,64,64]{1,2,0:T(8,128)(2,1)S(1)} %get-tuple-element.24), channel_id=1, source_target_pairs={{0,4},{4,8},{8,12},{12,0},{1,5},{5,9},{9,13},{13,1},{2,6},{6,10},{... | collective-permute-start | bytes 221192 | tf_op jit(solution)/shard_map/ppermute | solution.py:60
  51.3 1.6 %collective-permute-start.11 = (bf16[9,64,64]{1,2,0:T(8,128)(2,1)S(1)}, bf16[9,64,64]{1,2,0:T(8,128)(2,1)S(1)}, u32[]{:S(2)}, u32[]{:S(2)}) collective-permute-start(bf16[9,64,64]{1,2,0:T(8,128)(2,1)S(1)} %get-tuple-element.26), channel_id=1, source_target_pairs={{0,8},{4,12},{8,0},{12,4},{1,9},{5,13},{9,1},{13,5},{2,10},{6,14},... | collective-permute-start | bytes 221192 | tf_op jit(solution)/shard_map/ppermute | solution.py:60
  52.9 0.0 collective-permute-start.12
  52.9 6.1 %shard_map.105 = bf16[1,2,64,2304]{3,2,1,0:T(8,128)(2,1)} custom-call(s32[1]{0:T(128)} %bitcast.1.first_ref, s32[16,12]{1,0:T(8,128)} %src_ref.5, s32[16,12]{1,0:T(8,128)} %start_ref.5, s32[16,12]{1,0:T(8,128)} %span_ref.5, s32[16,12]{1,0:T(8,128)} %basis_ref.5, f32[16,12]{1,0:T(8,128)} %rsqrt_multiply_fusion.scale_ref, ...), custom_call_target="tpu_custom_call" | custom-call | tf_op jit(solution)/shard_map/pallas_call | solution.py:174
  59.0 1.4 %convolution_bitcast_fusion.1 = f32[1,2,64,256]{3,2,1,0:T(8,128)S(1)} fusion(bf16[2304,256,1]{1,0,2:T(8,128)(2,1)S(1)} %bitcast.64, bf16[1,2,64,2304]{3,2,1,0:T(8,128)(2,1)} %shard_map.105), kind=kOutput, calls=%fused_computation.13 | convolution fusion | flops 150994944 | bytes 1900544 | tf_op jit(solution)/shard_map/bpwq,qc->bpwc/dot_general | solution.py:271
  60.4 0.7 %pad_maximum_fusion.1 = f32[1,4,64,256]{3,2,1,0:T(8,128)} fusion(f32[1,2,64,256]{3,2,1,0:T(8,128)S(1)} %convolution_bitcast_fusion.1, f32[1,2,64,256]{3,2,1,0:T(8,128)S(1)} %convolution_bitcast_fusion.2), kind=kLoop, calls=%fused_computation.27 | loop fusion | flops 65536 | bytes 524288 | tf_op jit(solution)/shard_map/concatenate | solution.py:279
  61.1 0.2 collective-permute-done.10
  61.3 2.2 %collective-permute-done.11 = bf16[9,64,64]{1,2,0:T(8,128)(2,1)S(1)} collective-permute-done((bf16[9,64,64]{1,2,0:T(8,128)(2,1)S(1)}, bf16[9,64,64]{1,2,0:T(8,128)(2,1)S(1)}, u32[]{:S(2)}, u32[]{:S(2)}) %collective-permute-start.11) | collective-permute-done | bytes 73760 | tf_op jit(solution)/shard_map/ppermute | solution.py:60
  63.6 2.3 %collective-permute-done.12 = bf16[9,64,64]{1,2,0:T(8,128)(2,1)S(1)} collective-permute-done((bf16[9,64,64]{1,2,0:T(8,128)(2,1)S(1)}, bf16[9,64,64]{1,2,0:T(8,128)(2,1)S(1)}, u32[]{:S(2)}, u32[]{:S(2)}) %collective-permute-start.12) | collective-permute-done | bytes 73760 | tf_op jit(solution)/shard_map/ppermute | solution.py:60
  65.8 0.1 add_multiply_fusion
  65.9 0.9 %copy.19 = f32[9,64,64]{2,1,0:T(8,128)} copy(f32[9,64,64]{1,2,0:T(8,128)S(1)} %add_multiply_fusion) | data formatting | bytes 294912
  (6 shorter events, 0.1 us)
Async XLA Ops:
  2.5 0.7 %copy-start.2 = (bf16[1,4,64,512]{3,2,1,0:T(8,128)(2,1)}, bf16[1,4,64,512]{3,2,1,0:T(8,128)(2,1)S(1)}, u32[]{:S(2)}) copy-start(bf16[1,4,64,512]{3,2,1,0:T(8,128)(2,1)S(1)} %constant_dynamic-update-slice_fusion) | copy-start | bytes 786436
  3.9 9.0 %collective-permute-start = (bf16[1,2,64,512]{3,2,1,0:T(8,128)(2,1)}, bf16[1,2,64,512]{3,2,1,0:T(8,128)(2,1)}, u32[]{:S(2)}, u32[]{:S(2)}) collective-permute-start(bf16[1,2,64,512]{3,2,1,0:T(8,128)(2,1)} %get-tuple-element.27), channel_id=1, source_target_pairs={{0,4},{4,8},{8,12},{1,5},{5,9},{9,13},{2,6},{6,10},{10,14},{3,7},{... | collective-permute-start | bytes 393224 | tf_op jit(solution)/shard_map/ppermute | solution.py:23
  7.1 6.0 %collective-permute-start.1 = (bf16[1,2,64,512]{3,2,1,0:T(8,128)(2,1)}, bf16[1,2,64,512]{3,2,1,0:T(8,128)(2,1)}, u32[]{:S(2)}, u32[]{:S(2)}) collective-permute-start(bf16[1,2,64,512]{3,2,1,0:T(8,128)(2,1)} %get-tuple-element.28), channel_id=1, source_target_pairs={{4,0},{8,4},{12,8},{5,1},{9,5},{13,9},{6,2},{10,6},{14,10},{7,3},{... | collective-permute-start | bytes 393224 | tf_op jit(solution)/shard_map/ppermute | solution.py:26
  9.9 1.7 %copy-start.5 = (s32[16,12]{1,0:T(8,128)S(1)}, s32[16,12]{1,0:T(8,128)}, u32[]{:S(2)}) copy-start(s32[16,12]{1,0:T(8,128)} %span_ref.5) | copy-start | bytes 2308
  9.9 1.7 %copy-start.6 = (f32[16,12]{1,0:T(8,128)S(1)}, f32[16,12]{1,0:T(8,128)}, u32[]{:S(2)}) copy-start(f32[16,12]{1,0:T(8,128)} %param.15) | copy-start | bytes 2308
  9.9 2.3 %copy-start.1 = (bf16[9,256,256]{2,1,0:T(8,128)(2,1)S(1)}, bf16[9,256,256]{2,1,0:T(8,128)(2,1)}, u32[]{:S(2)}) copy-start(bf16[9,256,256]{2,1,0:T(8,128)(2,1)} %param.10) | copy-start | bytes 3538948
  12.2 1.0 %copy-start.3 = (bf16[1,4,64,512]{3,2,1,0:T(8,128)(2,1)S(1)}, bf16[1,4,64,512]{3,2,1,0:T(8,128)(2,1)}, u32[]{:S(2)}) copy-start(bf16[1,4,64,512]{3,2,1,0:T(8,128)(2,1)} %copy-done.2) | copy-start | bytes 786436
  14.3 5.3 %collective-permute-start.4 = (f32[2,1,4,256]{3,0,2,1:T(2,128)S(1)}, f32[2,1,4,256]{3,0,2,1:T(2,128)S(1)}, u32[]{:S(2)}, u32[]{:S(2)}) collective-permute-start(f32[2,1,4,256]{3,0,2,1:T(2,128)S(1)} %pad_maximum_fusion.2), channel_id=1, source_target_pairs={{0,1},{1,2},{2,3},{3,0},{4,5},{5,6},{6,7},{7,4},{8,9},{9,10},{10,1... | collective-permute-start | bytes 24584 | tf_op jit(solution)/shard_map/ppermute | solution.py:36
  17.5 2.5 %collective-permute-start.5 = (f32[2,1,4,256]{3,0,2,1:T(2,128)S(1)}, f32[2,1,4,256]{3,0,2,1:T(2,128)S(1)}, u32[]{:S(2)}, u32[]{:S(2)}) collective-permute-start(f32[2,1,4,256]{3,0,2,1:T(2,128)S(1)} %pad_maximum_fusion.2), channel_id=1, source_target_pairs={{0,2},{1,3},{2,0},{3,1},{4,6},{5,7},{6,4},{7,5},{8,10},{9,11},{10,... | collective-permute-start | bytes 24584 | tf_op jit(solution)/shard_map/ppermute | solution.py:36
  17.8 3.1 %collective-permute-start.6 = (f32[2,1,4,256]{3,0,2,1:T(2,128)S(1)}, f32[2,1,4,256]{3,0,2,1:T(2,128)S(1)}, u32[]{:S(2)}, u32[]{:S(2)}) collective-permute-start(f32[2,1,4,256]{3,0,2,1:T(2,128)S(1)} %pad_maximum_fusion.2), channel_id=1, source_target_pairs={{0,3},{1,0},{2,1},{3,2},{4,7},{5,4},{6,5},{7,6},{8,11},{9,8},{10,9... | collective-permute-start | bytes 24584 | tf_op jit(solution)/shard_map/ppermute | solution.py:36
  18.0 3.5 %collective-permute-start.2 = (bf16[1,8,16,512]{3,2,1,0:T(8,128)(2,1)S(1)}, bf16[1,8,16,512]{3,2,1,0:T(8,128)(2,1)S(1)}, u32[]{:S(2)}, u32[]{:S(2)}) collective-permute-start(bf16[1,8,16,512]{3,2,1,0:T(8,128)(2,1)S(1)} %get-tuple-element.22), channel_id=1, source_target_pairs={{0,1},{1,2},{2,3},{3,0},{4,5},{5,6},{6,7},{7,4},{8,9},{9,10},{10,1... | collective-permute-start | bytes 393224 | tf_op jit(solution)/shard_map/ppermute | solution.py:23
  19.6 5.0 %collective-permute-start.3 = (bf16[1,8,16,512]{3,2,1,0:T(8,128)(2,1)S(1)}, bf16[1,8,16,512]{3,2,1,0:T(8,128)(2,1)S(1)}, u32[]{:S(2)}, u32[]{:S(2)}) collective-permute-start(bf16[1,8,16,512]{3,2,1,0:T(8,128)(2,1)S(1)} %get-tuple-element.23), channel_id=1, source_target_pairs={{1,0},{2,1},{3,2},{0,3},{5,4},{6,5},{7,6},{4,7},{9,8},{10,9},{11,1... | collective-permute-start | bytes 393224 | tf_op jit(solution)/shard_map/ppermute | solution.py:26
  25.6 4.3 %copy-start.4 = (bf16[1,4,64,256]{3,2,1,0:T(8,128)(2,1)S(1)}, bf16[1,4,64,256]{3,2,1,0:T(8,128)(2,1)}, u32[]{:S(2)}) copy-start(bf16[1,4,64,256]{3,2,1,0:T(8,128)(2,1)} %param.9) | copy-start | bytes 393220
  33.4 9.5 %collective-permute-start.7 = (bf16[9,256,64]{1,2,0:T(8,128)(2,1)S(1)}, bf16[9,256,64]{1,2,0:T(8,128)(2,1)}, u32[]{:S(2)}, u32[]{:S(2)}) collective-permute-start(bf16[9,256,64]{1,2,0:T(8,128)(2,1)S(1)} %get-tuple-element.19), channel_id=1, source_target_pairs={{0,1},{1,2},{2,3},{3,0},{4,5},{5,6},{6,7},{7,4},{8,9},{9,10},{10,1... | collective-permute-start | bytes 884744 | tf_op jit(solution)/shard_map/ppermute | solution.py:60
  33.4 13.7 %collective-permute-start.8 = (bf16[9,256,64]{1,2,0:T(8,128)(2,1)S(1)}, bf16[9,256,64]{1,2,0:T(8,128)(2,1)}, u32[]{:S(2)}, u32[]{:S(2)}) collective-permute-start(bf16[9,256,64]{1,2,0:T(8,128)(2,1)S(1)} %get-tuple-element.21), channel_id=1, source_target_pairs={{0,2},{1,3},{2,0},{3,1},{4,6},{5,7},{6,4},{7,5},{8,10},{9,11},{10,... | collective-permute-start | bytes 884744 | tf_op jit(solution)/shard_map/ppermute | solution.py:60
  34.7 13.7 %collective-permute-start.9 = (bf16[9,256,64]{1,2,0:T(8,128)(2,1)S(1)}, bf16[9,256,64]{1,2,0:T(8,128)(2,1)}, u32[]{:S(2)}, u32[]{:S(2)}) collective-permute-start(bf16[9,256,64]{1,2,0:T(8,128)(2,1)S(1)} %get-tuple-element.20), channel_id=1, source_target_pairs={{0,3},{1,0},{2,1},{3,2},{4,7},{5,4},{6,5},{7,6},{8,11},{9,8},{10,9... | collective-permute-start | bytes 884744 | tf_op jit(solution)/shard_map/ppermute | solution.py:60
  40.2 1.5 %copy-start = (bf16[1,4,64,2304]{3,2,1,0:T(8,128)(2,1)S(1)}, bf16[1,4,64,2304]{3,2,1,0:T(8,128)(2,1)}, u32[]{:S(2)}) copy-start(bf16[1,4,64,2304]{3,2,1,0:T(8,128)(2,1)} %shard_map.103) | copy-start | bytes 3538948
  50.0 11.3 %collective-permute-start.10 = (bf16[9,64,64]{1,2,0:T(8,128)(2,1)S(1)}, bf16[9,64,64]{1,2,0:T(8,128)(2,1)S(1)}, u32[]{:S(2)}, u32[]{:S(2)}) collective-permute-start(bf16[9,64,64]{1,2,0:T(8,128)(2,1)S(1)} %get-tuple-element.24), channel_id=1, source_target_pairs={{0,4},{4,8},{8,12},{12,0},{1,5},{5,9},{9,13},{13,1},{2,6},{6,10},{... | collective-permute-start | bytes 221192 | tf_op jit(solution)/shard_map/ppermute | solution.py:60
  51.3 12.2 %collective-permute-start.11 = (bf16[9,64,64]{1,2,0:T(8,128)(2,1)S(1)}, bf16[9,64,64]{1,2,0:T(8,128)(2,1)S(1)}, u32[]{:S(2)}, u32[]{:S(2)}) collective-permute-start(bf16[9,64,64]{1,2,0:T(8,128)(2,1)S(1)} %get-tuple-element.26), channel_id=1, source_target_pairs={{0,8},{4,12},{8,0},{12,4},{1,9},{5,13},{9,1},{13,5},{2,10},{6,14},... | collective-permute-start | bytes 221192 | tf_op jit(solution)/shard_map/ppermute | solution.py:60
  52.9 12.9 %collective-permute-start.12 = (bf16[9,64,64]{1,2,0:T(8,128)(2,1)S(1)}, bf16[9,64,64]{1,2,0:T(8,128)(2,1)S(1)}, u32[]{:S(2)}, u32[]{:S(2)}) collective-permute-start(bf16[9,64,64]{1,2,0:T(8,128)(2,1)S(1)} %get-tuple-element.25), channel_id=1, source_target_pairs={{0,12},{4,0},{8,4},{12,8},{1,13},{5,1},{9,5},{13,9},{2,14},{6,2},{... | collective-permute-start | bytes 221192 | tf_op jit(solution)/shard_map/ppermute | solution.py:60
